TPU v7x, 512 devices: a whole 4x8x8 slice. The times are simulated.
512 devices in a mesh: col: 64 (over z_lo, y, core), row: 8 (over x, z_hi).
Axes of the slice: x: 4, y: 8, z: 8 (z_hi: 2, z_lo: 4; z = z_hi * 4 + z_lo), core: 2. Of those that a mesh axis runs over, the one named last changes fastest.
Arguments:
- image: bfloat16 [96, 64, 8192], P(None, 'row', 'col'), may hold values from -6 to 6
- cotangent: bfloat16 [96, 64, 8192], P(None, 'row', 'col'), may hold values from -6 to 6
- dw_kernel: float32 [96, 7, 7], replicated, may hold values from -0.875 to 0.875
- dw_bias: float32 [96], replicated, may hold values from -3 to 3
- ln_gain: float32 [96], replicated, may hold values from 0.1 to 1.9
- ln_bias: float32 [96], replicated, may hold values from -3 to 3
- w_in: bfloat16 [96, 384], replicated, may hold values from -0.625 to 0.625
- b_in: float32 [384], replicated, may hold values from -3 to 3
- w_out: bfloat16 [384, 96], replicated, may hold values from -0.3125 to 0.3125
- layer_scale: float32 [96], replicated, may hold values from 0.5 to 2
Outputs:
- block_out: bfloat16 [96, 64, 8192], P(None, 'row', 'col')
- image_grad: bfloat16 [96, 64, 8192], P(None, 'row', 'col')
- kernel_grad: float32 [96, 7, 7], replicated
- dw_bias_grad: float32 [96], replicated
- gain_grad: float32 [96], replicated
- ln_bias_grad: float32 [96], replicated
- w_in_grad: float32 [96, 384], replicated
- b_in_grad: float32 [384], replicated
- w_out_grad: float32 [384, 96], replicated
- scale_grad: float32 [96], replicated
All inputs are finite; a program needn't handle non-finite values.
Results may differ from a plain program's by a relative error of at most 0.0065.
Values may be sent and summed in bfloat16 or wider, within the bound.
No kernel may reach another device: no remote copies, remote signals or barrier semaphores. Data moves between devices by JAX's collectives and lax.ppermute only.
A program may use at most 64 MiB of HBM per device.

v0:
```python
import math

import jax
import jax.numpy as jnp
from jax import lax
from jax.sharding import PartitionSpec as P


def padded_2(block, sides, width):
    for axis, dim in sides:
        count = lax.axis_size(axis)
        forward = [(i, i + 1) for i in range(count - 1)]
        backward = [(target, source) for source, target in forward]
        low = lax.ppermute(
            lax.slice_in_dim(block, block.shape[dim] - width, None, axis=dim), axis, forward
        )
        high = lax.ppermute(lax.slice_in_dim(block, 0, width, axis=dim), axis, backward)
        block = jnp.concatenate([low, block, high], axis=dim)
    return block


def from_behind(value, axis, steps):
    count = lax.axis_size(axis)
    initial, last = (max(0, -steps), min(count, count - steps))
    return lax.ppermute(value, axis, [(source, source + steps) for source in range(initial, last)])


def conv_seven(padded, kernel):
    height = padded.shape[1] - 6
    breadth = padded.shape[2] - 6
    summed = jnp.zeros((padded.shape[0], height, breadth), jnp.float32)
    for row_step in range(7):
        for col_step in range(7):
            summed = (
                summed
                + kernel[:, row_step, col_step][:, None, None]
                * padded[:, row_step : row_step + height, col_step : col_step + breadth]
            )
    return summed


def kernel_terms(conv_grad, padded):
    height, breadth = (conv_grad.shape[1], conv_grad.shape[2])
    pieces = []
    for row_step in range(7):
        for col_step in range(7):
            pieces.append(
                jnp.sum(
                    conv_grad
                    * padded[:, row_step : row_step + height, col_step : col_step + breadth],
                    axis=(1, 2),
                )
            )
    return jnp.stack(pieces, axis=1).reshape(conv_grad.shape[0], 7, 7)


def product(form, left, right):
    return jnp.einsum(form, left, right, preferred_element_type=jnp.float32)


def mixing(conv_flat, image_flat, cotan_flat, ln_gain, ln_bias, w_in, b_in, w_out, layer_scale):
    average = jnp.mean(conv_flat, axis=0, keepdims=True)
    centred = conv_flat - average
    spread = jnp.mean(centred * centred, axis=0, keepdims=True)
    inverse = lax.rsqrt(spread + 1e-06)
    normed = centred * inverse
    ln_out = (normed * ln_gain[:, None] + ln_bias[:, None]).astype(jnp.bfloat16)
    pre_act = product("ch,cp->hp", w_in, ln_out) + b_in[:, None]
    act_out, gelu_pull = jax.vjp(jax.nn.gelu, pre_act)
    activ = act_out.astype(jnp.bfloat16)
    branch = product("hc,hp->cp", w_out, activ)
    scale_col = layer_scale[:, None]
    block_out = (image_flat.astype(jnp.float32) + scale_col * branch).astype(jnp.bfloat16)
    upstream = cotan_flat.astype(jnp.float32)
    scale_sum = jnp.sum(upstream * branch, axis=1)
    branch_grad = (scale_col * upstream).astype(jnp.bfloat16)
    w_out_sum = product("hp,cp->hc", activ, branch_grad)
    act_grad = product("hc,cp->hp", w_out, branch_grad)
    pre_grad = gelu_pull(act_grad)[0].astype(jnp.bfloat16)
    b_in_sum = jnp.sum(pre_grad.astype(jnp.float32), axis=1)
    w_in_sum = product("cp,hp->ch", ln_out, pre_grad)
    ln_grad = product("ch,hp->cp", w_in, pre_grad)
    gain_sum = jnp.sum(ln_grad * normed, axis=1)
    shift_sum = jnp.sum(ln_grad, axis=1)
    normed_grad = ln_grad * ln_gain[:, None]
    conv_grad = inverse * (
        normed_grad
        - jnp.mean(normed_grad, axis=0, keepdims=True)
        - normed * jnp.mean(normed_grad * normed, axis=0, keepdims=True)
    )
    return (block_out, conv_grad, (gain_sum, shift_sum, w_in_sum, b_in_sum, w_out_sum, scale_sum))


def local(image, cotangent, dw_kernel, dw_bias, ln_gain, ln_bias, w_in, b_in, w_out, layer_scale):
    channels, height, breadth = image.shape
    pixels = height * breadth
    padded = padded_2(image, (("col", 2), ("row", 1)), 3)
    conv_out = conv_seven(padded, dw_kernel) + dw_bias[:, None, None]
    block_flat, grad_flat, sums = mixing(
        conv_out.reshape(channels, pixels),
        image.reshape(channels, pixels),
        cotangent.reshape(channels, pixels),
        ln_gain,
        ln_bias,
        w_in,
        b_in,
        w_out,
        layer_scale,
    )
    gain_sum, shift_sum, w_in_sum, b_in_sum, w_out_sum, scale_sum = sums
    block_out = block_flat.reshape(channels, height, breadth)
    conv_grad = grad_flat.reshape(channels, height, breadth)
    flipped = dw_kernel[:, ::-1, ::-1]
    extended = conv_seven(jnp.pad(conv_grad, ((0, 0), (6, 6), (6, 6))), flipped)
    from_above = from_behind(extended[:, height + 3 :, :].astype(jnp.bfloat16), "row", 1).astype(
        jnp.float32
    )
    from_below = from_behind(extended[:, :3, :].astype(jnp.bfloat16), "row", -1).astype(jnp.float32)
    middle = extended[:, 3 : height + 3, :]
    middle = middle.at[:, :3, :].add(from_above)
    middle = middle.at[:, height - 3 :, :].add(from_below)
    from_left = from_behind(middle[:, :, breadth + 3 :], "col", 1)
    from_right = from_behind(middle[:, :, :3], "col", -1)
    back = middle[:, :, 3 : breadth + 3]
    back = back.at[:, :, :3].add(from_left)
    back = back.at[:, :, breadth - 3 :].add(from_right)
    image_grad = (cotangent.astype(jnp.float32) + back).astype(jnp.bfloat16)
    kernel_sum = kernel_terms(conv_grad, padded)
    bias_sum = jnp.sum(conv_grad, axis=(1, 2))
    kernel_sum, bias_sum, gain_sum, shift_sum, w_in_sum, b_in_sum, w_out_sum, scale_sum = lax.psum(
        (kernel_sum, bias_sum, gain_sum, shift_sum, w_in_sum, b_in_sum, w_out_sum, scale_sum),
        ("col", "row"),
    )
    factor = 1.0 / math.sqrt(height * lax.axis_size("row") * breadth * lax.axis_size("col"))
    return (
        block_out,
        image_grad,
        factor * kernel_sum,
        factor * bias_sum,
        factor * gain_sum,
        factor * shift_sum,
        factor * w_in_sum,
        factor * b_in_sum,
        factor * w_out_sum,
        factor * scale_sum,
    )


def solution(mesh):
    in_specs = (
        P(None, "row", "col"),
        P(None, "row", "col"),
        P(),
        P(),
        P(),
        P(),
        P(),
        P(),
        P(),
        P(),
    )
    out_specs = (
        P(None, "row", "col"),
        P(None, "row", "col"),
        P(),
        P(),
        P(),
        P(),
        P(),
        P(),
        P(),
        P(),
    )
    return jax.shard_map(local, mesh=mesh, in_specs=in_specs, out_specs=out_specs, check_vma=False)
```

profile of v0, /device:TPU:57, one launch (start us, length us, event | category | flops | bytes accessed | tf_op | source)
XLA Modules:
  0.0 489.5 jit_solution(10161626249035542997)
XLA Ops:
  7.2 1.1 copy.20
  8.4 3.8 collective-permute-start
  12.2 1.9 collective-permute-start.1
  14.1 1.0 slice_bitcast_fusion.48
  15.1 1.0 slice_bitcast_fusion.47
  16.1 3.1 collective-permute-done.1
  19.3 9.7 %collective-permute-start.2 = (bf16[96,3,134]{0,2,1:T(8,128)(2,1)S(1)}, bf16[96,3,134]{0,2,1:T(8,128)(2,1)S(1)}, u32[]{:S(2)}, u32[]{:S(2)}) collective-permute-start(bf16[96,3,134]{0,2,1:T(8,128)(2,1)S(1)} %get-tuple-element.142), channel_id=1, source_target_pairs={{0,1},{1,2},{2,3},{3,4},{4,5},{5,6},{6,7},{8,9},{9,10},{10,11},{11... | collective-permute-start | bytes 231560 | tf_op jit(solution)/shard_map/ppermute | solution.py:14
  29.1 1.3 collective-permute-start.3
  30.4 0.9 slice_bitcast_fusion.46
  31.3 1.0 convert.8
  32.2 0.9 copy.77
  33.2 7.2 %collective-permute-done.3 = bf16[96,3,134]{0,2,1:T(8,128)(2,1)S(1)} collective-permute-done((bf16[96,3,134]{0,2,1:T(8,128)(2,1)S(1)}, bf16[96,3,134]{0,2,1:T(8,128)(2,1)S(1)}, u32[]{:S(2)}, u32[]{:S(2)}) %collective-permute-start.3) | collective-permute-done | bytes 77216 | tf_op jit(solution)/shard_map/ppermute | solution.py:17
  40.6 4.3 fusion.223
  45.5 1.7 fusion.107
  47.2 2.0 convert_reduce_fusion
  49.2 1.0 fusion.220
  50.2 0.4 fusion.208
  51.2 1.9 fusion.203
  53.0 1.9 fusion.153
  54.9 0.8 fusion.135
  55.9 23.9 %fusion.221 = (bf16[96,14,134]{2,1,0:T(8,128)(2,1)}, f32[96,14,134]{2,1,0:T(8,128)S(1)}) fusion(f32[96]{0:T(128)S(1)} %get-tuple-element.146, f32[96]{0:T(128)S(1)} %get-tuple-element.165, f32[96]{0:T(128)S(1)} %get-tuple-element.184, f32[96]{0:T(128)S(1)} %get-tuple-element.192, f32[96]{0:T(128)S(1)} %get-tuple-element.191, f32[96]{0:T(128)S(1)} %get-tuple-element.190, ...), kind=kLoop, calls=%fused_computation.460 | loop fusion | flops 17649408 | bytes 1492608 | tf_op jit(solution)/shard_map/convert.3
  80.1 1.0 fusion.215
  81.1 1.0 fusion.185
  82.7 1.9 fusion.206
  84.5 98.8 %all-reduce.1 = (f32[96,7,7]{0,2,1:T(8,128)S(1)}, f32[96]{0:T(128)S(1)}, f32[96]{0:T(128)S(1)}, f32[96]{0:T(128)S(1)}, f32[384]{0:T(512)S(1)}, /*index=5*/f32[96]{0:T(128)S(1)}) all-reduce(f32[96,7,7]{0,2,1:T(8,128)S(1)} %reshape.203, f32[96]{0:T(128)S(1)} %get-tuple-element.101, ...), channel_id=1, replica_groups=mesh['col'=64,'row'=8] {'col','row'}, use_global_device_ids=true, to_apply=%region_53.54 | all-reduce | flops 5472 | bytes 43776 | tf_op jit(solution)/shard_map/psum | solution.py:130
  183.3 0.6 broadcast_multiply_fusion.2
  183.9 0.6 broadcast_multiply_fusion.6
  184.5 0.5 broadcast_multiply_fusion.10
  185.0 0.5 broadcast_multiply_fusion.7
  185.7 2.9 collective-permute-start.4
  188.7 0.5 broadcast_multiply_fusion.8
  189.3 1.3 collective-permute-start.5
  190.6 4.9 %collective-permute-done.4 = bf16[96,3,134]{2,1,0:T(4,128)(2,1)S(1)} collective-permute-done((bf16[96,3,134]{2,1,0:T(4,128)(2,1)S(1)}, bf16[96,3,134]{2,1,0:T(4,128)(2,1)S(1)}, u32[]{:S(2)}, u32[]{:S(2)}) %collective-permute-start.4) | collective-permute-done | bytes 77216 | tf_op jit(solution)/shard_map/ppermute | solution.py:25
  195.6 2.6 scatter-add.14
  198.2 7.7 %collective-permute-done.5 = bf16[96,3,134]{2,1,0:T(4,128)(2,1)S(1)} collective-permute-done((bf16[96,3,134]{2,1,0:T(4,128)(2,1)S(1)}, bf16[96,3,134]{2,1,0:T(4,128)(2,1)S(1)}, u32[]{:S(2)}, u32[]{:S(2)}) %collective-permute-start.5) | collective-permute-done | bytes 77216 | tf_op jit(solution)/shard_map/ppermute | solution.py:25
  206.0 2.6 scatter-add.15
  208.7 8.0 %collective-permute-start.6 = (f32[96,8,3]{2,1,0:T(8,128)S(1)}, f32[96,8,3]{2,1,0:T(8,128)S(1)}, u32[]{:S(2)}, u32[]{:S(2)}) collective-permute-start(f32[96,8,3]{2,1,0:T(8,128)S(1)} %get-tuple-element.135), channel_id=1, source_target_pairs={{0,8},{8,16},{16,24},{24,32},{32,40},{40,48},{48,56},{56,64},{64,7... | collective-permute-start | bytes 27656 | tf_op jit(solution)/shard_map/ppermute | solution.py:25
  216.8 0.5 broadcast_multiply_fusion.9
  217.3 0.7 copy.79
  218.2 1.9 collective-permute-start.7
  220.1 1.4 collective-permute-done.6
  221.7 6.1 %scatter-add.16 = f32[96,8,128]{2,1,0:T(8,128)S(1)} dynamic-update-slice(f32[96,8,128]{2,1,0:T(8,128)S(1)} %slice.979, f32[96,8,3]{2,1,0:T(8,128)S(1)} %slice_add_fusion.1, s32[]{:T(128)} %constant.134.clone.1, s32[]{:T(128)} %constant.134.clone.1, s32[]{:T(128)} %constant.134.clone.1) | dynamic-update-slice | bytes 18436 | tf_op jit(solution)/shard_map/scatter-add | solution.py:125
  227.7 1.7 collective-permute-done.7
  229.6 18.6 %scatter-add.19 = f32[96,8,128]{2,1,0:T(8,128)S(1)} dynamic-update-slice(f32[96,8,128]{2,1,0:T(8,128)S(1)} %scatter-add.16, f32[96,8,3]{2,1,0:T(8,128)S(1)} %slice_add_fusion, s32[]{:T(128)} %constant.134.clone.1, s32[]{:T(128)} %constant.134.clone.1, s32[]{:T(128)} %constant.136.clone.1) | dynamic-update-slice | bytes 18436 | tf_op jit(solution)/shard_map/scatter-add | solution.py:126
  248.2 0.7 add_convert_fusion
  248.9 230.5 %all-reduce.5.cloned.1.call-done = (f32[96,384]{1,0:T(8,128)}, f32[384,96]{0,1:T(8,128)}) async-done(((f32[96,384]{1,0:T(8,128)}, f32[384,96]{0,1:T(8,128)}), (f32[96,384]{1,0:T(8,128)}, f32[384,96]{0,1:T(8,128)})) %all-reduce.5.cloned.1.call-update) | async-done | bytes 294928 | tf_op jit(solution)/shard_map/psum | solution.py:130
  479.5 1.6 broadcast_multiply_fusion
  481.0 1.6 broadcast_multiply_fusion.1
  (114 shorter events, 3.3 us)
Async XLA Ops:
  7.2 38.3 %copy-start = (bf16[96,384]{1,0:T(8,128)(2,1)S(1)}, bf16[96,384]{1,0:T(8,128)(2,1)}, u32[]{:S(2)}) copy-start(bf16[96,384]{1,0:T(8,128)(2,1)} %param.24) | copy-start | bytes 221188
  7.2 472.3 %all-reduce.5.cloned.1.call-start = ((), (), s32[]{:S(2)}) async-start(), calls=%async_computation | async-start | bytes 589824 | tf_op jit(solution)/shard_map/psum | solution.py:130
  8.4 32.2 %copy-start.41 = (f32[96]{0:T(128)S(1)}, f32[96]{0:T(128)}, u32[]{:S(2)}) copy-start(f32[96]{0:T(128)} %param.21) | copy-start | bytes 1156
  8.4 7.7 %collective-permute-start = (bf16[96,8,3]{0,2,1:T(4,128)(2,1)S(1)}, bf16[96,8,3]{0,2,1:T(4,128)(2,1)S(1)}, u32[]{:S(2)}, u32[]{:S(2)}) collective-permute-start(bf16[96,8,3]{0,2,1:T(4,128)(2,1)S(1)} %get-tuple-element.144), channel_id=1, source_target_pairs={{0,8},{8,16},{16,24},{24,32},{32,40},{40,48},{48,56},{56,64},{64,7... | collective-permute-start | bytes 13832 | tf_op jit(solution)/shard_map/ppermute | solution.py:14
  12.2 7.1 %collective-permute-start.1 = (bf16[96,8,3]{0,2,1:T(4,128)(2,1)S(1)}, bf16[96,8,3]{0,2,1:T(4,128)(2,1)S(1)}, u32[]{:S(2)}, u32[]{:S(2)}) collective-permute-start(bf16[96,8,3]{0,2,1:T(4,128)(2,1)S(1)} %get-tuple-element.145), channel_id=1, source_target_pairs={{8,0},{16,8},{24,16},{32,24},{40,32},{48,40},{56,48},{64,56},{72,6... | collective-permute-start | bytes 13832 | tf_op jit(solution)/shard_map/ppermute | solution.py:17
  19.3 13.8 %collective-permute-start.2 = (bf16[96,3,134]{0,2,1:T(8,128)(2,1)S(1)}, bf16[96,3,134]{0,2,1:T(8,128)(2,1)S(1)}, u32[]{:S(2)}, u32[]{:S(2)}) collective-permute-start(bf16[96,3,134]{0,2,1:T(8,128)(2,1)S(1)} %get-tuple-element.142), channel_id=1, source_target_pairs={{0,1},{1,2},{2,3},{3,4},{4,5},{5,6},{6,7},{8,9},{9,10},{10,11},{11... | collective-permute-start | bytes 231560 | tf_op jit(solution)/shard_map/ppermute | solution.py:14
  29.1 11.3 %collective-permute-start.3 = (bf16[96,3,134]{0,2,1:T(8,128)(2,1)S(1)}, bf16[96,3,134]{0,2,1:T(8,128)(2,1)S(1)}, u32[]{:S(2)}, u32[]{:S(2)}) collective-permute-start(bf16[96,3,134]{0,2,1:T(8,128)(2,1)S(1)} %get-tuple-element.143), channel_id=1, source_target_pairs={{1,0},{2,1},{3,2},{4,3},{5,4},{6,5},{7,6},{9,8},{10,9},{11,10},{12... | collective-permute-start | bytes 231560 | tf_op jit(solution)/shard_map/ppermute | solution.py:17
  32.2 15.0 %copy-start.3 = (f32[12,8,8,128]{3,2,1,0:T(8,128)}, f32[12,8,8,128]{3,2,1,0:T(8,128)S(1)}, u32[]{:S(2)}) copy-start(f32[12,8,8,128]{3,2,1,0:T(8,128)S(1)} %convert.8) | copy-start | bytes 1179652
  40.5 4.9 %copy-start.9 = (f32[96]{0:T(128)S(1)}, f32[96]{0:T(128)}, u32[]{:S(2)}) copy-start(f32[96]{0:T(128)} %param.22) | copy-start | bytes 1156
  40.6 4.9 %copy-start.42 = (f32[96]{0:T(128)S(1)}, f32[96]{0:T(128)}, u32[]{:S(2)}) copy-start(f32[96]{0:T(128)} %param.23) | copy-start | bytes 1156
  40.6 4.9 %copy-start.43 = (f32[384]{0:T(512)S(1)}, f32[384]{0:T(512)}, u32[]{:S(2)}) copy-start(f32[384]{0:T(512)} %param.25) | copy-start | bytes 4612
  55.9 24.2 %copy-start.4 = (f32[12,8,8,128]{3,2,1,0:T(8,128)S(1)}, f32[12,8,8,128]{3,2,1,0:T(8,128)}, u32[]{:S(2)}) copy-start(f32[12,8,8,128]{3,2,1,0:T(8,128)} %copy-done.3) | copy-start | bytes 1179652
  55.9 24.2 %copy-start.5 = (bf16[384,1024]{0,1:T(8,128)(2,1)S(1)}, bf16[384,1024]{0,1:T(8,128)(2,1)}, u32[]{:S(2)}) copy-start(bf16[384,1024]{0,1:T(8,128)(2,1)} %get-tuple-element.197) | copy-start | bytes 2359300
  79.8 2.3 copy-start.12
  79.8 2.3 copy-start.13
  79.8 2.3 copy-start.14
  79.8 2.3 copy-start.15
  79.9 2.3 copy-start.16
  79.9 2.3 copy-start.17
  79.9 2.3 copy-start.18
  79.9 2.3 copy-start.19
  79.9 2.3 copy-start.20
  79.9 2.3 copy-start.21
  79.9 2.3 copy-start.22
  79.9 2.3 copy-start.23
  79.9 2.3 copy-start.24
  80.0 2.3 copy-start.25
  80.0 2.3 copy-start.26
  80.0 2.3 copy-start.27
  80.0 2.3 copy-start.28
  80.0 2.3 copy-start.29
  80.0 2.3 copy-start.30
  80.0 2.3 copy-start.31
  80.0 2.3 copy-start.32
  80.0 2.3 copy-start.33
  80.0 2.3 copy-start.34
  80.1 2.3 copy-start.35
  80.1 2.3 copy-start.36
  80.1 2.3 copy-start.37
  80.1 2.3 copy-start.38
  80.1 2.3 copy-start.39
  82.1 2.4 copy-start.40
  82.1 103.4 %copy-start.6 = (bf16[96,14,134]{2,1,0:T(8,128)(2,1)S(1)}, bf16[96,14,134]{2,1,0:T(8,128)(2,1)}, u32[]{:S(2)}) copy-start(bf16[96,14,134]{2,1,0:T(8,128)(2,1)} %get-tuple-element.129) | copy-start | bytes 1080580
  185.7 9.8 %collective-permute-start.4 = (bf16[96,3,134]{2,1,0:T(4,128)(2,1)S(1)}, bf16[96,3,134]{2,1,0:T(4,128)(2,1)S(1)}, u32[]{:S(2)}, u32[]{:S(2)}) collective-permute-start(bf16[96,3,134]{2,1,0:T(4,128)(2,1)S(1)} %get-tuple-element.137), channel_id=1, source_target_pairs={{0,1},{1,2},{2,3},{3,4},{4,5},{5,6},{6,7},{8,9},{9,10},{10,11},{11... | collective-permute-start | bytes 231560 | tf_op jit(solution)/shard_map/ppermute | solution.py:25
  189.3 16.6 %collective-permute-start.5 = (bf16[96,3,134]{2,1,0:T(4,128)(2,1)S(1)}, bf16[96,3,134]{2,1,0:T(4,128)(2,1)S(1)}, u32[]{:S(2)}, u32[]{:S(2)}) collective-permute-start(bf16[96,3,134]{2,1,0:T(4,128)(2,1)S(1)} %get-tuple-element.136), channel_id=1, source_target_pairs={{1,0},{2,1},{3,2},{4,3},{5,4},{6,5},{7,6},{9,8},{10,9},{11,10},{12... | collective-permute-start | bytes 231560 | tf_op jit(solution)/shard_map/ppermute | solution.py:25
  208.7 12.7 %collective-permute-start.6 = (f32[96,8,3]{2,1,0:T(8,128)S(1)}, f32[96,8,3]{2,1,0:T(8,128)S(1)}, u32[]{:S(2)}, u32[]{:S(2)}) collective-permute-start(f32[96,8,3]{2,1,0:T(8,128)S(1)} %get-tuple-element.135), channel_id=1, source_target_pairs={{0,8},{8,16},{16,24},{24,32},{32,40},{40,48},{48,56},{56,64},{64,7... | collective-permute-start | bytes 27656 | tf_op jit(solution)/shard_map/ppermute | solution.py:25
  218.2 11.3 %collective-permute-start.7 = (f32[96,8,3]{2,1,0:T(8,128)S(1)}, f32[96,8,3]{2,1,0:T(8,128)S(1)}, u32[]{:S(2)}, u32[]{:S(2)}) collective-permute-start(f32[96,8,3]{2,1,0:T(8,128)S(1)} %get-tuple-element.134), channel_id=1, source_target_pairs={{8,0},{16,8},{24,16},{32,24},{40,32},{48,40},{56,48},{64,56},{72,6... | collective-permute-start | bytes 27656 | tf_op jit(solution)/shard_map/ppermute | solution.py:25
  221.6 26.6 %copy-start.7 = (bf16[96,8,128]{2,1,0:T(8,128)(2,1)S(1)}, bf16[96,8,128]{2,1,0:T(8,128)(2,1)}, u32[]{:S(2)}) copy-start(bf16[96,8,128]{2,1,0:T(8,128)(2,1)} %param.19) | copy-start | bytes 589828
  (5 other events, 8.9 us)
Sparse Core Ops, SparseCore 0:
  218.1 261.2 all-reduce.4
where the time goes:
time: 493 us; the launch traced here: 489 us
  waiting for transfers between devices  257 us (52%)
  blocking collectives  98.8 us (20%)
  other arithmetic  43.3 us (9%)
  local copies, waits for them, and re-layouts  37.1 us (8%)
  starting transfers between devices  30.9 us (6%)
  between operations  14.9 us (3%)
  matrix products  7.91 us (2%)
    psum x1, waiting for transfers between devices, local(): lax.psum((kernel_sum, bias_sum, gain_sum, shift_sum, w_in_sum, b_in_sum,...  231 us
    psum x1, blocking collectives, local(): lax.psum((kernel_sum, bias_sum, gain_sum, shift_sum, w_in_sum, b_in_sum,...  98.8 us
    another operation x1, other arithmetic  23.9 us
    scatter-add x1, local copies, waits for them, and re-layouts, local(): back = back.at[:, :, breadth - 3:].add(from_right)  18.6 us
    ppermute x4, waiting for transfers between devices, from_behind(): lax.ppermute(value, axis, [(source, source + steps) for source in range(i...  15.6 us
    ppermute x4, starting transfers between devices, from_behind(): lax.ppermute(value, axis, [(source, source + steps) for source in range(i...  14.2 us
    ppermute x2, starting transfers between devices, padded_2(): lax.ppermute(lax.slice_in_dim(block, block.shape[dim] - width, None, axis...  13.5 us
    ppermute x2, waiting for transfers between devices, padded_2(): lax.ppermute(lax.slice_in_dim(block, 0, width, axis=dim), axis, backward)  10.4 us
  transfers between devices with their start and end apart: 9, of which 7 were waited for; matrix products, arithmetic and copies ran while one was open for 7% of the time, Pallas kernels for 0%

commit v1 on v0

--- a/solution.py
+++ b/solution.py
@@ -52,6 +52,24 @@
                 )
             )
     return jnp.stack(pieces, axis=1).reshape(conv_grad.shape[0], 7, 7)
+
+
+def butterfly_sum(parts):
+    shapes = [p.shape for p in parts]
+    flat = jnp.concatenate([p.reshape(-1) for p in parts])
+    for axis in ("col", "row"):
+        count = lax.axis_size(axis)
+        bit = 1
+        while bit < count:
+            pairs = [(i, i ^ bit) for i in range(count)]
+            flat = flat + lax.ppermute(flat, axis, pairs)
+            bit *= 2
+    out, start = [], 0
+    for shape in shapes:
+        size = math.prod(shape)
+        out.append(flat[start : start + size].reshape(shape))
+        start += size
+    return tuple(out)
 
 
 def product(form, left, right):
@@ -117,19 +135,24 @@
     )
     from_below = from_behind(extended[:, :3, :].astype(jnp.bfloat16), "row", -1).astype(jnp.float32)
     middle = extended[:, 3 : height + 3, :]
-    middle = middle.at[:, :3, :].add(from_above)
-    middle = middle.at[:, height - 3 :, :].add(from_below)
+    middle = (
+        middle
+        + jnp.pad(from_above, ((0, 0), (0, height - 3), (0, 0)))
+        + jnp.pad(from_below, ((0, 0), (height - 3, 0), (0, 0)))
+    )
     from_left = from_behind(middle[:, :, breadth + 3 :], "col", 1)
     from_right = from_behind(middle[:, :, :3], "col", -1)
     back = middle[:, :, 3 : breadth + 3]
-    back = back.at[:, :, :3].add(from_left)
-    back = back.at[:, :, breadth - 3 :].add(from_right)
+    back = (
+        back
+        + jnp.pad(from_left, ((0, 0), (0, 0), (0, breadth - 3)))
+        + jnp.pad(from_right, ((0, 0), (0, 0), (breadth - 3, 0)))
+    )
     image_grad = (cotangent.astype(jnp.float32) + back).astype(jnp.bfloat16)
     kernel_sum = kernel_terms(conv_grad, padded)
     bias_sum = jnp.sum(conv_grad, axis=(1, 2))
-    kernel_sum, bias_sum, gain_sum, shift_sum, w_in_sum, b_in_sum, w_out_sum, scale_sum = lax.psum(
-        (kernel_sum, bias_sum, gain_sum, shift_sum, w_in_sum, b_in_sum, w_out_sum, scale_sum),
-        ("col", "row"),
+    kernel_sum, bias_sum, gain_sum, shift_sum, w_in_sum, b_in_sum, w_out_sum, scale_sum = butterfly_sum(
+        (kernel_sum, bias_sum, gain_sum, shift_sum, w_in_sum, b_in_sum, w_out_sum, scale_sum)
     )
     factor = 1.0 / math.sqrt(height * lax.axis_size("row") * breadth * lax.axis_size("col"))
     return (

time: 493 us -> 218 us (0.44)
  waiting for transfers between devices: 257 us -> 90.5 us
  blocking collectives: 98.8 us -> 0 us
  starting transfers between devices: 30.9 us -> 65.7 us
  local copies, waits for them, and re-layouts: 37.1 us -> 11.7 us
  between operations: 14.9 us -> 3 us
    psum x1 -> x0, waiting for transfers between devices: 231 us -> none  [local(): lax.psum((kernel_sum, bias_sum, gain_sum, shift_sum, w_in_sum, b_in_sum,...]
    psum x1 -> x0, blocking collectives: 98.8 us -> none  [local(): lax.psum((kernel_sum, bias_sum, gain_sum, shift_sum, w_in_sum, b_in_sum,...]
    ppermute x0 -> x9, waiting for transfers between devices: none -> 65.5 us  [butterfly_sum(): flat = flat + lax.ppermute(flat, axis, pairs)]
    ppermute x0 -> x9, starting transfers between devices: none -> 38.9 us  [butterfly_sum(): flat = flat + lax.ppermute(flat, axis, pairs)]
    scatter-add x4 -> x0, local copies, waits for them, and re-layouts: 29.8 us -> none  [the longest x1 18.6 us: local(): back = back.at[:, :, breadth - 3:].add(from_right)]
  transfers between devices with their start and end apart: 9 -> 17, of which waited for: 7 -> 13; matrix products, arithmetic and copies ran while one was open for 7% -> 14% of each run, Pallas kernels for 0% -> 0%
where the time goes in v1:
time: 218 us; the launch traced here: 216 us
  waiting for transfers between devices  90.5 us (42%)
  starting transfers between devices  65.7 us (30%)
  other arithmetic  38.5 us (18%)
  local copies, waits for them, and re-layouts  11.7 us (5%)
  matrix products  6.46 us (3%)
  between operations  3 us (1%)
    ppermute x9, waiting for transfers between devices, butterfly_sum(): flat = flat + lax.ppermute(flat, axis, pairs)  65.5 us
    ppermute x9, starting transfers between devices, butterfly_sum(): flat = flat + lax.ppermute(flat, axis, pairs)  38.9 us
    another operation x1, other arithmetic  23.4 us
    ppermute x4, waiting for transfers between devices, from_behind(): lax.ppermute(value, axis, [(source, source + steps) for source in range(i...  13.9 us
    ppermute x2, starting transfers between devices, padded_2(): lax.ppermute(lax.slice_in_dim(block, block.shape[dim] - width, None, axis...  13.5 us
    ppermute x2, waiting for transfers between devices, padded_2(): lax.ppermute(lax.slice_in_dim(block, 0, width, axis=dim), axis, backward)  10.5 us
    ppermute x4, starting transfers between devices, from_behind(): lax.ppermute(value, axis, [(source, source + steps) for source in range(i...  10.1 us
    dot_general x6, matrix products, product(): return jnp.einsum(form, left, right, preferred_element_type=jnp.float32)  6.46 us
  transfers between devices with their start and end apart: 17, of which 13 were waited for; matrix products, arithmetic and copies ran while one was open for 14% of the time, Pallas kernels for 0%

profile of v1, /device:TPU:57, one launch (start us, length us, event | category | flops | bytes accessed | tf_op | source)
XLA Modules:
  0.0 215.9 jit_solution(7469816301686327922)
XLA Ops:
  0.7 1.2 copy.24
  1.8 3.8 %collective-permute-start = (bf16[96,8,3]{0,2,1:T(4,128)(2,1)S(1)}, bf16[96,8,3]{0,2,1:T(4,128)(2,1)S(1)}, u32[]{:S(2)}, u32[]{:S(2)}) collective-permute-start(bf16[96,8,3]{0,2,1:T(4,128)(2,1)S(1)} %get-tuple-element.114), channel_id=1, source_target_pairs={{0,8},{8,16},{16,24},{24,32},{32,40},{40,48},{48,56},{56,64},{64,7... | collective-permute-start | bytes 13832 | tf_op jit(solution)/shard_map/ppermute | solution.py:14
  5.6 1.9 collective-permute-start.1
  7.5 1.0 slice_bitcast_fusion.48
  8.6 1.0 slice_bitcast_fusion.47
  9.8 2.9 %collective-permute-done.1 = bf16[96,8,3]{0,2,1:T(4,128)(2,1)S(1)} collective-permute-done((bf16[96,8,3]{0,2,1:T(4,128)(2,1)S(1)}, bf16[96,8,3]{0,2,1:T(4,128)(2,1)S(1)}, u32[]{:S(2)}, u32[]{:S(2)}) %collective-permute-start.1) | collective-permute-done | bytes 4640 | tf_op jit(solution)/shard_map/ppermute | solution.py:17
  12.8 9.7 %collective-permute-start.2 = (bf16[96,3,134]{0,2,1:T(8,128)(2,1)S(1)}, bf16[96,3,134]{0,2,1:T(8,128)(2,1)S(1)}, u32[]{:S(2)}, u32[]{:S(2)}) collective-permute-start(bf16[96,3,134]{0,2,1:T(8,128)(2,1)S(1)} %get-tuple-element.112), channel_id=1, source_target_pairs={{0,1},{1,2},{2,3},{3,4},{4,5},{5,6},{6,7},{8,9},{9,10},{10,11},{11... | collective-permute-start | bytes 231560 | tf_op jit(solution)/shard_map/ppermute | solution.py:14
  22.5 1.3 collective-permute-start.3
  23.8 0.9 slice_bitcast_fusion.46
  24.9 1.0 convert.12
  26.5 7.7 %collective-permute-done.3 = bf16[96,3,134]{0,2,1:T(8,128)(2,1)S(1)} collective-permute-done((bf16[96,3,134]{0,2,1:T(8,128)(2,1)S(1)}, bf16[96,3,134]{0,2,1:T(8,128)(2,1)S(1)}, u32[]{:S(2)}, u32[]{:S(2)}) %collective-permute-start.3) | collective-permute-done | bytes 77216 | tf_op jit(solution)/shard_map/ppermute | solution.py:17
  34.3 4.3 %fusion.227 = (f32[8,128]{1,0:T(8,128)S(1)}, f32[96,8,128]{0,2,1:T(8,128)S(1)}) fusion(f32[96]{0:T(128)S(1)} %copy-done.126, bf16[96,11,134]{0,2,1:T(8,128)(2,1)S(1)} %get-tuple-element.111, f32[96]{0:T(128)S(1)} %get-tuple-element.163, f32[96]{0:T(128)S(1)} %get-tuple-element.164, f32[96]{0:T(128)S(1)} %get-tuple-element.117, ...), kind=kLoop, calls=%fused_computation.462 | loop fusion | flops 16317440 | bytes 8879872 | tf_op jit(solution)/shard_map/reduce_sum | solution.py:80
  39.7 1.7 fusion.107
  41.4 2.0 convert_reduce_fusion
  44.1 0.9 fusion.211
  45.3 1.9 fusion.204
  47.1 1.9 fusion.154
  49.0 0.8 fusion.136
  50.2 1.0 fusion.186
  51.6 0.8 stack.199
  52.8 1.6 fusion.219
  55.1 1.6 concatenate.68
  56.7 2.4 %collective-permute-start.8 = (f32[79200]{0:T(1024)S(1)}, f32[79200]{0:T(1024)S(1)}, u32[]{:S(2)}, u32[]{:S(2)}) collective-permute-start(f32[79200]{0:T(1024)S(1)} %concatenate.68), channel_id=1, source_target_pairs={{0,8},{8,0},{16,24},{24,16},{32,40},{40,32},{48,56},{56,48},{64,72... | collective-permute-start | bytes 950408 | tf_op jit(solution)/shard_map/ppermute | solution.py:65
  59.1 1.2 collective-permute-done.8
  60.3 2.1 collective-permute-start.9
  62.5 8.5 %collective-permute-done.9 = f32[79200]{0:T(1024)S(1)} collective-permute-done((f32[79200]{0:T(1024)S(1)}, f32[79200]{0:T(1024)S(1)}, u32[]{:S(2)}, u32[]{:S(2)}) %collective-permute-start.9) | collective-permute-done | bytes 316832 | tf_op jit(solution)/shard_map/ppermute | solution.py:65
  71.0 3.1 %collective-permute-start.10 = (f32[79200]{0:T(1024)S(1)}, f32[79200]{0:T(1024)S(1)}, u32[]{:S(2)}, u32[]{:S(2)}) collective-permute-start(f32[79200]{0:T(1024)S(1)} %add.503), channel_id=1, source_target_pairs={{0,32},{8,40},{16,48},{24,56},{32,0},{40,8},{48,16},{56,24},{64,96... | collective-permute-start | bytes 950408 | tf_op jit(solution)/shard_map/ppermute | solution.py:65
  74.1 16.1 %collective-permute-done.10 = f32[79200]{0:T(1024)S(1)} collective-permute-done((f32[79200]{0:T(1024)S(1)}, f32[79200]{0:T(1024)S(1)}, u32[]{:S(2)}, u32[]{:S(2)}) %collective-permute-start.10) | collective-permute-done | bytes 316832 | tf_op jit(solution)/shard_map/ppermute | solution.py:65
  90.7 3.6 %collective-permute-start.11 = (f32[79200]{0:T(1024)S(1)}, f32[79200]{0:T(1024)S(1)}, u32[]{:S(2)}, u32[]{:S(2)}) collective-permute-start(f32[79200]{0:T(1024)S(1)} %add.504), channel_id=1, source_target_pairs={{0,64},{8,72},{16,80},{24,88},{32,96},{40,104},{48,112},{56,120},{... | collective-permute-start | bytes 950408 | tf_op jit(solution)/shard_map/ppermute | solution.py:65
  94.3 17.1 %collective-permute-done.11 = f32[79200]{0:T(1024)S(1)} collective-permute-done((f32[79200]{0:T(1024)S(1)}, f32[79200]{0:T(1024)S(1)}, u32[]{:S(2)}, u32[]{:S(2)}) %collective-permute-start.11) | collective-permute-done | bytes 316832 | tf_op jit(solution)/shard_map/ppermute | solution.py:65
  111.4 3.8 %collective-permute-start.12 = (f32[79200]{0:T(1024)S(1)}, f32[79200]{0:T(1024)S(1)}, u32[]{:S(2)}, u32[]{:S(2)}) collective-permute-start(f32[79200]{0:T(1024)S(1)} %add.505), channel_id=1, source_target_pairs={{0,128},{8,136},{16,144},{24,152},{32,160},{40,168},{48,176},{56,1... | collective-permute-start | bytes 950408 | tf_op jit(solution)/shard_map/ppermute | solution.py:65
  115.2 6.6 %collective-permute-done.12 = f32[79200]{0:T(1024)S(1)} collective-permute-done((f32[79200]{0:T(1024)S(1)}, f32[79200]{0:T(1024)S(1)}, u32[]{:S(2)}, u32[]{:S(2)}) %collective-permute-start.12) | collective-permute-done | bytes 316832 | tf_op jit(solution)/shard_map/ppermute | solution.py:65
  121.8 5.2 %collective-permute-start.13 = (f32[79200]{0:T(1024)S(1)}, f32[79200]{0:T(1024)S(1)}, u32[]{:S(2)}, u32[]{:S(2)}) collective-permute-start(f32[79200]{0:T(1024)S(1)} %add.506), channel_id=1, source_target_pairs={{0,256},{8,264},{16,272},{24,280},{32,288},{40,296},{48,304},{56,3... | collective-permute-start | bytes 950408 | tf_op jit(solution)/shard_map/ppermute | solution.py:65
  127.1 14.8 %collective-permute-done.13 = f32[79200]{0:T(1024)S(1)} collective-permute-done((f32[79200]{0:T(1024)S(1)}, f32[79200]{0:T(1024)S(1)}, u32[]{:S(2)}, u32[]{:S(2)}) %collective-permute-start.13) | collective-permute-done | bytes 316832 | tf_op jit(solution)/shard_map/ppermute | solution.py:65
  141.9 5.3 %collective-permute-start.14 = (f32[79200]{0:T(1024)S(1)}, f32[79200]{0:T(1024)S(1)}, u32[]{:S(2)}, u32[]{:S(2)}) collective-permute-start(f32[79200]{0:T(1024)S(1)} %add.507), channel_id=1, source_target_pairs={{0,1},{1,0},{2,3},{3,2},{4,5},{5,4},{6,7},{7,6},{8,9},{9,8},{10,11... | collective-permute-start | bytes 950408 | tf_op jit(solution)/shard_map/ppermute | solution.py:65
  147.6 23.4 %fusion.225 = (bf16[96,14,134]{2,1,0:T(8,128)(2,1)S(1)}, f32[96,14,134]{2,1,0:T(8,128)S(1)}) fusion(f32[96]{0:T(128)S(1)} %get-tuple-element.116, f32[96]{0:T(128)S(1)} %copy-done.25, f32[96]{0:T(128)S(1)} %copy-done.63, f32[96]{0:T(128)S(1)} %copy-done.79, f32[96]{0:T(128)S(1)} %copy-done.77, f32[96]{0:T(128)S(1)} %copy-done.75, f32[96]{0:T(128)S(1)} %copy-done.73, ...), kind=kLoop, calls=%fused_computation.461 | loop fusion | flops 17649408 | bytes 1492608 | tf_op jit(solution)/shard_map/convert.7
  171.1 3.9 %collective-permute-start.4 = (bf16[96,3,134]{2,1,0:T(4,128)(2,1)S(1)}, bf16[96,3,134]{2,1,0:T(4,128)(2,1)S(1)}, u32[]{:S(2)}, u32[]{:S(2)}) collective-permute-start(bf16[96,3,134]{2,1,0:T(4,128)(2,1)S(1)} %get-tuple-element.100), channel_id=1, source_target_pairs={{0,1},{1,2},{2,3},{3,4},{4,5},{5,6},{6,7},{8,9},{9,10},{10,11},{11... | collective-permute-start | bytes 231560 | tf_op jit(solution)/shard_map/ppermute | solution.py:25
  175.1 1.3 collective-permute-start.5
  176.4 8.0 %collective-permute-start.15 = (f32[79200]{0:T(1024)S(1)}, f32[79200]{0:T(1024)S(1)}, u32[]{:S(2)}, u32[]{:S(2)}) collective-permute-start(f32[79200]{0:T(1024)S(1)} %add.508), channel_id=1, source_target_pairs={{0,2},{1,3},{2,0},{3,1},{4,6},{5,7},{6,4},{7,5},{8,10},{9,11},{10,... | collective-permute-start | bytes 950408 | tf_op jit(solution)/shard_map/ppermute | solution.py:65
  184.4 6.4 %collective-permute-done.5 = bf16[96,3,134]{2,1,0:T(4,128)(2,1)S(1)} collective-permute-done((bf16[96,3,134]{2,1,0:T(4,128)(2,1)S(1)}, bf16[96,3,134]{2,1,0:T(4,128)(2,1)S(1)}, u32[]{:S(2)}, u32[]{:S(2)}) %collective-permute-start.5) | collective-permute-done | bytes 77216 | tf_op jit(solution)/shard_map/ppermute | solution.py:25
  191.1 1.2 collective-permute-done.15
  192.4 5.4 %collective-permute-start.16 = (f32[79200]{0:T(1024)S(1)}, f32[79200]{0:T(1024)S(1)}, u32[]{:S(2)}, u32[]{:S(2)}) collective-permute-start(f32[79200]{0:T(1024)S(1)} %add.509), channel_id=1, source_target_pairs={{0,4},{1,5},{2,6},{3,7},{4,0},{5,1},{6,2},{7,3},{8,12},{9,13},{10,... | collective-permute-start | bytes 950408 | tf_op jit(solution)/shard_map/ppermute | solution.py:65
  197.9 1.9 collective-permute-start.6
  199.9 3.0 %collective-permute-start.7 = (f32[96,8,3]{2,1,0:T(8,128)S(1)}, f32[96,8,3]{2,1,0:T(8,128)S(1)}, u32[]{:S(2)}, u32[]{:S(2)}) collective-permute-start(f32[96,8,3]{2,1,0:T(8,128)S(1)} %get-tuple-element.99), channel_id=1, source_target_pairs={{8,0},{16,8},{24,16},{32,24},{40,32},{48,40},{56,48},{64,56},{72,6... | collective-permute-start | bytes 27656 | tf_op jit(solution)/shard_map/ppermute | solution.py:25
  203.6 1.0 collective-permute-done.6
  204.6 6.5 %collective-permute-done.7 = f32[96,8,3]{2,1,0:T(8,128)S(1)} collective-permute-done((f32[96,8,3]{2,1,0:T(8,128)S(1)}, f32[96,8,3]{2,1,0:T(8,128)S(1)}, u32[]{:S(2)}, u32[]{:S(2)}) %collective-permute-start.7) | collective-permute-done | bytes 9248 | tf_op jit(solution)/shard_map/ppermute | solution.py:25
  211.1 1.0 fusion.210
  213.4 0.8 copy.84
  (303 shorter events, 8.8 us)
Async XLA Ops:
  1.8 8.0 %collective-permute-start = (bf16[96,8,3]{0,2,1:T(4,128)(2,1)S(1)}, bf16[96,8,3]{0,2,1:T(4,128)(2,1)S(1)}, u32[]{:S(2)}, u32[]{:S(2)}) collective-permute-start(bf16[96,8,3]{0,2,1:T(4,128)(2,1)S(1)} %get-tuple-element.114), channel_id=1, source_target_pairs={{0,8},{8,16},{16,24},{24,32},{32,40},{40,48},{48,56},{56,64},{64,7... | collective-permute-start | bytes 13832 | tf_op jit(solution)/shard_map/ppermute | solution.py:14
  5.6 7.1 %collective-permute-start.1 = (bf16[96,8,3]{0,2,1:T(4,128)(2,1)S(1)}, bf16[96,8,3]{0,2,1:T(4,128)(2,1)S(1)}, u32[]{:S(2)}, u32[]{:S(2)}) collective-permute-start(bf16[96,8,3]{0,2,1:T(4,128)(2,1)S(1)} %get-tuple-element.115), channel_id=1, source_target_pairs={{8,0},{16,8},{24,16},{32,24},{40,32},{48,40},{56,48},{64,56},{72,6... | collective-permute-start | bytes 13832 | tf_op jit(solution)/shard_map/ppermute | solution.py:17
  12.8 13.7 %collective-permute-start.2 = (bf16[96,3,134]{0,2,1:T(8,128)(2,1)S(1)}, bf16[96,3,134]{0,2,1:T(8,128)(2,1)S(1)}, u32[]{:S(2)}, u32[]{:S(2)}) collective-permute-start(bf16[96,3,134]{0,2,1:T(8,128)(2,1)S(1)} %get-tuple-element.112), channel_id=1, source_target_pairs={{0,1},{1,2},{2,3},{3,4},{4,5},{5,6},{6,7},{8,9},{9,10},{10,11},{11... | collective-permute-start | bytes 231560 | tf_op jit(solution)/shard_map/ppermute | solution.py:14
  22.5 11.6 %collective-permute-start.3 = (bf16[96,3,134]{0,2,1:T(8,128)(2,1)S(1)}, bf16[96,3,134]{0,2,1:T(8,128)(2,1)S(1)}, u32[]{:S(2)}, u32[]{:S(2)}) collective-permute-start(bf16[96,3,134]{0,2,1:T(8,128)(2,1)S(1)} %get-tuple-element.113), channel_id=1, source_target_pairs={{1,0},{2,1},{3,2},{4,3},{5,4},{6,5},{7,6},{9,8},{10,9},{11,10},{12... | collective-permute-start | bytes 231560 | tf_op jit(solution)/shard_map/ppermute | solution.py:17
  56.7 3.6 %collective-permute-start.8 = (f32[79200]{0:T(1024)S(1)}, f32[79200]{0:T(1024)S(1)}, u32[]{:S(2)}, u32[]{:S(2)}) collective-permute-start(f32[79200]{0:T(1024)S(1)} %concatenate.68), channel_id=1, source_target_pairs={{0,8},{8,0},{16,24},{24,16},{32,40},{40,32},{48,56},{56,48},{64,72... | collective-permute-start | bytes 950408 | tf_op jit(solution)/shard_map/ppermute | solution.py:65
  60.3 10.6 %collective-permute-start.9 = (f32[79200]{0:T(1024)S(1)}, f32[79200]{0:T(1024)S(1)}, u32[]{:S(2)}, u32[]{:S(2)}) collective-permute-start(f32[79200]{0:T(1024)S(1)} %add.502), channel_id=1, source_target_pairs={{0,16},{8,24},{16,0},{24,8},{32,48},{40,56},{48,32},{56,40},{64,80... | collective-permute-start | bytes 950408 | tf_op jit(solution)/shard_map/ppermute | solution.py:65
  71.0 19.2 %collective-permute-start.10 = (f32[79200]{0:T(1024)S(1)}, f32[79200]{0:T(1024)S(1)}, u32[]{:S(2)}, u32[]{:S(2)}) collective-permute-start(f32[79200]{0:T(1024)S(1)} %add.503), channel_id=1, source_target_pairs={{0,32},{8,40},{16,48},{24,56},{32,0},{40,8},{48,16},{56,24},{64,96... | collective-permute-start | bytes 950408 | tf_op jit(solution)/shard_map/ppermute | solution.py:65
  90.3 56.9 %copy-start.7 = (f32[96]{0:T(128)S(1)}, f32[96]{0:T(128)}, u32[]{:S(2)}) copy-start(f32[96]{0:T(128)} %copy-done.6) | copy-start | bytes 1156
  90.3 56.9 %copy-start.9 = (f32[96]{0:T(128)S(1)}, f32[96]{0:T(128)}, u32[]{:S(2)}) copy-start(f32[96]{0:T(128)} %copy-done.8) | copy-start | bytes 1156
  90.3 56.9 %copy-start.11 = (f32[96]{0:T(128)S(1)}, f32[96]{0:T(128)}, u32[]{:S(2)}) copy-start(f32[96]{0:T(128)} %copy-done.10) | copy-start | bytes 1156
  90.3 56.9 %copy-start.13 = (f32[96]{0:T(128)S(1)}, f32[96]{0:T(128)}, u32[]{:S(2)}) copy-start(f32[96]{0:T(128)} %copy-done.12) | copy-start | bytes 1156
  90.3 56.9 %copy-start.15 = (f32[96]{0:T(128)S(1)}, f32[96]{0:T(128)}, u32[]{:S(2)}) copy-start(f32[96]{0:T(128)} %copy-done.14) | copy-start | bytes 1156
  90.3 56.9 %copy-start.17 = (f32[96]{0:T(128)S(1)}, f32[96]{0:T(128)}, u32[]{:S(2)}) copy-start(f32[96]{0:T(128)} %copy-done.16) | copy-start | bytes 1156
  90.3 56.9 %copy-start.19 = (f32[96]{0:T(128)S(1)}, f32[96]{0:T(128)}, u32[]{:S(2)}) copy-start(f32[96]{0:T(128)} %copy-done.18) | copy-start | bytes 1156
  90.3 56.9 %copy-start.21 = (f32[96]{0:T(128)S(1)}, f32[96]{0:T(128)}, u32[]{:S(2)}) copy-start(f32[96]{0:T(128)} %copy-done.20) | copy-start | bytes 1156
  90.3 56.9 %copy-start.23 = (f32[96]{0:T(128)S(1)}, f32[96]{0:T(128)}, u32[]{:S(2)}) copy-start(f32[96]{0:T(128)} %copy-done.22) | copy-start | bytes 1156
  90.4 56.9 %copy-start.25 = (f32[96]{0:T(128)S(1)}, f32[96]{0:T(128)}, u32[]{:S(2)}) copy-start(f32[96]{0:T(128)} %copy-done.24) | copy-start | bytes 1156
  90.4 56.9 %copy-start.27 = (f32[96]{0:T(128)S(1)}, f32[96]{0:T(128)}, u32[]{:S(2)}) copy-start(f32[96]{0:T(128)} %copy-done.26) | copy-start | bytes 1156
  90.4 56.9 %copy-start.29 = (f32[96]{0:T(128)S(1)}, f32[96]{0:T(128)}, u32[]{:S(2)}) copy-start(f32[96]{0:T(128)} %copy-done.28) | copy-start | bytes 1156
  90.4 56.9 %copy-start.31 = (f32[96]{0:T(128)S(1)}, f32[96]{0:T(128)}, u32[]{:S(2)}) copy-start(f32[96]{0:T(128)} %copy-done.30) | copy-start | bytes 1156
  90.4 56.9 %copy-start.33 = (f32[96]{0:T(128)S(1)}, f32[96]{0:T(128)}, u32[]{:S(2)}) copy-start(f32[96]{0:T(128)} %copy-done.32) | copy-start | bytes 1156
  90.4 56.9 %copy-start.35 = (f32[96]{0:T(128)S(1)}, f32[96]{0:T(128)}, u32[]{:S(2)}) copy-start(f32[96]{0:T(128)} %copy-done.34) | copy-start | bytes 1156
  90.4 56.9 %copy-start.37 = (f32[96]{0:T(128)S(1)}, f32[96]{0:T(128)}, u32[]{:S(2)}) copy-start(f32[96]{0:T(128)} %copy-done.36) | copy-start | bytes 1156
  90.4 56.9 %copy-start.39 = (f32[96]{0:T(128)S(1)}, f32[96]{0:T(128)}, u32[]{:S(2)}) copy-start(f32[96]{0:T(128)} %copy-done.38) | copy-start | bytes 1156
  90.4 56.9 %copy-start.41 = (f32[96]{0:T(128)S(1)}, f32[96]{0:T(128)}, u32[]{:S(2)}) copy-start(f32[96]{0:T(128)} %copy-done.40) | copy-start | bytes 1156
  90.4 56.9 %copy-start.43 = (f32[96]{0:T(128)S(1)}, f32[96]{0:T(128)}, u32[]{:S(2)}) copy-start(f32[96]{0:T(128)} %copy-done.42) | copy-start | bytes 1156
  90.5 56.9 %copy-start.45 = (f32[96]{0:T(128)S(1)}, f32[96]{0:T(128)}, u32[]{:S(2)}) copy-start(f32[96]{0:T(128)} %copy-done.44) | copy-start | bytes 1156
  90.5 56.9 %copy-start.47 = (f32[96]{0:T(128)S(1)}, f32[96]{0:T(128)}, u32[]{:S(2)}) copy-start(f32[96]{0:T(128)} %copy-done.46) | copy-start | bytes 1156
  90.5 56.9 %copy-start.49 = (f32[96]{0:T(128)S(1)}, f32[96]{0:T(128)}, u32[]{:S(2)}) copy-start(f32[96]{0:T(128)} %copy-done.48) | copy-start | bytes 1156
  90.5 56.9 %copy-start.51 = (f32[96]{0:T(128)S(1)}, f32[96]{0:T(128)}, u32[]{:S(2)}) copy-start(f32[96]{0:T(128)} %copy-done.50) | copy-start | bytes 1156
  90.5 56.9 %copy-start.53 = (f32[96]{0:T(128)S(1)}, f32[96]{0:T(128)}, u32[]{:S(2)}) copy-start(f32[96]{0:T(128)} %copy-done.52) | copy-start | bytes 1156
  90.5 56.9 %copy-start.55 = (f32[96]{0:T(128)S(1)}, f32[96]{0:T(128)}, u32[]{:S(2)}) copy-start(f32[96]{0:T(128)} %copy-done.54) | copy-start | bytes 1156
  90.5 56.9 %copy-start.57 = (f32[96]{0:T(128)S(1)}, f32[96]{0:T(128)}, u32[]{:S(2)}) copy-start(f32[96]{0:T(128)} %copy-done.56) | copy-start | bytes 1156
  90.5 56.9 %copy-start.59 = (f32[96]{0:T(128)S(1)}, f32[96]{0:T(128)}, u32[]{:S(2)}) copy-start(f32[96]{0:T(128)} %copy-done.58) | copy-start | bytes 1156
  90.5 56.9 %copy-start.61 = (f32[96]{0:T(128)S(1)}, f32[96]{0:T(128)}, u32[]{:S(2)}) copy-start(f32[96]{0:T(128)} %copy-done.60) | copy-start | bytes 1156
  90.5 56.9 %copy-start.63 = (f32[96]{0:T(128)S(1)}, f32[96]{0:T(128)}, u32[]{:S(2)}) copy-start(f32[96]{0:T(128)} %copy-done.62) | copy-start | bytes 1156
  90.6 56.9 %copy-start.65 = (f32[96]{0:T(128)S(1)}, f32[96]{0:T(128)}, u32[]{:S(2)}) copy-start(f32[96]{0:T(128)} %copy-done.64) | copy-start | bytes 1156
  90.6 56.9 %copy-start.67 = (f32[96]{0:T(128)S(1)}, f32[96]{0:T(128)}, u32[]{:S(2)}) copy-start(f32[96]{0:T(128)} %copy-done.66) | copy-start | bytes 1156
  90.7 20.7 %collective-permute-start.11 = (f32[79200]{0:T(1024)S(1)}, f32[79200]{0:T(1024)S(1)}, u32[]{:S(2)}, u32[]{:S(2)}) collective-permute-start(f32[79200]{0:T(1024)S(1)} %add.504), channel_id=1, source_target_pairs={{0,64},{8,72},{16,80},{24,88},{32,96},{40,104},{48,112},{56,120},{... | collective-permute-start | bytes 950408 | tf_op jit(solution)/shard_map/ppermute | solution.py:65
  111.4 10.4 %collective-permute-start.12 = (f32[79200]{0:T(1024)S(1)}, f32[79200]{0:T(1024)S(1)}, u32[]{:S(2)}, u32[]{:S(2)}) collective-permute-start(f32[79200]{0:T(1024)S(1)} %add.505), channel_id=1, source_target_pairs={{0,128},{8,136},{16,144},{24,152},{32,160},{40,168},{48,176},{56,1... | collective-permute-start | bytes 950408 | tf_op jit(solution)/shard_map/ppermute | solution.py:65
  121.8 20.0 %collective-permute-start.13 = (f32[79200]{0:T(1024)S(1)}, f32[79200]{0:T(1024)S(1)}, u32[]{:S(2)}, u32[]{:S(2)}) collective-permute-start(f32[79200]{0:T(1024)S(1)} %add.506), channel_id=1, source_target_pairs={{0,256},{8,264},{16,272},{24,280},{32,288},{40,296},{48,304},{56,3... | collective-permute-start | bytes 950408 | tf_op jit(solution)/shard_map/ppermute | solution.py:65
  141.9 34.5 %collective-permute-start.14 = (f32[79200]{0:T(1024)S(1)}, f32[79200]{0:T(1024)S(1)}, u32[]{:S(2)}, u32[]{:S(2)}) collective-permute-start(f32[79200]{0:T(1024)S(1)} %add.507), channel_id=1, source_target_pairs={{0,1},{1,0},{2,3},{3,2},{4,5},{5,4},{6,7},{7,6},{8,9},{9,8},{10,11... | collective-permute-start | bytes 950408 | tf_op jit(solution)/shard_map/ppermute | solution.py:65
  171.1 13.3 %collective-permute-start.4 = (bf16[96,3,134]{2,1,0:T(4,128)(2,1)S(1)}, bf16[96,3,134]{2,1,0:T(4,128)(2,1)S(1)}, u32[]{:S(2)}, u32[]{:S(2)}) collective-permute-start(bf16[96,3,134]{2,1,0:T(4,128)(2,1)S(1)} %get-tuple-element.100), channel_id=1, source_target_pairs={{0,1},{1,2},{2,3},{3,4},{4,5},{5,6},{6,7},{8,9},{9,10},{10,11},{11... | collective-permute-start | bytes 231560 | tf_op jit(solution)/shard_map/ppermute | solution.py:25
  175.1 15.7 %collective-permute-start.5 = (bf16[96,3,134]{2,1,0:T(4,128)(2,1)S(1)}, bf16[96,3,134]{2,1,0:T(4,128)(2,1)S(1)}, u32[]{:S(2)}, u32[]{:S(2)}) collective-permute-start(bf16[96,3,134]{2,1,0:T(4,128)(2,1)S(1)} %get-tuple-element.101), channel_id=1, source_target_pairs={{1,0},{2,1},{3,2},{4,3},{5,4},{6,5},{7,6},{9,8},{10,9},{11,10},{12... | collective-permute-start | bytes 231560 | tf_op jit(solution)/shard_map/ppermute | solution.py:25
  176.4 15.9 %collective-permute-start.15 = (f32[79200]{0:T(1024)S(1)}, f32[79200]{0:T(1024)S(1)}, u32[]{:S(2)}, u32[]{:S(2)}) collective-permute-start(f32[79200]{0:T(1024)S(1)} %add.508), channel_id=1, source_target_pairs={{0,2},{1,3},{2,0},{3,1},{4,6},{5,7},{6,4},{7,5},{8,10},{9,11},{10,... | collective-permute-start | bytes 950408 | tf_op jit(solution)/shard_map/ppermute | solution.py:65
  192.4 19.6 %collective-permute-start.16 = (f32[79200]{0:T(1024)S(1)}, f32[79200]{0:T(1024)S(1)}, u32[]{:S(2)}, u32[]{:S(2)}) collective-permute-start(f32[79200]{0:T(1024)S(1)} %add.509), channel_id=1, source_target_pairs={{0,4},{1,5},{2,6},{3,7},{4,0},{5,1},{6,2},{7,3},{8,12},{9,13},{10,... | collective-permute-start | bytes 950408 | tf_op jit(solution)/shard_map/ppermute | solution.py:65
  197.9 6.6 %collective-permute-start.6 = (f32[96,8,3]{2,1,0:T(8,128)S(1)}, f32[96,8,3]{2,1,0:T(8,128)S(1)}, u32[]{:S(2)}, u32[]{:S(2)}) collective-permute-start(f32[96,8,3]{2,1,0:T(8,128)S(1)} %get-tuple-element.98), channel_id=1, source_target_pairs={{0,8},{8,16},{16,24},{24,32},{32,40},{40,48},{48,56},{56,64},{64,7... | collective-permute-start | bytes 27656 | tf_op jit(solution)/shard_map/ppermute | solution.py:25
  199.9 11.2 %collective-permute-start.7 = (f32[96,8,3]{2,1,0:T(8,128)S(1)}, f32[96,8,3]{2,1,0:T(8,128)S(1)}, u32[]{:S(2)}, u32[]{:S(2)}) collective-permute-start(f32[96,8,3]{2,1,0:T(8,128)S(1)} %get-tuple-element.99), channel_id=1, source_target_pairs={{8,0},{16,8},{24,16},{32,24},{40,32},{48,40},{56,48},{64,56},{72,6... | collective-permute-start | bytes 27656 | tf_op jit(solution)/shard_map/ppermute | solution.py:25
  (98 other events, 1612.5 us)

commit v2 on v1

--- a/solution.py
+++ b/solution.py
@@ -54,16 +54,36 @@
     return jnp.stack(pieces, axis=1).reshape(conv_grad.shape[0], 7, 7)
 
 
-def butterfly_sum(parts):
+def xor_partner(value, axis, mask):
+    return lax.ppermute(value, axis, [(i, i ^ mask) for i in range(lax.axis_size(axis))])
+
+
+def butterfly_sum(parts, halving=(("col", 1), ("col", 2))):
     shapes = [p.shape for p in parts]
     flat = jnp.concatenate([p.reshape(-1) for p in parts])
+    total = flat.shape[0]
+    unit = 2 ** len(halving)
+    flat = jnp.pad(flat, (0, -total % unit))
+    doubling = []
     for axis in ("col", "row"):
-        count = lax.axis_size(axis)
-        bit = 1
-        while bit < count:
-            pairs = [(i, i ^ bit) for i in range(count)]
-            flat = flat + lax.ppermute(flat, axis, pairs)
-            bit *= 2
+        mask = 1
+        while mask < lax.axis_size(axis):
+            if (axis, mask) not in halving:
+                doubling.append((axis, mask))
+            mask *= 2
+    sides = []
+    for axis, mask in halving:
+        half = flat.shape[0] // 2
+        side = (lax.axis_index(axis) // mask) % 2
+        keep = lax.dynamic_slice_in_dim(flat, side * half, half)
+        send = lax.dynamic_slice_in_dim(flat, (1 - side) * half, half)
+        flat = keep + xor_partner(send, axis, mask)
+        sides.append(side)
+    for axis, mask in doubling:
+        flat = flat + xor_partner(flat, axis, mask)
+    for (axis, mask), side in zip(reversed(halving), reversed(sides)):
+        other = xor_partner(flat, axis, mask)
+        flat = jnp.where(side == 0, jnp.concatenate([flat, other]), jnp.concatenate([other, flat]))
     out, start = [], 0
     for shape in shapes:
         size = math.prod(shape)

time: 218 us -> 182 us (0.83)
  waiting for transfers between devices: 90.5 us -> 38 us
  starting transfers between devices: 65.7 us -> 78.4 us
  local copies, waits for them, and re-layouts: 11.7 us -> 15.7 us
    ppermute x9 -> x11, waiting for transfers between devices: 65.5 us -> 18.8 us  [xor_partner(): lax.ppermute(value, axis, [(i, i ^ mask) for i in range(lax.axis_size(axi...]
    ppermute x4, starting transfers between devices: 10.1 us -> 17.2 us  [from_behind(): lax.ppermute(value, axis, [(source, source + steps) for source in range(i...]
    ppermute x4, waiting for transfers between devices: 13.9 us -> 8.23 us  [from_behind(): lax.ppermute(value, axis, [(source, source + steps) for source in range(i...]
    ppermute x9 -> x11, starting transfers between devices: 38.9 us -> 44.5 us  [xor_partner(): lax.ppermute(value, axis, [(i, i ^ mask) for i in range(lax.axis_size(axi...]
  transfers between devices with their start and end apart: 17 -> 19, of which waited for: 13 -> 13; matrix products, arithmetic and copies ran while one was open for 14% -> 17% of each run, Pallas kernels for 0% -> 0%
where the time goes in v2:
time: 182 us
  starting transfers between devices  78.4 us (43%)
  other arithmetic  40 us (22%)
  waiting for transfers between devices  38 us (21%)
  local copies, waits for them, and re-layouts  15.7 us (9%)
  matrix products  6.46 us (4%)
  between operations  2.87 us (2%)
    ppermute x11, starting transfers between devices, xor_partner(): lax.ppermute(value, axis, [(i, i ^ mask) for i in range(lax.axis_size(axi...  44.5 us
    another operation x1, other arithmetic  24.1 us
    ppermute x11, waiting for transfers between devices, xor_partner(): lax.ppermute(value, axis, [(i, i ^ mask) for i in range(lax.axis_size(axi...  18.8 us
    ppermute x4, starting transfers between devices, from_behind(): lax.ppermute(value, axis, [(source, source + steps) for source in range(i...  17.2 us
    ppermute x2, starting transfers between devices, padded_2(): lax.ppermute(lax.slice_in_dim(block, block.shape[dim] - width, None, axis...  13.5 us
    ppermute x2, waiting for transfers between devices, padded_2(): lax.ppermute(lax.slice_in_dim(block, 0, width, axis=dim), axis, backward)  10.5 us
    ppermute x4, waiting for transfers between devices, from_behind(): lax.ppermute(value, axis, [(source, source + steps) for source in range(i...  8.23 us
    dot_general x6, matrix products, product(): return jnp.einsum(form, left, right, preferred_element_type=jnp.float32)  6.46 us
  transfers between devices with their start and end apart: 19, of which 13 were waited for; matrix products, arithmetic and copies ran while one was open for 17% of the time, Pallas kernels for 0%

profile of v2, /device:TPU:57, one launch (start us, length us, event | category | flops | bytes accessed | tf_op | source)
XLA Modules:
  0.0 181.5 jit_solution(7042523879594998132)
XLA Ops:
  0.7 1.2 copy.24
  1.8 3.8 %collective-permute-start = (bf16[96,8,3]{0,2,1:T(4,128)(2,1)S(1)}, bf16[96,8,3]{0,2,1:T(4,128)(2,1)S(1)}, u32[]{:S(2)}, u32[]{:S(2)}) collective-permute-start(bf16[96,8,3]{0,2,1:T(4,128)(2,1)S(1)} %get-tuple-element.114), channel_id=1, source_target_pairs={{0,8},{8,16},{16,24},{24,32},{32,40},{40,48},{48,56},{56,64},{64,7... | collective-permute-start | bytes 13832 | tf_op jit(solution)/shard_map/ppermute | solution.py:14
  5.6 1.9 %collective-permute-start.1 = (bf16[96,8,3]{0,2,1:T(4,128)(2,1)S(1)}, bf16[96,8,3]{0,2,1:T(4,128)(2,1)S(1)}, u32[]{:S(2)}, u32[]{:S(2)}) collective-permute-start(bf16[96,8,3]{0,2,1:T(4,128)(2,1)S(1)} %get-tuple-element.115), channel_id=1, source_target_pairs={{8,0},{16,8},{24,16},{32,24},{40,32},{48,40},{56,48},{64,56},{72,6... | collective-permute-start | bytes 13832 | tf_op jit(solution)/shard_map/ppermute | solution.py:17
  7.5 1.0 slice_bitcast_fusion.48
  8.6 1.0 slice_bitcast_fusion.47
  9.8 2.9 %collective-permute-done.1 = bf16[96,8,3]{0,2,1:T(4,128)(2,1)S(1)} collective-permute-done((bf16[96,8,3]{0,2,1:T(4,128)(2,1)S(1)}, bf16[96,8,3]{0,2,1:T(4,128)(2,1)S(1)}, u32[]{:S(2)}, u32[]{:S(2)}) %collective-permute-start.1) | collective-permute-done | bytes 4640 | tf_op jit(solution)/shard_map/ppermute | solution.py:17
  12.8 9.7 %collective-permute-start.2 = (bf16[96,3,134]{0,2,1:T(8,128)(2,1)S(1)}, bf16[96,3,134]{0,2,1:T(8,128)(2,1)S(1)}, u32[]{:S(2)}, u32[]{:S(2)}) collective-permute-start(bf16[96,3,134]{0,2,1:T(8,128)(2,1)S(1)} %get-tuple-element.112), channel_id=1, source_target_pairs={{0,1},{1,2},{2,3},{3,4},{4,5},{5,6},{6,7},{8,9},{9,10},{10,11},{11... | collective-permute-start | bytes 231560 | tf_op jit(solution)/shard_map/ppermute | solution.py:14
  22.5 1.3 collective-permute-start.3
  23.8 0.9 slice_bitcast_fusion.46
  24.8 1.0 convert.12
  26.5 7.7 %collective-permute-done.3 = bf16[96,3,134]{0,2,1:T(8,128)(2,1)S(1)} collective-permute-done((bf16[96,3,134]{0,2,1:T(8,128)(2,1)S(1)}, bf16[96,3,134]{0,2,1:T(8,128)(2,1)S(1)}, u32[]{:S(2)}, u32[]{:S(2)}) %collective-permute-start.3) | collective-permute-done | bytes 77216 | tf_op jit(solution)/shard_map/ppermute | solution.py:17
  34.4 4.3 %fusion.227 = (f32[8,128]{1,0:T(8,128)S(1)}, f32[96,8,128]{0,2,1:T(8,128)S(1)}) fusion(f32[96]{0:T(128)S(1)} %copy-done.109, bf16[96,11,134]{0,2,1:T(8,128)(2,1)S(1)} %get-tuple-element.111, f32[96]{0:T(128)S(1)} %get-tuple-element.163, f32[96]{0:T(128)S(1)} %get-tuple-element.164, f32[96]{0:T(128)S(1)} %get-tuple-element.117, ...), kind=kLoop, calls=%fused_computation.466 | loop fusion | flops 16317440 | bytes 8879872 | tf_op jit(solution)/shard_map/reduce_sum | solution.py:100
  39.7 1.7 fusion.107
  41.4 2.0 %convert_reduce_fusion = (f32[384]{0:T(512)}, bf16[384,1024]{0,1:T(8,128)(2,1)S(1)}) fusion(f32[1024,384]{1,0:T(8,128)S(1)} %get-tuple-element.168, bf16[384,96]{0,1:T(8,128)(2,1)S(1)} %copy-done.4, f32[12,8,8,128]{3,2,1,0:T(8,128)S(1)} %convert.12, f32[96]{0:T(128)S(1)} %copy-done.85), kind=kOutput, calls=%fused_computation.162 | convolution fusion | flops 84344448 | bytes 2828160 | tf_op jit(solution)/shard_map/hc,cp->hp/dot_general | solution.py:96
  44.1 0.9 fusion.211
  45.3 1.9 %fusion.204 = (f32[96]{0:T(128)}, f32[96]{0:T(128)}, f32[96]{0:T(128)}, f32[96]{0:T(128)}, f32[96]{0:T(128)}, /*index=5*/f32[96]{0:T(128)}, f32[96]{0:T(128)}, f...) fusion(f32[96,8,128]{0,2,1:T(8,128)S(1)} %copy.32, ...), kind=kLoop, calls=%fused_computation.358 | loop fusion | flops 5306688 | bytes 3939072 | tf_op jit(solution)/shard_map/reduce_sum | solution.py:48
  47.1 1.9 %fusion.154 = (f32[96]{0:T(128)}, f32[96]{0:T(128)}, f32[96]{0:T(128)}, f32[96]{0:T(128)}, f32[96]{0:T(128)}, /*index=5*/f32[96]{0:T(128)}, f32[96]{0:T(128)}, f...) fusion(f32[96,8,128]{0,2,1:T(8,128)S(1)} %copy.32, ...), kind=kLoop, calls=%fused_computation.308 | loop fusion | flops 5306688 | bytes 3939072 | tf_op jit(solution)/shard_map/reduce_sum | solution.py:48
  49.0 0.8 fusion.136
  50.1 1.5 fusion.186
  51.8 2.8 %stack.199 = f32[96,49]{0,1:T(8,128)S(1)} concatenate(f32[96,1]{0,1:T(1,128)S(1)} %bitcast.270, f32[96,1]{0,1:T(1,128)S(1)} %bitcast.269, f32[96,1]{0,1:T(1,128)S(1)} %bitcast.268, f32[96,1]{0,1:T(1,128)S(1)} %bitcast.267, f32[96,1]{0,1:T(1,128)S(1)} %bitcast.266, f32[96,1]{0,1:T(1,128)S(1)} %bitcast.265, f32[96,1]{0,1:T(1,128)S(1)} %bitcast.264, f32[96,1]{0,1:T(1,128)S(1)} %bitcast.263, ...), dimensions={1} | concatenate | bytes 37632 | tf_op jit(solution)/shard_map/stack | solution.py:54
  55.1 1.6 fusion.219
  57.7 3.5 %concatenate.80 = f32[79200]{0:T(1024)S(1)} concatenate(f32[4704]{0:T(1024)S(1)} %reshape_reshape.3, f32[96]{0:T(128)} %get-tuple-element.73, f32[96]{0:T(128)} %get-tuple-element.72, f32[96]{0:T(128)S(1)} %reduce_sum.577, f32[36864]{0:T(1024)S(1)} %reshape.104, f32[384]{0:T(512)} %get-tuple-element.170, f32[36864]{0:T(1024)S(1)} %reshape.105, f32[96]{0:T(128)S(1)} %get-tuple-element.102), dimensions={0} | concatenate | bytes 633600 | tf_op jit(solution)/shard_map/concatenate | solution.py:63
  61.3 2.4 %collective-permute-start.8 = (f32[39600]{0:T(1024)S(1)}, f32[39600]{0:T(1024)S(1)}, u32[]{:S(2)}, u32[]{:S(2)}) collective-permute-start(f32[39600]{0:T(1024)S(1)} %dynamic_slice.13), channel_id=1, source_target_pairs={{0,8},{8,0},{16,24},{24,16},{32,40},{40,32},{48,56},{56,48},{64,72... | collective-permute-start | bytes 475208 | tf_op jit(solution)/shard_map/ppermute | solution.py:58
  63.8 1.0 collective-permute-done.8
  65.0 2.3 %collective-permute-start.9 = (f32[19800]{0:T(1024)S(1)}, f32[19800]{0:T(1024)S(1)}, u32[]{:S(2)}, u32[]{:S(2)}) collective-permute-start(f32[19800]{0:T(1024)S(1)} %dynamic_slice.15), channel_id=1, source_target_pairs={{0,16},{8,24},{16,0},{24,8},{32,48},{40,56},{48,32},{56,40},{64,80... | collective-permute-start | bytes 237608 | tf_op jit(solution)/shard_map/ppermute | solution.py:58
  67.3 3.4 %collective-permute-done.9 = f32[19800]{0:T(1024)S(1)} collective-permute-done((f32[19800]{0:T(1024)S(1)}, f32[19800]{0:T(1024)S(1)}, u32[]{:S(2)}, u32[]{:S(2)}) %collective-permute-start.9) | collective-permute-done | bytes 79232 | tf_op jit(solution)/shard_map/ppermute | solution.py:58
  70.8 2.9 %collective-permute-start.10 = (f32[19800]{0:T(1024)S(1)}, f32[19800]{0:T(1024)S(1)}, u32[]{:S(2)}, u32[]{:S(2)}) collective-permute-start(f32[19800]{0:T(1024)S(1)} %dynamic-slice_add_fusion.1), channel_id=1, source_target_pairs={{0,32},{8,40},{16,48},{24,56},{32,0},{40,8},{48,16},{56,24},{64,96... | collective-permute-start | bytes 237608 | tf_op jit(solution)/shard_map/ppermute | solution.py:58
  73.7 4.0 %collective-permute-done.10 = f32[19800]{0:T(1024)S(1)} collective-permute-done((f32[19800]{0:T(1024)S(1)}, f32[19800]{0:T(1024)S(1)}, u32[]{:S(2)}, u32[]{:S(2)}) %collective-permute-start.10) | collective-permute-done | bytes 79232 | tf_op jit(solution)/shard_map/ppermute | solution.py:58
  77.7 4.5 %collective-permute-start.11 = (f32[19800]{0:T(1024)S(1)}, f32[19800]{0:T(1024)S(1)}, u32[]{:S(2)}, u32[]{:S(2)}) collective-permute-start(f32[19800]{0:T(1024)S(1)} %add.531), channel_id=1, source_target_pairs={{0,64},{8,72},{16,80},{24,88},{32,96},{40,104},{48,112},{56,120},{... | collective-permute-start | bytes 237608 | tf_op jit(solution)/shard_map/ppermute | solution.py:58
  82.3 5.0 %collective-permute-done.11 = f32[19800]{0:T(1024)S(1)} collective-permute-done((f32[19800]{0:T(1024)S(1)}, f32[19800]{0:T(1024)S(1)}, u32[]{:S(2)}, u32[]{:S(2)}) %collective-permute-start.11) | collective-permute-done | bytes 79232 | tf_op jit(solution)/shard_map/ppermute | solution.py:58
  87.2 3.2 %collective-permute-start.12 = (f32[19800]{0:T(1024)S(1)}, f32[19800]{0:T(1024)S(1)}, u32[]{:S(2)}, u32[]{:S(2)}) collective-permute-start(f32[19800]{0:T(1024)S(1)} %add.532), channel_id=1, source_target_pairs={{0,128},{8,136},{16,144},{24,152},{32,160},{40,168},{48,176},{56,1... | collective-permute-start | bytes 237608 | tf_op jit(solution)/shard_map/ppermute | solution.py:58
  90.4 2.0 %collective-permute-done.12 = f32[19800]{0:T(1024)S(1)} collective-permute-done((f32[19800]{0:T(1024)S(1)}, f32[19800]{0:T(1024)S(1)}, u32[]{:S(2)}, u32[]{:S(2)}) %collective-permute-start.12) | collective-permute-done | bytes 79232 | tf_op jit(solution)/shard_map/ppermute | solution.py:58
  92.4 4.5 %collective-permute-start.13 = (f32[19800]{0:T(1024)S(1)}, f32[19800]{0:T(1024)S(1)}, u32[]{:S(2)}, u32[]{:S(2)}) collective-permute-start(f32[19800]{0:T(1024)S(1)} %add.533), channel_id=1, source_target_pairs={{0,256},{8,264},{16,272},{24,280},{32,288},{40,296},{48,304},{56,3... | collective-permute-start | bytes 237608 | tf_op jit(solution)/shard_map/ppermute | solution.py:58
  96.9 2.7 %collective-permute-done.13 = f32[19800]{0:T(1024)S(1)} collective-permute-done((f32[19800]{0:T(1024)S(1)}, f32[19800]{0:T(1024)S(1)}, u32[]{:S(2)}, u32[]{:S(2)}) %collective-permute-start.13) | collective-permute-done | bytes 79232 | tf_op jit(solution)/shard_map/ppermute | solution.py:58
  99.6 5.5 %collective-permute-start.14 = (f32[19800]{0:T(1024)S(1)}, f32[19800]{0:T(1024)S(1)}, u32[]{:S(2)}, u32[]{:S(2)}) collective-permute-start(f32[19800]{0:T(1024)S(1)} %add.534), channel_id=1, source_target_pairs={{0,1},{1,0},{2,3},{3,2},{4,5},{5,4},{6,7},{7,6},{8,9},{9,8},{10,11... | collective-permute-start | bytes 237608 | tf_op jit(solution)/shard_map/ppermute | solution.py:58
  105.5 24.1 %fusion.225 = (bf16[96,14,134]{2,1,0:T(8,128)(2,1)S(1)}, f32[96,14,134]{2,1,0:T(8,128)}) fusion(f32[96]{0:T(128)S(1)} %get-tuple-element.116, f32[96]{0:T(128)S(1)} %copy-done.26, f32[96]{0:T(128)S(1)} %copy-done.64, f32[96]{0:T(128)S(1)} %copy-done.80, f32[96]{0:T(128)S(1)} %copy-done.78, f32[96]{0:T(128)S(1)} %copy-done.76, f32[96]{0:T(128)S(1)} %copy-done.74, ...), kind=kLoop, calls=%fused_computation.465 | loop fusion | flops 17649408 | bytes 1492608 | tf_op jit(solution)/shard_map/convert.7
  129.6 3.3 %collective-permute-start.15 = (f32[19800]{0:T(1024)S(1)}, f32[19800]{0:T(1024)S(1)}, u32[]{:S(2)}, u32[]{:S(2)}) collective-permute-start(f32[19800]{0:T(1024)S(1)} %add.535), channel_id=1, source_target_pairs={{0,2},{1,3},{2,0},{3,1},{4,6},{5,7},{6,4},{7,5},{8,10},{9,11},{10,... | collective-permute-start | bytes 237608 | tf_op jit(solution)/shard_map/ppermute | solution.py:58
  133.1 2.7 %collective-permute-start.4 = (bf16[96,3,134]{2,1,0:T(4,128)(2,1)S(1)}, bf16[96,3,134]{2,1,0:T(4,128)(2,1)S(1)}, u32[]{:S(2)}, u32[]{:S(2)}) collective-permute-start(bf16[96,3,134]{2,1,0:T(4,128)(2,1)S(1)} %get-tuple-element.100), channel_id=1, source_target_pairs={{0,1},{1,2},{2,3},{3,4},{4,5},{5,6},{6,7},{8,9},{9,10},{10,11},{11... | collective-permute-start | bytes 231560 | tf_op jit(solution)/shard_map/ppermute | solution.py:25
  135.7 1.3 collective-permute-start.5
  137.8 9.8 %collective-permute-start.16 = (f32[19800]{0:T(1024)S(1)}, f32[19800]{0:T(1024)S(1)}, u32[]{:S(2)}, u32[]{:S(2)}) collective-permute-start(f32[19800]{0:T(1024)S(1)} %add.536), channel_id=1, source_target_pairs={{0,4},{1,5},{2,6},{3,7},{4,0},{5,1},{6,2},{7,3},{8,12},{9,13},{10,... | collective-permute-start | bytes 237608 | tf_op jit(solution)/shard_map/ppermute | solution.py:58
  147.6 1.0 collective-permute-done.5
  149.6 4.2 %collective-permute-start.17 = (f32[19800]{0:T(1024)S(1)}, f32[19800]{0:T(1024)S(1)}, u32[]{:S(2)}, u32[]{:S(2)}) collective-permute-start(f32[19800]{0:T(1024)S(1)} %add.537), channel_id=1, source_target_pairs={{0,16},{8,24},{16,0},{24,8},{32,48},{40,56},{48,32},{56,40},{64,80... | collective-permute-start | bytes 237608 | tf_op jit(solution)/shard_map/ppermute | solution.py:58
  154.0 11.3 %collective-permute-start.6 = (f32[96,8,3]{2,1,0:T(8,128)S(1)}, f32[96,8,3]{2,1,0:T(8,128)S(1)}, u32[]{:S(2)}, u32[]{:S(2)}) collective-permute-start(f32[96,8,3]{2,1,0:T(8,128)S(1)} %get-tuple-element.98), channel_id=1, source_target_pairs={{0,8},{8,16},{16,24},{24,32},{32,40},{40,48},{48,56},{56,64},{64,7... | collective-permute-start | bytes 27656 | tf_op jit(solution)/shard_map/ppermute | solution.py:25
  165.4 1.9 %collective-permute-start.7 = (f32[96,8,3]{2,1,0:T(8,128)S(1)}, f32[96,8,3]{2,1,0:T(8,128)S(1)}, u32[]{:S(2)}, u32[]{:S(2)}) collective-permute-start(f32[96,8,3]{2,1,0:T(8,128)S(1)} %get-tuple-element.99), channel_id=1, source_target_pairs={{8,0},{16,8},{24,16},{32,24},{40,32},{48,40},{56,48},{64,56},{72,6... | collective-permute-start | bytes 27656 | tf_op jit(solution)/shard_map/ppermute | solution.py:25
  167.4 1.9 %collective-permute-start.18 = (f32[39600]{0:T(1024)S(1)}, f32[39600]{0:T(1024)S(1)}, u32[]{:S(2)}, u32[]{:S(2)}) collective-permute-start(f32[39600]{0:T(1024)S(1)} %maximum_select_fusion.1), channel_id=1, source_target_pairs={{0,8},{8,0},{16,24},{24,16},{32,40},{40,32},{48,56},{56,48},{64,72... | collective-permute-start | bytes 475208 | tf_op jit(solution)/shard_map/ppermute | solution.py:58
  170.1 6.5 %collective-permute-done.7 = f32[96,8,3]{2,1,0:T(8,128)S(1)} collective-permute-done((f32[96,8,3]{2,1,0:T(8,128)S(1)}, f32[96,8,3]{2,1,0:T(8,128)S(1)}, u32[]{:S(2)}, u32[]{:S(2)}) %collective-permute-start.7) | collective-permute-done | bytes 9248 | tf_op jit(solution)/shard_map/ppermute | solution.py:25
  176.6 1.0 fusion.210
  179.0 0.8 copy.84
  (277 shorter events, 10.5 us)
Async XLA Ops:
  1.8 8.0 %collective-permute-start = (bf16[96,8,3]{0,2,1:T(4,128)(2,1)S(1)}, bf16[96,8,3]{0,2,1:T(4,128)(2,1)S(1)}, u32[]{:S(2)}, u32[]{:S(2)}) collective-permute-start(bf16[96,8,3]{0,2,1:T(4,128)(2,1)S(1)} %get-tuple-element.114), channel_id=1, source_target_pairs={{0,8},{8,16},{16,24},{24,32},{32,40},{40,48},{48,56},{56,64},{64,7... | collective-permute-start | bytes 13832 | tf_op jit(solution)/shard_map/ppermute | solution.py:14
  5.6 7.1 %collective-permute-start.1 = (bf16[96,8,3]{0,2,1:T(4,128)(2,1)S(1)}, bf16[96,8,3]{0,2,1:T(4,128)(2,1)S(1)}, u32[]{:S(2)}, u32[]{:S(2)}) collective-permute-start(bf16[96,8,3]{0,2,1:T(4,128)(2,1)S(1)} %get-tuple-element.115), channel_id=1, source_target_pairs={{8,0},{16,8},{24,16},{32,24},{40,32},{48,40},{56,48},{64,56},{72,6... | collective-permute-start | bytes 13832 | tf_op jit(solution)/shard_map/ppermute | solution.py:17
  12.8 13.7 %collective-permute-start.2 = (bf16[96,3,134]{0,2,1:T(8,128)(2,1)S(1)}, bf16[96,3,134]{0,2,1:T(8,128)(2,1)S(1)}, u32[]{:S(2)}, u32[]{:S(2)}) collective-permute-start(bf16[96,3,134]{0,2,1:T(8,128)(2,1)S(1)} %get-tuple-element.112), channel_id=1, source_target_pairs={{0,1},{1,2},{2,3},{3,4},{4,5},{5,6},{6,7},{8,9},{9,10},{10,11},{11... | collective-permute-start | bytes 231560 | tf_op jit(solution)/shard_map/ppermute | solution.py:14
  22.5 11.6 %collective-permute-start.3 = (bf16[96,3,134]{0,2,1:T(8,128)(2,1)S(1)}, bf16[96,3,134]{0,2,1:T(8,128)(2,1)S(1)}, u32[]{:S(2)}, u32[]{:S(2)}) collective-permute-start(bf16[96,3,134]{0,2,1:T(8,128)(2,1)S(1)} %get-tuple-element.113), channel_id=1, source_target_pairs={{1,0},{2,1},{3,2},{4,3},{5,4},{6,5},{7,6},{9,8},{10,9},{11,10},{12... | collective-permute-start | bytes 231560 | tf_op jit(solution)/shard_map/ppermute | solution.py:17
  57.3 47.8 %copy-start.8 = (f32[96]{0:T(128)S(1)}, f32[96]{0:T(128)}, u32[]{:S(2)}) copy-start(f32[96]{0:T(128)} %copy-done.7) | copy-start | bytes 1156
  57.3 47.8 %copy-start.10 = (f32[96]{0:T(128)S(1)}, f32[96]{0:T(128)}, u32[]{:S(2)}) copy-start(f32[96]{0:T(128)} %copy-done.9) | copy-start | bytes 1156
  57.3 47.8 %copy-start.12 = (f32[96]{0:T(128)S(1)}, f32[96]{0:T(128)}, u32[]{:S(2)}) copy-start(f32[96]{0:T(128)} %copy-done.11) | copy-start | bytes 1156
  57.3 47.8 %copy-start.14 = (f32[96]{0:T(128)S(1)}, f32[96]{0:T(128)}, u32[]{:S(2)}) copy-start(f32[96]{0:T(128)} %copy-done.13) | copy-start | bytes 1156
  57.3 47.8 %copy-start.16 = (f32[96]{0:T(128)S(1)}, f32[96]{0:T(128)}, u32[]{:S(2)}) copy-start(f32[96]{0:T(128)} %copy-done.15) | copy-start | bytes 1156
  57.4 47.8 %copy-start.18 = (f32[96]{0:T(128)S(1)}, f32[96]{0:T(128)}, u32[]{:S(2)}) copy-start(f32[96]{0:T(128)} %copy-done.17) | copy-start | bytes 1156
  57.4 47.8 %copy-start.20 = (f32[96]{0:T(128)S(1)}, f32[96]{0:T(128)}, u32[]{:S(2)}) copy-start(f32[96]{0:T(128)} %copy-done.19) | copy-start | bytes 1156
  57.4 47.8 %copy-start.22 = (f32[96]{0:T(128)S(1)}, f32[96]{0:T(128)}, u32[]{:S(2)}) copy-start(f32[96]{0:T(128)} %copy-done.21) | copy-start | bytes 1156
  57.4 47.8 %copy-start.24 = (f32[96]{0:T(128)S(1)}, f32[96]{0:T(128)}, u32[]{:S(2)}) copy-start(f32[96]{0:T(128)} %copy-done.23) | copy-start | bytes 1156
  57.4 47.8 %copy-start.26 = (f32[96]{0:T(128)S(1)}, f32[96]{0:T(128)}, u32[]{:S(2)}) copy-start(f32[96]{0:T(128)} %copy-done.25) | copy-start | bytes 1156
  57.4 47.8 %copy-start.28 = (f32[96]{0:T(128)S(1)}, f32[96]{0:T(128)}, u32[]{:S(2)}) copy-start(f32[96]{0:T(128)} %copy-done.27) | copy-start | bytes 1156
  57.4 47.8 %copy-start.30 = (f32[96]{0:T(128)S(1)}, f32[96]{0:T(128)}, u32[]{:S(2)}) copy-start(f32[96]{0:T(128)} %copy-done.29) | copy-start | bytes 1156
  57.4 47.8 %copy-start.32 = (f32[96]{0:T(128)S(1)}, f32[96]{0:T(128)}, u32[]{:S(2)}) copy-start(f32[96]{0:T(128)} %copy-done.31) | copy-start | bytes 1156
  57.4 47.8 %copy-start.34 = (f32[96]{0:T(128)S(1)}, f32[96]{0:T(128)}, u32[]{:S(2)}) copy-start(f32[96]{0:T(128)} %copy-done.33) | copy-start | bytes 1156
  57.5 47.8 %copy-start.36 = (f32[96]{0:T(128)S(1)}, f32[96]{0:T(128)}, u32[]{:S(2)}) copy-start(f32[96]{0:T(128)} %copy-done.35) | copy-start | bytes 1156
  57.5 47.8 %copy-start.38 = (f32[96]{0:T(128)S(1)}, f32[96]{0:T(128)}, u32[]{:S(2)}) copy-start(f32[96]{0:T(128)} %copy-done.37) | copy-start | bytes 1156
  57.5 47.8 %copy-start.40 = (f32[96]{0:T(128)S(1)}, f32[96]{0:T(128)}, u32[]{:S(2)}) copy-start(f32[96]{0:T(128)} %copy-done.39) | copy-start | bytes 1156
  57.5 47.8 %copy-start.42 = (f32[96]{0:T(128)S(1)}, f32[96]{0:T(128)}, u32[]{:S(2)}) copy-start(f32[96]{0:T(128)} %copy-done.41) | copy-start | bytes 1156
  57.5 47.8 %copy-start.44 = (f32[96]{0:T(128)S(1)}, f32[96]{0:T(128)}, u32[]{:S(2)}) copy-start(f32[96]{0:T(128)} %copy-done.43) | copy-start | bytes 1156
  57.5 47.8 %copy-start.46 = (f32[96]{0:T(128)S(1)}, f32[96]{0:T(128)}, u32[]{:S(2)}) copy-start(f32[96]{0:T(128)} %copy-done.45) | copy-start | bytes 1156
  57.5 47.8 %copy-start.48 = (f32[96]{0:T(128)S(1)}, f32[96]{0:T(128)}, u32[]{:S(2)}) copy-start(f32[96]{0:T(128)} %copy-done.47) | copy-start | bytes 1156
  57.5 47.8 %copy-start.50 = (f32[96]{0:T(128)S(1)}, f32[96]{0:T(128)}, u32[]{:S(2)}) copy-start(f32[96]{0:T(128)} %copy-done.49) | copy-start | bytes 1156
  57.5 47.8 %copy-start.52 = (f32[96]{0:T(128)S(1)}, f32[96]{0:T(128)}, u32[]{:S(2)}) copy-start(f32[96]{0:T(128)} %copy-done.51) | copy-start | bytes 1156
  57.5 47.8 %copy-start.54 = (f32[96]{0:T(128)S(1)}, f32[96]{0:T(128)}, u32[]{:S(2)}) copy-start(f32[96]{0:T(128)} %copy-done.53) | copy-start | bytes 1156
  57.6 47.8 %copy-start.56 = (f32[96]{0:T(128)S(1)}, f32[96]{0:T(128)}, u32[]{:S(2)}) copy-start(f32[96]{0:T(128)} %copy-done.55) | copy-start | bytes 1156
  57.6 47.8 %copy-start.58 = (f32[96]{0:T(128)S(1)}, f32[96]{0:T(128)}, u32[]{:S(2)}) copy-start(f32[96]{0:T(128)} %copy-done.57) | copy-start | bytes 1156
  57.6 47.8 %copy-start.60 = (f32[96]{0:T(128)S(1)}, f32[96]{0:T(128)}, u32[]{:S(2)}) copy-start(f32[96]{0:T(128)} %copy-done.59) | copy-start | bytes 1156
  57.6 47.8 %copy-start.62 = (f32[96]{0:T(128)S(1)}, f32[96]{0:T(128)}, u32[]{:S(2)}) copy-start(f32[96]{0:T(128)} %copy-done.61) | copy-start | bytes 1156
  57.6 47.8 %copy-start.64 = (f32[96]{0:T(128)S(1)}, f32[96]{0:T(128)}, u32[]{:S(2)}) copy-start(f32[96]{0:T(128)} %copy-done.63) | copy-start | bytes 1156
  61.3 3.4 %collective-permute-start.8 = (f32[39600]{0:T(1024)S(1)}, f32[39600]{0:T(1024)S(1)}, u32[]{:S(2)}, u32[]{:S(2)}) collective-permute-start(f32[39600]{0:T(1024)S(1)} %dynamic_slice.13), channel_id=1, source_target_pairs={{0,8},{8,0},{16,24},{24,16},{32,40},{40,32},{48,56},{56,48},{64,72... | collective-permute-start | bytes 475208 | tf_op jit(solution)/shard_map/ppermute | solution.py:58
  65.0 5.7 %collective-permute-start.9 = (f32[19800]{0:T(1024)S(1)}, f32[19800]{0:T(1024)S(1)}, u32[]{:S(2)}, u32[]{:S(2)}) collective-permute-start(f32[19800]{0:T(1024)S(1)} %dynamic_slice.15), channel_id=1, source_target_pairs={{0,16},{8,24},{16,0},{24,8},{32,48},{40,56},{48,32},{56,40},{64,80... | collective-permute-start | bytes 237608 | tf_op jit(solution)/shard_map/ppermute | solution.py:58
  70.8 6.9 %collective-permute-start.10 = (f32[19800]{0:T(1024)S(1)}, f32[19800]{0:T(1024)S(1)}, u32[]{:S(2)}, u32[]{:S(2)}) collective-permute-start(f32[19800]{0:T(1024)S(1)} %dynamic-slice_add_fusion.1), channel_id=1, source_target_pairs={{0,32},{8,40},{16,48},{24,56},{32,0},{40,8},{48,16},{56,24},{64,96... | collective-permute-start | bytes 237608 | tf_op jit(solution)/shard_map/ppermute | solution.py:58
  77.7 9.5 %collective-permute-start.11 = (f32[19800]{0:T(1024)S(1)}, f32[19800]{0:T(1024)S(1)}, u32[]{:S(2)}, u32[]{:S(2)}) collective-permute-start(f32[19800]{0:T(1024)S(1)} %add.531), channel_id=1, source_target_pairs={{0,64},{8,72},{16,80},{24,88},{32,96},{40,104},{48,112},{56,120},{... | collective-permute-start | bytes 237608 | tf_op jit(solution)/shard_map/ppermute | solution.py:58
  87.2 5.2 %collective-permute-start.12 = (f32[19800]{0:T(1024)S(1)}, f32[19800]{0:T(1024)S(1)}, u32[]{:S(2)}, u32[]{:S(2)}) collective-permute-start(f32[19800]{0:T(1024)S(1)} %add.532), channel_id=1, source_target_pairs={{0,128},{8,136},{16,144},{24,152},{32,160},{40,168},{48,176},{56,1... | collective-permute-start | bytes 237608 | tf_op jit(solution)/shard_map/ppermute | solution.py:58
  92.4 7.2 %collective-permute-start.13 = (f32[19800]{0:T(1024)S(1)}, f32[19800]{0:T(1024)S(1)}, u32[]{:S(2)}, u32[]{:S(2)}) collective-permute-start(f32[19800]{0:T(1024)S(1)} %add.533), channel_id=1, source_target_pairs={{0,256},{8,264},{16,272},{24,280},{32,288},{40,296},{48,304},{56,3... | collective-permute-start | bytes 237608 | tf_op jit(solution)/shard_map/ppermute | solution.py:58
  99.6 30.0 %collective-permute-start.14 = (f32[19800]{0:T(1024)S(1)}, f32[19800]{0:T(1024)S(1)}, u32[]{:S(2)}, u32[]{:S(2)}) collective-permute-start(f32[19800]{0:T(1024)S(1)} %add.534), channel_id=1, source_target_pairs={{0,1},{1,0},{2,3},{3,2},{4,5},{5,4},{6,7},{7,6},{8,9},{9,8},{10,11... | collective-permute-start | bytes 237608 | tf_op jit(solution)/shard_map/ppermute | solution.py:58
  129.6 8.1 %collective-permute-start.15 = (f32[19800]{0:T(1024)S(1)}, f32[19800]{0:T(1024)S(1)}, u32[]{:S(2)}, u32[]{:S(2)}) collective-permute-start(f32[19800]{0:T(1024)S(1)} %add.535), channel_id=1, source_target_pairs={{0,2},{1,3},{2,0},{3,1},{4,6},{5,7},{6,4},{7,5},{8,10},{9,11},{10,... | collective-permute-start | bytes 237608 | tf_op jit(solution)/shard_map/ppermute | solution.py:58
  133.1 14.5 %collective-permute-start.4 = (bf16[96,3,134]{2,1,0:T(4,128)(2,1)S(1)}, bf16[96,3,134]{2,1,0:T(4,128)(2,1)S(1)}, u32[]{:S(2)}, u32[]{:S(2)}) collective-permute-start(bf16[96,3,134]{2,1,0:T(4,128)(2,1)S(1)} %get-tuple-element.100), channel_id=1, source_target_pairs={{0,1},{1,2},{2,3},{3,4},{4,5},{5,6},{6,7},{8,9},{9,10},{10,11},{11... | collective-permute-start | bytes 231560 | tf_op jit(solution)/shard_map/ppermute | solution.py:25
  135.7 12.9 %collective-permute-start.5 = (bf16[96,3,134]{2,1,0:T(4,128)(2,1)S(1)}, bf16[96,3,134]{2,1,0:T(4,128)(2,1)S(1)}, u32[]{:S(2)}, u32[]{:S(2)}) collective-permute-start(bf16[96,3,134]{2,1,0:T(4,128)(2,1)S(1)} %get-tuple-element.101), channel_id=1, source_target_pairs={{1,0},{2,1},{3,2},{4,3},{5,4},{6,5},{7,6},{9,8},{10,9},{11,10},{12... | collective-permute-start | bytes 231560 | tf_op jit(solution)/shard_map/ppermute | solution.py:25
  137.8 11.8 %collective-permute-start.16 = (f32[19800]{0:T(1024)S(1)}, f32[19800]{0:T(1024)S(1)}, u32[]{:S(2)}, u32[]{:S(2)}) collective-permute-start(f32[19800]{0:T(1024)S(1)} %add.536), channel_id=1, source_target_pairs={{0,4},{1,5},{2,6},{3,7},{4,0},{5,1},{6,2},{7,3},{8,12},{9,13},{10,... | collective-permute-start | bytes 237608 | tf_op jit(solution)/shard_map/ppermute | solution.py:58
  149.6 17.7 %collective-permute-start.17 = (f32[19800]{0:T(1024)S(1)}, f32[19800]{0:T(1024)S(1)}, u32[]{:S(2)}, u32[]{:S(2)}) collective-permute-start(f32[19800]{0:T(1024)S(1)} %add.537), channel_id=1, source_target_pairs={{0,16},{8,24},{16,0},{24,8},{32,48},{40,56},{48,32},{56,40},{64,80... | collective-permute-start | bytes 237608 | tf_op jit(solution)/shard_map/ppermute | solution.py:58
  154.0 16.0 %collective-permute-start.6 = (f32[96,8,3]{2,1,0:T(8,128)S(1)}, f32[96,8,3]{2,1,0:T(8,128)S(1)}, u32[]{:S(2)}, u32[]{:S(2)}) collective-permute-start(f32[96,8,3]{2,1,0:T(8,128)S(1)} %get-tuple-element.98), channel_id=1, source_target_pairs={{0,8},{8,16},{16,24},{24,32},{32,40},{40,48},{48,56},{56,64},{64,7... | collective-permute-start | bytes 27656 | tf_op jit(solution)/shard_map/ppermute | solution.py:25
  165.4 11.2 %collective-permute-start.7 = (f32[96,8,3]{2,1,0:T(8,128)S(1)}, f32[96,8,3]{2,1,0:T(8,128)S(1)}, u32[]{:S(2)}, u32[]{:S(2)}) collective-permute-start(f32[96,8,3]{2,1,0:T(8,128)S(1)} %get-tuple-element.99), channel_id=1, source_target_pairs={{8,0},{16,8},{24,16},{32,24},{40,32},{48,40},{56,48},{64,56},{72,6... | collective-permute-start | bytes 27656 | tf_op jit(solution)/shard_map/ppermute | solution.py:25
  167.4 10.1 %collective-permute-start.18 = (f32[39600]{0:T(1024)S(1)}, f32[39600]{0:T(1024)S(1)}, u32[]{:S(2)}, u32[]{:S(2)}) collective-permute-start(f32[39600]{0:T(1024)S(1)} %maximum_select_fusion.1), channel_id=1, source_target_pairs={{0,8},{8,0},{16,24},{24,16},{32,40},{40,32},{48,56},{56,48},{64,72... | collective-permute-start | bytes 475208 | tf_op jit(solution)/shard_map/ppermute | solution.py:58
  (83 other events, 1606.1 us)

commit v3 on v2

--- a/solution.py
+++ b/solution.py
@@ -149,25 +149,12 @@
     block_out = block_flat.reshape(channels, height, breadth)
     conv_grad = grad_flat.reshape(channels, height, breadth)
     flipped = dw_kernel[:, ::-1, ::-1]
-    extended = conv_seven(jnp.pad(conv_grad, ((0, 0), (6, 6), (6, 6))), flipped)
-    from_above = from_behind(extended[:, height + 3 :, :].astype(jnp.bfloat16), "row", 1).astype(
-        jnp.float32
-    )
-    from_below = from_behind(extended[:, :3, :].astype(jnp.bfloat16), "row", -1).astype(jnp.float32)
-    middle = extended[:, 3 : height + 3, :]
-    middle = (
-        middle
-        + jnp.pad(from_above, ((0, 0), (0, height - 3), (0, 0)))
-        + jnp.pad(from_below, ((0, 0), (height - 3, 0), (0, 0)))
-    )
-    from_left = from_behind(middle[:, :, breadth + 3 :], "col", 1)
-    from_right = from_behind(middle[:, :, :3], "col", -1)
-    back = middle[:, :, 3 : breadth + 3]
-    back = (
-        back
-        + jnp.pad(from_left, ((0, 0), (0, 0), (0, breadth - 3)))
-        + jnp.pad(from_right, ((0, 0), (0, 0), (breadth - 3, 0)))
-    )
+    grad_col = padded_2(conv_grad, (("col", 2),), 3)
+    grad_rows = padded_2(grad_col.astype(jnp.bfloat16), (("row", 1),), 3).astype(jnp.float32)
+    grad_padded = jnp.concatenate(
+        [grad_rows[:, :3, :], grad_col, grad_rows[:, height + 3 :, :]], axis=1
+    )
+    back = conv_seven(grad_padded, flipped)
     image_grad = (cotangent.astype(jnp.float32) + back).astype(jnp.bfloat16)
     kernel_sum = kernel_terms(conv_grad, padded)
     bias_sum = jnp.sum(conv_grad, axis=(1, 2))

time: 182 us -> 155 us (0.85); the launches traced: 182 us -> 152 us
  other arithmetic: 40 us -> 17.4 us
  waiting for transfers between devices: 38 us -> 34.4 us
    another operation x1 -> x0, other arithmetic: 24.1 us -> none
    ppermute x4 -> x0, starting transfers between devices: 17.2 us -> none  [from_behind(): lax.ppermute(value, axis, [(source, source + steps) for source in range(i...]
    ppermute x2 -> x4, starting transfers between devices: 13.5 us -> 24.7 us  [padded_2(): lax.ppermute(lax.slice_in_dim(block, block.shape[dim] - width, None, axis...]
    ppermute x4 -> x0, waiting for transfers between devices: 8.23 us -> none  [from_behind(): lax.ppermute(value, axis, [(source, source + steps) for source in range(i...]
    ppermute x11, waiting for transfers between devices: 18.8 us -> 24.2 us  [xor_partner(): lax.ppermute(value, axis, [(i, i ^ mask) for i in range(lax.axis_size(axi...]
    ppermute x2 -> x4, starting transfers between devices: 3.21 us -> 6.57 us  [padded_2(): lax.ppermute(lax.slice_in_dim(block, 0, width, axis=dim), axis, backward)]
    convert_element_type x1, other arithmetic: 0.95 us -> 3.98 us  [local(): image_grad = (cotangent.astype(jnp.float32) + back).astype(jnp.bfloat16)]
    ppermute x11, starting transfers between devices: 44.5 us -> 47.3 us  [xor_partner(): lax.ppermute(value, axis, [(i, i ^ mask) for i in range(lax.axis_size(axi...]
  transfers between devices with their start and end apart: 19 -> 19, of which waited for: 13 -> 11; matrix products, arithmetic and copies ran while one was open for 17% -> 7% of each run, Pallas kernels for 0% -> 0%
where the time goes in v3:
time: 155 us; the launch traced here: 152 us
  starting transfers between devices  78.5 us (51%)
  waiting for transfers between devices  34.4 us (22%)
  other arithmetic  17.4 us (11%)
  local copies, waits for them, and re-layouts  14.5 us (9%)
  matrix products  5.05 us (3%)
  between operations  2.41 us (2%)
    ppermute x11, starting transfers between devices, xor_partner(): lax.ppermute(value, axis, [(i, i ^ mask) for i in range(lax.axis_size(axi...  47.3 us
    ppermute x4, starting transfers between devices, padded_2(): lax.ppermute(lax.slice_in_dim(block, block.shape[dim] - width, None, axis...  24.7 us
    ppermute x11, waiting for transfers between devices, xor_partner(): lax.ppermute(value, axis, [(i, i ^ mask) for i in range(lax.axis_size(axi...  24.2 us
    ppermute x4, waiting for transfers between devices, padded_2(): lax.ppermute(lax.slice_in_dim(block, 0, width, axis=dim), axis, backward)  10.2 us
    ppermute x4, starting transfers between devices, padded_2(): lax.ppermute(lax.slice_in_dim(block, 0, width, axis=dim), axis, backward)  6.57 us
    unnamed x166, local copies, waits for them, and re-layouts  5.8 us
    dot_general x6, matrix products, product(): return jnp.einsum(form, left, right, preferred_element_type=jnp.float32)  5.05 us
    reduce_sum x4, other arithmetic, kernel_terms(): jnp.sum(conv_grad * padded[:, row_step:row_step + height, col_step:col_st...  4.87 us
  transfers between devices with their start and end apart: 19, of which 11 were waited for; matrix products, arithmetic and copies ran while one was open for 7% of the time, Pallas kernels for 0%

profile of v3, /device:TPU:57, one launch (start us, length us, event | category | flops | bytes accessed | tf_op | source)
XLA Modules:
  0.0 152.2 jit_solution(16380990868338596720)
XLA Ops:
  0.7 1.2 copy.24
  1.8 3.8 %collective-permute-start = (bf16[96,8,3]{0,2,1:T(4,128)(2,1)S(1)}, bf16[96,8,3]{0,2,1:T(4,128)(2,1)S(1)}, u32[]{:S(2)}, u32[]{:S(2)}) collective-permute-start(bf16[96,8,3]{0,2,1:T(4,128)(2,1)S(1)} %get-tuple-element.112), channel_id=1, source_target_pairs={{0,8},{8,16},{16,24},{24,32},{32,40},{40,48},{48,56},{56,64},{64,7... | collective-permute-start | bytes 13832 | tf_op jit(solution)/shard_map/ppermute | solution.py:14
  5.6 1.9 %collective-permute-start.1 = (bf16[96,8,3]{0,2,1:T(4,128)(2,1)S(1)}, bf16[96,8,3]{0,2,1:T(4,128)(2,1)S(1)}, u32[]{:S(2)}, u32[]{:S(2)}) collective-permute-start(bf16[96,8,3]{0,2,1:T(4,128)(2,1)S(1)} %get-tuple-element.113), channel_id=1, source_target_pairs={{8,0},{16,8},{24,16},{32,24},{40,32},{48,40},{56,48},{64,56},{72,6... | collective-permute-start | bytes 13832 | tf_op jit(solution)/shard_map/ppermute | solution.py:17
  7.5 1.0 slice_bitcast_fusion.48
  8.5 1.0 slice_bitcast_fusion.47
  9.6 3.0 %collective-permute-done.1 = bf16[96,8,3]{0,2,1:T(4,128)(2,1)S(1)} collective-permute-done((bf16[96,8,3]{0,2,1:T(4,128)(2,1)S(1)}, bf16[96,8,3]{0,2,1:T(4,128)(2,1)S(1)}, u32[]{:S(2)}, u32[]{:S(2)}) %collective-permute-start.1) | collective-permute-done | bytes 4640 | tf_op jit(solution)/shard_map/ppermute | solution.py:17
  12.8 9.7 %collective-permute-start.2 = (bf16[96,3,134]{0,2,1:T(8,128)(2,1)S(1)}, bf16[96,3,134]{0,2,1:T(8,128)(2,1)S(1)}, u32[]{:S(2)}, u32[]{:S(2)}) collective-permute-start(bf16[96,3,134]{0,2,1:T(8,128)(2,1)S(1)} %get-tuple-element.110), channel_id=1, source_target_pairs={{0,1},{1,2},{2,3},{3,4},{4,5},{5,6},{6,7},{8,9},{9,10},{10,11},{11... | collective-permute-start | bytes 231560 | tf_op jit(solution)/shard_map/ppermute | solution.py:14
  22.5 1.3 collective-permute-start.3
  23.8 0.9 slice_bitcast_fusion.46
  24.8 1.1 copy.32
  26.1 0.9 copy.95
  27.0 6.9 %collective-permute-done.3 = bf16[96,3,134]{0,2,1:T(8,128)(2,1)S(1)} collective-permute-done((bf16[96,3,134]{0,2,1:T(8,128)(2,1)S(1)}, bf16[96,3,134]{0,2,1:T(8,128)(2,1)S(1)}, u32[]{:S(2)}, u32[]{:S(2)}) %collective-permute-start.3) | collective-permute-done | bytes 77216 | tf_op jit(solution)/shard_map/ppermute | solution.py:17
  34.4 4.3 %fusion.180 = (f32[8,128]{1,0:T(8,128)S(1)}, f32[96,8,128]{0,2,1:T(8,128)S(1)}) fusion(f32[96]{0:T(128)S(1)} %copy-done.77, bf16[96,11,134]{0,2,1:T(8,128)(2,1)S(1)} %get-tuple-element.109, f32[96]{0:T(128)S(1)} %get-tuple-element.161, f32[96]{0:T(128)S(1)} %get-tuple-element.162, f32[96]{0:T(128)S(1)} %get-tuple-element.115, f32[96]{0:T(128)S(1)} %get-tuple-element.116, ...), kind=kLoop, calls=%fused_computation.429 | loop fusion | flops 16317440 | bytes 8879872 | tf_op jit(solution)/shard_map/reduce_sum | solution.py:100
  39.3 0.8 fusion.10
  40.2 2.0 %convert_reduce_fusion = (f32[384]{0:T(512)}, bf16[384,1024]{0,1:T(8,128)(2,1)S(1)}) fusion(f32[1024,384]{1,0:T(8,128)S(1)} %get-tuple-element.166, bf16[384,96]{0,1:T(8,128)(2,1)S(1)} %copy-done.4, f32[96,1024]{1,0:T(8,128)S(1)} %copy.97, f32[96]{0:T(128)S(1)} %copy-done.48), kind=kOutput, calls=%fused_computation.16 | convolution fusion | flops 84344448 | bytes 2828160 | tf_op jit(solution)/shard_map/hc,cp->hp/dot_general | solution.py:96
  42.5 1.0 fusion.168
  43.5 1.5 fusion.179
  45.0 1.2 copy.98
  46.2 1.1 fusion.123
  47.3 1.9 %fusion.141 = (f32[96]{0:T(128)}, f32[96]{0:T(128)}, f32[96]{0:T(128)}, f32[96]{0:T(128)}, f32[96]{0:T(128)}, /*index=5*/f32[96]{0:T(128)}, f32[96]{0:T(128)}, f...) fusion(bf16[96,11,134]{0,2,1:T(8,128)(2,1)S(1)} %get-tuple-elem, ...), kind=kLoop, calls=%fused_computation.256 | loop fusion | flops 5306688 | bytes 3939072 | tf_op jit(solution)/shard_map/reduce_sum | solution.py:48
  49.4 1.3 fusion.91
  53.2 1.6 %concatenate.149 = f32[79200]{0:T(1024)S(1)} concatenate(f32[4704]{0:T(1024)S(1)} %reshape_reshape.3, f32[96]{0:T(128)S(1)} %copy-done.52, f32[96]{0:T(128)S(1)} %copy-done.51, f32[96]{0:T(128)S(1)} %reduce_sum.577, f32[36864]{0:T(1024)S(1)} %reshape.104, f32[384]{0:T(512)S(1)} %copy-done.50, f32[36864]{0:T(1024)S(1)} %reshape.105, f32[96]{0:T(128)S(1)} %get-tuple-element.98), dimensions={0} | concatenate | bytes 633600 | tf_op jit(solution)/shard_map/concatenate | solution.py:63
  54.9 2.4 %collective-permute-start.8 = (f32[39600]{0:T(1024)S(1)}, f32[39600]{0:T(1024)S(1)}, u32[]{:S(2)}, u32[]{:S(2)}) collective-permute-start(f32[39600]{0:T(1024)S(1)} %dynamic_slice.13), channel_id=1, source_target_pairs={{0,8},{8,0},{16,24},{24,16},{32,40},{40,32},{48,56},{56,48},{64,72... | collective-permute-start | bytes 475208 | tf_op jit(solution)/shard_map/ppermute | solution.py:58
  57.4 1.0 collective-permute-done.8
  58.6 2.3 %collective-permute-start.9 = (f32[19800]{0:T(1024)S(1)}, f32[19800]{0:T(1024)S(1)}, u32[]{:S(2)}, u32[]{:S(2)}) collective-permute-start(f32[19800]{0:T(1024)S(1)} %dynamic_slice.15), channel_id=1, source_target_pairs={{0,16},{8,24},{16,0},{24,8},{32,48},{40,56},{48,32},{56,40},{64,80... | collective-permute-start | bytes 237608 | tf_op jit(solution)/shard_map/ppermute | solution.py:58
  60.9 3.2 %collective-permute-done.9 = f32[19800]{0:T(1024)S(1)} collective-permute-done((f32[19800]{0:T(1024)S(1)}, f32[19800]{0:T(1024)S(1)}, u32[]{:S(2)}, u32[]{:S(2)}) %collective-permute-start.9) | collective-permute-done | bytes 79232 | tf_op jit(solution)/shard_map/ppermute | solution.py:58
  64.2 3.1 %collective-permute-start.10 = (f32[19800]{0:T(1024)S(1)}, f32[19800]{0:T(1024)S(1)}, u32[]{:S(2)}, u32[]{:S(2)}) collective-permute-start(f32[19800]{0:T(1024)S(1)} %dynamic-slice_add_fusion.1), channel_id=1, source_target_pairs={{0,32},{8,40},{16,48},{24,56},{32,0},{40,8},{48,16},{56,24},{64,96... | collective-permute-start | bytes 237608 | tf_op jit(solution)/shard_map/ppermute | solution.py:58
  67.3 4.2 %collective-permute-done.10 = f32[19800]{0:T(1024)S(1)} collective-permute-done((f32[19800]{0:T(1024)S(1)}, f32[19800]{0:T(1024)S(1)}, u32[]{:S(2)}, u32[]{:S(2)}) %collective-permute-start.10) | collective-permute-done | bytes 79232 | tf_op jit(solution)/shard_map/ppermute | solution.py:58
  71.6 4.2 %collective-permute-start.11 = (f32[19800]{0:T(1024)S(1)}, f32[19800]{0:T(1024)S(1)}, u32[]{:S(2)}, u32[]{:S(2)}) collective-permute-start(f32[19800]{0:T(1024)S(1)} %add.505), channel_id=1, source_target_pairs={{0,64},{8,72},{16,80},{24,88},{32,96},{40,104},{48,112},{56,120},{... | collective-permute-start | bytes 237608 | tf_op jit(solution)/shard_map/ppermute | solution.py:58
  75.7 4.9 %collective-permute-done.11 = f32[19800]{0:T(1024)S(1)} collective-permute-done((f32[19800]{0:T(1024)S(1)}, f32[19800]{0:T(1024)S(1)}, u32[]{:S(2)}, u32[]{:S(2)}) %collective-permute-start.11) | collective-permute-done | bytes 79232 | tf_op jit(solution)/shard_map/ppermute | solution.py:58
  80.7 3.0 %collective-permute-start.12 = (f32[19800]{0:T(1024)S(1)}, f32[19800]{0:T(1024)S(1)}, u32[]{:S(2)}, u32[]{:S(2)}) collective-permute-start(f32[19800]{0:T(1024)S(1)} %add.506), channel_id=1, source_target_pairs={{0,128},{8,136},{16,144},{24,152},{32,160},{40,168},{48,176},{56,1... | collective-permute-start | bytes 237608 | tf_op jit(solution)/shard_map/ppermute | solution.py:58
  83.7 2.1 %collective-permute-done.12 = f32[19800]{0:T(1024)S(1)} collective-permute-done((f32[19800]{0:T(1024)S(1)}, f32[19800]{0:T(1024)S(1)}, u32[]{:S(2)}, u32[]{:S(2)}) %collective-permute-start.12) | collective-permute-done | bytes 79232 | tf_op jit(solution)/shard_map/ppermute | solution.py:58
  85.9 4.5 %collective-permute-start.13 = (f32[19800]{0:T(1024)S(1)}, f32[19800]{0:T(1024)S(1)}, u32[]{:S(2)}, u32[]{:S(2)}) collective-permute-start(f32[19800]{0:T(1024)S(1)} %add.507), channel_id=1, source_target_pairs={{0,256},{8,264},{16,272},{24,280},{32,288},{40,296},{48,304},{56,3... | collective-permute-start | bytes 237608 | tf_op jit(solution)/shard_map/ppermute | solution.py:58
  90.4 7.5 %collective-permute-start.4 = (f32[96,8,3]{0,2,1:T(4,128)S(1)}, f32[96,8,3]{0,2,1:T(4,128)S(1)}, u32[]{:S(2)}, u32[]{:S(2)}) collective-permute-start(f32[96,8,3]{0,2,1:T(4,128)S(1)} %get-tuple-element.94), channel_id=1, source_target_pairs={{0,8},{8,16},{16,24},{24,32},{32,40},{40,48},{48,56},{56,64},{64,7... | collective-permute-start | bytes 27656 | tf_op jit(solution)/shard_map/ppermute | solution.py:14
  97.9 2.1 %collective-permute-start.5 = (f32[96,8,3]{0,2,1:T(4,128)S(1)}, f32[96,8,3]{0,2,1:T(4,128)S(1)}, u32[]{:S(2)}, u32[]{:S(2)}) collective-permute-start(f32[96,8,3]{0,2,1:T(4,128)S(1)} %get-tuple-element.95), channel_id=1, source_target_pairs={{8,0},{16,8},{24,16},{32,24},{40,32},{48,40},{56,48},{64,56},{72,6... | collective-permute-start | bytes 27656 | tf_op jit(solution)/shard_map/ppermute | solution.py:17
  100.0 4.8 %collective-permute-start.14 = (f32[19800]{0:T(1024)S(1)}, f32[19800]{0:T(1024)S(1)}, u32[]{:S(2)}, u32[]{:S(2)}) collective-permute-start(f32[19800]{0:T(1024)S(1)} %add.508), channel_id=1, source_target_pairs={{0,1},{1,0},{2,3},{3,2},{4,5},{5,4},{6,7},{7,6},{8,9},{9,8},{10,11... | collective-permute-start | bytes 237608 | tf_op jit(solution)/shard_map/ppermute | solution.py:58
  105.1 4.0 %collective-permute-done.14 = f32[19800]{0:T(1024)S(1)} collective-permute-done((f32[19800]{0:T(1024)S(1)}, f32[19800]{0:T(1024)S(1)}, u32[]{:S(2)}, u32[]{:S(2)}) %collective-permute-start.14) | collective-permute-done | bytes 79232 | tf_op jit(solution)/shard_map/ppermute | solution.py:58
  109.2 4.1 %collective-permute-start.15 = (f32[19800]{0:T(1024)S(1)}, f32[19800]{0:T(1024)S(1)}, u32[]{:S(2)}, u32[]{:S(2)}) collective-permute-start(f32[19800]{0:T(1024)S(1)} %add.509), channel_id=1, source_target_pairs={{0,2},{1,3},{2,0},{3,1},{4,6},{5,7},{6,4},{7,5},{8,10},{9,11},{10,... | collective-permute-start | bytes 237608 | tf_op jit(solution)/shard_map/ppermute | solution.py:58
  113.3 3.6 %collective-permute-start.6 = (bf16[96,3,134]{0,2,1:T(8,128)(2,1)S(1)}, bf16[96,3,134]{0,2,1:T(8,128)(2,1)S(1)}, u32[]{:S(2)}, u32[]{:S(2)}) collective-permute-start(bf16[96,3,134]{0,2,1:T(8,128)(2,1)S(1)} %get-tuple-element.106), channel_id=1, source_target_pairs={{0,1},{1,2},{2,3},{3,4},{4,5},{5,6},{6,7},{8,9},{9,10},{10,11},{11... | collective-permute-start | bytes 231560 | tf_op jit(solution)/shard_map/ppermute | solution.py:14
  117.0 1.3 collective-permute-start.7
  119.0 10.7 %collective-permute-start.16 = (f32[19800]{0:T(1024)S(1)}, f32[19800]{0:T(1024)S(1)}, u32[]{:S(2)}, u32[]{:S(2)}) collective-permute-start(f32[19800]{0:T(1024)S(1)} %add.510), channel_id=1, source_target_pairs={{0,4},{1,5},{2,6},{3,7},{4,0},{5,1},{6,2},{7,3},{8,12},{9,13},{10,... | collective-permute-start | bytes 237608 | tf_op jit(solution)/shard_map/ppermute | solution.py:58
  130.0 1.7 %collective-permute-done.16 = f32[19800]{0:T(1024)S(1)} collective-permute-done((f32[19800]{0:T(1024)S(1)}, f32[19800]{0:T(1024)S(1)}, u32[]{:S(2)}, u32[]{:S(2)}) %collective-permute-start.16) | collective-permute-done | bytes 79232 | tf_op jit(solution)/shard_map/ppermute | solution.py:58
  131.7 2.0 %collective-permute-start.17 = (f32[19800]{0:T(1024)S(1)}, f32[19800]{0:T(1024)S(1)}, u32[]{:S(2)}, u32[]{:S(2)}) collective-permute-start(f32[19800]{0:T(1024)S(1)} %add.511), channel_id=1, source_target_pairs={{0,16},{8,24},{16,0},{24,8},{32,48},{40,56},{48,32},{56,40},{64,80... | collective-permute-start | bytes 237608 | tf_op jit(solution)/shard_map/ppermute | solution.py:58
  133.9 3.0 %collective-permute-done.17 = f32[19800]{0:T(1024)S(1)} collective-permute-done((f32[19800]{0:T(1024)S(1)}, f32[19800]{0:T(1024)S(1)}, u32[]{:S(2)}, u32[]{:S(2)}) %collective-permute-start.17) | collective-permute-done | bytes 79232 | tf_op jit(solution)/shard_map/ppermute | solution.py:58
  137.0 6.1 %collective-permute-start.18 = (f32[39600]{0:T(1024)S(1)}, f32[39600]{0:T(1024)S(1)}, u32[]{:S(2)}, u32[]{:S(2)}) collective-permute-start(f32[39600]{0:T(1024)S(1)} %maximum_select_fusion.1), channel_id=1, source_target_pairs={{0,8},{8,0},{16,24},{24,16},{32,40},{40,32},{48,56},{56,48},{64,72... | collective-permute-start | bytes 475208 | tf_op jit(solution)/shard_map/ppermute | solution.py:58
  143.4 4.0 %fusion.144 = bf16[96,8,128]{0,2,1:T(8,128)(2,1)S(1)} fusion(f32[96,11,134]{0,2,1:T(8,128)S(1)} %get-tuple-element.93, f32[96,8,3]{0,2,1:T(4,128)S(1)} %collective-permute-done.5, f32[96,8,128]{0,2,1:T(8,128)S(1)} %bitcast.262, f32[96,8,3]{0,2,1:T(4,128)S(1)} %collective-permute-done.4, f32[96,11,134]{0,2,1:T(8,128)S(1)} %get-tuple-element.92, ...), kind=kLoop, calls=%fused_computation.260 | loop fusion | flops 10420224 | bytes 17338752 | tf_op jit(solution)/shard_map/convert_element_type | solution.py:158
  147.4 0.8 copy.91
  149.7 0.8 copy.93
  (215 shorter events, 8.8 us)
Async XLA Ops:
  0.6 38.6 %copy-start = (bf16[96,384]{1,0:T(8,128)(2,1)S(1)}, bf16[96,384]{1,0:T(8,128)(2,1)}, u32[]{:S(2)}) copy-start(bf16[96,384]{1,0:T(8,128)(2,1)} %param.16) | copy-start | bytes 221188
  1.8 7.8 %collective-permute-start = (bf16[96,8,3]{0,2,1:T(4,128)(2,1)S(1)}, bf16[96,8,3]{0,2,1:T(4,128)(2,1)S(1)}, u32[]{:S(2)}, u32[]{:S(2)}) collective-permute-start(bf16[96,8,3]{0,2,1:T(4,128)(2,1)S(1)} %get-tuple-element.112), channel_id=1, source_target_pairs={{0,8},{8,16},{16,24},{24,32},{32,40},{40,48},{48,56},{56,64},{64,7... | collective-permute-start | bytes 13832 | tf_op jit(solution)/shard_map/ppermute | solution.py:14
  5.6 7.1 %collective-permute-start.1 = (bf16[96,8,3]{0,2,1:T(4,128)(2,1)S(1)}, bf16[96,8,3]{0,2,1:T(4,128)(2,1)S(1)}, u32[]{:S(2)}, u32[]{:S(2)}) collective-permute-start(bf16[96,8,3]{0,2,1:T(4,128)(2,1)S(1)} %get-tuple-element.113), channel_id=1, source_target_pairs={{8,0},{16,8},{24,16},{32,24},{40,32},{48,40},{56,48},{64,56},{72,6... | collective-permute-start | bytes 13832 | tf_op jit(solution)/shard_map/ppermute | solution.py:17
  9.5 24.6 %copy-start.6 = (f32[96]{0:T(128)}, f32[96]{0:T(128)S(1)}, u32[]{:S(2)}) copy-start(f32[96]{0:T(128)S(1)} %get-tuple-element.142) | copy-start | bytes 1156
  9.5 24.6 %copy-start.8 = (f32[96]{0:T(128)}, f32[96]{0:T(128)S(1)}, u32[]{:S(2)}) copy-start(f32[96]{0:T(128)S(1)} %get-tuple-element.143) | copy-start | bytes 1156
  9.6 24.6 %copy-start.10 = (f32[96]{0:T(128)}, f32[96]{0:T(128)S(1)}, u32[]{:S(2)}) copy-start(f32[96]{0:T(128)S(1)} %get-tuple-element.144) | copy-start | bytes 1156
  9.6 24.6 %copy-start.12 = (f32[96]{0:T(128)}, f32[96]{0:T(128)S(1)}, u32[]{:S(2)}) copy-start(f32[96]{0:T(128)S(1)} %get-tuple-element.145) | copy-start | bytes 1156
  9.6 24.6 %copy-start.14 = (f32[96]{0:T(128)}, f32[96]{0:T(128)S(1)}, u32[]{:S(2)}) copy-start(f32[96]{0:T(128)S(1)} %get-tuple-element.146) | copy-start | bytes 1156
  9.6 24.6 %copy-start.16 = (f32[96]{0:T(128)}, f32[96]{0:T(128)S(1)}, u32[]{:S(2)}) copy-start(f32[96]{0:T(128)S(1)} %get-tuple-element.147) | copy-start | bytes 1156
  9.6 24.6 %copy-start.18 = (f32[96]{0:T(128)}, f32[96]{0:T(128)S(1)}, u32[]{:S(2)}) copy-start(f32[96]{0:T(128)S(1)} %get-tuple-element.148) | copy-start | bytes 1156
  9.6 24.6 %copy-start.20 = (f32[96]{0:T(128)}, f32[96]{0:T(128)S(1)}, u32[]{:S(2)}) copy-start(f32[96]{0:T(128)S(1)} %get-tuple-element.149) | copy-start | bytes 1156
  9.6 24.6 %copy-start.22 = (f32[96]{0:T(128)}, f32[96]{0:T(128)S(1)}, u32[]{:S(2)}) copy-start(f32[96]{0:T(128)S(1)} %get-tuple-element.150) | copy-start | bytes 1156
  9.6 24.6 %copy-start.24 = (f32[96]{0:T(128)}, f32[96]{0:T(128)S(1)}, u32[]{:S(2)}) copy-start(f32[96]{0:T(128)S(1)} %get-tuple-element.151) | copy-start | bytes 1156
  12.8 14.2 %collective-permute-start.2 = (bf16[96,3,134]{0,2,1:T(8,128)(2,1)S(1)}, bf16[96,3,134]{0,2,1:T(8,128)(2,1)S(1)}, u32[]{:S(2)}, u32[]{:S(2)}) collective-permute-start(bf16[96,3,134]{0,2,1:T(8,128)(2,1)S(1)} %get-tuple-element.110), channel_id=1, source_target_pairs={{0,1},{1,2},{2,3},{3,4},{4,5},{5,6},{6,7},{8,9},{9,10},{10,11},{11... | collective-permute-start | bytes 231560 | tf_op jit(solution)/shard_map/ppermute | solution.py:14
  22.5 11.4 %collective-permute-start.3 = (bf16[96,3,134]{0,2,1:T(8,128)(2,1)S(1)}, bf16[96,3,134]{0,2,1:T(8,128)(2,1)S(1)}, u32[]{:S(2)}, u32[]{:S(2)}) collective-permute-start(bf16[96,3,134]{0,2,1:T(8,128)(2,1)S(1)} %get-tuple-element.111), channel_id=1, source_target_pairs={{1,0},{2,1},{3,2},{4,3},{5,4},{6,5},{7,6},{9,8},{10,9},{11,10},{12... | collective-permute-start | bytes 231560 | tf_op jit(solution)/shard_map/ppermute | solution.py:17
  54.9 3.4 %collective-permute-start.8 = (f32[39600]{0:T(1024)S(1)}, f32[39600]{0:T(1024)S(1)}, u32[]{:S(2)}, u32[]{:S(2)}) collective-permute-start(f32[39600]{0:T(1024)S(1)} %dynamic_slice.13), channel_id=1, source_target_pairs={{0,8},{8,0},{16,24},{24,16},{32,40},{40,32},{48,56},{56,48},{64,72... | collective-permute-start | bytes 475208 | tf_op jit(solution)/shard_map/ppermute | solution.py:58
  58.6 5.6 %collective-permute-start.9 = (f32[19800]{0:T(1024)S(1)}, f32[19800]{0:T(1024)S(1)}, u32[]{:S(2)}, u32[]{:S(2)}) collective-permute-start(f32[19800]{0:T(1024)S(1)} %dynamic_slice.15), channel_id=1, source_target_pairs={{0,16},{8,24},{16,0},{24,8},{32,48},{40,56},{48,32},{56,40},{64,80... | collective-permute-start | bytes 237608 | tf_op jit(solution)/shard_map/ppermute | solution.py:58
  64.2 7.3 %collective-permute-start.10 = (f32[19800]{0:T(1024)S(1)}, f32[19800]{0:T(1024)S(1)}, u32[]{:S(2)}, u32[]{:S(2)}) collective-permute-start(f32[19800]{0:T(1024)S(1)} %dynamic-slice_add_fusion.1), channel_id=1, source_target_pairs={{0,32},{8,40},{16,48},{24,56},{32,0},{40,8},{48,16},{56,24},{64,96... | collective-permute-start | bytes 237608 | tf_op jit(solution)/shard_map/ppermute | solution.py:58
  71.6 9.1 %collective-permute-start.11 = (f32[19800]{0:T(1024)S(1)}, f32[19800]{0:T(1024)S(1)}, u32[]{:S(2)}, u32[]{:S(2)}) collective-permute-start(f32[19800]{0:T(1024)S(1)} %add.505), channel_id=1, source_target_pairs={{0,64},{8,72},{16,80},{24,88},{32,96},{40,104},{48,112},{56,120},{... | collective-permute-start | bytes 237608 | tf_op jit(solution)/shard_map/ppermute | solution.py:58
  80.7 5.2 %collective-permute-start.12 = (f32[19800]{0:T(1024)S(1)}, f32[19800]{0:T(1024)S(1)}, u32[]{:S(2)}, u32[]{:S(2)}) collective-permute-start(f32[19800]{0:T(1024)S(1)} %add.506), channel_id=1, source_target_pairs={{0,128},{8,136},{16,144},{24,152},{32,160},{40,168},{48,176},{56,1... | collective-permute-start | bytes 237608 | tf_op jit(solution)/shard_map/ppermute | solution.py:58
  85.9 14.1 %collective-permute-start.13 = (f32[19800]{0:T(1024)S(1)}, f32[19800]{0:T(1024)S(1)}, u32[]{:S(2)}, u32[]{:S(2)}) collective-permute-start(f32[19800]{0:T(1024)S(1)} %add.507), channel_id=1, source_target_pairs={{0,256},{8,264},{16,272},{24,280},{32,288},{40,296},{48,304},{56,3... | collective-permute-start | bytes 237608 | tf_op jit(solution)/shard_map/ppermute | solution.py:58
  90.4 14.5 %collective-permute-start.4 = (f32[96,8,3]{0,2,1:T(4,128)S(1)}, f32[96,8,3]{0,2,1:T(4,128)S(1)}, u32[]{:S(2)}, u32[]{:S(2)}) collective-permute-start(f32[96,8,3]{0,2,1:T(4,128)S(1)} %get-tuple-element.94), channel_id=1, source_target_pairs={{0,8},{8,16},{16,24},{24,32},{32,40},{40,48},{48,56},{56,64},{64,7... | collective-permute-start | bytes 27656 | tf_op jit(solution)/shard_map/ppermute | solution.py:14
  97.9 7.2 %collective-permute-start.5 = (f32[96,8,3]{0,2,1:T(4,128)S(1)}, f32[96,8,3]{0,2,1:T(4,128)S(1)}, u32[]{:S(2)}, u32[]{:S(2)}) collective-permute-start(f32[96,8,3]{0,2,1:T(4,128)S(1)} %get-tuple-element.95), channel_id=1, source_target_pairs={{8,0},{16,8},{24,16},{32,24},{40,32},{48,40},{56,48},{64,56},{72,6... | collective-permute-start | bytes 27656 | tf_op jit(solution)/shard_map/ppermute | solution.py:17
  100.0 9.2 %collective-permute-start.14 = (f32[19800]{0:T(1024)S(1)}, f32[19800]{0:T(1024)S(1)}, u32[]{:S(2)}, u32[]{:S(2)}) collective-permute-start(f32[19800]{0:T(1024)S(1)} %add.508), channel_id=1, source_target_pairs={{0,1},{1,0},{2,3},{3,2},{4,5},{5,4},{6,7},{7,6},{8,9},{9,8},{10,11... | collective-permute-start | bytes 237608 | tf_op jit(solution)/shard_map/ppermute | solution.py:58
  109.2 9.8 %collective-permute-start.15 = (f32[19800]{0:T(1024)S(1)}, f32[19800]{0:T(1024)S(1)}, u32[]{:S(2)}, u32[]{:S(2)}) collective-permute-start(f32[19800]{0:T(1024)S(1)} %add.509), channel_id=1, source_target_pairs={{0,2},{1,3},{2,0},{3,1},{4,6},{5,7},{6,4},{7,5},{8,10},{9,11},{10,... | collective-permute-start | bytes 237608 | tf_op jit(solution)/shard_map/ppermute | solution.py:58
  113.3 16.4 %collective-permute-start.6 = (bf16[96,3,134]{0,2,1:T(8,128)(2,1)S(1)}, bf16[96,3,134]{0,2,1:T(8,128)(2,1)S(1)}, u32[]{:S(2)}, u32[]{:S(2)}) collective-permute-start(bf16[96,3,134]{0,2,1:T(8,128)(2,1)S(1)} %get-tuple-element.106), channel_id=1, source_target_pairs={{0,1},{1,2},{2,3},{3,4},{4,5},{5,6},{6,7},{8,9},{9,10},{10,11},{11... | collective-permute-start | bytes 231560 | tf_op jit(solution)/shard_map/ppermute | solution.py:14
  117.0 12.8 %collective-permute-start.7 = (bf16[96,3,134]{0,2,1:T(8,128)(2,1)S(1)}, bf16[96,3,134]{0,2,1:T(8,128)(2,1)S(1)}, u32[]{:S(2)}, u32[]{:S(2)}) collective-permute-start(bf16[96,3,134]{0,2,1:T(8,128)(2,1)S(1)} %get-tuple-element.107), channel_id=1, source_target_pairs={{1,0},{2,1},{3,2},{4,3},{5,4},{6,5},{7,6},{9,8},{10,9},{11,10},{12... | collective-permute-start | bytes 231560 | tf_op jit(solution)/shard_map/ppermute | solution.py:17
  119.0 12.7 %collective-permute-start.16 = (f32[19800]{0:T(1024)S(1)}, f32[19800]{0:T(1024)S(1)}, u32[]{:S(2)}, u32[]{:S(2)}) collective-permute-start(f32[19800]{0:T(1024)S(1)} %add.510), channel_id=1, source_target_pairs={{0,4},{1,5},{2,6},{3,7},{4,0},{5,1},{6,2},{7,3},{8,12},{9,13},{10,... | collective-permute-start | bytes 237608 | tf_op jit(solution)/shard_map/ppermute | solution.py:58
  129.8 13.3 %copy-start.2 = (bf16[96,8,128]{0,2,1:T(8,128)(2,1)S(1)}, bf16[96,8,128]{0,2,1:T(8,128)(2,1)}, u32[]{:S(2)}) copy-start(bf16[96,8,128]{0,2,1:T(8,128)(2,1)} %copy-done.1) | copy-start | bytes 589828
  129.8 13.3 %copy-start.7 = (f32[96]{0:T(128)S(1)}, f32[96]{0:T(128)}, u32[]{:S(2)}) copy-start(f32[96]{0:T(128)} %copy-done.6) | copy-start | bytes 1156
  129.8 13.3 %copy-start.9 = (f32[96]{0:T(128)S(1)}, f32[96]{0:T(128)}, u32[]{:S(2)}) copy-start(f32[96]{0:T(128)} %copy-done.8) | copy-start | bytes 1156
  129.8 13.3 %copy-start.11 = (f32[96]{0:T(128)S(1)}, f32[96]{0:T(128)}, u32[]{:S(2)}) copy-start(f32[96]{0:T(128)} %copy-done.10) | copy-start | bytes 1156
  129.9 13.3 %copy-start.13 = (f32[96]{0:T(128)S(1)}, f32[96]{0:T(128)}, u32[]{:S(2)}) copy-start(f32[96]{0:T(128)} %copy-done.12) | copy-start | bytes 1156
  129.9 13.3 %copy-start.15 = (f32[96]{0:T(128)S(1)}, f32[96]{0:T(128)}, u32[]{:S(2)}) copy-start(f32[96]{0:T(128)} %copy-done.14) | copy-start | bytes 1156
  129.9 13.3 %copy-start.17 = (f32[96]{0:T(128)S(1)}, f32[96]{0:T(128)}, u32[]{:S(2)}) copy-start(f32[96]{0:T(128)} %copy-done.16) | copy-start | bytes 1156
  129.9 13.3 %copy-start.19 = (f32[96]{0:T(128)S(1)}, f32[96]{0:T(128)}, u32[]{:S(2)}) copy-start(f32[96]{0:T(128)} %copy-done.18) | copy-start | bytes 1156
  129.9 13.3 %copy-start.21 = (f32[96]{0:T(128)S(1)}, f32[96]{0:T(128)}, u32[]{:S(2)}) copy-start(f32[96]{0:T(128)} %copy-done.20) | copy-start | bytes 1156
  129.9 13.3 %copy-start.23 = (f32[96]{0:T(128)S(1)}, f32[96]{0:T(128)}, u32[]{:S(2)}) copy-start(f32[96]{0:T(128)} %copy-done.22) | copy-start | bytes 1156
  129.9 13.3 %copy-start.25 = (f32[96]{0:T(128)S(1)}, f32[96]{0:T(128)}, u32[]{:S(2)}) copy-start(f32[96]{0:T(128)} %copy-done.24) | copy-start | bytes 1156
  129.9 13.3 %copy-start.27 = (f32[96]{0:T(128)S(1)}, f32[96]{0:T(128)}, u32[]{:S(2)}) copy-start(f32[96]{0:T(128)} %copy-done.26) | copy-start | bytes 1156
  129.9 13.3 %copy-start.29 = (f32[96]{0:T(128)S(1)}, f32[96]{0:T(128)}, u32[]{:S(2)}) copy-start(f32[96]{0:T(128)} %copy-done.28) | copy-start | bytes 1156
  129.9 13.3 %copy-start.31 = (f32[96]{0:T(128)S(1)}, f32[96]{0:T(128)}, u32[]{:S(2)}) copy-start(f32[96]{0:T(128)} %copy-done.30) | copy-start | bytes 1156
  130.0 13.3 %copy-start.33 = (f32[96]{0:T(128)S(1)}, f32[96]{0:T(128)}, u32[]{:S(2)}) copy-start(f32[96]{0:T(128)} %copy-done.32) | copy-start | bytes 1156
  130.0 13.3 %copy-start.35 = (f32[96]{0:T(128)S(1)}, f32[96]{0:T(128)}, u32[]{:S(2)}) copy-start(f32[96]{0:T(128)} %copy-done.34) | copy-start | bytes 1156
  130.0 13.3 %copy-start.37 = (f32[96]{0:T(128)S(1)}, f32[96]{0:T(128)}, u32[]{:S(2)}) copy-start(f32[96]{0:T(128)} %copy-done.36) | copy-start | bytes 1156
  130.0 13.3 %copy-start.39 = (f32[96]{0:T(128)S(1)}, f32[96]{0:T(128)}, u32[]{:S(2)}) copy-start(f32[96]{0:T(128)} %copy-done.38) | copy-start | bytes 1156
  131.7 5.2 %collective-permute-start.17 = (f32[19800]{0:T(1024)S(1)}, f32[19800]{0:T(1024)S(1)}, u32[]{:S(2)}, u32[]{:S(2)}) collective-permute-start(f32[19800]{0:T(1024)S(1)} %add.511), channel_id=1, source_target_pairs={{0,16},{8,24},{16,0},{24,8},{32,48},{40,56},{48,32},{56,40},{64,80... | collective-permute-start | bytes 237608 | tf_op jit(solution)/shard_map/ppermute | solution.py:58
  137.0 11.2 %collective-permute-start.18 = (f32[39600]{0:T(1024)S(1)}, f32[39600]{0:T(1024)S(1)}, u32[]{:S(2)}, u32[]{:S(2)}) collective-permute-start(f32[39600]{0:T(1024)S(1)} %maximum_select_fusion.1), channel_id=1, source_target_pairs={{0,8},{8,0},{16,24},{24,16},{32,40},{40,32},{48,56},{56,48},{64,72... | collective-permute-start | bytes 475208 | tf_op jit(solution)/shard_map/ppermute | solution.py:58
  (51 other events, 250.8 us)

commit v4 on v3

--- a/solution.py
+++ b/solution.py
@@ -132,22 +132,43 @@
 def local(image, cotangent, dw_kernel, dw_bias, ln_gain, ln_bias, w_in, b_in, w_out, layer_scale):
     channels, height, breadth = image.shape
     pixels = height * breadth
-    padded = padded_2(image, (("col", 2), ("row", 1)), 3)
-    conv_out = conv_seven(padded, dw_kernel) + dw_bias[:, None, None]
-    block_flat, grad_flat, sums = mixing(
-        conv_out.reshape(channels, pixels),
-        image.reshape(channels, pixels),
-        cotangent.reshape(channels, pixels),
-        ln_gain,
-        ln_bias,
-        w_in,
-        b_in,
-        w_out,
-        layer_scale,
-    )
+    padded_c = padded_2(image, (("col", 2),), 3)
+    count = lax.axis_size("row")
+    forward = [(i, i + 1) for i in range(count - 1)]
+    backward = [(target, source) for source, target in forward]
+    above = lax.ppermute(padded_c[:, height - 3 :, :], "row", forward)
+    below = lax.ppermute(padded_c[:, :3, :], "row", backward)
+    padded = jnp.concatenate([above, padded_c, below], axis=1)
+    bias = dw_bias[:, None, None]
+    conv_mid = conv_seven(padded_c, dw_kernel) + bias
+    conv_top = conv_seven(jnp.concatenate([above, padded_c[:, :6, :]], axis=1), dw_kernel) + bias
+    conv_bot = (
+        conv_seven(jnp.concatenate([padded_c[:, height - 6 :, :], below], axis=1), dw_kernel) + bias
+    )
+    params = (ln_gain, ln_bias, w_in, b_in, w_out, layer_scale)
+
+    def flat(field):
+        return field.reshape(channels, -1)
+
+    def edges(field):
+        return jnp.concatenate([field[:, :3, :], field[:, height - 3 :, :]], axis=1)
+
+    mid_out, mid_grad, mid_sums = mixing(
+        flat(conv_mid), flat(image[:, 3 : height - 3, :]), flat(cotangent[:, 3 : height - 3, :]), *params
+    )
+    edge_out, edge_grad, edge_sums = mixing(
+        flat(jnp.concatenate([conv_top, conv_bot], axis=1)), flat(edges(image)), flat(edges(cotangent)), *params
+    )
+    sums = tuple(x + y for x, y in zip(edge_sums, mid_sums))
     gain_sum, shift_sum, w_in_sum, b_in_sum, w_out_sum, scale_sum = sums
-    block_out = block_flat.reshape(channels, height, breadth)
-    conv_grad = grad_flat.reshape(channels, height, breadth)
+
+    def assemble(edge_flat, mid_flat):
+        edge_rows = edge_flat.reshape(channels, 6, breadth)
+        mid_rows = mid_flat.reshape(channels, height - 6, breadth)
+        return jnp.concatenate([edge_rows[:, :3], mid_rows, edge_rows[:, 3:]], axis=1)
+
+    block_out = assemble(edge_out, mid_out)
+    conv_grad = assemble(edge_grad, mid_grad)
     flipped = dw_kernel[:, ::-1, ::-1]
     grad_col = padded_2(conv_grad, (("col", 2),), 3)
     grad_rows = padded_2(grad_col.astype(jnp.bfloat16), (("row", 1),), 3).astype(jnp.float32)

time: 155 us -> 166 us (1.071)
  other arithmetic: 17.4 us -> 27.1 us
  matrix products: 5.05 us -> 10.1 us
  waiting for transfers between devices: 34.4 us -> 39 us
  starting transfers between devices: 78.5 us -> 74.2 us
  local copies, waits for them, and re-layouts: 14.5 us -> 11 us
    ppermute x0 -> x2, starting transfers between devices: none -> 12.1 us  [the longest x1 10.7 us: local(): above = lax.ppermute(padded_c[:, height - 3:, :], 'row', forward)]
    ppermute x4 -> x3, starting transfers between devices: 24.7 us -> 14 us  [padded_2(): lax.ppermute(lax.slice_in_dim(block, block.shape[dim] - width, None, axis...]
    ppermute x4 -> x3, waiting for transfers between devices: 10.2 us -> 0.01 us  [padded_2(): lax.ppermute(lax.slice_in_dim(block, 0, width, axis=dim), axis, backward)]
    ppermute x0 -> x2, waiting for transfers between devices: none -> 7.69 us  [the longest x1 7.69 us: local(): below = lax.ppermute(padded_c[:, :3, :], 'row', backward)]
    ppermute x11, waiting for transfers between devices: 24.2 us -> 31.3 us  [xor_partner(): lax.ppermute(value, axis, [(i, i ^ mask) for i in range(lax.axis_size(axi...]
    add x0 -> x6, other arithmetic: none -> 5.68 us  [the longest x1 2.94 us: local(): conv_seven(jnp.concatenate([padded_c[:, height - 6:, :], below], axis=1),...]
    ppermute x11, starting transfers between devices: 47.3 us -> 42 us  [xor_partner(): lax.ppermute(value, axis, [(i, i ^ mask) for i in range(lax.axis_size(axi...]
    dot_general x6 -> x12, matrix products: 5.05 us -> 10.1 us  [product(): return jnp.einsum(form, left, right, preferred_element_type=jnp.float32)]
  transfers between devices with their start and end apart: 19 -> 19, of which waited for: 11 -> 9; matrix products, arithmetic and copies ran while one was open for 7% -> 10% of each run, Pallas kernels for 0% -> 0%
where the time goes in v4:
time: 166 us; the launch traced here: 164 us
  starting transfers between devices  74.2 us (45%)
  waiting for transfers between devices  39 us (23%)
  other arithmetic  27.1 us (16%)
  local copies, waits for them, and re-layouts  11 us (7%)
  matrix products  10.1 us (6%)
  between operations  3.03 us (2%)
    ppermute x11, starting transfers between devices, xor_partner(): lax.ppermute(value, axis, [(i, i ^ mask) for i in range(lax.axis_size(axi...  42 us
    ppermute x11, waiting for transfers between devices, xor_partner(): lax.ppermute(value, axis, [(i, i ^ mask) for i in range(lax.axis_size(axi...  31.3 us
    ppermute x3, starting transfers between devices, padded_2(): lax.ppermute(lax.slice_in_dim(block, block.shape[dim] - width, None, axis...  14 us
    ppermute x1, starting transfers between devices, local(): above = lax.ppermute(padded_c[:, height - 3:, :], 'row', forward)  10.7 us
    dot_general x12, matrix products, product(): return jnp.einsum(form, left, right, preferred_element_type=jnp.float32)  10.1 us
    ppermute x1, waiting for transfers between devices, local(): below = lax.ppermute(padded_c[:, :3, :], 'row', backward)  7.69 us
    convert_element_type x1, other arithmetic, local(): image_grad = (cotangent.astype(jnp.float32) + back).astype(jnp.bfloat16)  6.52 us
    ppermute x3, starting transfers between devices, padded_2(): lax.ppermute(lax.slice_in_dim(block, 0, width, axis=dim), axis, backward)  6.02 us
  transfers between devices with their start and end apart: 19, of which 9 were waited for; matrix products, arithmetic and copies ran while one was open for 10% of the time, Pallas kernels for 0%

profile of v4, /device:TPU:57, one launch (start us, length us, event | category | flops | bytes accessed | tf_op | source)
XLA Modules:
  0.0 164.4 jit_solution(502689378195233334)
XLA Ops:
  0.7 1.0 constant_dynamic-update-slice_fusion.1
  1.8 2.6 %collective-permute-start.1 = (bf16[96,8,3]{2,0,1:T(8,128)(2,1)S(1)}, bf16[96,8,3]{2,0,1:T(8,128)(2,1)S(1)}, u32[]{:S(2)}, u32[]{:S(2)}) collective-permute-start(bf16[96,8,3]{2,0,1:T(8,128)(2,1)S(1)} %get-tuple-element.163), channel_id=1, source_target_pairs={{8,0},{16,8},{24,16},{32,24},{40,32},{48,40},{56,48},{64,56},{72,6... | collective-permute-start | bytes 13832 | tf_op jit(solution)/shard_map/ppermute | solution.py:17
  4.4 5.1 %collective-permute-start = (bf16[96,8,3]{2,0,1:T(8,128)(2,1)S(1)}, bf16[96,8,3]{2,0,1:T(8,128)(2,1)S(1)}, u32[]{:S(2)}, u32[]{:S(2)}) collective-permute-start(bf16[96,8,3]{2,0,1:T(8,128)(2,1)S(1)} %get-tuple-element.162), channel_id=1, source_target_pairs={{0,8},{8,16},{16,24},{24,32},{32,40},{40,48},{48,56},{56,64},{64,7... | collective-permute-start | bytes 13832 | tf_op jit(solution)/shard_map/ppermute | solution.py:14
  11.3 0.8 maximum_convert_fusion.1
  13.0 2.3 %fusion.234 = (f32[2,128]{1,0:T(2,128)S(1)}, f32[96,2,128]{2,0,1:T(8,128)S(1)}) fusion(f32[96]{0:T(128)S(1)} %copy-done.97, bf16[96,8,131]{2,0,1:T(8,128)(2,1)S(1)} %constant_dynamic-update-slice_fusion, f32[96]{0:T(128)S(1)} %get-tuple-element.215, f32[96]{0:T(128)} %get-tuple-element.216, f32[96]{0:T(128)S(1)} %get-tuple-element.169, ...), kind=kLoop, calls=%fused_computation.626 | loop fusion | flops 5185280 | bytes 1894272 | tf_op jit(solution)/shard_map/reduce_sum | solution.py:100
  15.9 1.1 convert_reduce_fusion.1
  16.9 0.9 fusion.231
  18.0 0.9 fusion.226
  18.9 1.5 fusion.153
  20.4 10.7 %collective-permute-start.2 = (bf16[96,3,134]{2,0,1:T(8,128)(2,1)S(1)}, bf16[96,3,134]{2,0,1:T(8,128)(2,1)S(1)}, u32[]{:S(2)}, u32[]{:S(2)}) collective-permute-start(bf16[96,3,134]{2,0,1:T(8,128)(2,1)S(1)} %get-tuple-element.141), channel_id=1, source_target_pairs={{0,1},{1,2},{2,3},{3,4},{4,5},{5,6},{6,7},{8,9},{9,10},{10,11},{11... | collective-permute-start | bytes 231560 | tf_op jit(solution)/shard_map/ppermute | solution.py:139
  31.0 1.5 collective-permute-start.3
  33.2 1.3 fusion.156
  34.6 2.7 %fusion.100 = f32[96,3,128]{2,0,1:T(8,128)S(1)} fusion(bf16[96,6,134]{2,0,1:T(8,128)(2,1)S(1)} %get-tuple-element.143, bf16[96,3,134]{2,0,1:T(8,128)(2,1)S(1)} %collective-permute-done.2, bf16[96,8,3]{2,0,1:T(8,128)(2,1)S(1)} %collective-permute-done, bf16[96,8,128]{2,0,1:T(8,128)(2,1)S(1)} %get-tuple-element.161, ...), kind=kLoop, calls=%fused_computation.403 | loop fusion | flops 8294400 | bytes 2704256 | tf_op jit(solution)/shard_map/add | solution.py:144
  37.3 7.7 %collective-permute-done.3 = bf16[96,3,134]{2,0,1:T(8,128)(2,1)S(1)} collective-permute-done((bf16[96,3,134]{2,0,1:T(8,128)(2,1)S(1)}, bf16[96,3,134]{2,0,1:T(8,128)(2,1)S(1)}, u32[]{:S(2)}, u32[]{:S(2)}) %collective-permute-start.3) | collective-permute-done | bytes 77216 | tf_op jit(solution)/shard_map/ppermute | solution.py:140
  45.4 2.9 %add_add_fusion = f32[96,3,128]{2,0,1:T(8,128)S(1)} fusion(bf16[96,6,134]{2,0,1:T(8,128)(2,1)S(1)} %get-tuple-element.144, bf16[96,3,134]{2,0,1:T(8,128)(2,1)S(1)} %collective-permute-done.3, bf16[96,8,3]{2,0,1:T(8,128)(2,1)S(1)} %collective-permute-done, bf16[96,8,128]{2,0,1:T(8,128)(2,1)S(1)} %get-tuple-element.161, ...), kind=kLoop, calls=%fused_computation.437 | loop fusion | flops 8294400 | bytes 2704256 | tf_op jit(solution)/shard_map/add | solution.py:146
  49.3 1.7 %convert_reduce_fusion = (f32[384]{0:T(512)}, bf16[384,768]{0,1:T(8,128)(2,1)S(1)}) fusion(f32[384,768]{0,1:T(8,128)S(1)} %fusion, bf16[384,96]{0,1:T(8,128)(2,1)S(1)} %copy-done.13, f32[12,8,6,128]{3,2,1,0:T(8,128)S(1)} %bitcast.303, f32[96]{0:T(128)S(1)} %copy-done.106), kind=kOutput, calls=%fused_computation.123 | convolution fusion | flops 63258240 | bytes 2140032 | tf_op jit(solution)/shard_map/hc,cp->hp/dot_general | solution.py:96
  51.0 0.9 fusion.80
  53.7 0.8 slice_reduce_fusion.1
  55.0 1.3 multiply_reduce_fusion
  56.3 1.3 multiply_reduce_fusion.28
  57.7 1.1 multiply_reduce_fusion.18
  60.4 1.3 fusion.77
  61.8 1.6 concatenate.267
  63.5 3.2 %collective-permute-start.8 = (f32[39600]{0:T(1024)S(1)}, f32[39600]{0:T(1024)S(1)}, u32[]{:S(2)}, u32[]{:S(2)}) collective-permute-start(f32[39600]{0:T(1024)S(1)} %dynamic_slice.13), channel_id=1, source_target_pairs={{0,8},{8,0},{16,24},{24,16},{32,40},{40,32},{48,56},{56,48},{64,72... | collective-permute-start | bytes 475208 | tf_op jit(solution)/shard_map/ppermute | solution.py:58
  66.7 1.0 collective-permute-done.8
  67.9 1.9 %collective-permute-start.9 = (f32[19800]{0:T(1024)S(1)}, f32[19800]{0:T(1024)S(1)}, u32[]{:S(2)}, u32[]{:S(2)}) collective-permute-start(f32[19800]{0:T(1024)S(1)} %dynamic_slice.15), channel_id=1, source_target_pairs={{0,16},{8,24},{16,0},{24,8},{32,48},{40,56},{48,32},{56,40},{64,80... | collective-permute-start | bytes 237608 | tf_op jit(solution)/shard_map/ppermute | solution.py:58
  69.9 3.6 %collective-permute-done.9 = f32[19800]{0:T(1024)S(1)} collective-permute-done((f32[19800]{0:T(1024)S(1)}, f32[19800]{0:T(1024)S(1)}, u32[]{:S(2)}, u32[]{:S(2)}) %collective-permute-start.9) | collective-permute-done | bytes 79232 | tf_op jit(solution)/shard_map/ppermute | solution.py:58
  73.6 1.9 %collective-permute-start.10 = (f32[19800]{0:T(1024)S(1)}, f32[19800]{0:T(1024)S(1)}, u32[]{:S(2)}, u32[]{:S(2)}) collective-permute-start(f32[19800]{0:T(1024)S(1)} %dynamic-slice_add_fusion.1), channel_id=1, source_target_pairs={{0,32},{8,40},{16,48},{24,56},{32,0},{40,8},{48,16},{56,24},{64,96... | collective-permute-start | bytes 237608 | tf_op jit(solution)/shard_map/ppermute | solution.py:58
  75.5 6.5 %collective-permute-done.10 = f32[19800]{0:T(1024)S(1)} collective-permute-done((f32[19800]{0:T(1024)S(1)}, f32[19800]{0:T(1024)S(1)}, u32[]{:S(2)}, u32[]{:S(2)}) %collective-permute-start.10) | collective-permute-done | bytes 79232 | tf_op jit(solution)/shard_map/ppermute | solution.py:58
  82.0 3.6 %collective-permute-start.11 = (f32[19800]{0:T(1024)S(1)}, f32[19800]{0:T(1024)S(1)}, u32[]{:S(2)}, u32[]{:S(2)}) collective-permute-start(f32[19800]{0:T(1024)S(1)} %add.981), channel_id=1, source_target_pairs={{0,64},{8,72},{16,80},{24,88},{32,96},{40,104},{48,112},{56,120},{... | collective-permute-start | bytes 237608 | tf_op jit(solution)/shard_map/ppermute | solution.py:58
  85.9 6.2 %collective-permute-start.4 = (f32[96,8,3]{2,0,1:T(8,128)S(1)}, f32[96,8,3]{2,0,1:T(8,128)S(1)}, u32[]{:S(2)}, u32[]{:S(2)}) collective-permute-start(f32[96,8,3]{2,0,1:T(8,128)S(1)} %get-tuple-element.139), channel_id=1, source_target_pairs={{0,8},{8,16},{16,24},{24,32},{32,40},{40,48},{48,56},{56,64},{64,7... | collective-permute-start | bytes 27656 | tf_op jit(solution)/shard_map/ppermute | solution.py:14
  92.0 2.1 %collective-permute-start.5 = (f32[96,8,3]{2,0,1:T(8,128)S(1)}, f32[96,8,3]{2,0,1:T(8,128)S(1)}, u32[]{:S(2)}, u32[]{:S(2)}) collective-permute-start(f32[96,8,3]{2,0,1:T(8,128)S(1)} %get-tuple-element.140), channel_id=1, source_target_pairs={{8,0},{16,8},{24,16},{32,24},{40,32},{48,40},{56,48},{64,56},{72,6... | collective-permute-start | bytes 27656 | tf_op jit(solution)/shard_map/ppermute | solution.py:17
  94.4 2.2 %collective-permute-start.12 = (f32[19800]{0:T(1024)S(1)}, f32[19800]{0:T(1024)S(1)}, u32[]{:S(2)}, u32[]{:S(2)}) collective-permute-start(f32[19800]{0:T(1024)S(1)} %add.982), channel_id=1, source_target_pairs={{0,128},{8,136},{16,144},{24,152},{32,160},{40,168},{48,176},{56,1... | collective-permute-start | bytes 237608 | tf_op jit(solution)/shard_map/ppermute | solution.py:58
  96.7 7.6 %collective-permute-done.12 = f32[19800]{0:T(1024)S(1)} collective-permute-done((f32[19800]{0:T(1024)S(1)}, f32[19800]{0:T(1024)S(1)}, u32[]{:S(2)}, u32[]{:S(2)}) %collective-permute-start.12) | collective-permute-done | bytes 79232 | tf_op jit(solution)/shard_map/ppermute | solution.py:58
  104.3 1.9 %collective-permute-start.13 = (f32[19800]{0:T(1024)S(1)}, f32[19800]{0:T(1024)S(1)}, u32[]{:S(2)}, u32[]{:S(2)}) collective-permute-start(f32[19800]{0:T(1024)S(1)} %add.983), channel_id=1, source_target_pairs={{0,256},{8,264},{16,272},{24,280},{32,288},{40,296},{48,304},{56,3... | collective-permute-start | bytes 237608 | tf_op jit(solution)/shard_map/ppermute | solution.py:58
  106.6 6.0 %collective-permute-done.13 = f32[19800]{0:T(1024)S(1)} collective-permute-done((f32[19800]{0:T(1024)S(1)}, f32[19800]{0:T(1024)S(1)}, u32[]{:S(2)}, u32[]{:S(2)}) %collective-permute-start.13) | collective-permute-done | bytes 79232 | tf_op jit(solution)/shard_map/ppermute | solution.py:58
  112.6 6.4 %collective-permute-start.14 = (f32[19800]{0:T(1024)S(1)}, f32[19800]{0:T(1024)S(1)}, u32[]{:S(2)}, u32[]{:S(2)}) collective-permute-start(f32[19800]{0:T(1024)S(1)} %add.984), channel_id=1, source_target_pairs={{0,1},{1,0},{2,3},{3,2},{4,5},{5,4},{6,7},{7,6},{8,9},{9,8},{10,11... | collective-permute-start | bytes 237608 | tf_op jit(solution)/shard_map/ppermute | solution.py:58
  119.0 2.8 %collective-permute-start.6 = (bf16[96,3,134]{2,0,1:T(8,128)(2,1)S(1)}, bf16[96,3,134]{2,0,1:T(8,128)(2,1)S(1)}, u32[]{:S(2)}, u32[]{:S(2)}) collective-permute-start(bf16[96,3,134]{2,0,1:T(8,128)(2,1)S(1)} %get-tuple-element.137), channel_id=1, source_target_pairs={{0,1},{1,2},{2,3},{3,4},{4,5},{5,6},{6,7},{8,9},{9,10},{10,11},{11... | collective-permute-start | bytes 231560 | tf_op jit(solution)/shard_map/ppermute | solution.py:14
  121.8 1.3 collective-permute-start.7
  123.1 9.1 %collective-permute-start.15 = (f32[19800]{0:T(1024)S(1)}, f32[19800]{0:T(1024)S(1)}, u32[]{:S(2)}, u32[]{:S(2)}) collective-permute-start(f32[19800]{0:T(1024)S(1)} %add.985), channel_id=1, source_target_pairs={{0,2},{1,3},{2,0},{3,1},{4,6},{5,7},{6,4},{7,5},{8,10},{9,11},{10,... | collective-permute-start | bytes 237608 | tf_op jit(solution)/shard_map/ppermute | solution.py:58
  132.2 0.8 pad_maximum_fusion.7
  133.1 1.2 collective-permute-done.15
  134.3 3.3 %collective-permute-start.16 = (f32[19800]{0:T(1024)S(1)}, f32[19800]{0:T(1024)S(1)}, u32[]{:S(2)}, u32[]{:S(2)}) collective-permute-start(f32[19800]{0:T(1024)S(1)} %add.986), channel_id=1, source_target_pairs={{0,4},{1,5},{2,6},{3,7},{4,0},{5,1},{6,2},{7,3},{8,12},{9,13},{10,... | collective-permute-start | bytes 237608 | tf_op jit(solution)/shard_map/ppermute | solution.py:58
  137.7 3.3 %collective-permute-done.16 = f32[19800]{0:T(1024)S(1)} collective-permute-done((f32[19800]{0:T(1024)S(1)}, f32[19800]{0:T(1024)S(1)}, u32[]{:S(2)}, u32[]{:S(2)}) %collective-permute-start.16) | collective-permute-done | bytes 79232 | tf_op jit(solution)/shard_map/ppermute | solution.py:58
  141.0 1.9 %collective-permute-start.17 = (f32[19800]{0:T(1024)S(1)}, f32[19800]{0:T(1024)S(1)}, u32[]{:S(2)}, u32[]{:S(2)}) collective-permute-start(f32[19800]{0:T(1024)S(1)} %add.987), channel_id=1, source_target_pairs={{0,16},{8,24},{16,0},{24,8},{32,48},{40,56},{48,32},{56,40},{64,80... | collective-permute-start | bytes 237608 | tf_op jit(solution)/shard_map/ppermute | solution.py:58
  144.0 2.2 %collective-permute-done.17 = f32[19800]{0:T(1024)S(1)} collective-permute-done((f32[19800]{0:T(1024)S(1)}, f32[19800]{0:T(1024)S(1)}, u32[]{:S(2)}, u32[]{:S(2)}) %collective-permute-start.17) | collective-permute-done | bytes 79232 | tf_op jit(solution)/shard_map/ppermute | solution.py:58
  146.3 6.4 %collective-permute-start.18 = (f32[39600]{0:T(1024)S(1)}, f32[39600]{0:T(1024)S(1)}, u32[]{:S(2)}, u32[]{:S(2)}) collective-permute-start(f32[39600]{0:T(1024)S(1)} %maximum_select_fusion.1), channel_id=1, source_target_pairs={{0,8},{8,0},{16,24},{24,16},{32,40},{40,32},{48,56},{56,48},{64,72... | collective-permute-start | bytes 475208 | tf_op jit(solution)/shard_map/ppermute | solution.py:58
  153.1 6.5 %fusion.52 = bf16[96,8,128]{2,0,1:T(8,128)(2,1)S(1)} fusion(f32[96,11,134]{2,0,1:T(8,128)S(1)} %get-tuple-element.130, f32[96,8,3]{2,0,1:T(8,128)S(1)} %collective-permute-done.5, f32[96,8,128]{2,0,1:T(8,128)S(1)} %copy_dynamic-update-slice_fusion, f32[96,8,3]{2,0,1:T(8,128)S(1)} %collective-permute-done.4, f32[96,11,134]{2,0,1:T(8,128)S(1)} %get-tuple-element.129, ...), kind=kLoop, calls=%fused_computation.214 | loop fusion | flops 10420224 | bytes 17338752 | tf_op jit(solution)/shard_map/convert_element_type | solution.py:179
  (311 shorter events, 15.4 us)
Async XLA Ops:
  1.8 10.2 %collective-permute-start.1 = (bf16[96,8,3]{2,0,1:T(8,128)(2,1)S(1)}, bf16[96,8,3]{2,0,1:T(8,128)(2,1)S(1)}, u32[]{:S(2)}, u32[]{:S(2)}) collective-permute-start(bf16[96,8,3]{2,0,1:T(8,128)(2,1)S(1)} %get-tuple-element.163), channel_id=1, source_target_pairs={{8,0},{16,8},{24,16},{32,24},{40,32},{48,40},{56,48},{64,56},{72,6... | collective-permute-start | bytes 13832 | tf_op jit(solution)/shard_map/ppermute | solution.py:17
  4.4 7.7 %collective-permute-start = (bf16[96,8,3]{2,0,1:T(8,128)(2,1)S(1)}, bf16[96,8,3]{2,0,1:T(8,128)(2,1)S(1)}, u32[]{:S(2)}, u32[]{:S(2)}) collective-permute-start(bf16[96,8,3]{2,0,1:T(8,128)(2,1)S(1)} %get-tuple-element.162), channel_id=1, source_target_pairs={{0,8},{8,16},{16,24},{24,32},{32,40},{40,48},{48,56},{56,64},{64,7... | collective-permute-start | bytes 13832 | tf_op jit(solution)/shard_map/ppermute | solution.py:14
  9.6 35.4 %copy-start.19 = (f32[96]{0:T(128)}, f32[96]{0:T(128)S(1)}, u32[]{:S(2)}) copy-start(f32[96]{0:T(128)S(1)} %get-tuple-element.177) | copy-start | bytes 1156
  9.6 35.4 %copy-start.21 = (f32[96]{0:T(128)}, f32[96]{0:T(128)S(1)}, u32[]{:S(2)}) copy-start(f32[96]{0:T(128)S(1)} %get-tuple-element.178) | copy-start | bytes 1156
  9.6 35.4 %copy-start.23 = (f32[96]{0:T(128)}, f32[96]{0:T(128)S(1)}, u32[]{:S(2)}) copy-start(f32[96]{0:T(128)S(1)} %get-tuple-element.179) | copy-start | bytes 1156
  9.6 35.4 %copy-start.25 = (f32[96]{0:T(128)}, f32[96]{0:T(128)S(1)}, u32[]{:S(2)}) copy-start(f32[96]{0:T(128)S(1)} %get-tuple-element.180) | copy-start | bytes 1156
  9.6 35.4 %copy-start.27 = (f32[96]{0:T(128)}, f32[96]{0:T(128)S(1)}, u32[]{:S(2)}) copy-start(f32[96]{0:T(128)S(1)} %get-tuple-element.181) | copy-start | bytes 1156
  9.6 35.4 %copy-start.29 = (f32[96]{0:T(128)}, f32[96]{0:T(128)S(1)}, u32[]{:S(2)}) copy-start(f32[96]{0:T(128)S(1)} %get-tuple-element.182) | copy-start | bytes 1156
  9.6 35.4 %copy-start.31 = (f32[96]{0:T(128)}, f32[96]{0:T(128)S(1)}, u32[]{:S(2)}) copy-start(f32[96]{0:T(128)S(1)} %get-tuple-element.183) | copy-start | bytes 1156
  9.6 35.4 %copy-start.33 = (f32[96]{0:T(128)}, f32[96]{0:T(128)S(1)}, u32[]{:S(2)}) copy-start(f32[96]{0:T(128)S(1)} %get-tuple-element.184) | copy-start | bytes 1156
  9.6 35.4 %copy-start.35 = (f32[96]{0:T(128)}, f32[96]{0:T(128)S(1)}, u32[]{:S(2)}) copy-start(f32[96]{0:T(128)S(1)} %get-tuple-element.185) | copy-start | bytes 1156
  9.7 35.4 %copy-start.37 = (f32[96]{0:T(128)}, f32[96]{0:T(128)S(1)}, u32[]{:S(2)}) copy-start(f32[96]{0:T(128)S(1)} %get-tuple-element.186) | copy-start | bytes 1156
  9.7 35.4 %copy-start.39 = (f32[96]{0:T(128)}, f32[96]{0:T(128)S(1)}, u32[]{:S(2)}) copy-start(f32[96]{0:T(128)S(1)} %get-tuple-element.187) | copy-start | bytes 1156
  9.7 35.4 %copy-start.41 = (f32[96]{0:T(128)}, f32[96]{0:T(128)S(1)}, u32[]{:S(2)}) copy-start(f32[96]{0:T(128)S(1)} %get-tuple-element.188) | copy-start | bytes 1156
  9.7 35.4 %copy-start.43 = (f32[96]{0:T(128)}, f32[96]{0:T(128)S(1)}, u32[]{:S(2)}) copy-start(f32[96]{0:T(128)S(1)} %get-tuple-element.189) | copy-start | bytes 1156
  9.7 35.4 %copy-start.45 = (f32[96]{0:T(128)}, f32[96]{0:T(128)S(1)}, u32[]{:S(2)}) copy-start(f32[96]{0:T(128)S(1)} %get-tuple-element.190) | copy-start | bytes 1156
  9.7 35.4 %copy-start.47 = (f32[96]{0:T(128)}, f32[96]{0:T(128)S(1)}, u32[]{:S(2)}) copy-start(f32[96]{0:T(128)S(1)} %get-tuple-element.191) | copy-start | bytes 1156
  9.7 35.4 %copy-start.49 = (f32[96]{0:T(128)}, f32[96]{0:T(128)S(1)}, u32[]{:S(2)}) copy-start(f32[96]{0:T(128)S(1)} %get-tuple-element.192) | copy-start | bytes 1156
  9.7 35.4 %copy-start.51 = (f32[96]{0:T(128)}, f32[96]{0:T(128)S(1)}, u32[]{:S(2)}) copy-start(f32[96]{0:T(128)S(1)} %get-tuple-element.193) | copy-start | bytes 1156
  9.8 35.4 %copy-start.53 = (f32[96]{0:T(128)}, f32[96]{0:T(128)S(1)}, u32[]{:S(2)}) copy-start(f32[96]{0:T(128)S(1)} %get-tuple-element.194) | copy-start | bytes 1156
  9.8 35.4 %copy-start.55 = (f32[96]{0:T(128)}, f32[96]{0:T(128)S(1)}, u32[]{:S(2)}) copy-start(f32[96]{0:T(128)S(1)} %get-tuple-element.195) | copy-start | bytes 1156
  9.8 35.4 %copy-start.57 = (f32[96]{0:T(128)}, f32[96]{0:T(128)S(1)}, u32[]{:S(2)}) copy-start(f32[96]{0:T(128)S(1)} %get-tuple-element.196) | copy-start | bytes 1156
  9.8 35.4 %copy-start.59 = (f32[96]{0:T(128)}, f32[96]{0:T(128)S(1)}, u32[]{:S(2)}) copy-start(f32[96]{0:T(128)S(1)} %get-tuple-element.197) | copy-start | bytes 1156
  9.8 35.4 %copy-start.61 = (f32[96]{0:T(128)}, f32[96]{0:T(128)S(1)}, u32[]{:S(2)}) copy-start(f32[96]{0:T(128)S(1)} %get-tuple-element.198) | copy-start | bytes 1156
  9.8 35.4 %copy-start.63 = (f32[96]{0:T(128)}, f32[96]{0:T(128)S(1)}, u32[]{:S(2)}) copy-start(f32[96]{0:T(128)S(1)} %get-tuple-element.199) | copy-start | bytes 1156
  9.8 35.4 %copy-start.65 = (f32[96]{0:T(128)}, f32[96]{0:T(128)S(1)}, u32[]{:S(2)}) copy-start(f32[96]{0:T(128)S(1)} %get-tuple-element.200) | copy-start | bytes 1156
  9.8 35.4 %copy-start.67 = (f32[96]{0:T(128)}, f32[96]{0:T(128)S(1)}, u32[]{:S(2)}) copy-start(f32[96]{0:T(128)S(1)} %get-tuple-element.201) | copy-start | bytes 1156
  9.8 35.4 %copy-start.69 = (f32[96]{0:T(128)}, f32[96]{0:T(128)S(1)}, u32[]{:S(2)}) copy-start(f32[96]{0:T(128)S(1)} %get-tuple-element.202) | copy-start | bytes 1156
  9.8 35.4 %copy-start.71 = (f32[96]{0:T(128)}, f32[96]{0:T(128)S(1)}, u32[]{:S(2)}) copy-start(f32[96]{0:T(128)S(1)} %get-tuple-element.203) | copy-start | bytes 1156
  9.9 35.4 %copy-start.73 = (f32[96]{0:T(128)}, f32[96]{0:T(128)S(1)}, u32[]{:S(2)}) copy-start(f32[96]{0:T(128)S(1)} %get-tuple-element.204) | copy-start | bytes 1156
  9.9 35.4 %copy-start.75 = (f32[96]{0:T(128)}, f32[96]{0:T(128)S(1)}, u32[]{:S(2)}) copy-start(f32[96]{0:T(128)S(1)} %get-tuple-element.205) | copy-start | bytes 1156
  20.4 14.2 %collective-permute-start.2 = (bf16[96,3,134]{2,0,1:T(8,128)(2,1)S(1)}, bf16[96,3,134]{2,0,1:T(8,128)(2,1)S(1)}, u32[]{:S(2)}, u32[]{:S(2)}) collective-permute-start(bf16[96,3,134]{2,0,1:T(8,128)(2,1)S(1)} %get-tuple-element.141), channel_id=1, source_target_pairs={{0,1},{1,2},{2,3},{3,4},{4,5},{5,6},{6,7},{8,9},{9,10},{10,11},{11... | collective-permute-start | bytes 231560 | tf_op jit(solution)/shard_map/ppermute | solution.py:139
  31.0 13.9 %collective-permute-start.3 = (bf16[96,3,134]{2,0,1:T(8,128)(2,1)S(1)}, bf16[96,3,134]{2,0,1:T(8,128)(2,1)S(1)}, u32[]{:S(2)}, u32[]{:S(2)}) collective-permute-start(bf16[96,3,134]{2,0,1:T(8,128)(2,1)S(1)} %get-tuple-element.142), channel_id=1, source_target_pairs={{1,0},{2,1},{3,2},{4,3},{5,4},{6,5},{7,6},{9,8},{10,9},{11,10},{12... | collective-permute-start | bytes 231560 | tf_op jit(solution)/shard_map/ppermute | solution.py:140
  63.5 4.2 %collective-permute-start.8 = (f32[39600]{0:T(1024)S(1)}, f32[39600]{0:T(1024)S(1)}, u32[]{:S(2)}, u32[]{:S(2)}) collective-permute-start(f32[39600]{0:T(1024)S(1)} %dynamic_slice.13), channel_id=1, source_target_pairs={{0,8},{8,0},{16,24},{24,16},{32,40},{40,32},{48,56},{56,48},{64,72... | collective-permute-start | bytes 475208 | tf_op jit(solution)/shard_map/ppermute | solution.py:58
  67.9 5.6 %collective-permute-start.9 = (f32[19800]{0:T(1024)S(1)}, f32[19800]{0:T(1024)S(1)}, u32[]{:S(2)}, u32[]{:S(2)}) collective-permute-start(f32[19800]{0:T(1024)S(1)} %dynamic_slice.15), channel_id=1, source_target_pairs={{0,16},{8,24},{16,0},{24,8},{32,48},{40,56},{48,32},{56,40},{64,80... | collective-permute-start | bytes 237608 | tf_op jit(solution)/shard_map/ppermute | solution.py:58
  73.6 8.4 %collective-permute-start.10 = (f32[19800]{0:T(1024)S(1)}, f32[19800]{0:T(1024)S(1)}, u32[]{:S(2)}, u32[]{:S(2)}) collective-permute-start(f32[19800]{0:T(1024)S(1)} %dynamic-slice_add_fusion.1), channel_id=1, source_target_pairs={{0,32},{8,40},{16,48},{24,56},{32,0},{40,8},{48,16},{56,24},{64,96... | collective-permute-start | bytes 237608 | tf_op jit(solution)/shard_map/ppermute | solution.py:58
  82.0 12.4 %collective-permute-start.11 = (f32[19800]{0:T(1024)S(1)}, f32[19800]{0:T(1024)S(1)}, u32[]{:S(2)}, u32[]{:S(2)}) collective-permute-start(f32[19800]{0:T(1024)S(1)} %add.981), channel_id=1, source_target_pairs={{0,64},{8,72},{16,80},{24,88},{32,96},{40,104},{48,112},{56,120},{... | collective-permute-start | bytes 237608 | tf_op jit(solution)/shard_map/ppermute | solution.py:58
  85.9 20.4 %collective-permute-start.4 = (f32[96,8,3]{2,0,1:T(8,128)S(1)}, f32[96,8,3]{2,0,1:T(8,128)S(1)}, u32[]{:S(2)}, u32[]{:S(2)}) collective-permute-start(f32[96,8,3]{2,0,1:T(8,128)S(1)} %get-tuple-element.139), channel_id=1, source_target_pairs={{0,8},{8,16},{16,24},{24,32},{32,40},{40,48},{48,56},{56,64},{64,7... | collective-permute-start | bytes 27656 | tf_op jit(solution)/shard_map/ppermute | solution.py:14
  92.0 14.3 %collective-permute-start.5 = (f32[96,8,3]{2,0,1:T(8,128)S(1)}, f32[96,8,3]{2,0,1:T(8,128)S(1)}, u32[]{:S(2)}, u32[]{:S(2)}) collective-permute-start(f32[96,8,3]{2,0,1:T(8,128)S(1)} %get-tuple-element.140), channel_id=1, source_target_pairs={{8,0},{16,8},{24,16},{32,24},{40,32},{48,40},{56,48},{64,56},{72,6... | collective-permute-start | bytes 27656 | tf_op jit(solution)/shard_map/ppermute | solution.py:17
  94.4 9.9 %collective-permute-start.12 = (f32[19800]{0:T(1024)S(1)}, f32[19800]{0:T(1024)S(1)}, u32[]{:S(2)}, u32[]{:S(2)}) collective-permute-start(f32[19800]{0:T(1024)S(1)} %add.982), channel_id=1, source_target_pairs={{0,128},{8,136},{16,144},{24,152},{32,160},{40,168},{48,176},{56,1... | collective-permute-start | bytes 237608 | tf_op jit(solution)/shard_map/ppermute | solution.py:58
  104.3 8.2 %collective-permute-start.13 = (f32[19800]{0:T(1024)S(1)}, f32[19800]{0:T(1024)S(1)}, u32[]{:S(2)}, u32[]{:S(2)}) collective-permute-start(f32[19800]{0:T(1024)S(1)} %add.983), channel_id=1, source_target_pairs={{0,256},{8,264},{16,272},{24,280},{32,288},{40,296},{48,304},{56,3... | collective-permute-start | bytes 237608 | tf_op jit(solution)/shard_map/ppermute | solution.py:58
  112.6 10.5 %collective-permute-start.14 = (f32[19800]{0:T(1024)S(1)}, f32[19800]{0:T(1024)S(1)}, u32[]{:S(2)}, u32[]{:S(2)}) collective-permute-start(f32[19800]{0:T(1024)S(1)} %add.984), channel_id=1, source_target_pairs={{0,1},{1,0},{2,3},{3,2},{4,5},{5,4},{6,7},{7,6},{8,9},{9,8},{10,11... | collective-permute-start | bytes 237608 | tf_op jit(solution)/shard_map/ppermute | solution.py:58
  119.0 18.6 %collective-permute-start.6 = (bf16[96,3,134]{2,0,1:T(8,128)(2,1)S(1)}, bf16[96,3,134]{2,0,1:T(8,128)(2,1)S(1)}, u32[]{:S(2)}, u32[]{:S(2)}) collective-permute-start(bf16[96,3,134]{2,0,1:T(8,128)(2,1)S(1)} %get-tuple-element.137), channel_id=1, source_target_pairs={{0,1},{1,2},{2,3},{3,4},{4,5},{5,6},{6,7},{8,9},{9,10},{10,11},{11... | collective-permute-start | bytes 231560 | tf_op jit(solution)/shard_map/ppermute | solution.py:14
  121.8 15.8 %collective-permute-start.7 = (bf16[96,3,134]{2,0,1:T(8,128)(2,1)S(1)}, bf16[96,3,134]{2,0,1:T(8,128)(2,1)S(1)}, u32[]{:S(2)}, u32[]{:S(2)}) collective-permute-start(bf16[96,3,134]{2,0,1:T(8,128)(2,1)S(1)} %get-tuple-element.138), channel_id=1, source_target_pairs={{1,0},{2,1},{3,2},{4,3},{5,4},{6,5},{7,6},{9,8},{10,9},{11,10},{12... | collective-permute-start | bytes 231560 | tf_op jit(solution)/shard_map/ppermute | solution.py:17
  123.1 11.1 %collective-permute-start.15 = (f32[19800]{0:T(1024)S(1)}, f32[19800]{0:T(1024)S(1)}, u32[]{:S(2)}, u32[]{:S(2)}) collective-permute-start(f32[19800]{0:T(1024)S(1)} %add.985), channel_id=1, source_target_pairs={{0,2},{1,3},{2,0},{3,1},{4,6},{5,7},{6,4},{7,5},{8,10},{9,11},{10,... | collective-permute-start | bytes 237608 | tf_op jit(solution)/shard_map/ppermute | solution.py:58
  134.3 6.7 %collective-permute-start.16 = (f32[19800]{0:T(1024)S(1)}, f32[19800]{0:T(1024)S(1)}, u32[]{:S(2)}, u32[]{:S(2)}) collective-permute-start(f32[19800]{0:T(1024)S(1)} %add.986), channel_id=1, source_target_pairs={{0,4},{1,5},{2,6},{3,7},{4,0},{5,1},{6,2},{7,3},{8,12},{9,13},{10,... | collective-permute-start | bytes 237608 | tf_op jit(solution)/shard_map/ppermute | solution.py:58
  141.0 5.2 %collective-permute-start.17 = (f32[19800]{0:T(1024)S(1)}, f32[19800]{0:T(1024)S(1)}, u32[]{:S(2)}, u32[]{:S(2)}) collective-permute-start(f32[19800]{0:T(1024)S(1)} %add.987), channel_id=1, source_target_pairs={{0,16},{8,24},{16,0},{24,8},{32,48},{40,56},{48,32},{56,40},{64,80... | collective-permute-start | bytes 237608 | tf_op jit(solution)/shard_map/ppermute | solution.py:58
  146.3 14.1 %collective-permute-start.18 = (f32[39600]{0:T(1024)S(1)}, f32[39600]{0:T(1024)S(1)}, u32[]{:S(2)}, u32[]{:S(2)}) collective-permute-start(f32[39600]{0:T(1024)S(1)} %maximum_select_fusion.1), channel_id=1, source_target_pairs={{0,8},{8,0},{16,24},{24,16},{32,40},{40,32},{48,56},{56,48},{64,72... | collective-permute-start | bytes 475208 | tf_op jit(solution)/shard_map/ppermute | solution.py:58
  (84 other events, 858.7 us)

commit v5 on v4

--- a/solution.py
+++ b/solution.py
@@ -132,12 +132,14 @@
 def local(image, cotangent, dw_kernel, dw_bias, ln_gain, ln_bias, w_in, b_in, w_out, layer_scale):
     channels, height, breadth = image.shape
     pixels = height * breadth
-    padded_c = padded_2(image, (("col", 2),), 3)
     count = lax.axis_size("row")
     forward = [(i, i + 1) for i in range(count - 1)]
     backward = [(target, source) for source, target in forward]
-    above = lax.ppermute(padded_c[:, height - 3 :, :], "row", forward)
-    below = lax.ppermute(padded_c[:, :3, :], "row", backward)
+    above_raw = lax.ppermute(image[:, height - 3 :, :], "row", forward)
+    below_raw = lax.ppermute(image[:, :3, :], "row", backward)
+    padded_c = padded_2(image, (("col", 2),), 3)
+    strips = padded_2(jnp.concatenate([above_raw, below_raw], axis=1), (("col", 2),), 3)
+    above, below = strips[:, :3, :], strips[:, 3:, :]
     padded = jnp.concatenate([above, padded_c, below], axis=1)
     bias = dw_bias[:, None, None]
     conv_mid = conv_seven(padded_c, dw_kernel) + bias

time: 166 us -> 166 us (level)
  waiting for transfers between devices: 39 us -> 31.8 us
  starting transfers between devices: 74.2 us -> 81.3 us
    ppermute x2, waiting for transfers between devices: 7.69 us -> 0.01 us  [the longest x1 0.01 us: local(): above_raw = lax.ppermute(image[:, height - 3:, :], 'row', forward)]
    ppermute x11, starting transfers between devices: 42 us -> 47.5 us  [xor_partner(): lax.ppermute(value, axis, [(i, i ^ mask) for i in range(lax.axis_size(axi...]
    ppermute x3 -> x4, waiting for transfers between devices: 0.01 us -> 4.16 us  [padded_2(): lax.ppermute(lax.slice_in_dim(block, 0, width, axis=dim), axis, backward)]
    ppermute x11, waiting for transfers between devices: 31.3 us -> 27.7 us  [xor_partner(): lax.ppermute(value, axis, [(i, i ^ mask) for i in range(lax.axis_size(axi...]
    ppermute x3 -> x4, starting transfers between devices: 6.02 us -> 8.1 us  [padded_2(): lax.ppermute(lax.slice_in_dim(block, 0, width, axis=dim), axis, backward)]
    unnamed x232 -> x229, local copies, waits for them, and re-layouts: 4.78 us -> 4.3 us
    ppermute x3 -> x4, starting transfers between devices: 14 us -> 13.8 us  [padded_2(): lax.ppermute(lax.slice_in_dim(block, block.shape[dim] - width, None, axis...]
  transfers between devices with their start and end apart: 19 -> 21, of which waited for: 9 -> 9; matrix products, arithmetic and copies ran while one was open for 10% -> 13% of each run, Pallas kernels for 0% -> 0%
where the time goes in v5:
time: 166 us; the launch traced here: 165 us
  starting transfers between devices  81.3 us (49%)
  waiting for transfers between devices  31.8 us (19%)
  other arithmetic  28 us (17%)
  matrix products  10.7 us (6%)
  local copies, waits for them, and re-layouts  9.99 us (6%)
  between operations  3.07 us (2%)
    ppermute x11, starting transfers between devices, xor_partner(): lax.ppermute(value, axis, [(i, i ^ mask) for i in range(lax.axis_size(axi...  47.5 us
    ppermute x11, waiting for transfers between devices, xor_partner(): lax.ppermute(value, axis, [(i, i ^ mask) for i in range(lax.axis_size(axi...  27.7 us
    ppermute x4, starting transfers between devices, padded_2(): lax.ppermute(lax.slice_in_dim(block, block.shape[dim] - width, None, axis...  13.8 us
    dot_general x12, matrix products, product(): return jnp.einsum(form, left, right, preferred_element_type=jnp.float32)  10.7 us
    ppermute x1, starting transfers between devices, local(): above_raw = lax.ppermute(image[:, height - 3:, :], 'row', forward)  10.6 us
    ppermute x4, starting transfers between devices, padded_2(): lax.ppermute(lax.slice_in_dim(block, 0, width, axis=dim), axis, backward)  8.1 us
    convert_element_type x1, other arithmetic, local(): image_grad = (cotangent.astype(jnp.float32) + back).astype(jnp.bfloat16)  6.56 us
    unnamed x229, local copies, waits for them, and re-layouts  4.3 us
  transfers between devices with their start and end apart: 21, of which 9 were waited for; matrix products, arithmetic and copies ran while one was open for 13% of the time, Pallas kernels for 0%

profile of v5, /device:TPU:57, one launch (start us, length us, event | category | flops | bytes accessed | tf_op | source)
XLA Modules:
  0.0 165.0 jit_solution(728076206581873470)
XLA Ops:
  0.7 1.0 constant_dynamic-update-slice_fusion.3
  1.9 2.6 %collective-permute-start.5 = (bf16[96,8,3]{2,0,1:T(8,128)(2,1)S(1)}, bf16[96,8,3]{2,0,1:T(8,128)(2,1)S(1)}, u32[]{:S(2)}, u32[]{:S(2)}) collective-permute-start(bf16[96,8,3]{2,0,1:T(8,128)(2,1)S(1)} %get-tuple-element.163), channel_id=1, source_target_pairs={{8,0},{16,8},{24,16},{32,24},{40,32},{48,40},{56,48},{64,56},{72,6... | collective-permute-start | bytes 13832 | tf_op jit(solution)/shard_map/ppermute | solution.py:17
  4.4 5.1 %collective-permute-start.4 = (bf16[96,8,3]{2,0,1:T(8,128)(2,1)S(1)}, bf16[96,8,3]{2,0,1:T(8,128)(2,1)S(1)}, u32[]{:S(2)}, u32[]{:S(2)}) collective-permute-start(bf16[96,8,3]{2,0,1:T(8,128)(2,1)S(1)} %get-tuple-element.162), channel_id=1, source_target_pairs={{0,8},{8,16},{16,24},{24,32},{32,40},{40,48},{48,56},{56,64},{64,7... | collective-permute-start | bytes 13832 | tf_op jit(solution)/shard_map/ppermute | solution.py:14
  9.6 10.6 %collective-permute-start = (bf16[96,3,128]{2,0,1:T(8,128)(2,1)S(1)}, bf16[96,3,128]{2,0,1:T(8,128)(2,1)S(1)}, u32[]{:S(2)}, u32[]{:S(2)}) collective-permute-start(bf16[96,3,128]{2,0,1:T(8,128)(2,1)S(1)} %get-tuple-element.165), channel_id=1, source_target_pairs={{0,1},{1,2},{2,3},{3,4},{4,5},{5,6},{6,7},{8,9},{9,10},{10,11},{11... | collective-permute-start | bytes 221192 | tf_op jit(solution)/shard_map/ppermute | solution.py:138
  20.2 1.3 collective-permute-start.1
  23.5 2.4 %fusion.244 = (f32[2,128]{1,0:T(2,128)S(1)}, f32[96,2,128]{2,0,1:T(8,128)S(1)}) fusion(f32[96]{0:T(128)S(1)} %copy-done.94, bf16[96,8,131]{2,0,1:T(8,128)(2,1)S(1)} %constant_dynamic-update-slice_fusion.2, f32[96]{0:T(128)} %get-tuple-element.217, f32[96]{0:T(128)} %get-tuple-element.218, f32[96]{0:T(128)S(1)} %get-tuple-element.171, ...), kind=kLoop, calls=%fused_computation.661 | loop fusion | flops 5185280 | bytes 1894016 | tf_op jit(solution)/shard_map/reduce_sum | solution.py:100
  26.5 1.1 convert_reduce_fusion.1
  27.5 0.9 fusion.241
  28.7 0.9 fusion.236
  29.5 1.5 fusion.153
  31.5 2.2 %collective-permute-start.2 = (bf16[96,6,3]{2,0,1:T(8,128)(2,1)S(1)}, bf16[96,6,3]{2,0,1:T(8,128)(2,1)S(1)}, u32[]{:S(2)}, u32[]{:S(2)}) collective-permute-start(bf16[96,6,3]{2,0,1:T(8,128)(2,1)S(1)} %get-tuple-element.166), channel_id=1, source_target_pairs={{0,8},{8,16},{16,24},{24,32},{32,40},{40,48},{48,56},{56,64},{64,7... | collective-permute-start | bytes 10376 | tf_op jit(solution)/shard_map/ppermute | solution.py:14
  33.8 2.3 %collective-permute-start.3 = (bf16[96,6,3]{2,0,1:T(8,128)(2,1)S(1)}, bf16[96,6,3]{2,0,1:T(8,128)(2,1)S(1)}, u32[]{:S(2)}, u32[]{:S(2)}) collective-permute-start(bf16[96,6,3]{2,0,1:T(8,128)(2,1)S(1)} %get-tuple-element.167), channel_id=1, source_target_pairs={{8,0},{16,8},{24,16},{32,24},{40,32},{48,40},{56,48},{64,56},{72,6... | collective-permute-start | bytes 10376 | tf_op jit(solution)/shard_map/ppermute | solution.py:17
  36.1 1.4 fusion.156
  38.2 4.2 %collective-permute-done.3 = bf16[96,6,3]{2,0,1:T(8,128)(2,1)S(1)} collective-permute-done((bf16[96,6,3]{2,0,1:T(8,128)(2,1)S(1)}, bf16[96,6,3]{2,0,1:T(8,128)(2,1)S(1)}, u32[]{:S(2)}, u32[]{:S(2)}) %collective-permute-start.3) | collective-permute-done | bytes 3488 | tf_op jit(solution)/shard_map/ppermute | solution.py:17
  42.6 3.0 %fusion.100 = f32[96,3,128]{2,0,1:T(8,128)S(1)} fusion(bf16[96,3,128]{2,0,1:T(8,128)(2,1)S(1)} %collective-permute-done, bf16[96,6,128]{2,0,1:T(8,128)(2,1)S(1)} %constant_dynamic-update-slice_fusion, bf16[96,6,3]{2,0,1:T(8,128)(2,1)S(1)} %collective-permute-done.3, bf16[96,6,3]{2,0,1:T(8,128)(2,1)S(1)} %collective-permute-done.2, ...), kind=kLoop, calls=%fused_computation.424 | loop fusion | flops 8957952 | bytes 2704000 | tf_op jit(solution)/shard_map/add | solution.py:146
  45.9 3.1 %add_add_fusion = f32[96,3,128]{2,0,1:T(8,128)S(1)} fusion(bf16[96,3,128]{2,0,1:T(8,128)(2,1)S(1)} %collective-permute-done.1, bf16[96,6,128]{2,0,1:T(8,128)(2,1)S(1)} %constant_dynamic-update-slice_fusion, bf16[96,6,3]{2,0,1:T(8,128)(2,1)S(1)} %collective-permute-done.3, bf16[96,6,3]{2,0,1:T(8,128)(2,1)S(1)} %collective-permute-done.2, ...), kind=kLoop, calls=%fused_computation.458 | loop fusion | flops 8957952 | bytes 2704000 | tf_op jit(solution)/shard_map/add | solution.py:148
  50.1 1.7 %convert_reduce_fusion = (f32[384]{0:T(512)}, bf16[384,768]{0,1:T(8,128)(2,1)S(1)}) fusion(f32[384,768]{0,1:T(8,128)S(1)} %fusion, bf16[384,96]{0,1:T(8,128)(2,1)S(1)} %copy-done.13, f32[12,8,6,128]{3,2,1,0:T(8,128)S(1)} %bitcast.303, f32[96]{0:T(128)S(1)} %copy-done.103), kind=kOutput, calls=%fused_computation.123 | convolution fusion | flops 63258240 | bytes 2140032 | tf_op jit(solution)/shard_map/hc,cp->hp/dot_general | solution.py:96
  51.8 1.8 %fusion.77 = (f32[96]{0:T(128)}, bf16[96,768]{1,0:T(8,128)(2,1)}) fusion(f32[12,8,6,128]{3,2,1,0:T(8,128)S(1)} %bitcast.304, f32[96]{0:T(128)S(1)} %copy-done.103, bf16[384,96]{0,1:T(8,128)(2,1)S(1)} %copy-done.13, f32[384,768]{0,1:T(8,128)S(1)} %fusion, bf16[96,3,128]{2,0,1:T(8,128)(2,1)S(1)} %copy-done.17, bf16[96,3,128]{2,0,1:T(8,128)(2,1)S(1)} %copy-done.15), kind=kOutput, calls=%fused_computation.357 | convolution fusion | flops 59793312 | bytes 1843968 | tf_op jit(solution)/shard_map/hc,hp->cp/dot_general | solution.py:96
  53.6 1.0 fusion.80
  57.7 1.3 multiply_reduce_fusion
  59.0 1.3 multiply_reduce_fusion.28
  60.4 1.1 multiply_reduce_fusion.18
  63.1 1.6 concatenate.293
  64.8 1.9 %collective-permute-start.10 = (f32[39600]{0:T(1024)S(1)}, f32[39600]{0:T(1024)S(1)}, u32[]{:S(2)}, u32[]{:S(2)}) collective-permute-start(f32[39600]{0:T(1024)S(1)} %dynamic_slice.13), channel_id=1, source_target_pairs={{0,8},{8,0},{16,24},{24,16},{32,40},{40,32},{48,56},{56,48},{64,72... | collective-permute-start | bytes 475208 | tf_op jit(solution)/shard_map/ppermute | solution.py:58
  66.8 1.3 collective-permute-done.10
  68.3 1.9 %collective-permute-start.11 = (f32[19800]{0:T(1024)S(1)}, f32[19800]{0:T(1024)S(1)}, u32[]{:S(2)}, u32[]{:S(2)}) collective-permute-start(f32[19800]{0:T(1024)S(1)} %dynamic_slice.15), channel_id=1, source_target_pairs={{0,16},{8,24},{16,0},{24,8},{32,48},{40,56},{48,32},{56,40},{64,80... | collective-permute-start | bytes 237608 | tf_op jit(solution)/shard_map/ppermute | solution.py:58
  70.3 3.9 %collective-permute-done.11 = f32[19800]{0:T(1024)S(1)} collective-permute-done((f32[19800]{0:T(1024)S(1)}, f32[19800]{0:T(1024)S(1)}, u32[]{:S(2)}, u32[]{:S(2)}) %collective-permute-start.11) | collective-permute-done | bytes 79232 | tf_op jit(solution)/shard_map/ppermute | solution.py:58
  74.2 1.9 %collective-permute-start.12 = (f32[19800]{0:T(1024)S(1)}, f32[19800]{0:T(1024)S(1)}, u32[]{:S(2)}, u32[]{:S(2)}) collective-permute-start(f32[19800]{0:T(1024)S(1)} %dynamic-slice_add_fusion.1), channel_id=1, source_target_pairs={{0,32},{8,40},{16,48},{24,56},{32,0},{40,8},{48,16},{56,24},{64,96... | collective-permute-start | bytes 237608 | tf_op jit(solution)/shard_map/ppermute | solution.py:58
  76.2 6.7 %collective-permute-done.12 = f32[19800]{0:T(1024)S(1)} collective-permute-done((f32[19800]{0:T(1024)S(1)}, f32[19800]{0:T(1024)S(1)}, u32[]{:S(2)}, u32[]{:S(2)}) %collective-permute-start.12) | collective-permute-done | bytes 79232 | tf_op jit(solution)/shard_map/ppermute | solution.py:58
  82.9 3.6 %collective-permute-start.13 = (f32[19800]{0:T(1024)S(1)}, f32[19800]{0:T(1024)S(1)}, u32[]{:S(2)}, u32[]{:S(2)}) collective-permute-start(f32[19800]{0:T(1024)S(1)} %add.981), channel_id=1, source_target_pairs={{0,64},{8,72},{16,80},{24,88},{32,96},{40,104},{48,112},{56,120},{... | collective-permute-start | bytes 237608 | tf_op jit(solution)/shard_map/ppermute | solution.py:58
  86.7 4.6 %collective-permute-start.6 = (f32[96,8,3]{2,0,1:T(8,128)S(1)}, f32[96,8,3]{2,0,1:T(8,128)S(1)}, u32[]{:S(2)}, u32[]{:S(2)}) collective-permute-start(f32[96,8,3]{2,0,1:T(8,128)S(1)} %get-tuple-element.139), channel_id=1, source_target_pairs={{0,8},{8,16},{16,24},{24,32},{32,40},{40,48},{48,56},{56,64},{64,7... | collective-permute-start | bytes 27656 | tf_op jit(solution)/shard_map/ppermute | solution.py:14
  91.3 1.9 %collective-permute-start.7 = (f32[96,8,3]{2,0,1:T(8,128)S(1)}, f32[96,8,3]{2,0,1:T(8,128)S(1)}, u32[]{:S(2)}, u32[]{:S(2)}) collective-permute-start(f32[96,8,3]{2,0,1:T(8,128)S(1)} %get-tuple-element.140), channel_id=1, source_target_pairs={{8,0},{16,8},{24,16},{32,24},{40,32},{48,40},{56,48},{64,56},{72,6... | collective-permute-start | bytes 27656 | tf_op jit(solution)/shard_map/ppermute | solution.py:17
  93.5 3.1 %collective-permute-start.14 = (f32[19800]{0:T(1024)S(1)}, f32[19800]{0:T(1024)S(1)}, u32[]{:S(2)}, u32[]{:S(2)}) collective-permute-start(f32[19800]{0:T(1024)S(1)} %add.982), channel_id=1, source_target_pairs={{0,128},{8,136},{16,144},{24,152},{32,160},{40,168},{48,176},{56,1... | collective-permute-start | bytes 237608 | tf_op jit(solution)/shard_map/ppermute | solution.py:58
  96.7 6.7 %collective-permute-done.14 = f32[19800]{0:T(1024)S(1)} collective-permute-done((f32[19800]{0:T(1024)S(1)}, f32[19800]{0:T(1024)S(1)}, u32[]{:S(2)}, u32[]{:S(2)}) %collective-permute-start.14) | collective-permute-done | bytes 79232 | tf_op jit(solution)/shard_map/ppermute | solution.py:58
  103.5 3.4 %collective-permute-start.15 = (f32[19800]{0:T(1024)S(1)}, f32[19800]{0:T(1024)S(1)}, u32[]{:S(2)}, u32[]{:S(2)}) collective-permute-start(f32[19800]{0:T(1024)S(1)} %add.983), channel_id=1, source_target_pairs={{0,256},{8,264},{16,272},{24,280},{32,288},{40,296},{48,304},{56,3... | collective-permute-start | bytes 237608 | tf_op jit(solution)/shard_map/ppermute | solution.py:58
  107.1 3.8 %collective-permute-done.15 = f32[19800]{0:T(1024)S(1)} collective-permute-done((f32[19800]{0:T(1024)S(1)}, f32[19800]{0:T(1024)S(1)}, u32[]{:S(2)}, u32[]{:S(2)}) %collective-permute-start.15) | collective-permute-done | bytes 79232 | tf_op jit(solution)/shard_map/ppermute | solution.py:58
  111.0 8.2 %collective-permute-start.16 = (f32[19800]{0:T(1024)S(1)}, f32[19800]{0:T(1024)S(1)}, u32[]{:S(2)}, u32[]{:S(2)}) collective-permute-start(f32[19800]{0:T(1024)S(1)} %add.984), channel_id=1, source_target_pairs={{0,1},{1,0},{2,3},{3,2},{4,5},{5,4},{6,7},{7,6},{8,9},{9,8},{10,11... | collective-permute-start | bytes 237608 | tf_op jit(solution)/shard_map/ppermute | solution.py:58
  119.2 1.9 %collective-permute-start.8 = (bf16[96,3,134]{2,0,1:T(8,128)(2,1)S(1)}, bf16[96,3,134]{2,0,1:T(8,128)(2,1)S(1)}, u32[]{:S(2)}, u32[]{:S(2)}) collective-permute-start(bf16[96,3,134]{2,0,1:T(8,128)(2,1)S(1)} %get-tuple-element.137), channel_id=1, source_target_pairs={{0,1},{1,2},{2,3},{3,4},{4,5},{5,6},{6,7},{8,9},{9,10},{10,11},{11... | collective-permute-start | bytes 231560 | tf_op jit(solution)/shard_map/ppermute | solution.py:14
  121.2 1.3 collective-permute-start.9
  122.5 10.0 %collective-permute-start.17 = (f32[19800]{0:T(1024)S(1)}, f32[19800]{0:T(1024)S(1)}, u32[]{:S(2)}, u32[]{:S(2)}) collective-permute-start(f32[19800]{0:T(1024)S(1)} %add.985), channel_id=1, source_target_pairs={{0,2},{1,3},{2,0},{3,1},{4,6},{5,7},{6,4},{7,5},{8,10},{9,11},{10,... | collective-permute-start | bytes 237608 | tf_op jit(solution)/shard_map/ppermute | solution.py:58
  132.5 0.8 pad_maximum_fusion.8
  133.3 1.0 collective-permute-done.17
  134.3 5.2 %collective-permute-start.18 = (f32[19800]{0:T(1024)S(1)}, f32[19800]{0:T(1024)S(1)}, u32[]{:S(2)}, u32[]{:S(2)}) collective-permute-start(f32[19800]{0:T(1024)S(1)} %add.986), channel_id=1, source_target_pairs={{0,4},{1,5},{2,6},{3,7},{4,0},{5,1},{6,2},{7,3},{8,12},{9,13},{10,... | collective-permute-start | bytes 237608 | tf_op jit(solution)/shard_map/ppermute | solution.py:58
  139.6 2.1 %collective-permute-done.18 = f32[19800]{0:T(1024)S(1)} collective-permute-done((f32[19800]{0:T(1024)S(1)}, f32[19800]{0:T(1024)S(1)}, u32[]{:S(2)}, u32[]{:S(2)}) %collective-permute-start.18) | collective-permute-done | bytes 79232 | tf_op jit(solution)/shard_map/ppermute | solution.py:58
  141.7 1.9 %collective-permute-start.19 = (f32[19800]{0:T(1024)S(1)}, f32[19800]{0:T(1024)S(1)}, u32[]{:S(2)}, u32[]{:S(2)}) collective-permute-start(f32[19800]{0:T(1024)S(1)} %add.987), channel_id=1, source_target_pairs={{0,16},{8,24},{16,0},{24,8},{32,48},{40,56},{48,32},{56,40},{64,80... | collective-permute-start | bytes 237608 | tf_op jit(solution)/shard_map/ppermute | solution.py:58
  144.7 2.2 %collective-permute-done.19 = f32[19800]{0:T(1024)S(1)} collective-permute-done((f32[19800]{0:T(1024)S(1)}, f32[19800]{0:T(1024)S(1)}, u32[]{:S(2)}, u32[]{:S(2)}) %collective-permute-start.19) | collective-permute-done | bytes 79232 | tf_op jit(solution)/shard_map/ppermute | solution.py:58
  147.0 6.3 %collective-permute-start.20 = (f32[39600]{0:T(1024)S(1)}, f32[39600]{0:T(1024)S(1)}, u32[]{:S(2)}, u32[]{:S(2)}) collective-permute-start(f32[39600]{0:T(1024)S(1)} %maximum_select_fusion.1), channel_id=1, source_target_pairs={{0,8},{8,0},{16,24},{24,16},{32,40},{40,32},{48,56},{56,48},{64,72... | collective-permute-start | bytes 475208 | tf_op jit(solution)/shard_map/ppermute | solution.py:58
  153.7 6.6 %fusion.52 = bf16[96,8,128]{2,0,1:T(8,128)(2,1)S(1)} fusion(f32[96,11,134]{2,0,1:T(8,128)S(1)} %get-tuple-element.130, f32[96,8,3]{2,0,1:T(8,128)S(1)} %collective-permute-done.7, f32[96,8,128]{2,0,1:T(8,128)S(1)} %copy_dynamic-update-slice_fusion, f32[96,8,3]{2,0,1:T(8,128)S(1)} %collective-permute-done.6, f32[96,11,134]{2,0,1:T(8,128)S(1)} %get-tuple-element.129, ...), kind=kLoop, calls=%fused_computation.234 | loop fusion | flops 10420224 | bytes 17338752 | tf_op jit(solution)/shard_map/convert_element_type | solution.py:181
  (315 shorter events, 16.2 us)
Async XLA Ops:
  0.6 25.3 %copy-start = (bf16[96,384]{1,0:T(8,128)(2,1)S(1)}, bf16[96,384]{1,0:T(8,128)(2,1)}, u32[]{:S(2)}) copy-start(bf16[96,384]{1,0:T(8,128)(2,1)} %param.16) | copy-start | bytes 221188
  1.9 21.6 %collective-permute-start.5 = (bf16[96,8,3]{2,0,1:T(8,128)(2,1)S(1)}, bf16[96,8,3]{2,0,1:T(8,128)(2,1)S(1)}, u32[]{:S(2)}, u32[]{:S(2)}) collective-permute-start(bf16[96,8,3]{2,0,1:T(8,128)(2,1)S(1)} %get-tuple-element.163), channel_id=1, source_target_pairs={{8,0},{16,8},{24,16},{32,24},{40,32},{48,40},{56,48},{64,56},{72,6... | collective-permute-start | bytes 13832 | tf_op jit(solution)/shard_map/ppermute | solution.py:17
  4.4 19.0 %collective-permute-start.4 = (bf16[96,8,3]{2,0,1:T(8,128)(2,1)S(1)}, bf16[96,8,3]{2,0,1:T(8,128)(2,1)S(1)}, u32[]{:S(2)}, u32[]{:S(2)}) collective-permute-start(bf16[96,8,3]{2,0,1:T(8,128)(2,1)S(1)} %get-tuple-element.162), channel_id=1, source_target_pairs={{0,8},{8,16},{16,24},{24,32},{32,40},{40,48},{48,56},{56,64},{64,7... | collective-permute-start | bytes 13832 | tf_op jit(solution)/shard_map/ppermute | solution.py:14
  9.6 21.8 %collective-permute-start = (bf16[96,3,128]{2,0,1:T(8,128)(2,1)S(1)}, bf16[96,3,128]{2,0,1:T(8,128)(2,1)S(1)}, u32[]{:S(2)}, u32[]{:S(2)}) collective-permute-start(bf16[96,3,128]{2,0,1:T(8,128)(2,1)S(1)} %get-tuple-element.165), channel_id=1, source_target_pairs={{0,1},{1,2},{2,3},{3,4},{4,5},{5,6},{6,7},{8,9},{9,10},{10,11},{11... | collective-permute-start | bytes 221192 | tf_op jit(solution)/shard_map/ppermute | solution.py:138
  20.2 11.2 %collective-permute-start.1 = (bf16[96,3,128]{2,0,1:T(8,128)(2,1)S(1)}, bf16[96,3,128]{2,0,1:T(8,128)(2,1)S(1)}, u32[]{:S(2)}, u32[]{:S(2)}) collective-permute-start(bf16[96,3,128]{2,0,1:T(8,128)(2,1)S(1)} %get-tuple-element.164), channel_id=1, source_target_pairs={{1,0},{2,1},{3,2},{4,3},{5,4},{6,5},{7,6},{9,8},{10,9},{11,10},{12... | collective-permute-start | bytes 221192 | tf_op jit(solution)/shard_map/ppermute | solution.py:139
  21.6 24.0 %copy-start.20 = (f32[96]{0:T(128)}, f32[96]{0:T(128)S(1)}, u32[]{:S(2)}) copy-start(f32[96]{0:T(128)S(1)} %get-tuple-element.179) | copy-start | bytes 1156
  21.6 24.0 %copy-start.22 = (f32[96]{0:T(128)}, f32[96]{0:T(128)S(1)}, u32[]{:S(2)}) copy-start(f32[96]{0:T(128)S(1)} %get-tuple-element.180) | copy-start | bytes 1156
  21.6 24.0 %copy-start.24 = (f32[96]{0:T(128)}, f32[96]{0:T(128)S(1)}, u32[]{:S(2)}) copy-start(f32[96]{0:T(128)S(1)} %get-tuple-element.181) | copy-start | bytes 1156
  21.6 24.0 %copy-start.26 = (f32[96]{0:T(128)}, f32[96]{0:T(128)S(1)}, u32[]{:S(2)}) copy-start(f32[96]{0:T(128)S(1)} %get-tuple-element.182) | copy-start | bytes 1156
  21.6 24.0 %copy-start.28 = (f32[96]{0:T(128)}, f32[96]{0:T(128)S(1)}, u32[]{:S(2)}) copy-start(f32[96]{0:T(128)S(1)} %get-tuple-element.183) | copy-start | bytes 1156
  21.6 24.0 %copy-start.30 = (f32[96]{0:T(128)}, f32[96]{0:T(128)S(1)}, u32[]{:S(2)}) copy-start(f32[96]{0:T(128)S(1)} %get-tuple-element.184) | copy-start | bytes 1156
  21.6 24.0 %copy-start.32 = (f32[96]{0:T(128)}, f32[96]{0:T(128)S(1)}, u32[]{:S(2)}) copy-start(f32[96]{0:T(128)S(1)} %get-tuple-element.185) | copy-start | bytes 1156
  21.6 24.0 %copy-start.34 = (f32[96]{0:T(128)}, f32[96]{0:T(128)S(1)}, u32[]{:S(2)}) copy-start(f32[96]{0:T(128)S(1)} %get-tuple-element.186) | copy-start | bytes 1156
  21.6 24.0 %copy-start.36 = (f32[96]{0:T(128)}, f32[96]{0:T(128)S(1)}, u32[]{:S(2)}) copy-start(f32[96]{0:T(128)S(1)} %get-tuple-element.187) | copy-start | bytes 1156
  21.7 24.0 %copy-start.38 = (f32[96]{0:T(128)}, f32[96]{0:T(128)S(1)}, u32[]{:S(2)}) copy-start(f32[96]{0:T(128)S(1)} %get-tuple-element.188) | copy-start | bytes 1156
  21.7 24.0 %copy-start.40 = (f32[96]{0:T(128)}, f32[96]{0:T(128)S(1)}, u32[]{:S(2)}) copy-start(f32[96]{0:T(128)S(1)} %get-tuple-element.189) | copy-start | bytes 1156
  21.7 24.0 %copy-start.42 = (f32[96]{0:T(128)}, f32[96]{0:T(128)S(1)}, u32[]{:S(2)}) copy-start(f32[96]{0:T(128)S(1)} %get-tuple-element.190) | copy-start | bytes 1156
  21.7 24.0 %copy-start.44 = (f32[96]{0:T(128)}, f32[96]{0:T(128)S(1)}, u32[]{:S(2)}) copy-start(f32[96]{0:T(128)S(1)} %get-tuple-element.191) | copy-start | bytes 1156
  21.7 24.0 %copy-start.46 = (f32[96]{0:T(128)}, f32[96]{0:T(128)S(1)}, u32[]{:S(2)}) copy-start(f32[96]{0:T(128)S(1)} %get-tuple-element.192) | copy-start | bytes 1156
  21.7 24.0 %copy-start.48 = (f32[96]{0:T(128)}, f32[96]{0:T(128)S(1)}, u32[]{:S(2)}) copy-start(f32[96]{0:T(128)S(1)} %get-tuple-element.193) | copy-start | bytes 1156
  21.7 24.0 %copy-start.50 = (f32[96]{0:T(128)}, f32[96]{0:T(128)S(1)}, u32[]{:S(2)}) copy-start(f32[96]{0:T(128)S(1)} %get-tuple-element.194) | copy-start | bytes 1156
  21.7 24.0 %copy-start.52 = (f32[96]{0:T(128)}, f32[96]{0:T(128)S(1)}, u32[]{:S(2)}) copy-start(f32[96]{0:T(128)S(1)} %get-tuple-element.195) | copy-start | bytes 1156
  21.8 24.0 %copy-start.54 = (f32[96]{0:T(128)}, f32[96]{0:T(128)S(1)}, u32[]{:S(2)}) copy-start(f32[96]{0:T(128)S(1)} %get-tuple-element.196) | copy-start | bytes 1156
  21.8 24.0 %copy-start.56 = (f32[96]{0:T(128)}, f32[96]{0:T(128)S(1)}, u32[]{:S(2)}) copy-start(f32[96]{0:T(128)S(1)} %get-tuple-element.197) | copy-start | bytes 1156
  21.8 24.0 %copy-start.58 = (f32[96]{0:T(128)}, f32[96]{0:T(128)S(1)}, u32[]{:S(2)}) copy-start(f32[96]{0:T(128)S(1)} %get-tuple-element.198) | copy-start | bytes 1156
  21.8 24.0 %copy-start.60 = (f32[96]{0:T(128)}, f32[96]{0:T(128)S(1)}, u32[]{:S(2)}) copy-start(f32[96]{0:T(128)S(1)} %get-tuple-element.199) | copy-start | bytes 1156
  21.8 24.0 %copy-start.62 = (f32[96]{0:T(128)}, f32[96]{0:T(128)S(1)}, u32[]{:S(2)}) copy-start(f32[96]{0:T(128)S(1)} %get-tuple-element.200) | copy-start | bytes 1156
  21.8 24.0 %copy-start.64 = (f32[96]{0:T(128)}, f32[96]{0:T(128)S(1)}, u32[]{:S(2)}) copy-start(f32[96]{0:T(128)S(1)} %get-tuple-element.201) | copy-start | bytes 1156
  21.8 24.0 %copy-start.66 = (f32[96]{0:T(128)}, f32[96]{0:T(128)S(1)}, u32[]{:S(2)}) copy-start(f32[96]{0:T(128)S(1)} %get-tuple-element.202) | copy-start | bytes 1156
  21.8 24.0 %copy-start.68 = (f32[96]{0:T(128)}, f32[96]{0:T(128)S(1)}, u32[]{:S(2)}) copy-start(f32[96]{0:T(128)S(1)} %get-tuple-element.203) | copy-start | bytes 1156
  31.5 6.6 %collective-permute-start.2 = (bf16[96,6,3]{2,0,1:T(8,128)(2,1)S(1)}, bf16[96,6,3]{2,0,1:T(8,128)(2,1)S(1)}, u32[]{:S(2)}, u32[]{:S(2)}) collective-permute-start(bf16[96,6,3]{2,0,1:T(8,128)(2,1)S(1)} %get-tuple-element.166), channel_id=1, source_target_pairs={{0,8},{8,16},{16,24},{24,32},{32,40},{40,48},{48,56},{56,64},{64,7... | collective-permute-start | bytes 10376 | tf_op jit(solution)/shard_map/ppermute | solution.py:14
  33.8 8.6 %collective-permute-start.3 = (bf16[96,6,3]{2,0,1:T(8,128)(2,1)S(1)}, bf16[96,6,3]{2,0,1:T(8,128)(2,1)S(1)}, u32[]{:S(2)}, u32[]{:S(2)}) collective-permute-start(bf16[96,6,3]{2,0,1:T(8,128)(2,1)S(1)} %get-tuple-element.167), channel_id=1, source_target_pairs={{8,0},{16,8},{24,16},{32,24},{40,32},{48,40},{56,48},{64,56},{72,6... | collective-permute-start | bytes 10376 | tf_op jit(solution)/shard_map/ppermute | solution.py:17
  64.8 3.3 %collective-permute-start.10 = (f32[39600]{0:T(1024)S(1)}, f32[39600]{0:T(1024)S(1)}, u32[]{:S(2)}, u32[]{:S(2)}) collective-permute-start(f32[39600]{0:T(1024)S(1)} %dynamic_slice.13), channel_id=1, source_target_pairs={{0,8},{8,0},{16,24},{24,16},{32,40},{40,32},{48,56},{56,48},{64,72... | collective-permute-start | bytes 475208 | tf_op jit(solution)/shard_map/ppermute | solution.py:58
  68.2 25.1 %copy-start.10 = (bf16[96,768]{1,0:T(8,128)(2,1)S(1)}, bf16[96,768]{1,0:T(8,128)(2,1)}, u32[]{:S(2)}) copy-start(bf16[96,768]{1,0:T(8,128)(2,1)} %get-tuple-element.150) | copy-start | bytes 442372
  68.3 5.8 %collective-permute-start.11 = (f32[19800]{0:T(1024)S(1)}, f32[19800]{0:T(1024)S(1)}, u32[]{:S(2)}, u32[]{:S(2)}) collective-permute-start(f32[19800]{0:T(1024)S(1)} %dynamic_slice.15), channel_id=1, source_target_pairs={{0,16},{8,24},{16,0},{24,8},{32,48},{40,56},{48,32},{56,40},{64,80... | collective-permute-start | bytes 237608 | tf_op jit(solution)/shard_map/ppermute | solution.py:58
  74.2 8.7 %collective-permute-start.12 = (f32[19800]{0:T(1024)S(1)}, f32[19800]{0:T(1024)S(1)}, u32[]{:S(2)}, u32[]{:S(2)}) collective-permute-start(f32[19800]{0:T(1024)S(1)} %dynamic-slice_add_fusion.1), channel_id=1, source_target_pairs={{0,32},{8,40},{16,48},{24,56},{32,0},{40,8},{48,16},{56,24},{64,96... | collective-permute-start | bytes 237608 | tf_op jit(solution)/shard_map/ppermute | solution.py:58
  82.9 10.6 %collective-permute-start.13 = (f32[19800]{0:T(1024)S(1)}, f32[19800]{0:T(1024)S(1)}, u32[]{:S(2)}, u32[]{:S(2)}) collective-permute-start(f32[19800]{0:T(1024)S(1)} %add.981), channel_id=1, source_target_pairs={{0,64},{8,72},{16,80},{24,88},{32,96},{40,104},{48,112},{56,120},{... | collective-permute-start | bytes 237608 | tf_op jit(solution)/shard_map/ppermute | solution.py:58
  86.7 20.1 %collective-permute-start.6 = (f32[96,8,3]{2,0,1:T(8,128)S(1)}, f32[96,8,3]{2,0,1:T(8,128)S(1)}, u32[]{:S(2)}, u32[]{:S(2)}) collective-permute-start(f32[96,8,3]{2,0,1:T(8,128)S(1)} %get-tuple-element.139), channel_id=1, source_target_pairs={{0,8},{8,16},{16,24},{24,32},{32,40},{40,48},{48,56},{56,64},{64,7... | collective-permute-start | bytes 27656 | tf_op jit(solution)/shard_map/ppermute | solution.py:14
  91.3 15.5 %collective-permute-start.7 = (f32[96,8,3]{2,0,1:T(8,128)S(1)}, f32[96,8,3]{2,0,1:T(8,128)S(1)}, u32[]{:S(2)}, u32[]{:S(2)}) collective-permute-start(f32[96,8,3]{2,0,1:T(8,128)S(1)} %get-tuple-element.140), channel_id=1, source_target_pairs={{8,0},{16,8},{24,16},{32,24},{40,32},{48,40},{56,48},{64,56},{72,6... | collective-permute-start | bytes 27656 | tf_op jit(solution)/shard_map/ppermute | solution.py:17
  93.5 10.0 %collective-permute-start.14 = (f32[19800]{0:T(1024)S(1)}, f32[19800]{0:T(1024)S(1)}, u32[]{:S(2)}, u32[]{:S(2)}) collective-permute-start(f32[19800]{0:T(1024)S(1)} %add.982), channel_id=1, source_target_pairs={{0,128},{8,136},{16,144},{24,152},{32,160},{40,168},{48,176},{56,1... | collective-permute-start | bytes 237608 | tf_op jit(solution)/shard_map/ppermute | solution.py:58
  103.5 7.5 %collective-permute-start.15 = (f32[19800]{0:T(1024)S(1)}, f32[19800]{0:T(1024)S(1)}, u32[]{:S(2)}, u32[]{:S(2)}) collective-permute-start(f32[19800]{0:T(1024)S(1)} %add.983), channel_id=1, source_target_pairs={{0,256},{8,264},{16,272},{24,280},{32,288},{40,296},{48,304},{56,3... | collective-permute-start | bytes 237608 | tf_op jit(solution)/shard_map/ppermute | solution.py:58
  111.0 11.5 %collective-permute-start.16 = (f32[19800]{0:T(1024)S(1)}, f32[19800]{0:T(1024)S(1)}, u32[]{:S(2)}, u32[]{:S(2)}) collective-permute-start(f32[19800]{0:T(1024)S(1)} %add.984), channel_id=1, source_target_pairs={{0,1},{1,0},{2,3},{3,2},{4,5},{5,4},{6,7},{7,6},{8,9},{9,8},{10,11... | collective-permute-start | bytes 237608 | tf_op jit(solution)/shard_map/ppermute | solution.py:58
  119.2 20.3 %collective-permute-start.8 = (bf16[96,3,134]{2,0,1:T(8,128)(2,1)S(1)}, bf16[96,3,134]{2,0,1:T(8,128)(2,1)S(1)}, u32[]{:S(2)}, u32[]{:S(2)}) collective-permute-start(bf16[96,3,134]{2,0,1:T(8,128)(2,1)S(1)} %get-tuple-element.137), channel_id=1, source_target_pairs={{0,1},{1,2},{2,3},{3,4},{4,5},{5,6},{6,7},{8,9},{9,10},{10,11},{11... | collective-permute-start | bytes 231560 | tf_op jit(solution)/shard_map/ppermute | solution.py:14
  121.2 18.4 %collective-permute-start.9 = (bf16[96,3,134]{2,0,1:T(8,128)(2,1)S(1)}, bf16[96,3,134]{2,0,1:T(8,128)(2,1)S(1)}, u32[]{:S(2)}, u32[]{:S(2)}) collective-permute-start(bf16[96,3,134]{2,0,1:T(8,128)(2,1)S(1)} %get-tuple-element.138), channel_id=1, source_target_pairs={{1,0},{2,1},{3,2},{4,3},{5,4},{6,5},{7,6},{9,8},{10,9},{11,10},{12... | collective-permute-start | bytes 231560 | tf_op jit(solution)/shard_map/ppermute | solution.py:17
  122.5 11.8 %collective-permute-start.17 = (f32[19800]{0:T(1024)S(1)}, f32[19800]{0:T(1024)S(1)}, u32[]{:S(2)}, u32[]{:S(2)}) collective-permute-start(f32[19800]{0:T(1024)S(1)} %add.985), channel_id=1, source_target_pairs={{0,2},{1,3},{2,0},{3,1},{4,6},{5,7},{6,4},{7,5},{8,10},{9,11},{10,... | collective-permute-start | bytes 237608 | tf_op jit(solution)/shard_map/ppermute | solution.py:58
  134.3 7.4 %collective-permute-start.18 = (f32[19800]{0:T(1024)S(1)}, f32[19800]{0:T(1024)S(1)}, u32[]{:S(2)}, u32[]{:S(2)}) collective-permute-start(f32[19800]{0:T(1024)S(1)} %add.986), channel_id=1, source_target_pairs={{0,4},{1,5},{2,6},{3,7},{4,0},{5,1},{6,2},{7,3},{8,12},{9,13},{10,... | collective-permute-start | bytes 237608 | tf_op jit(solution)/shard_map/ppermute | solution.py:58
  141.7 5.2 %collective-permute-start.19 = (f32[19800]{0:T(1024)S(1)}, f32[19800]{0:T(1024)S(1)}, u32[]{:S(2)}, u32[]{:S(2)}) collective-permute-start(f32[19800]{0:T(1024)S(1)} %add.987), channel_id=1, source_target_pairs={{0,16},{8,24},{16,0},{24,8},{32,48},{40,56},{48,32},{56,40},{64,80... | collective-permute-start | bytes 237608 | tf_op jit(solution)/shard_map/ppermute | solution.py:58
  147.0 14.0 %collective-permute-start.20 = (f32[39600]{0:T(1024)S(1)}, f32[39600]{0:T(1024)S(1)}, u32[]{:S(2)}, u32[]{:S(2)}) collective-permute-start(f32[39600]{0:T(1024)S(1)} %maximum_select_fusion.1), channel_id=1, source_target_pairs={{0,8},{8,0},{16,24},{24,16},{32,40},{40,32},{48,56},{56,48},{64,72... | collective-permute-start | bytes 475208 | tf_op jit(solution)/shard_map/ppermute | solution.py:58
  (84 other events, 806.4 us)

commit v6 on v3

--- a/solution.py
+++ b/solution.py
@@ -17,6 +17,35 @@
         high = lax.ppermute(lax.slice_in_dim(block, 0, width, axis=dim), axis, backward)
         block = jnp.concatenate([low, block, high], axis=dim)
     return block
+
+
+def padded_one_round(block, width):
+    cols, rows = lax.axis_size("col"), lax.axis_size("row")
+    height, breadth = block.shape[1], block.shape[2]
+    top, bottom = slice(0, width), slice(height - width, height)
+    first, last = slice(0, width), slice(breadth - width, breadth)
+
+    def moved(piece, dc, dr):
+        pairs = [
+            (c * rows + r, (c + dc) * rows + (r + dr))
+            for c in range(cols)
+            for r in range(rows)
+            if 0 <= c + dc < cols and 0 <= r + dr < rows
+        ]
+        return lax.ppermute(piece, ("col", "row"), pairs)
+
+    above = lax.ppermute(block[:, bottom, :], "row", [(i, i + 1) for i in range(rows - 1)])
+    below = lax.ppermute(block[:, top, :], "row", [(i + 1, i) for i in range(rows - 1)])
+    left = lax.ppermute(block[:, :, last], "col", [(i, i + 1) for i in range(cols - 1)])
+    right = lax.ppermute(block[:, :, first], "col", [(i + 1, i) for i in range(cols - 1)])
+    top_left = moved(block[:, bottom, last], 1, 1)
+    top_right = moved(block[:, bottom, first], -1, 1)
+    bottom_left = moved(block[:, top, last], 1, -1)
+    bottom_right = moved(block[:, top, first], -1, -1)
+    upper = jnp.concatenate([top_left, above, top_right], axis=2)
+    middle = jnp.concatenate([left, block, right], axis=2)
+    lower = jnp.concatenate([bottom_left, below, bottom_right], axis=2)
+    return jnp.concatenate([upper, middle, lower], axis=1)
 
 
 def from_behind(value, axis, steps):
@@ -132,7 +161,7 @@
 def local(image, cotangent, dw_kernel, dw_bias, ln_gain, ln_bias, w_in, b_in, w_out, layer_scale):
     channels, height, breadth = image.shape
     pixels = height * breadth
-    padded = padded_2(image, (("col", 2), ("row", 1)), 3)
+    padded = padded_one_round(image, 3)
     conv_out = conv_seven(padded, dw_kernel) + dw_bias[:, None, None]
     block_flat, grad_flat, sums = mixing(
         conv_out.reshape(channels, pixels),

time: 155 us -> 176 us (1.14)
  starting transfers between devices: 78.5 us -> 109 us
  waiting for transfers between devices: 34.4 us -> 25.2 us
    ppermute x0 -> x8, starting transfers between devices: none -> 32.4 us  [the longest x4 16.3 us: moved(): return lax.ppermute(piece, ('col', 'row'), pairs)]
    ppermute x11, starting transfers between devices: 47.3 us -> 60.6 us  [xor_partner(): lax.ppermute(value, axis, [(i, i ^ mask) for i in range(lax.axis_size(axi...]
    ppermute x4 -> x2, starting transfers between devices: 24.7 us -> 11.7 us  [padded_2(): lax.ppermute(lax.slice_in_dim(block, block.shape[dim] - width, None, axis...]
    ppermute x4 -> x2, waiting for transfers between devices: 10.2 us -> 0.01 us  [padded_2(): lax.ppermute(lax.slice_in_dim(block, 0, width, axis=dim), axis, backward)]
    ppermute x0 -> x8, waiting for transfers between devices: none -> 9.34 us  [the longest x1 9.32 us: padded_one_round(): lax.ppermute(block[:, top, :], 'row', [(i + 1, i) for i in range(rows - 1)])]
    ppermute x11, waiting for transfers between devices: 24.2 us -> 15.9 us  [xor_partner(): lax.ppermute(value, axis, [(i, i ^ mask) for i in range(lax.axis_size(axi...]
    ppermute x4 -> x2, starting transfers between devices: 6.57 us -> 4.14 us  [padded_2(): lax.ppermute(lax.slice_in_dim(block, 0, width, axis=dim), axis, backward)]
  transfers between devices with their start and end apart: 19 -> 23, of which waited for: 11 -> 9; matrix products, arithmetic and copies ran while one was open for 7% -> 6% of each run, Pallas kernels for 0% -> 0%
where the time goes in v6:
time: 176 us; the launch traced here: 173 us
  starting transfers between devices  109 us (62%)
  waiting for transfers between devices  25.2 us (14%)
  other arithmetic  17.3 us (10%)
  local copies, waits for them, and re-layouts  14.5 us (8%)
  matrix products  5.07 us (3%)
  between operations  2.49 us (1%)
    ppermute x11, starting transfers between devices, xor_partner(): lax.ppermute(value, axis, [(i, i ^ mask) for i in range(lax.axis_size(axi...  60.6 us
    ppermute x4, starting transfers between devices, moved(): return lax.ppermute(piece, ('col', 'row'), pairs)  16.3 us
    ppermute x11, waiting for transfers between devices, xor_partner(): lax.ppermute(value, axis, [(i, i ^ mask) for i in range(lax.axis_size(axi...  15.9 us
    ppermute x2, starting transfers between devices, padded_2(): lax.ppermute(lax.slice_in_dim(block, block.shape[dim] - width, None, axis...  11.7 us
    ppermute x1, waiting for transfers between devices, padded_one_round(): lax.ppermute(block[:, top, :], 'row', [(i + 1, i) for i in range(rows - 1)])  9.32 us
    ppermute x1, starting transfers between devices, padded_one_round(): lax.ppermute(block[:, bottom, :], 'row', [(i, i + 1) for i in range(rows...  9.11 us
    unnamed x166, local copies, waits for them, and re-layouts  5.8 us
    dot_general x6, matrix products, product(): return jnp.einsum(form, left, right, preferred_element_type=jnp.float32)  5.07 us
  transfers between devices with their start and end apart: 23, of which 9 were waited for; matrix products, arithmetic and copies ran while one was open for 6% of the time, Pallas kernels for 0%

profile of v6, /device:TPU:57, one launch (start us, length us, event | category | flops | bytes accessed | tf_op | source)
XLA Modules:
  0.0 173.4 jit_solution(2151571287260711874)
XLA Ops:
  0.7 1.2 copy.24
  1.8 3.8 %collective-permute-start.3 = (bf16[96,8,3]{0,2,1:T(4,128)(2,1)S(1)}, bf16[96,8,3]{0,2,1:T(4,128)(2,1)S(1)}, u32[]{:S(2)}, u32[]{:S(2)}) collective-permute-start(bf16[96,8,3]{0,2,1:T(4,128)(2,1)S(1)} %get-tuple-element.116), channel_id=1, source_target_pairs={{0,8},{8,16},{16,24},{24,32},{32,40},{40,48},{48,56},{56,64},{64,7... | collective-permute-start | bytes 13832 | tf_op jit(solution)/shard_map/ppermute | solution.py:39
  5.6 1.9 %collective-permute-start.4 = (bf16[96,8,3]{0,2,1:T(4,128)(2,1)S(1)}, bf16[96,8,3]{0,2,1:T(4,128)(2,1)S(1)}, u32[]{:S(2)}, u32[]{:S(2)}) collective-permute-start(bf16[96,8,3]{0,2,1:T(4,128)(2,1)S(1)} %get-tuple-element.117), channel_id=1, source_target_pairs={{8,0},{16,8},{24,16},{32,24},{40,32},{48,40},{56,48},{64,56},{72,6... | collective-permute-start | bytes 13832 | tf_op jit(solution)/shard_map/ppermute | solution.py:40
  7.6 12.4 %collective-permute-start = (bf16[96,3,3]{0,2,1:T(4,128)(2,1)S(1)}, bf16[96,3,3]{0,2,1:T(4,128)(2,1)S(1)}, u32[]{:S(2)}, u32[]{:S(2)}) collective-permute-start(bf16[96,3,3]{0,2,1:T(4,128)(2,1)S(1)} %get-tuple-element.110), channel_id=1, source_target_pairs={{0,9},{1,10},{2,11},{3,12},{4,13},{5,14},{6,15},{8,17},{9,18},{10,... | collective-permute-start | bytes 5192 | tf_op jit(solution)/shard_map/ppermute | solution.py:35
  20.0 1.3 collective-permute-start.2
  21.3 1.3 collective-permute-start.5
  22.6 1.0 slice_bitcast_fusion.48
  23.6 1.0 slice_bitcast_fusion.47
  24.7 1.3 collective-permute-start.7
  26.0 9.1 %collective-permute-start.1 = (bf16[96,3,128]{0,2,1:T(8,128)(2,1)S(1)}, bf16[96,3,128]{0,2,1:T(8,128)(2,1)S(1)}, u32[]{:S(2)}, u32[]{:S(2)}) collective-permute-start(bf16[96,3,128]{0,2,1:T(8,128)(2,1)S(1)} %get-tuple-element.114), channel_id=1, source_target_pairs={{0,1},{1,2},{2,3},{3,4},{4,5},{5,6},{6,7},{8,9},{9,10},{10,11},{11... | collective-permute-start | bytes 221192 | tf_op jit(solution)/shard_map/ppermute | solution.py:37
  35.1 1.3 collective-permute-start.6
  36.4 0.9 slice_bitcast_fusion.46
  37.5 1.1 copy.38
  38.7 0.9 copy.101
  39.6 9.3 %collective-permute-done.6 = bf16[96,3,128]{0,2,1:T(8,128)(2,1)S(1)} collective-permute-done((bf16[96,3,128]{0,2,1:T(8,128)(2,1)S(1)}, bf16[96,3,128]{0,2,1:T(8,128)(2,1)S(1)}, u32[]{:S(2)}, u32[]{:S(2)}) %collective-permute-start.6) | collective-permute-done | bytes 73760 | tf_op jit(solution)/shard_map/ppermute | solution.py:38
  49.4 4.3 %fusion.180 = (f32[8,128]{1,0:T(8,128)S(1)}, f32[96,8,128]{0,2,1:T(8,128)S(1)}) fusion(f32[96]{0:T(128)S(1)} %copy-done.77, bf16[96,11,134]{0,2,1:T(8,128)(2,1)S(1)} %get-tuple-element.109, f32[96]{0:T(128)S(1)} %get-tuple-element.165, f32[96]{0:T(128)S(1)} %get-tuple-element.166, f32[96]{0:T(128)S(1)} %get-tuple-element.119, f32[96]{0:T(128)S(1)} %get-tuple-element.120, ...), kind=kLoop, calls=%fused_computation.426 | loop fusion | flops 16317440 | bytes 8879872 | tf_op jit(solution)/shard_map/reduce_sum | solution.py:129
  55.2 2.0 %convert_reduce_fusion = (f32[384]{0:T(512)}, bf16[384,1024]{0,1:T(8,128)(2,1)S(1)}) fusion(f32[1024,384]{1,0:T(8,128)S(1)} %get-tuple-element.170, bf16[384,96]{0,1:T(8,128)(2,1)S(1)} %copy-done.4, f32[96,1024]{1,0:T(8,128)S(1)} %copy.103, f32[96]{0:T(128)S(1)} %copy-done.48), kind=kOutput, calls=%fused_computation.16 | convolution fusion | flops 84344448 | bytes 2828160 | tf_op jit(solution)/shard_map/hc,cp->hp/dot_general | solution.py:125
  57.5 1.0 fusion.168
  58.5 1.5 fusion.179
  60.0 1.2 copy.104
  61.2 1.1 fusion.123
  62.4 1.9 %fusion.141 = (f32[96]{0:T(128)}, f32[96]{0:T(128)}, f32[96]{0:T(128)}, f32[96]{0:T(128)}, f32[96]{0:T(128)}, /*index=5*/f32[96]{0:T(128)}, f32[96]{0:T(128)}, f...) fusion(bf16[96,11,134]{0,2,1:T(8,128)(2,1)S(1)} %get-tuple-elem, ...), kind=kLoop, calls=%fused_computation.256 | loop fusion | flops 5306688 | bytes 3939072 | tf_op jit(solution)/shard_map/reduce_sum | solution.py:77
  64.4 1.3 fusion.91
  68.3 1.6 concatenate.157
  70.0 1.9 %collective-permute-start.12 = (f32[39600]{0:T(1024)S(1)}, f32[39600]{0:T(1024)S(1)}, u32[]{:S(2)}, u32[]{:S(2)}) collective-permute-start(f32[39600]{0:T(1024)S(1)} %dynamic_slice.13), channel_id=1, source_target_pairs={{0,8},{8,0},{16,24},{24,16},{32,40},{40,32},{48,56},{56,48},{64,72... | collective-permute-start | bytes 475208 | tf_op jit(solution)/shard_map/ppermute | solution.py:87
  72.0 1.3 collective-permute-done.12
  73.5 1.9 %collective-permute-start.13 = (f32[19800]{0:T(1024)S(1)}, f32[19800]{0:T(1024)S(1)}, u32[]{:S(2)}, u32[]{:S(2)}) collective-permute-start(f32[19800]{0:T(1024)S(1)} %dynamic_slice.15), channel_id=1, source_target_pairs={{0,16},{8,24},{16,0},{24,8},{32,48},{40,56},{48,32},{56,40},{64,80... | collective-permute-start | bytes 237608 | tf_op jit(solution)/shard_map/ppermute | solution.py:87
  75.4 3.9 %collective-permute-done.13 = f32[19800]{0:T(1024)S(1)} collective-permute-done((f32[19800]{0:T(1024)S(1)}, f32[19800]{0:T(1024)S(1)}, u32[]{:S(2)}, u32[]{:S(2)}) %collective-permute-start.13) | collective-permute-done | bytes 79232 | tf_op jit(solution)/shard_map/ppermute | solution.py:87
  79.4 5.0 %collective-permute-start.14 = (f32[19800]{0:T(1024)S(1)}, f32[19800]{0:T(1024)S(1)}, u32[]{:S(2)}, u32[]{:S(2)}) collective-permute-start(f32[19800]{0:T(1024)S(1)} %dynamic-slice_add_fusion.1), channel_id=1, source_target_pairs={{0,32},{8,40},{16,48},{24,56},{32,0},{40,8},{48,16},{56,24},{64,96... | collective-permute-start | bytes 237608 | tf_op jit(solution)/shard_map/ppermute | solution.py:87
  84.4 1.8 %collective-permute-done.14 = f32[19800]{0:T(1024)S(1)} collective-permute-done((f32[19800]{0:T(1024)S(1)}, f32[19800]{0:T(1024)S(1)}, u32[]{:S(2)}, u32[]{:S(2)}) %collective-permute-start.14) | collective-permute-done | bytes 79232 | tf_op jit(solution)/shard_map/ppermute | solution.py:87
  86.3 8.1 %collective-permute-start.15 = (f32[19800]{0:T(1024)S(1)}, f32[19800]{0:T(1024)S(1)}, u32[]{:S(2)}, u32[]{:S(2)}) collective-permute-start(f32[19800]{0:T(1024)S(1)} %add.505), channel_id=1, source_target_pairs={{0,64},{8,72},{16,80},{24,88},{32,96},{40,104},{48,112},{56,120},{... | collective-permute-start | bytes 237608 | tf_op jit(solution)/shard_map/ppermute | solution.py:87
  94.3 1.9 %collective-permute-done.15 = f32[19800]{0:T(1024)S(1)} collective-permute-done((f32[19800]{0:T(1024)S(1)}, f32[19800]{0:T(1024)S(1)}, u32[]{:S(2)}, u32[]{:S(2)}) %collective-permute-start.15) | collective-permute-done | bytes 79232 | tf_op jit(solution)/shard_map/ppermute | solution.py:87
  96.3 6.0 %collective-permute-start.16 = (f32[19800]{0:T(1024)S(1)}, f32[19800]{0:T(1024)S(1)}, u32[]{:S(2)}, u32[]{:S(2)}) collective-permute-start(f32[19800]{0:T(1024)S(1)} %add.506), channel_id=1, source_target_pairs={{0,128},{8,136},{16,144},{24,152},{32,160},{40,168},{48,176},{56,1... | collective-permute-start | bytes 237608 | tf_op jit(solution)/shard_map/ppermute | solution.py:87
  102.3 1.8 %collective-permute-done.16 = f32[19800]{0:T(1024)S(1)} collective-permute-done((f32[19800]{0:T(1024)S(1)}, f32[19800]{0:T(1024)S(1)}, u32[]{:S(2)}, u32[]{:S(2)}) %collective-permute-start.16) | collective-permute-done | bytes 79232 | tf_op jit(solution)/shard_map/ppermute | solution.py:87
  104.1 3.9 %collective-permute-start.17 = (f32[19800]{0:T(1024)S(1)}, f32[19800]{0:T(1024)S(1)}, u32[]{:S(2)}, u32[]{:S(2)}) collective-permute-start(f32[19800]{0:T(1024)S(1)} %add.507), channel_id=1, source_target_pairs={{0,256},{8,264},{16,272},{24,280},{32,288},{40,296},{48,304},{56,3... | collective-permute-start | bytes 237608 | tf_op jit(solution)/shard_map/ppermute | solution.py:87
  108.0 7.0 %collective-permute-start.8 = (f32[96,8,3]{0,2,1:T(4,128)S(1)}, f32[96,8,3]{0,2,1:T(4,128)S(1)}, u32[]{:S(2)}, u32[]{:S(2)}) collective-permute-start(f32[96,8,3]{0,2,1:T(4,128)S(1)} %get-tuple-element.94), channel_id=1, source_target_pairs={{0,8},{8,16},{16,24},{24,32},{32,40},{40,48},{48,56},{56,64},{64,7... | collective-permute-start | bytes 27656 | tf_op jit(solution)/shard_map/ppermute | solution.py:14
  115.1 2.8 %collective-permute-start.9 = (f32[96,8,3]{0,2,1:T(4,128)S(1)}, f32[96,8,3]{0,2,1:T(4,128)S(1)}, u32[]{:S(2)}, u32[]{:S(2)}) collective-permute-start(f32[96,8,3]{0,2,1:T(4,128)S(1)} %get-tuple-element.95), channel_id=1, source_target_pairs={{8,0},{16,8},{24,16},{32,24},{40,32},{48,40},{56,48},{64,56},{72,6... | collective-permute-start | bytes 27656 | tf_op jit(solution)/shard_map/ppermute | solution.py:17
  118.0 9.2 %collective-permute-start.18 = (f32[19800]{0:T(1024)S(1)}, f32[19800]{0:T(1024)S(1)}, u32[]{:S(2)}, u32[]{:S(2)}) collective-permute-start(f32[19800]{0:T(1024)S(1)} %add.508), channel_id=1, source_target_pairs={{0,1},{1,0},{2,3},{3,2},{4,5},{5,4},{6,7},{7,6},{8,9},{9,8},{10,11... | collective-permute-start | bytes 237608 | tf_op jit(solution)/shard_map/ppermute | solution.py:87
  127.2 1.6 collective-permute-done.18
  128.9 5.2 %collective-permute-start.19 = (f32[19800]{0:T(1024)S(1)}, f32[19800]{0:T(1024)S(1)}, u32[]{:S(2)}, u32[]{:S(2)}) collective-permute-start(f32[19800]{0:T(1024)S(1)} %add.509), channel_id=1, source_target_pairs={{0,2},{1,3},{2,0},{3,1},{4,6},{5,7},{6,4},{7,5},{8,10},{9,11},{10,... | collective-permute-start | bytes 237608 | tf_op jit(solution)/shard_map/ppermute | solution.py:87
  134.1 4.7 %collective-permute-start.10 = (bf16[96,3,134]{0,2,1:T(8,128)(2,1)S(1)}, bf16[96,3,134]{0,2,1:T(8,128)(2,1)S(1)}, u32[]{:S(2)}, u32[]{:S(2)}) collective-permute-start(bf16[96,3,134]{0,2,1:T(8,128)(2,1)S(1)} %get-tuple-element.106), channel_id=1, source_target_pairs={{0,1},{1,2},{2,3},{3,4},{4,5},{5,6},{6,7},{8,9},{9,10},{10,11},{11... | collective-permute-start | bytes 231560 | tf_op jit(solution)/shard_map/ppermute | solution.py:14
  138.8 1.3 collective-permute-start.11
  140.9 9.0 %collective-permute-start.20 = (f32[19800]{0:T(1024)S(1)}, f32[19800]{0:T(1024)S(1)}, u32[]{:S(2)}, u32[]{:S(2)}) collective-permute-start(f32[19800]{0:T(1024)S(1)} %add.510), channel_id=1, source_target_pairs={{0,4},{1,5},{2,6},{3,7},{4,0},{5,1},{6,2},{7,3},{8,12},{9,13},{10,... | collective-permute-start | bytes 237608 | tf_op jit(solution)/shard_map/ppermute | solution.py:87
  150.1 1.8 %collective-permute-done.20 = f32[19800]{0:T(1024)S(1)} collective-permute-done((f32[19800]{0:T(1024)S(1)}, f32[19800]{0:T(1024)S(1)}, u32[]{:S(2)}, u32[]{:S(2)}) %collective-permute-start.20) | collective-permute-done | bytes 79232 | tf_op jit(solution)/shard_map/ppermute | solution.py:87
  152.0 3.4 %collective-permute-start.21 = (f32[19800]{0:T(1024)S(1)}, f32[19800]{0:T(1024)S(1)}, u32[]{:S(2)}, u32[]{:S(2)}) collective-permute-start(f32[19800]{0:T(1024)S(1)} %add.511), channel_id=1, source_target_pairs={{0,16},{8,24},{16,0},{24,8},{32,48},{40,56},{48,32},{56,40},{64,80... | collective-permute-start | bytes 237608 | tf_op jit(solution)/shard_map/ppermute | solution.py:87
  155.5 1.7 collective-permute-done.21
  157.3 7.0 %collective-permute-start.22 = (f32[39600]{0:T(1024)S(1)}, f32[39600]{0:T(1024)S(1)}, u32[]{:S(2)}, u32[]{:S(2)}) collective-permute-start(f32[39600]{0:T(1024)S(1)} %maximum_select_fusion.1), channel_id=1, source_target_pairs={{0,8},{8,0},{16,24},{24,16},{32,40},{40,32},{48,56},{56,48},{64,72... | collective-permute-start | bytes 475208 | tf_op jit(solution)/shard_map/ppermute | solution.py:87
  164.6 4.0 %fusion.144 = bf16[96,8,128]{0,2,1:T(8,128)(2,1)S(1)} fusion(f32[96,11,134]{0,2,1:T(8,128)S(1)} %get-tuple-element.93, f32[96,8,3]{0,2,1:T(4,128)S(1)} %collective-permute-done.9, f32[96,8,128]{0,2,1:T(8,128)S(1)} %bitcast.262, f32[96,8,3]{0,2,1:T(4,128)S(1)} %collective-permute-done.8, f32[96,11,134]{0,2,1:T(8,128)S(1)} %get-tuple-element.92, ...), kind=kLoop, calls=%fused_computation.260 | loop fusion | flops 10420224 | bytes 17338752 | tf_op jit(solution)/shard_map/convert_element_type | solution.py:187
  (224 shorter events, 11.1 us)
Async XLA Ops:
  0.6 53.6 %copy-start = (bf16[96,384]{1,0:T(8,128)(2,1)S(1)}, bf16[96,384]{1,0:T(8,128)(2,1)}, u32[]{:S(2)}) copy-start(bf16[96,384]{1,0:T(8,128)(2,1)} %param.16) | copy-start | bytes 221188
  1.8 37.8 %collective-permute-start.3 = (bf16[96,8,3]{0,2,1:T(4,128)(2,1)S(1)}, bf16[96,8,3]{0,2,1:T(4,128)(2,1)S(1)}, u32[]{:S(2)}, u32[]{:S(2)}) collective-permute-start(bf16[96,8,3]{0,2,1:T(4,128)(2,1)S(1)} %get-tuple-element.116), channel_id=1, source_target_pairs={{0,8},{8,16},{16,24},{24,32},{32,40},{40,48},{48,56},{56,64},{64,7... | collective-permute-start | bytes 13832 | tf_op jit(solution)/shard_map/ppermute | solution.py:39
  5.6 34.0 %collective-permute-start.4 = (bf16[96,8,3]{0,2,1:T(4,128)(2,1)S(1)}, bf16[96,8,3]{0,2,1:T(4,128)(2,1)S(1)}, u32[]{:S(2)}, u32[]{:S(2)}) collective-permute-start(bf16[96,8,3]{0,2,1:T(4,128)(2,1)S(1)} %get-tuple-element.117), channel_id=1, source_target_pairs={{8,0},{16,8},{24,16},{32,24},{40,32},{48,40},{56,48},{64,56},{72,6... | collective-permute-start | bytes 13832 | tf_op jit(solution)/shard_map/ppermute | solution.py:40
  7.6 17.1 %collective-permute-start = (bf16[96,3,3]{0,2,1:T(4,128)(2,1)S(1)}, bf16[96,3,3]{0,2,1:T(4,128)(2,1)S(1)}, u32[]{:S(2)}, u32[]{:S(2)}) collective-permute-start(bf16[96,3,3]{0,2,1:T(4,128)(2,1)S(1)} %get-tuple-element.110), channel_id=1, source_target_pairs={{0,9},{1,10},{2,11},{3,12},{4,13},{5,14},{6,15},{8,17},{9,18},{10,... | collective-permute-start | bytes 5192 | tf_op jit(solution)/shard_map/ppermute | solution.py:35
  20.0 6.0 %collective-permute-start.2 = (bf16[96,3,3]{0,2,1:T(4,128)(2,1)S(1)}, bf16[96,3,3]{0,2,1:T(4,128)(2,1)S(1)}, u32[]{:S(2)}, u32[]{:S(2)}) collective-permute-start(bf16[96,3,3]{0,2,1:T(4,128)(2,1)S(1)} %get-tuple-element.113), channel_id=1, source_target_pairs={{8,1},{9,2},{10,3},{11,4},{12,5},{13,6},{14,7},{16,9},{17,10},{18,... | collective-permute-start | bytes 5192 | tf_op jit(solution)/shard_map/ppermute | solution.py:35
  21.3 13.9 %collective-permute-start.5 = (bf16[96,3,3]{0,2,1:T(4,128)(2,1)S(1)}, bf16[96,3,3]{0,2,1:T(4,128)(2,1)S(1)}, u32[]{:S(2)}, u32[]{:S(2)}) collective-permute-start(bf16[96,3,3]{0,2,1:T(4,128)(2,1)S(1)} %get-tuple-element.112), channel_id=1, source_target_pairs={{1,8},{2,9},{3,10},{4,11},{5,12},{6,13},{7,14},{9,16},{10,17},{11,... | collective-permute-start | bytes 5192 | tf_op jit(solution)/shard_map/ppermute | solution.py:35
  24.6 24.6 %copy-start.6 = (f32[96]{0:T(128)}, f32[96]{0:T(128)S(1)}, u32[]{:S(2)}) copy-start(f32[96]{0:T(128)S(1)} %get-tuple-element.146) | copy-start | bytes 1156
  24.6 24.6 %copy-start.8 = (f32[96]{0:T(128)}, f32[96]{0:T(128)S(1)}, u32[]{:S(2)}) copy-start(f32[96]{0:T(128)S(1)} %get-tuple-element.147) | copy-start | bytes 1156
  24.6 24.6 %copy-start.10 = (f32[96]{0:T(128)}, f32[96]{0:T(128)S(1)}, u32[]{:S(2)}) copy-start(f32[96]{0:T(128)S(1)} %get-tuple-element.148) | copy-start | bytes 1156
  24.6 24.6 %copy-start.12 = (f32[96]{0:T(128)}, f32[96]{0:T(128)S(1)}, u32[]{:S(2)}) copy-start(f32[96]{0:T(128)S(1)} %get-tuple-element.149) | copy-start | bytes 1156
  24.6 24.6 %copy-start.14 = (f32[96]{0:T(128)}, f32[96]{0:T(128)S(1)}, u32[]{:S(2)}) copy-start(f32[96]{0:T(128)S(1)} %get-tuple-element.150) | copy-start | bytes 1156
  24.6 24.6 %copy-start.16 = (f32[96]{0:T(128)}, f32[96]{0:T(128)S(1)}, u32[]{:S(2)}) copy-start(f32[96]{0:T(128)S(1)} %get-tuple-element.151) | copy-start | bytes 1156
  24.6 24.6 %copy-start.18 = (f32[96]{0:T(128)}, f32[96]{0:T(128)S(1)}, u32[]{:S(2)}) copy-start(f32[96]{0:T(128)S(1)} %get-tuple-element.152) | copy-start | bytes 1156
  24.6 24.6 %copy-start.20 = (f32[96]{0:T(128)}, f32[96]{0:T(128)S(1)}, u32[]{:S(2)}) copy-start(f32[96]{0:T(128)S(1)} %get-tuple-element.153) | copy-start | bytes 1156
  24.7 24.6 %copy-start.22 = (f32[96]{0:T(128)}, f32[96]{0:T(128)S(1)}, u32[]{:S(2)}) copy-start(f32[96]{0:T(128)S(1)} %get-tuple-element.154) | copy-start | bytes 1156
  24.7 24.6 %copy-start.24 = (f32[96]{0:T(128)}, f32[96]{0:T(128)S(1)}, u32[]{:S(2)}) copy-start(f32[96]{0:T(128)S(1)} %get-tuple-element.155) | copy-start | bytes 1156
  24.7 14.9 %collective-permute-start.7 = (bf16[96,3,3]{0,2,1:T(4,128)(2,1)S(1)}, bf16[96,3,3]{0,2,1:T(4,128)(2,1)S(1)}, u32[]{:S(2)}, u32[]{:S(2)}) collective-permute-start(bf16[96,3,3]{0,2,1:T(4,128)(2,1)S(1)} %get-tuple-element.111), channel_id=1, source_target_pairs={{9,0},{10,1},{11,2},{12,3},{13,4},{14,5},{15,6},{17,8},{18,9},{19,... | collective-permute-start | bytes 5192 | tf_op jit(solution)/shard_map/ppermute | solution.py:35
  26.0 13.6 %collective-permute-start.1 = (bf16[96,3,128]{0,2,1:T(8,128)(2,1)S(1)}, bf16[96,3,128]{0,2,1:T(8,128)(2,1)S(1)}, u32[]{:S(2)}, u32[]{:S(2)}) collective-permute-start(bf16[96,3,128]{0,2,1:T(8,128)(2,1)S(1)} %get-tuple-element.114), channel_id=1, source_target_pairs={{0,1},{1,2},{2,3},{3,4},{4,5},{5,6},{6,7},{8,9},{9,10},{10,11},{11... | collective-permute-start | bytes 221192 | tf_op jit(solution)/shard_map/ppermute | solution.py:37
  35.1 13.8 %collective-permute-start.6 = (bf16[96,3,128]{0,2,1:T(8,128)(2,1)S(1)}, bf16[96,3,128]{0,2,1:T(8,128)(2,1)S(1)}, u32[]{:S(2)}, u32[]{:S(2)}) collective-permute-start(bf16[96,3,128]{0,2,1:T(8,128)(2,1)S(1)} %get-tuple-element.115), channel_id=1, source_target_pairs={{1,0},{2,1},{3,2},{4,3},{5,4},{6,5},{7,6},{9,8},{10,9},{11,10},{12... | collective-permute-start | bytes 221192 | tf_op jit(solution)/shard_map/ppermute | solution.py:38
  70.0 3.3 %collective-permute-start.12 = (f32[39600]{0:T(1024)S(1)}, f32[39600]{0:T(1024)S(1)}, u32[]{:S(2)}, u32[]{:S(2)}) collective-permute-start(f32[39600]{0:T(1024)S(1)} %dynamic_slice.13), channel_id=1, source_target_pairs={{0,8},{8,0},{16,24},{24,16},{32,40},{40,32},{48,56},{56,48},{64,72... | collective-permute-start | bytes 475208 | tf_op jit(solution)/shard_map/ppermute | solution.py:87
  73.5 5.8 %collective-permute-start.13 = (f32[19800]{0:T(1024)S(1)}, f32[19800]{0:T(1024)S(1)}, u32[]{:S(2)}, u32[]{:S(2)}) collective-permute-start(f32[19800]{0:T(1024)S(1)} %dynamic_slice.15), channel_id=1, source_target_pairs={{0,16},{8,24},{16,0},{24,8},{32,48},{40,56},{48,32},{56,40},{64,80... | collective-permute-start | bytes 237608 | tf_op jit(solution)/shard_map/ppermute | solution.py:87
  79.4 6.9 %collective-permute-start.14 = (f32[19800]{0:T(1024)S(1)}, f32[19800]{0:T(1024)S(1)}, u32[]{:S(2)}, u32[]{:S(2)}) collective-permute-start(f32[19800]{0:T(1024)S(1)} %dynamic-slice_add_fusion.1), channel_id=1, source_target_pairs={{0,32},{8,40},{16,48},{24,56},{32,0},{40,8},{48,16},{56,24},{64,96... | collective-permute-start | bytes 237608 | tf_op jit(solution)/shard_map/ppermute | solution.py:87
  86.3 10.0 %collective-permute-start.15 = (f32[19800]{0:T(1024)S(1)}, f32[19800]{0:T(1024)S(1)}, u32[]{:S(2)}, u32[]{:S(2)}) collective-permute-start(f32[19800]{0:T(1024)S(1)} %add.505), channel_id=1, source_target_pairs={{0,64},{8,72},{16,80},{24,88},{32,96},{40,104},{48,112},{56,120},{... | collective-permute-start | bytes 237608 | tf_op jit(solution)/shard_map/ppermute | solution.py:87
  96.3 7.9 %collective-permute-start.16 = (f32[19800]{0:T(1024)S(1)}, f32[19800]{0:T(1024)S(1)}, u32[]{:S(2)}, u32[]{:S(2)}) collective-permute-start(f32[19800]{0:T(1024)S(1)} %add.506), channel_id=1, source_target_pairs={{0,128},{8,136},{16,144},{24,152},{32,160},{40,168},{48,176},{56,1... | collective-permute-start | bytes 237608 | tf_op jit(solution)/shard_map/ppermute | solution.py:87
  104.1 13.8 %collective-permute-start.17 = (f32[19800]{0:T(1024)S(1)}, f32[19800]{0:T(1024)S(1)}, u32[]{:S(2)}, u32[]{:S(2)}) collective-permute-start(f32[19800]{0:T(1024)S(1)} %add.507), channel_id=1, source_target_pairs={{0,256},{8,264},{16,272},{24,280},{32,288},{40,296},{48,304},{56,3... | collective-permute-start | bytes 237608 | tf_op jit(solution)/shard_map/ppermute | solution.py:87
  108.0 19.1 %collective-permute-start.8 = (f32[96,8,3]{0,2,1:T(4,128)S(1)}, f32[96,8,3]{0,2,1:T(4,128)S(1)}, u32[]{:S(2)}, u32[]{:S(2)}) collective-permute-start(f32[96,8,3]{0,2,1:T(4,128)S(1)} %get-tuple-element.94), channel_id=1, source_target_pairs={{0,8},{8,16},{16,24},{24,32},{32,40},{40,48},{48,56},{56,64},{64,7... | collective-permute-start | bytes 27656 | tf_op jit(solution)/shard_map/ppermute | solution.py:14
  115.1 12.1 %collective-permute-start.9 = (f32[96,8,3]{0,2,1:T(4,128)S(1)}, f32[96,8,3]{0,2,1:T(4,128)S(1)}, u32[]{:S(2)}, u32[]{:S(2)}) collective-permute-start(f32[96,8,3]{0,2,1:T(4,128)S(1)} %get-tuple-element.95), channel_id=1, source_target_pairs={{8,0},{16,8},{24,16},{32,24},{40,32},{48,40},{56,48},{64,56},{72,6... | collective-permute-start | bytes 27656 | tf_op jit(solution)/shard_map/ppermute | solution.py:17
  118.0 10.9 %collective-permute-start.18 = (f32[19800]{0:T(1024)S(1)}, f32[19800]{0:T(1024)S(1)}, u32[]{:S(2)}, u32[]{:S(2)}) collective-permute-start(f32[19800]{0:T(1024)S(1)} %add.508), channel_id=1, source_target_pairs={{0,1},{1,0},{2,3},{3,2},{4,5},{5,4},{6,7},{7,6},{8,9},{9,8},{10,11... | collective-permute-start | bytes 237608 | tf_op jit(solution)/shard_map/ppermute | solution.py:87
  128.9 12.0 %collective-permute-start.19 = (f32[19800]{0:T(1024)S(1)}, f32[19800]{0:T(1024)S(1)}, u32[]{:S(2)}, u32[]{:S(2)}) collective-permute-start(f32[19800]{0:T(1024)S(1)} %add.509), channel_id=1, source_target_pairs={{0,2},{1,3},{2,0},{3,1},{4,6},{5,7},{6,4},{7,5},{8,10},{9,11},{10,... | collective-permute-start | bytes 237608 | tf_op jit(solution)/shard_map/ppermute | solution.py:87
  134.1 15.7 %collective-permute-start.10 = (bf16[96,3,134]{0,2,1:T(8,128)(2,1)S(1)}, bf16[96,3,134]{0,2,1:T(8,128)(2,1)S(1)}, u32[]{:S(2)}, u32[]{:S(2)}) collective-permute-start(bf16[96,3,134]{0,2,1:T(8,128)(2,1)S(1)} %get-tuple-element.106), channel_id=1, source_target_pairs={{0,1},{1,2},{2,3},{3,4},{4,5},{5,6},{6,7},{8,9},{9,10},{10,11},{11... | collective-permute-start | bytes 231560 | tf_op jit(solution)/shard_map/ppermute | solution.py:14
  138.8 11.0 %collective-permute-start.11 = (bf16[96,3,134]{0,2,1:T(8,128)(2,1)S(1)}, bf16[96,3,134]{0,2,1:T(8,128)(2,1)S(1)}, u32[]{:S(2)}, u32[]{:S(2)}) collective-permute-start(bf16[96,3,134]{0,2,1:T(8,128)(2,1)S(1)} %get-tuple-element.107), channel_id=1, source_target_pairs={{1,0},{2,1},{3,2},{4,3},{5,4},{6,5},{7,6},{9,8},{10,9},{11,10},{12... | collective-permute-start | bytes 231560 | tf_op jit(solution)/shard_map/ppermute | solution.py:17
  140.9 11.1 %collective-permute-start.20 = (f32[19800]{0:T(1024)S(1)}, f32[19800]{0:T(1024)S(1)}, u32[]{:S(2)}, u32[]{:S(2)}) collective-permute-start(f32[19800]{0:T(1024)S(1)} %add.510), channel_id=1, source_target_pairs={{0,4},{1,5},{2,6},{3,7},{4,0},{5,1},{6,2},{7,3},{8,12},{9,13},{10,... | collective-permute-start | bytes 237608 | tf_op jit(solution)/shard_map/ppermute | solution.py:87
  149.9 14.5 %copy-start.2 = (bf16[96,8,128]{0,2,1:T(8,128)(2,1)S(1)}, bf16[96,8,128]{0,2,1:T(8,128)(2,1)}, u32[]{:S(2)}) copy-start(bf16[96,8,128]{0,2,1:T(8,128)(2,1)} %copy-done.1) | copy-start | bytes 589828
  149.9 14.5 %copy-start.7 = (f32[96]{0:T(128)S(1)}, f32[96]{0:T(128)}, u32[]{:S(2)}) copy-start(f32[96]{0:T(128)} %copy-done.6) | copy-start | bytes 1156
  149.9 14.5 %copy-start.9 = (f32[96]{0:T(128)S(1)}, f32[96]{0:T(128)}, u32[]{:S(2)}) copy-start(f32[96]{0:T(128)} %copy-done.8) | copy-start | bytes 1156
  149.9 14.5 %copy-start.11 = (f32[96]{0:T(128)S(1)}, f32[96]{0:T(128)}, u32[]{:S(2)}) copy-start(f32[96]{0:T(128)} %copy-done.10) | copy-start | bytes 1156
  149.9 14.5 %copy-start.13 = (f32[96]{0:T(128)S(1)}, f32[96]{0:T(128)}, u32[]{:S(2)}) copy-start(f32[96]{0:T(128)} %copy-done.12) | copy-start | bytes 1156
  150.0 14.5 %copy-start.15 = (f32[96]{0:T(128)S(1)}, f32[96]{0:T(128)}, u32[]{:S(2)}) copy-start(f32[96]{0:T(128)} %copy-done.14) | copy-start | bytes 1156
  150.0 14.5 %copy-start.17 = (f32[96]{0:T(128)S(1)}, f32[96]{0:T(128)}, u32[]{:S(2)}) copy-start(f32[96]{0:T(128)} %copy-done.16) | copy-start | bytes 1156
  150.0 14.5 %copy-start.19 = (f32[96]{0:T(128)S(1)}, f32[96]{0:T(128)}, u32[]{:S(2)}) copy-start(f32[96]{0:T(128)} %copy-done.18) | copy-start | bytes 1156
  150.0 14.5 %copy-start.21 = (f32[96]{0:T(128)S(1)}, f32[96]{0:T(128)}, u32[]{:S(2)}) copy-start(f32[96]{0:T(128)} %copy-done.20) | copy-start | bytes 1156
  150.0 14.5 %copy-start.23 = (f32[96]{0:T(128)S(1)}, f32[96]{0:T(128)}, u32[]{:S(2)}) copy-start(f32[96]{0:T(128)} %copy-done.22) | copy-start | bytes 1156
  150.0 14.5 %copy-start.25 = (f32[96]{0:T(128)S(1)}, f32[96]{0:T(128)}, u32[]{:S(2)}) copy-start(f32[96]{0:T(128)} %copy-done.24) | copy-start | bytes 1156
  150.0 14.5 %copy-start.27 = (f32[96]{0:T(128)S(1)}, f32[96]{0:T(128)}, u32[]{:S(2)}) copy-start(f32[96]{0:T(128)} %copy-done.26) | copy-start | bytes 1156
  150.0 14.5 %copy-start.29 = (f32[96]{0:T(128)S(1)}, f32[96]{0:T(128)}, u32[]{:S(2)}) copy-start(f32[96]{0:T(128)} %copy-done.28) | copy-start | bytes 1156
  150.0 14.5 %copy-start.31 = (f32[96]{0:T(128)S(1)}, f32[96]{0:T(128)}, u32[]{:S(2)}) copy-start(f32[96]{0:T(128)} %copy-done.30) | copy-start | bytes 1156
  152.0 5.2 %collective-permute-start.21 = (f32[19800]{0:T(1024)S(1)}, f32[19800]{0:T(1024)S(1)}, u32[]{:S(2)}, u32[]{:S(2)}) collective-permute-start(f32[19800]{0:T(1024)S(1)} %add.511), channel_id=1, source_target_pairs={{0,16},{8,24},{16,0},{24,8},{32,48},{40,56},{48,32},{56,40},{64,80... | collective-permute-start | bytes 237608 | tf_op jit(solution)/shard_map/ppermute | solution.py:87
  157.3 12.1 %collective-permute-start.22 = (f32[39600]{0:T(1024)S(1)}, f32[39600]{0:T(1024)S(1)}, u32[]{:S(2)}, u32[]{:S(2)}) collective-permute-start(f32[39600]{0:T(1024)S(1)} %maximum_select_fusion.1), channel_id=1, source_target_pairs={{0,8},{8,0},{16,24},{24,16},{32,40},{40,32},{48,56},{56,48},{64,72... | collective-permute-start | bytes 475208 | tf_op jit(solution)/shard_map/ppermute | solution.py:87
  (55 other events, 344.9 us)

commit v7 on v3

--- a/solution.py
+++ b/solution.py
@@ -132,7 +132,7 @@
 def local(image, cotangent, dw_kernel, dw_bias, ln_gain, ln_bias, w_in, b_in, w_out, layer_scale):
     channels, height, breadth = image.shape
     pixels = height * breadth
-    padded = padded_2(image, (("col", 2), ("row", 1)), 3)
+    padded = padded_2(image, (("row", 1), ("col", 2)), 3)
     conv_out = conv_seven(padded, dw_kernel) + dw_bias[:, None, None]
     block_flat, grad_flat, sums = mixing(
         conv_out.reshape(channels, pixels),

time: 155 us -> 162 us (1.045)
  other arithmetic: 17.4 us -> 20.7 us
  starting transfers between devices: 78.5 us -> 75.3 us
  waiting for transfers between devices: 34.4 us -> 37.6 us
  local copies, waits for them, and re-layouts: 14.5 us -> 16.7 us
    ppermute x11, starting transfers between devices: 47.3 us -> 43 us  [xor_partner(): lax.ppermute(value, axis, [(i, i ^ mask) for i in range(lax.axis_size(axi...]
    ppermute x4, waiting for transfers between devices: 10.2 us -> 12.2 us  [padded_2(): lax.ppermute(lax.slice_in_dim(block, 0, width, axis=dim), axis, backward)]
    unnamed x166 -> x258, local copies, waits for them, and re-layouts: 5.8 us -> 5.98 us
  transfers between devices with their start and end apart: 19 -> 19, of which waited for: 11 -> 12; matrix products, arithmetic and copies ran while one was open for 7% -> 8% of each run, Pallas kernels for 0% -> 0%
where the time goes in v7:
time: 162 us; the launch traced here: 159 us
  starting transfers between devices  75.3 us (46%)
  waiting for transfers between devices  37.6 us (23%)
  other arithmetic  20.7 us (13%)
  local copies, waits for them, and re-layouts  16.7 us (10%)
  matrix products  5.73 us (4%)
  between operations  3.07 us (2%)
    ppermute x11, starting transfers between devices, xor_partner(): lax.ppermute(value, axis, [(i, i ^ mask) for i in range(lax.axis_size(axi...  43 us
    ppermute x4, starting transfers between devices, padded_2(): lax.ppermute(lax.slice_in_dim(block, block.shape[dim] - width, None, axis...  25.9 us
    ppermute x11, waiting for transfers between devices, xor_partner(): lax.ppermute(value, axis, [(i, i ^ mask) for i in range(lax.axis_size(axi...  25.4 us
    ppermute x4, waiting for transfers between devices, padded_2(): lax.ppermute(lax.slice_in_dim(block, 0, width, axis=dim), axis, backward)  12.2 us
    ppermute x4, starting transfers between devices, padded_2(): lax.ppermute(lax.slice_in_dim(block, 0, width, axis=dim), axis, backward)  6.43 us
    reduce_sum x4, other arithmetic, kernel_terms(): jnp.sum(conv_grad * padded[:, row_step:row_step + height, col_step:col_st...  6.15 us
    unnamed x258, local copies, waits for them, and re-layouts  5.98 us
    reduce_sum x1, other arithmetic, mixing(): average = jnp.mean(conv_flat, axis=0, keepdims=True)  5.75 us
  transfers between devices with their start and end apart: 19, of which 12 were waited for; matrix products, arithmetic and copies ran while one was open for 8% of the time, Pallas kernels for 0%

profile of v7, /device:TPU:57, one launch (start us, length us, event | category | flops | bytes accessed | tf_op | source)
XLA Modules:
  0.0 159.2 jit_solution(2078372046847196359)
XLA Ops:
  0.7 1.2 copy.24
  1.8 10.6 %collective-permute-start = (bf16[96,3,128]{0,2,1:T(8,128)(2,1)S(1)}, bf16[96,3,128]{0,2,1:T(8,128)(2,1)S(1)}, u32[]{:S(2)}, u32[]{:S(2)}) collective-permute-start(bf16[96,3,128]{0,2,1:T(8,128)(2,1)S(1)} %get-tuple-element.112), channel_id=1, source_target_pairs={{0,1},{1,2},{2,3},{3,4},{4,5},{5,6},{6,7},{8,9},{9,10},{10,11},{11... | collective-permute-start | bytes 221192 | tf_op jit(solution)/shard_map/ppermute | solution.py:14
  12.5 1.3 collective-permute-start.1
  13.8 1.0 slice_bitcast_fusion.48
  14.8 1.0 slice_bitcast_fusion.47
  16.1 8.8 %collective-permute-done.1 = bf16[96,3,128]{0,2,1:T(8,128)(2,1)S(1)} collective-permute-done((bf16[96,3,128]{0,2,1:T(8,128)(2,1)S(1)}, bf16[96,3,128]{0,2,1:T(8,128)(2,1)S(1)}, u32[]{:S(2)}, u32[]{:S(2)}) %collective-permute-start.1) | collective-permute-done | bytes 73760 | tf_op jit(solution)/shard_map/ppermute | solution.py:17
  24.9 3.3 %collective-permute-start.2 = (bf16[96,14,3]{0,2,1:T(4,128)(2,1)S(1)}, bf16[96,14,3]{0,2,1:T(4,128)(2,1)S(1)}, u32[]{:S(2)}, u32[]{:S(2)}) collective-permute-start(bf16[96,14,3]{0,2,1:T(4,128)(2,1)S(1)} %get-tuple-element.100), channel_id=1, source_target_pairs={{0,8},{8,16},{16,24},{24,32},{32,40},{40,48},{48,56},{56,64},{64,7... | collective-permute-start | bytes 24200 | tf_op jit(solution)/shard_map/ppermute | solution.py:14
  28.2 1.9 %collective-permute-start.3 = (bf16[96,14,3]{0,2,1:T(4,128)(2,1)S(1)}, bf16[96,14,3]{0,2,1:T(4,128)(2,1)S(1)}, u32[]{:S(2)}, u32[]{:S(2)}) collective-permute-start(bf16[96,14,3]{0,2,1:T(4,128)(2,1)S(1)} %get-tuple-element.101), channel_id=1, source_target_pairs={{8,0},{16,8},{24,16},{32,24},{40,32},{48,40},{56,48},{64,56},{72,6... | collective-permute-start | bytes 24200 | tf_op jit(solution)/shard_map/ppermute | solution.py:17
  30.1 1.4 slice_bitcast_fusion.46
  31.6 1.1 copy.32
  32.9 0.9 copy.95
  33.8 1.5 collective-permute-done.3
  36.0 5.8 %fusion.180 = (f32[8,128]{1,0:T(8,128)S(1)}, f32[96,8,128]{0,2,1:T(8,128)S(1)}) fusion(f32[96]{0:T(128)S(1)} %copy-done.123, bf16[96,14,131]{0,2,1:T(8,128)(2,1)S(1)} %get-tuple-element.99, f32[96]{0:T(128)S(1)} %get-tuple-element.161, f32[96]{0:T(128)} %get-tuple-element.162, f32[96]{0:T(128)S(1)} %get-tuple-element.115, ...), kind=kLoop, calls=%fused_computation.433 | loop fusion | flops 15137792 | bytes 9018112 | tf_op jit(solution)/shard_map/reduce_sum | solution.py:100
  43.3 2.0 %convert_reduce_fusion = (f32[384]{0:T(512)}, bf16[384,1024]{0,1:T(8,128)(2,1)S(1)}) fusion(f32[1024,384]{1,0:T(8,128)S(1)} %get-tuple-element.166, bf16[384,96]{0,1:T(8,128)(2,1)S(1)} %copy-done.7, f32[96,1024]{1,0:T(8,128)S(1)} %copy.97, f32[96]{0:T(128)S(1)} %copy-done.82), kind=kOutput, calls=%fused_computation.16 | convolution fusion | flops 84344448 | bytes 2828160 | tf_op jit(solution)/shard_map/hc,cp->hp/dot_general | solution.py:96
  45.2 1.0 fusion.178
  46.2 1.0 fusion.168
  47.2 1.5 fusion.179
  48.8 1.2 copy.98
  49.9 1.8 %fusion.137 = (f32[96]{0:T(128)}, f32[96]{0:T(128)}, f32[96]{0:T(128)}, f32[96]{0:T(128)}, f32[96]{0:T(128)}, /*index=5*/f32[96]{0:T(128)}, f32[96]{0:T(128)}, f...) fusion(bf16[96,14,131]{0,2,1:T(8,128)(2,1)S(1)} %get-tuple-elem, ...), kind=kLoop, calls=%fused_computation.252 | loop fusion | flops 5306688 | bytes 3939072 | tf_op jit(solution)/shard_map/reduce_sum | solution.py:48
  51.7 1.9 %fusion.141 = (f32[96]{0:T(128)}, f32[96]{0:T(128)}, f32[96]{0:T(128)}, f32[96]{0:T(128)}, f32[96]{0:T(128)}, /*index=5*/f32[96]{0:T(128)}, f32[96]{0:T(128)}, f...) fusion(bf16[96,14,131]{0,2,1:T(8,128)(2,1)S(1)} %get-tuple-elem, ...), kind=kLoop, calls=%fused_computation.256 | loop fusion | flops 5306688 | bytes 3939072 | tf_op jit(solution)/shard_map/reduce_sum | solution.py:48
  54.8 0.9 reshape.104
  55.7 1.7 %fusion.138 = (f32[96]{0:T(128)S(1)}, f32[96]{0:T(128)S(1)}, f32[96]{0:T(128)S(1)}, f32[96]{0:T(128)S(1)}, f32[96]{0:T(128)S(1)}, /*index=5*/f32[96]{0:T(128)S(1...) fusion(bf16[96,3,128]{0,2,1:T(8,128)(2,1)} %copy-done.5, bf16[96,8,128]{0,2,1:T(8,128)(2,1)S(1)} %copy.24, ...), kind=kLoop, calls=%fused_computation.253 | loop fusion | flops 3537984 | bytes 1330944 | tf_op jit(solution)/shard_map/reduce_sum | solution.py:48
  60.1 1.6 %concatenate.149 = f32[79200]{0:T(1024)S(1)} concatenate(f32[4704]{0:T(1024)S(1)} %reshape_reshape.3, f32[96]{0:T(128)S(1)} %copy-done.86, f32[96]{0:T(128)S(1)} %copy-done.85, f32[96]{0:T(128)S(1)} %reduce_sum.577, f32[36864]{0:T(1024)S(1)} %reshape.104, f32[384]{0:T(512)S(1)} %copy-done.84, f32[36864]{0:T(1024)S(1)} %reshape.105, f32[96]{0:T(128)S(1)} %get-tuple-element.102), dimensions={0} | concatenate | bytes 633600 | tf_op jit(solution)/shard_map/concatenate | solution.py:63
  61.8 1.9 %collective-permute-start.8 = (f32[39600]{0:T(1024)S(1)}, f32[39600]{0:T(1024)S(1)}, u32[]{:S(2)}, u32[]{:S(2)}) collective-permute-start(f32[39600]{0:T(1024)S(1)} %dynamic_slice.13), channel_id=1, source_target_pairs={{0,8},{8,0},{16,24},{24,16},{32,40},{40,32},{48,56},{56,48},{64,72... | collective-permute-start | bytes 475208 | tf_op jit(solution)/shard_map/ppermute | solution.py:58
  63.8 1.3 collective-permute-done.8
  65.3 2.0 %collective-permute-start.9 = (f32[19800]{0:T(1024)S(1)}, f32[19800]{0:T(1024)S(1)}, u32[]{:S(2)}, u32[]{:S(2)}) collective-permute-start(f32[19800]{0:T(1024)S(1)} %dynamic_slice.15), channel_id=1, source_target_pairs={{0,16},{8,24},{16,0},{24,8},{32,48},{40,56},{48,32},{56,40},{64,80... | collective-permute-start | bytes 237608 | tf_op jit(solution)/shard_map/ppermute | solution.py:58
  67.4 3.8 %collective-permute-done.9 = f32[19800]{0:T(1024)S(1)} collective-permute-done((f32[19800]{0:T(1024)S(1)}, f32[19800]{0:T(1024)S(1)}, u32[]{:S(2)}, u32[]{:S(2)}) %collective-permute-start.9) | collective-permute-done | bytes 79232 | tf_op jit(solution)/shard_map/ppermute | solution.py:58
  71.2 3.7 %collective-permute-start.10 = (f32[19800]{0:T(1024)S(1)}, f32[19800]{0:T(1024)S(1)}, u32[]{:S(2)}, u32[]{:S(2)}) collective-permute-start(f32[19800]{0:T(1024)S(1)} %dynamic-slice_add_fusion.1), channel_id=1, source_target_pairs={{0,32},{8,40},{16,48},{24,56},{32,0},{40,8},{48,16},{56,24},{64,96... | collective-permute-start | bytes 237608 | tf_op jit(solution)/shard_map/ppermute | solution.py:58
  75.0 4.7 %collective-permute-done.10 = f32[19800]{0:T(1024)S(1)} collective-permute-done((f32[19800]{0:T(1024)S(1)}, f32[19800]{0:T(1024)S(1)}, u32[]{:S(2)}, u32[]{:S(2)}) %collective-permute-start.10) | collective-permute-done | bytes 79232 | tf_op jit(solution)/shard_map/ppermute | solution.py:58
  79.7 5.4 %collective-permute-start.11 = (f32[19800]{0:T(1024)S(1)}, f32[19800]{0:T(1024)S(1)}, u32[]{:S(2)}, u32[]{:S(2)}) collective-permute-start(f32[19800]{0:T(1024)S(1)} %add.505), channel_id=1, source_target_pairs={{0,64},{8,72},{16,80},{24,88},{32,96},{40,104},{48,112},{56,120},{... | collective-permute-start | bytes 237608 | tf_op jit(solution)/shard_map/ppermute | solution.py:58
  85.1 6.0 %collective-permute-done.11 = f32[19800]{0:T(1024)S(1)} collective-permute-done((f32[19800]{0:T(1024)S(1)}, f32[19800]{0:T(1024)S(1)}, u32[]{:S(2)}, u32[]{:S(2)}) %collective-permute-start.11) | collective-permute-done | bytes 79232 | tf_op jit(solution)/shard_map/ppermute | solution.py:58
  91.1 2.1 %collective-permute-start.12 = (f32[19800]{0:T(1024)S(1)}, f32[19800]{0:T(1024)S(1)}, u32[]{:S(2)}, u32[]{:S(2)}) collective-permute-start(f32[19800]{0:T(1024)S(1)} %add.506), channel_id=1, source_target_pairs={{0,128},{8,136},{16,144},{24,152},{32,160},{40,168},{48,176},{56,1... | collective-permute-start | bytes 237608 | tf_op jit(solution)/shard_map/ppermute | solution.py:58
  93.2 3.1 %collective-permute-done.12 = f32[19800]{0:T(1024)S(1)} collective-permute-done((f32[19800]{0:T(1024)S(1)}, f32[19800]{0:T(1024)S(1)}, u32[]{:S(2)}, u32[]{:S(2)}) %collective-permute-start.12) | collective-permute-done | bytes 79232 | tf_op jit(solution)/shard_map/ppermute | solution.py:58
  96.3 1.9 %collective-permute-start.13 = (f32[19800]{0:T(1024)S(1)}, f32[19800]{0:T(1024)S(1)}, u32[]{:S(2)}, u32[]{:S(2)}) collective-permute-start(f32[19800]{0:T(1024)S(1)} %add.507), channel_id=1, source_target_pairs={{0,256},{8,264},{16,272},{24,280},{32,288},{40,296},{48,304},{56,3... | collective-permute-start | bytes 237608 | tf_op jit(solution)/shard_map/ppermute | solution.py:58
  98.2 7.3 %collective-permute-start.4 = (f32[96,8,3]{0,2,1:T(4,128)S(1)}, f32[96,8,3]{0,2,1:T(4,128)S(1)}, u32[]{:S(2)}, u32[]{:S(2)}) collective-permute-start(f32[96,8,3]{0,2,1:T(4,128)S(1)} %get-tuple-element.94), channel_id=1, source_target_pairs={{0,8},{8,16},{16,24},{24,32},{32,40},{40,48},{48,56},{56,64},{64,7... | collective-permute-start | bytes 27656 | tf_op jit(solution)/shard_map/ppermute | solution.py:14
  105.5 1.9 %collective-permute-start.5 = (f32[96,8,3]{0,2,1:T(4,128)S(1)}, f32[96,8,3]{0,2,1:T(4,128)S(1)}, u32[]{:S(2)}, u32[]{:S(2)}) collective-permute-start(f32[96,8,3]{0,2,1:T(4,128)S(1)} %get-tuple-element.95), channel_id=1, source_target_pairs={{8,0},{16,8},{24,16},{32,24},{40,32},{48,40},{56,48},{64,56},{72,6... | collective-permute-start | bytes 27656 | tf_op jit(solution)/shard_map/ppermute | solution.py:17
  107.4 4.7 %collective-permute-start.14 = (f32[19800]{0:T(1024)S(1)}, f32[19800]{0:T(1024)S(1)}, u32[]{:S(2)}, u32[]{:S(2)}) collective-permute-start(f32[19800]{0:T(1024)S(1)} %add.508), channel_id=1, source_target_pairs={{0,1},{1,0},{2,3},{3,2},{4,5},{5,4},{6,7},{7,6},{8,9},{9,8},{10,11... | collective-permute-start | bytes 237608 | tf_op jit(solution)/shard_map/ppermute | solution.py:58
  112.8 3.9 %collective-permute-done.14 = f32[19800]{0:T(1024)S(1)} collective-permute-done((f32[19800]{0:T(1024)S(1)}, f32[19800]{0:T(1024)S(1)}, u32[]{:S(2)}, u32[]{:S(2)}) %collective-permute-start.14) | collective-permute-done | bytes 79232 | tf_op jit(solution)/shard_map/ppermute | solution.py:58
  116.7 3.1 %collective-permute-start.15 = (f32[19800]{0:T(1024)S(1)}, f32[19800]{0:T(1024)S(1)}, u32[]{:S(2)}, u32[]{:S(2)}) collective-permute-start(f32[19800]{0:T(1024)S(1)} %add.509), channel_id=1, source_target_pairs={{0,2},{1,3},{2,0},{3,1},{4,6},{5,7},{6,4},{7,5},{8,10},{9,11},{10,... | collective-permute-start | bytes 237608 | tf_op jit(solution)/shard_map/ppermute | solution.py:58
  119.8 4.7 %collective-permute-start.6 = (bf16[96,3,134]{0,2,1:T(8,128)(2,1)S(1)}, bf16[96,3,134]{0,2,1:T(8,128)(2,1)S(1)}, u32[]{:S(2)}, u32[]{:S(2)}) collective-permute-start(bf16[96,3,134]{0,2,1:T(8,128)(2,1)S(1)} %get-tuple-element.110), channel_id=1, source_target_pairs={{0,1},{1,2},{2,3},{3,4},{4,5},{5,6},{6,7},{8,9},{9,10},{10,11},{11... | collective-permute-start | bytes 231560 | tf_op jit(solution)/shard_map/ppermute | solution.py:14
  124.5 1.3 collective-permute-start.7
  126.6 8.0 %collective-permute-start.16 = (f32[19800]{0:T(1024)S(1)}, f32[19800]{0:T(1024)S(1)}, u32[]{:S(2)}, u32[]{:S(2)}) collective-permute-start(f32[19800]{0:T(1024)S(1)} %add.510), channel_id=1, source_target_pairs={{0,4},{1,5},{2,6},{3,7},{4,0},{5,1},{6,2},{7,3},{8,12},{9,13},{10,... | collective-permute-start | bytes 237608 | tf_op jit(solution)/shard_map/ppermute | solution.py:58
  134.6 1.4 collective-permute-done.7
  136.4 0.9 collective-permute-done.16
  137.4 3.7 %collective-permute-start.17 = (f32[19800]{0:T(1024)S(1)}, f32[19800]{0:T(1024)S(1)}, u32[]{:S(2)}, u32[]{:S(2)}) collective-permute-start(f32[19800]{0:T(1024)S(1)} %add.511), channel_id=1, source_target_pairs={{0,16},{8,24},{16,0},{24,8},{32,48},{40,56},{48,32},{56,40},{64,80... | collective-permute-start | bytes 237608 | tf_op jit(solution)/shard_map/ppermute | solution.py:58
  141.2 1.7 %collective-permute-done.17 = f32[19800]{0:T(1024)S(1)} collective-permute-done((f32[19800]{0:T(1024)S(1)}, f32[19800]{0:T(1024)S(1)}, u32[]{:S(2)}, u32[]{:S(2)}) %collective-permute-start.17) | collective-permute-done | bytes 79232 | tf_op jit(solution)/shard_map/ppermute | solution.py:58
  143.0 6.4 %collective-permute-start.18 = (f32[39600]{0:T(1024)S(1)}, f32[39600]{0:T(1024)S(1)}, u32[]{:S(2)}, u32[]{:S(2)}) collective-permute-start(f32[39600]{0:T(1024)S(1)} %maximum_select_fusion.1), channel_id=1, source_target_pairs={{0,8},{8,0},{16,24},{24,16},{32,40},{40,32},{48,56},{56,48},{64,72... | collective-permute-start | bytes 475208 | tf_op jit(solution)/shard_map/ppermute | solution.py:58
  149.8 4.6 %fusion.144 = bf16[96,8,128]{0,2,1:T(8,128)(2,1)S(1)} fusion(f32[96,11,134]{0,2,1:T(8,128)S(1)} %get-tuple-element.93, f32[96,8,3]{0,2,1:T(4,128)S(1)} %collective-permute-done.5, f32[96,8,128]{0,2,1:T(8,128)S(1)} %bitcast.262, f32[96,8,3]{0,2,1:T(4,128)S(1)} %collective-permute-done.4, f32[96,11,134]{0,2,1:T(8,128)S(1)} %get-tuple-element.92, ...), kind=kLoop, calls=%fused_computation.260 | loop fusion | flops 10420224 | bytes 17338752 | tf_op jit(solution)/shard_map/convert_element_type | solution.py:158
  (307 shorter events, 12.3 us)
Async XLA Ops:
  0.6 41.7 %copy-start = (bf16[96,384]{1,0:T(8,128)(2,1)S(1)}, bf16[96,384]{1,0:T(8,128)(2,1)}, u32[]{:S(2)}) copy-start(bf16[96,384]{1,0:T(8,128)(2,1)} %param.16) | copy-start | bytes 221188
  1.8 14.2 %collective-permute-start = (bf16[96,3,128]{0,2,1:T(8,128)(2,1)S(1)}, bf16[96,3,128]{0,2,1:T(8,128)(2,1)S(1)}, u32[]{:S(2)}, u32[]{:S(2)}) collective-permute-start(bf16[96,3,128]{0,2,1:T(8,128)(2,1)S(1)} %get-tuple-element.112), channel_id=1, source_target_pairs={{0,1},{1,2},{2,3},{3,4},{4,5},{5,6},{6,7},{8,9},{9,10},{10,11},{11... | collective-permute-start | bytes 221192 | tf_op jit(solution)/shard_map/ppermute | solution.py:14
  12.5 12.4 %collective-permute-start.1 = (bf16[96,3,128]{0,2,1:T(8,128)(2,1)S(1)}, bf16[96,3,128]{0,2,1:T(8,128)(2,1)S(1)}, u32[]{:S(2)}, u32[]{:S(2)}) collective-permute-start(bf16[96,3,128]{0,2,1:T(8,128)(2,1)S(1)} %get-tuple-element.113), channel_id=1, source_target_pairs={{1,0},{2,1},{3,2},{4,3},{5,4},{6,5},{7,6},{9,8},{10,9},{11,10},{12... | collective-permute-start | bytes 221192 | tf_op jit(solution)/shard_map/ppermute | solution.py:17
  14.8 20.8 %copy-start.10 = (f32[96]{0:T(128)}, f32[96]{0:T(128)S(1)}, u32[]{:S(2)}) copy-start(f32[96]{0:T(128)S(1)} %get-tuple-element.126) | copy-start | bytes 1156
  14.8 20.8 %copy-start.12 = (f32[96]{0:T(128)}, f32[96]{0:T(128)S(1)}, u32[]{:S(2)}) copy-start(f32[96]{0:T(128)S(1)} %get-tuple-element.127) | copy-start | bytes 1156
  14.8 20.8 %copy-start.14 = (f32[96]{0:T(128)}, f32[96]{0:T(128)S(1)}, u32[]{:S(2)}) copy-start(f32[96]{0:T(128)S(1)} %get-tuple-element.128) | copy-start | bytes 1156
  14.8 20.8 %copy-start.16 = (f32[96]{0:T(128)}, f32[96]{0:T(128)S(1)}, u32[]{:S(2)}) copy-start(f32[96]{0:T(128)S(1)} %get-tuple-element.129) | copy-start | bytes 1156
  14.8 20.8 %copy-start.18 = (f32[96]{0:T(128)}, f32[96]{0:T(128)S(1)}, u32[]{:S(2)}) copy-start(f32[96]{0:T(128)S(1)} %get-tuple-element.130) | copy-start | bytes 1156
  14.8 20.8 %copy-start.20 = (f32[96]{0:T(128)}, f32[96]{0:T(128)S(1)}, u32[]{:S(2)}) copy-start(f32[96]{0:T(128)S(1)} %get-tuple-element.131) | copy-start | bytes 1156
  14.8 20.8 %copy-start.22 = (f32[96]{0:T(128)}, f32[96]{0:T(128)S(1)}, u32[]{:S(2)}) copy-start(f32[96]{0:T(128)S(1)} %get-tuple-element.132) | copy-start | bytes 1156
  15.8 19.8 %copy-start.24 = (f32[96]{0:T(128)}, f32[96]{0:T(128)S(1)}, u32[]{:S(2)}) copy-start(f32[96]{0:T(128)S(1)} %get-tuple-element.133) | copy-start | bytes 1156
  15.9 19.8 %copy-start.26 = (f32[96]{0:T(128)}, f32[96]{0:T(128)S(1)}, u32[]{:S(2)}) copy-start(f32[96]{0:T(128)S(1)} %get-tuple-element.134) | copy-start | bytes 1156
  15.9 19.8 %copy-start.28 = (f32[96]{0:T(128)}, f32[96]{0:T(128)S(1)}, u32[]{:S(2)}) copy-start(f32[96]{0:T(128)S(1)} %get-tuple-element.135) | copy-start | bytes 1156
  15.9 19.8 %copy-start.30 = (f32[96]{0:T(128)}, f32[96]{0:T(128)S(1)}, u32[]{:S(2)}) copy-start(f32[96]{0:T(128)S(1)} %get-tuple-element.136) | copy-start | bytes 1156
  15.9 19.8 %copy-start.32 = (f32[96]{0:T(128)}, f32[96]{0:T(128)S(1)}, u32[]{:S(2)}) copy-start(f32[96]{0:T(128)S(1)} %get-tuple-element.137) | copy-start | bytes 1156
  15.9 19.8 %copy-start.34 = (f32[96]{0:T(128)}, f32[96]{0:T(128)S(1)}, u32[]{:S(2)}) copy-start(f32[96]{0:T(128)S(1)} %get-tuple-element.138) | copy-start | bytes 1156
  15.9 19.8 %copy-start.36 = (f32[96]{0:T(128)}, f32[96]{0:T(128)S(1)}, u32[]{:S(2)}) copy-start(f32[96]{0:T(128)S(1)} %get-tuple-element.139) | copy-start | bytes 1156
  15.9 19.8 %copy-start.38 = (f32[96]{0:T(128)}, f32[96]{0:T(128)S(1)}, u32[]{:S(2)}) copy-start(f32[96]{0:T(128)S(1)} %get-tuple-element.140) | copy-start | bytes 1156
  15.9 19.8 %copy-start.40 = (f32[96]{0:T(128)}, f32[96]{0:T(128)S(1)}, u32[]{:S(2)}) copy-start(f32[96]{0:T(128)S(1)} %get-tuple-element.141) | copy-start | bytes 1156
  15.9 19.8 %copy-start.42 = (f32[96]{0:T(128)}, f32[96]{0:T(128)S(1)}, u32[]{:S(2)}) copy-start(f32[96]{0:T(128)S(1)} %get-tuple-element.142) | copy-start | bytes 1156
  15.9 19.8 %copy-start.44 = (f32[96]{0:T(128)}, f32[96]{0:T(128)S(1)}, u32[]{:S(2)}) copy-start(f32[96]{0:T(128)S(1)} %get-tuple-element.143) | copy-start | bytes 1156
  16.0 19.8 %copy-start.46 = (f32[96]{0:T(128)}, f32[96]{0:T(128)S(1)}, u32[]{:S(2)}) copy-start(f32[96]{0:T(128)S(1)} %get-tuple-element.144) | copy-start | bytes 1156
  16.0 19.8 %copy-start.48 = (f32[96]{0:T(128)}, f32[96]{0:T(128)S(1)}, u32[]{:S(2)}) copy-start(f32[96]{0:T(128)S(1)} %get-tuple-element.145) | copy-start | bytes 1156
  16.0 19.8 %copy-start.50 = (f32[96]{0:T(128)}, f32[96]{0:T(128)S(1)}, u32[]{:S(2)}) copy-start(f32[96]{0:T(128)S(1)} %get-tuple-element.146) | copy-start | bytes 1156
  16.0 19.8 %copy-start.52 = (f32[96]{0:T(128)}, f32[96]{0:T(128)S(1)}, u32[]{:S(2)}) copy-start(f32[96]{0:T(128)S(1)} %get-tuple-element.147) | copy-start | bytes 1156
  16.0 19.8 %copy-start.54 = (f32[96]{0:T(128)}, f32[96]{0:T(128)S(1)}, u32[]{:S(2)}) copy-start(f32[96]{0:T(128)S(1)} %get-tuple-element.148) | copy-start | bytes 1156
  16.0 19.8 %copy-start.56 = (f32[96]{0:T(128)}, f32[96]{0:T(128)S(1)}, u32[]{:S(2)}) copy-start(f32[96]{0:T(128)S(1)} %get-tuple-element.149) | copy-start | bytes 1156
  16.0 19.8 %copy-start.58 = (f32[96]{0:T(128)}, f32[96]{0:T(128)S(1)}, u32[]{:S(2)}) copy-start(f32[96]{0:T(128)S(1)} %get-tuple-element.150) | copy-start | bytes 1156
  16.0 19.8 %copy-start.60 = (f32[96]{0:T(128)}, f32[96]{0:T(128)S(1)}, u32[]{:S(2)}) copy-start(f32[96]{0:T(128)S(1)} %get-tuple-element.151) | copy-start | bytes 1156
  16.0 19.8 %copy-start.3 = (bf16[96,3,128]{0,2,1:T(8,128)(2,1)}, bf16[96,3,128]{0,2,1:T(8,128)(2,1)S(1)}, u32[]{:S(2)}) copy-start(bf16[96,3,128]{0,2,1:T(8,128)(2,1)S(1)} %collective-permute-done) | copy-start | bytes 221188
  24.9 8.9 %collective-permute-start.2 = (bf16[96,14,3]{0,2,1:T(4,128)(2,1)S(1)}, bf16[96,14,3]{0,2,1:T(4,128)(2,1)S(1)}, u32[]{:S(2)}, u32[]{:S(2)}) collective-permute-start(bf16[96,14,3]{0,2,1:T(4,128)(2,1)S(1)} %get-tuple-element.100), channel_id=1, source_target_pairs={{0,8},{8,16},{16,24},{24,32},{32,40},{40,48},{48,56},{56,64},{64,7... | collective-permute-start | bytes 24200 | tf_op jit(solution)/shard_map/ppermute | solution.py:14
  28.2 7.1 %collective-permute-start.3 = (bf16[96,14,3]{0,2,1:T(4,128)(2,1)S(1)}, bf16[96,14,3]{0,2,1:T(4,128)(2,1)S(1)}, u32[]{:S(2)}, u32[]{:S(2)}) collective-permute-start(bf16[96,14,3]{0,2,1:T(4,128)(2,1)S(1)} %get-tuple-element.101), channel_id=1, source_target_pairs={{8,0},{16,8},{24,16},{32,24},{40,32},{48,40},{56,48},{64,56},{72,6... | collective-permute-start | bytes 24200 | tf_op jit(solution)/shard_map/ppermute | solution.py:17
  61.8 3.3 %collective-permute-start.8 = (f32[39600]{0:T(1024)S(1)}, f32[39600]{0:T(1024)S(1)}, u32[]{:S(2)}, u32[]{:S(2)}) collective-permute-start(f32[39600]{0:T(1024)S(1)} %dynamic_slice.13), channel_id=1, source_target_pairs={{0,8},{8,0},{16,24},{24,16},{32,40},{40,32},{48,56},{56,48},{64,72... | collective-permute-start | bytes 475208 | tf_op jit(solution)/shard_map/ppermute | solution.py:58
  65.3 5.8 %collective-permute-start.9 = (f32[19800]{0:T(1024)S(1)}, f32[19800]{0:T(1024)S(1)}, u32[]{:S(2)}, u32[]{:S(2)}) collective-permute-start(f32[19800]{0:T(1024)S(1)} %dynamic_slice.15), channel_id=1, source_target_pairs={{0,16},{8,24},{16,0},{24,8},{32,48},{40,56},{48,32},{56,40},{64,80... | collective-permute-start | bytes 237608 | tf_op jit(solution)/shard_map/ppermute | solution.py:58
  71.2 8.4 %collective-permute-start.10 = (f32[19800]{0:T(1024)S(1)}, f32[19800]{0:T(1024)S(1)}, u32[]{:S(2)}, u32[]{:S(2)}) collective-permute-start(f32[19800]{0:T(1024)S(1)} %dynamic-slice_add_fusion.1), channel_id=1, source_target_pairs={{0,32},{8,40},{16,48},{24,56},{32,0},{40,8},{48,16},{56,24},{64,96... | collective-permute-start | bytes 237608 | tf_op jit(solution)/shard_map/ppermute | solution.py:58
  79.7 11.4 %collective-permute-start.11 = (f32[19800]{0:T(1024)S(1)}, f32[19800]{0:T(1024)S(1)}, u32[]{:S(2)}, u32[]{:S(2)}) collective-permute-start(f32[19800]{0:T(1024)S(1)} %add.505), channel_id=1, source_target_pairs={{0,64},{8,72},{16,80},{24,88},{32,96},{40,104},{48,112},{56,120},{... | collective-permute-start | bytes 237608 | tf_op jit(solution)/shard_map/ppermute | solution.py:58
  91.1 5.2 %collective-permute-start.12 = (f32[19800]{0:T(1024)S(1)}, f32[19800]{0:T(1024)S(1)}, u32[]{:S(2)}, u32[]{:S(2)}) collective-permute-start(f32[19800]{0:T(1024)S(1)} %add.506), channel_id=1, source_target_pairs={{0,128},{8,136},{16,144},{24,152},{32,160},{40,168},{48,176},{56,1... | collective-permute-start | bytes 237608 | tf_op jit(solution)/shard_map/ppermute | solution.py:58
  96.3 11.2 %collective-permute-start.13 = (f32[19800]{0:T(1024)S(1)}, f32[19800]{0:T(1024)S(1)}, u32[]{:S(2)}, u32[]{:S(2)}) collective-permute-start(f32[19800]{0:T(1024)S(1)} %add.507), channel_id=1, source_target_pairs={{0,256},{8,264},{16,272},{24,280},{32,288},{40,296},{48,304},{56,3... | collective-permute-start | bytes 237608 | tf_op jit(solution)/shard_map/ppermute | solution.py:58
  98.2 14.0 %collective-permute-start.4 = (f32[96,8,3]{0,2,1:T(4,128)S(1)}, f32[96,8,3]{0,2,1:T(4,128)S(1)}, u32[]{:S(2)}, u32[]{:S(2)}) collective-permute-start(f32[96,8,3]{0,2,1:T(4,128)S(1)} %get-tuple-element.94), channel_id=1, source_target_pairs={{0,8},{8,16},{16,24},{24,32},{32,40},{40,48},{48,56},{56,64},{64,7... | collective-permute-start | bytes 27656 | tf_op jit(solution)/shard_map/ppermute | solution.py:14
  105.5 7.2 %collective-permute-start.5 = (f32[96,8,3]{0,2,1:T(4,128)S(1)}, f32[96,8,3]{0,2,1:T(4,128)S(1)}, u32[]{:S(2)}, u32[]{:S(2)}) collective-permute-start(f32[96,8,3]{0,2,1:T(4,128)S(1)} %get-tuple-element.95), channel_id=1, source_target_pairs={{8,0},{16,8},{24,16},{32,24},{40,32},{48,40},{56,48},{64,56},{72,6... | collective-permute-start | bytes 27656 | tf_op jit(solution)/shard_map/ppermute | solution.py:17
  107.4 9.2 %collective-permute-start.14 = (f32[19800]{0:T(1024)S(1)}, f32[19800]{0:T(1024)S(1)}, u32[]{:S(2)}, u32[]{:S(2)}) collective-permute-start(f32[19800]{0:T(1024)S(1)} %add.508), channel_id=1, source_target_pairs={{0,1},{1,0},{2,3},{3,2},{4,5},{5,4},{6,7},{7,6},{8,9},{9,8},{10,11... | collective-permute-start | bytes 237608 | tf_op jit(solution)/shard_map/ppermute | solution.py:58
  116.7 9.9 %collective-permute-start.15 = (f32[19800]{0:T(1024)S(1)}, f32[19800]{0:T(1024)S(1)}, u32[]{:S(2)}, u32[]{:S(2)}) collective-permute-start(f32[19800]{0:T(1024)S(1)} %add.509), channel_id=1, source_target_pairs={{0,2},{1,3},{2,0},{3,1},{4,6},{5,7},{6,4},{7,5},{8,10},{9,11},{10,... | collective-permute-start | bytes 237608 | tf_op jit(solution)/shard_map/ppermute | solution.py:58
  119.8 14.8 %collective-permute-start.6 = (bf16[96,3,134]{0,2,1:T(8,128)(2,1)S(1)}, bf16[96,3,134]{0,2,1:T(8,128)(2,1)S(1)}, u32[]{:S(2)}, u32[]{:S(2)}) collective-permute-start(bf16[96,3,134]{0,2,1:T(8,128)(2,1)S(1)} %get-tuple-element.110), channel_id=1, source_target_pairs={{0,1},{1,2},{2,3},{3,4},{4,5},{5,6},{6,7},{8,9},{9,10},{10,11},{11... | collective-permute-start | bytes 231560 | tf_op jit(solution)/shard_map/ppermute | solution.py:14
  124.5 11.5 %collective-permute-start.7 = (bf16[96,3,134]{0,2,1:T(8,128)(2,1)S(1)}, bf16[96,3,134]{0,2,1:T(8,128)(2,1)S(1)}, u32[]{:S(2)}, u32[]{:S(2)}) collective-permute-start(bf16[96,3,134]{0,2,1:T(8,128)(2,1)S(1)} %get-tuple-element.111), channel_id=1, source_target_pairs={{1,0},{2,1},{3,2},{4,3},{5,4},{6,5},{7,6},{9,8},{10,9},{11,10},{12... | collective-permute-start | bytes 231560 | tf_op jit(solution)/shard_map/ppermute | solution.py:17
  126.6 10.8 %collective-permute-start.16 = (f32[19800]{0:T(1024)S(1)}, f32[19800]{0:T(1024)S(1)}, u32[]{:S(2)}, u32[]{:S(2)}) collective-permute-start(f32[19800]{0:T(1024)S(1)} %add.510), channel_id=1, source_target_pairs={{0,4},{1,5},{2,6},{3,7},{4,0},{5,1},{6,2},{7,3},{8,12},{9,13},{10,... | collective-permute-start | bytes 237608 | tf_op jit(solution)/shard_map/ppermute | solution.py:58
  136.0 13.4 %copy-start.2 = (bf16[96,8,128]{0,2,1:T(8,128)(2,1)S(1)}, bf16[96,8,128]{0,2,1:T(8,128)(2,1)}, u32[]{:S(2)}) copy-start(bf16[96,8,128]{0,2,1:T(8,128)(2,1)} %copy-done.1) | copy-start | bytes 589828
  137.4 5.5 %collective-permute-start.17 = (f32[19800]{0:T(1024)S(1)}, f32[19800]{0:T(1024)S(1)}, u32[]{:S(2)}, u32[]{:S(2)}) collective-permute-start(f32[19800]{0:T(1024)S(1)} %add.511), channel_id=1, source_target_pairs={{0,16},{8,24},{16,0},{24,8},{32,48},{40,56},{48,32},{56,40},{64,80... | collective-permute-start | bytes 237608 | tf_op jit(solution)/shard_map/ppermute | solution.py:58
  143.0 12.2 %collective-permute-start.18 = (f32[39600]{0:T(1024)S(1)}, f32[39600]{0:T(1024)S(1)}, u32[]{:S(2)}, u32[]{:S(2)}) collective-permute-start(f32[39600]{0:T(1024)S(1)} %maximum_select_fusion.1), channel_id=1, source_target_pairs={{0,8},{8,0},{16,24},{24,16},{32,40},{40,32},{48,56},{56,48},{64,72... | collective-permute-start | bytes 475208 | tf_op jit(solution)/shard_map/ppermute | solution.py:58
  (97 other events, 684.7 us)

commit v8 on v3

--- a/solution.py
+++ b/solution.py
@@ -65,7 +65,7 @@
     unit = 2 ** len(halving)
     flat = jnp.pad(flat, (0, -total % unit))
     doubling = []
-    for axis in ("col", "row"):
+    for axis in ("row", "col"):
         mask = 1
         while mask < lax.axis_size(axis):
             if (axis, mask) not in halving:

time: 155 us -> 155 us (level)
  the two profiles are of different devices: /device:TPU:57 before, /device:TPU:5 now
where the time goes in v8:
time: 155 us; the launch traced here: 154 us
  starting transfers between devices  78.7 us (51%)
  waiting for transfers between devices  36.5 us (24%)
  other arithmetic  17.4 us (11%)
  local copies, waits for them, and re-layouts  14.5 us (9%)
  matrix products  5.05 us (3%)
  between operations  2.41 us (2%)
    ppermute x11, starting transfers between devices, xor_partner(): lax.ppermute(value, axis, [(i, i ^ mask) for i in range(lax.axis_size(axi...  41.2 us
    ppermute x11, waiting for transfers between devices, xor_partner(): lax.ppermute(value, axis, [(i, i ^ mask) for i in range(lax.axis_size(axi...  26.6 us
    ppermute x4, starting transfers between devices, padded_2(): lax.ppermute(lax.slice_in_dim(block, block.shape[dim] - width, None, axis...  25.7 us
    ppermute x4, starting transfers between devices, padded_2(): lax.ppermute(lax.slice_in_dim(block, 0, width, axis=dim), axis, backward)  11.8 us
    ppermute x4, waiting for transfers between devices, padded_2(): lax.ppermute(lax.slice_in_dim(block, 0, width, axis=dim), axis, backward)  9.83 us
    unnamed x166, local copies, waits for them, and re-layouts  5.8 us
    dot_general x6, matrix products, product(): return jnp.einsum(form, left, right, preferred_element_type=jnp.float32)  5.05 us
    reduce_sum x4, other arithmetic, kernel_terms(): jnp.sum(conv_grad * padded[:, row_step:row_step + height, col_step:col_st...  4.87 us
  transfers between devices with their start and end apart: 19, of which 11 were waited for; matrix products, arithmetic and copies ran while one was open for 7% of the time, Pallas kernels for 0%

profile of v8, /device:TPU:5, one launch (start us, length us, event | category | flops | bytes accessed | tf_op | source)
XLA Modules:
  0.0 154.4 jit_solution(17166357464240121491)
XLA Ops:
  0.7 1.2 copy.24
  1.8 3.8 %collective-permute-start = (bf16[96,8,3]{0,2,1:T(4,128)(2,1)S(1)}, bf16[96,8,3]{0,2,1:T(4,128)(2,1)S(1)}, u32[]{:S(2)}, u32[]{:S(2)}) collective-permute-start(bf16[96,8,3]{0,2,1:T(4,128)(2,1)S(1)} %get-tuple-element.112), channel_id=1, source_target_pairs={{0,8},{8,16},{16,24},{24,32},{32,40},{40,48},{48,56},{56,64},{64,7... | collective-permute-start | bytes 13832 | tf_op jit(solution)/shard_map/ppermute | solution.py:14
  5.6 1.9 %collective-permute-start.1 = (bf16[96,8,3]{0,2,1:T(4,128)(2,1)S(1)}, bf16[96,8,3]{0,2,1:T(4,128)(2,1)S(1)}, u32[]{:S(2)}, u32[]{:S(2)}) collective-permute-start(bf16[96,8,3]{0,2,1:T(4,128)(2,1)S(1)} %get-tuple-element.113), channel_id=1, source_target_pairs={{8,0},{16,8},{24,16},{32,24},{40,32},{48,40},{56,48},{64,56},{72,6... | collective-permute-start | bytes 13832 | tf_op jit(solution)/shard_map/ppermute | solution.py:17
  7.5 1.0 slice_bitcast_fusion.48
  8.5 1.0 slice_bitcast_fusion.47
  9.6 0.9 collective-permute-done.1
  10.7 10.6 %collective-permute-start.2 = (bf16[96,3,134]{0,2,1:T(8,128)(2,1)S(1)}, bf16[96,3,134]{0,2,1:T(8,128)(2,1)S(1)}, u32[]{:S(2)}, u32[]{:S(2)}) collective-permute-start(bf16[96,3,134]{0,2,1:T(8,128)(2,1)S(1)} %get-tuple-element.110), channel_id=1, source_target_pairs={{0,1},{1,2},{2,3},{3,4},{4,5},{5,6},{6,7},{8,9},{9,10},{10,11},{11... | collective-permute-start | bytes 231560 | tf_op jit(solution)/shard_map/ppermute | solution.py:14
  21.3 1.9 %collective-permute-start.3 = (bf16[96,3,134]{0,2,1:T(8,128)(2,1)S(1)}, bf16[96,3,134]{0,2,1:T(8,128)(2,1)S(1)}, u32[]{:S(2)}, u32[]{:S(2)}) collective-permute-start(bf16[96,3,134]{0,2,1:T(8,128)(2,1)S(1)} %get-tuple-element.111), channel_id=1, source_target_pairs={{1,0},{2,1},{3,2},{4,3},{5,4},{6,5},{7,6},{9,8},{10,9},{11,10},{12... | collective-permute-start | bytes 231560 | tf_op jit(solution)/shard_map/ppermute | solution.py:17
  23.2 0.9 slice_bitcast_fusion.46
  24.3 1.1 copy.32
  25.5 0.9 copy.95
  26.4 6.6 %collective-permute-done.3 = bf16[96,3,134]{0,2,1:T(8,128)(2,1)S(1)} collective-permute-done((bf16[96,3,134]{0,2,1:T(8,128)(2,1)S(1)}, bf16[96,3,134]{0,2,1:T(8,128)(2,1)S(1)}, u32[]{:S(2)}, u32[]{:S(2)}) %collective-permute-start.3) | collective-permute-done | bytes 77216 | tf_op jit(solution)/shard_map/ppermute | solution.py:17
  33.4 4.3 %fusion.180 = (f32[8,128]{1,0:T(8,128)S(1)}, f32[96,8,128]{0,2,1:T(8,128)S(1)}) fusion(f32[96]{0:T(128)S(1)} %copy-done.77, bf16[96,11,134]{0,2,1:T(8,128)(2,1)S(1)} %get-tuple-element.109, f32[96]{0:T(128)S(1)} %get-tuple-element.161, f32[96]{0:T(128)S(1)} %get-tuple-element.162, f32[96]{0:T(128)S(1)} %get-tuple-element.115, f32[96]{0:T(128)S(1)} %get-tuple-element.116, ...), kind=kLoop, calls=%fused_computation.429 | loop fusion | flops 16317440 | bytes 8879872 | tf_op jit(solution)/shard_map/reduce_sum | solution.py:100
  38.3 0.8 fusion.10
  39.2 2.0 %convert_reduce_fusion = (f32[384]{0:T(512)}, bf16[384,1024]{0,1:T(8,128)(2,1)S(1)}) fusion(f32[1024,384]{1,0:T(8,128)S(1)} %get-tuple-element.166, bf16[384,96]{0,1:T(8,128)(2,1)S(1)} %copy-done.4, f32[96,1024]{1,0:T(8,128)S(1)} %copy.97, f32[96]{0:T(128)S(1)} %copy-done.48), kind=kOutput, calls=%fused_computation.16 | convolution fusion | flops 84344448 | bytes 2828160 | tf_op jit(solution)/shard_map/hc,cp->hp/dot_general | solution.py:96
  41.5 1.0 fusion.168
  42.5 1.5 fusion.179
  44.0 1.2 copy.98
  45.2 1.1 fusion.123
  46.3 1.9 %fusion.141 = (f32[96]{0:T(128)}, f32[96]{0:T(128)}, f32[96]{0:T(128)}, f32[96]{0:T(128)}, f32[96]{0:T(128)}, /*index=5*/f32[96]{0:T(128)}, f32[96]{0:T(128)}, f...) fusion(bf16[96,11,134]{0,2,1:T(8,128)(2,1)S(1)} %get-tuple-elem, ...), kind=kLoop, calls=%fused_computation.256 | loop fusion | flops 5306688 | bytes 3939072 | tf_op jit(solution)/shard_map/reduce_sum | solution.py:48
  48.4 1.3 fusion.91
  52.3 1.6 %concatenate.149 = f32[79200]{0:T(1024)S(1)} concatenate(f32[4704]{0:T(1024)S(1)} %reshape_reshape.3, f32[96]{0:T(128)S(1)} %copy-done.52, f32[96]{0:T(128)S(1)} %copy-done.51, f32[96]{0:T(128)S(1)} %reduce_sum.577, f32[36864]{0:T(1024)S(1)} %reshape.104, f32[384]{0:T(512)S(1)} %copy-done.50, f32[36864]{0:T(1024)S(1)} %reshape.105, f32[96]{0:T(128)S(1)} %get-tuple-element.98), dimensions={0} | concatenate | bytes 633600 | tf_op jit(solution)/shard_map/concatenate | solution.py:63
  54.0 2.4 %collective-permute-start.8 = (f32[39600]{0:T(1024)S(1)}, f32[39600]{0:T(1024)S(1)}, u32[]{:S(2)}, u32[]{:S(2)}) collective-permute-start(f32[39600]{0:T(1024)S(1)} %dynamic_slice.13), channel_id=1, source_target_pairs={{0,8},{8,0},{16,24},{24,16},{32,40},{40,32},{48,56},{56,48},{64,72... | collective-permute-start | bytes 475208 | tf_op jit(solution)/shard_map/ppermute | solution.py:58
  56.4 1.0 collective-permute-done.8
  57.6 4.3 %collective-permute-start.9 = (f32[19800]{0:T(1024)S(1)}, f32[19800]{0:T(1024)S(1)}, u32[]{:S(2)}, u32[]{:S(2)}) collective-permute-start(f32[19800]{0:T(1024)S(1)} %dynamic_slice.15), channel_id=1, source_target_pairs={{0,16},{8,24},{16,0},{24,8},{32,48},{40,56},{48,32},{56,40},{64,80... | collective-permute-start | bytes 237608 | tf_op jit(solution)/shard_map/ppermute | solution.py:58
  61.9 2.5 %collective-permute-done.9 = f32[19800]{0:T(1024)S(1)} collective-permute-done((f32[19800]{0:T(1024)S(1)}, f32[19800]{0:T(1024)S(1)}, u32[]{:S(2)}, u32[]{:S(2)}) %collective-permute-start.9) | collective-permute-done | bytes 79232 | tf_op jit(solution)/shard_map/ppermute | solution.py:58
  64.5 1.9 %collective-permute-start.10 = (f32[19800]{0:T(1024)S(1)}, f32[19800]{0:T(1024)S(1)}, u32[]{:S(2)}, u32[]{:S(2)}) collective-permute-start(f32[19800]{0:T(1024)S(1)} %dynamic-slice_add_fusion.1), channel_id=1, source_target_pairs={{0,1},{1,0},{2,3},{3,2},{4,5},{5,4},{6,7},{7,6},{8,9},{9,8},{10,11... | collective-permute-start | bytes 237608 | tf_op jit(solution)/shard_map/ppermute | solution.py:58
  66.5 7.3 %collective-permute-done.10 = f32[19800]{0:T(1024)S(1)} collective-permute-done((f32[19800]{0:T(1024)S(1)}, f32[19800]{0:T(1024)S(1)}, u32[]{:S(2)}, u32[]{:S(2)}) %collective-permute-start.10) | collective-permute-done | bytes 79232 | tf_op jit(solution)/shard_map/ppermute | solution.py:58
  73.7 1.9 %collective-permute-start.11 = (f32[19800]{0:T(1024)S(1)}, f32[19800]{0:T(1024)S(1)}, u32[]{:S(2)}, u32[]{:S(2)}) collective-permute-start(f32[19800]{0:T(1024)S(1)} %add.505), channel_id=1, source_target_pairs={{0,2},{1,3},{2,0},{3,1},{4,6},{5,7},{6,4},{7,5},{8,10},{9,11},{10,... | collective-permute-start | bytes 237608 | tf_op jit(solution)/shard_map/ppermute | solution.py:58
  75.7 3.3 %collective-permute-done.11 = f32[19800]{0:T(1024)S(1)} collective-permute-done((f32[19800]{0:T(1024)S(1)}, f32[19800]{0:T(1024)S(1)}, u32[]{:S(2)}, u32[]{:S(2)}) %collective-permute-start.11) | collective-permute-done | bytes 79232 | tf_op jit(solution)/shard_map/ppermute | solution.py:58
  78.9 2.1 %collective-permute-start.12 = (f32[19800]{0:T(1024)S(1)}, f32[19800]{0:T(1024)S(1)}, u32[]{:S(2)}, u32[]{:S(2)}) collective-permute-start(f32[19800]{0:T(1024)S(1)} %add.506), channel_id=1, source_target_pairs={{0,4},{1,5},{2,6},{3,7},{4,0},{5,1},{6,2},{7,3},{8,12},{9,13},{10,... | collective-permute-start | bytes 237608 | tf_op jit(solution)/shard_map/ppermute | solution.py:58
  81.0 4.6 %collective-permute-done.12 = f32[19800]{0:T(1024)S(1)} collective-permute-done((f32[19800]{0:T(1024)S(1)}, f32[19800]{0:T(1024)S(1)}, u32[]{:S(2)}, u32[]{:S(2)}) %collective-permute-start.12) | collective-permute-done | bytes 79232 | tf_op jit(solution)/shard_map/ppermute | solution.py:58
  85.7 4.0 %collective-permute-start.13 = (f32[19800]{0:T(1024)S(1)}, f32[19800]{0:T(1024)S(1)}, u32[]{:S(2)}, u32[]{:S(2)}) collective-permute-start(f32[19800]{0:T(1024)S(1)} %add.507), channel_id=1, source_target_pairs={{0,32},{8,40},{16,48},{24,56},{32,0},{40,8},{48,16},{56,24},{64,96... | collective-permute-start | bytes 237608 | tf_op jit(solution)/shard_map/ppermute | solution.py:58
  89.7 7.2 %collective-permute-start.4 = (f32[96,8,3]{0,2,1:T(4,128)S(1)}, f32[96,8,3]{0,2,1:T(4,128)S(1)}, u32[]{:S(2)}, u32[]{:S(2)}) collective-permute-start(f32[96,8,3]{0,2,1:T(4,128)S(1)} %get-tuple-element.94), channel_id=1, source_target_pairs={{0,8},{8,16},{16,24},{24,32},{32,40},{40,48},{48,56},{56,64},{64,7... | collective-permute-start | bytes 27656 | tf_op jit(solution)/shard_map/ppermute | solution.py:14
  96.9 1.9 %collective-permute-start.5 = (f32[96,8,3]{0,2,1:T(4,128)S(1)}, f32[96,8,3]{0,2,1:T(4,128)S(1)}, u32[]{:S(2)}, u32[]{:S(2)}) collective-permute-start(f32[96,8,3]{0,2,1:T(4,128)S(1)} %get-tuple-element.95), channel_id=1, source_target_pairs={{8,0},{16,8},{24,16},{32,24},{40,32},{48,40},{56,48},{64,56},{72,6... | collective-permute-start | bytes 27656 | tf_op jit(solution)/shard_map/ppermute | solution.py:17
  98.8 7.5 %collective-permute-start.14 = (f32[19800]{0:T(1024)S(1)}, f32[19800]{0:T(1024)S(1)}, u32[]{:S(2)}, u32[]{:S(2)}) collective-permute-start(f32[19800]{0:T(1024)S(1)} %add.508), channel_id=1, source_target_pairs={{0,64},{8,72},{16,80},{24,88},{32,96},{40,104},{48,112},{56,120},{... | collective-permute-start | bytes 237608 | tf_op jit(solution)/shard_map/ppermute | solution.py:58
  106.5 1.5 collective-permute-done.14
  108.0 5.8 %collective-permute-start.15 = (f32[19800]{0:T(1024)S(1)}, f32[19800]{0:T(1024)S(1)}, u32[]{:S(2)}, u32[]{:S(2)}) collective-permute-start(f32[19800]{0:T(1024)S(1)} %add.509), channel_id=1, source_target_pairs={{0,128},{8,136},{16,144},{24,152},{32,160},{40,168},{48,176},{56,1... | collective-permute-start | bytes 237608 | tf_op jit(solution)/shard_map/ppermute | solution.py:58
  113.8 4.1 %collective-permute-start.6 = (bf16[96,3,134]{0,2,1:T(8,128)(2,1)S(1)}, bf16[96,3,134]{0,2,1:T(8,128)(2,1)S(1)}, u32[]{:S(2)}, u32[]{:S(2)}) collective-permute-start(bf16[96,3,134]{0,2,1:T(8,128)(2,1)S(1)} %get-tuple-element.106), channel_id=1, source_target_pairs={{0,1},{1,2},{2,3},{3,4},{4,5},{5,6},{6,7},{8,9},{9,10},{10,11},{11... | collective-permute-start | bytes 231560 | tf_op jit(solution)/shard_map/ppermute | solution.py:14
  117.9 6.0 %collective-permute-start.7 = (bf16[96,3,134]{0,2,1:T(8,128)(2,1)S(1)}, bf16[96,3,134]{0,2,1:T(8,128)(2,1)S(1)}, u32[]{:S(2)}, u32[]{:S(2)}) collective-permute-start(bf16[96,3,134]{0,2,1:T(8,128)(2,1)S(1)} %get-tuple-element.107), channel_id=1, source_target_pairs={{1,0},{2,1},{3,2},{4,3},{5,4},{6,5},{7,6},{9,8},{10,9},{11,10},{12... | collective-permute-start | bytes 231560 | tf_op jit(solution)/shard_map/ppermute | solution.py:17
  124.7 1.9 %collective-permute-start.16 = (f32[19800]{0:T(1024)S(1)}, f32[19800]{0:T(1024)S(1)}, u32[]{:S(2)}, u32[]{:S(2)}) collective-permute-start(f32[19800]{0:T(1024)S(1)} %add.510), channel_id=1, source_target_pairs={{0,256},{8,264},{16,272},{24,280},{32,288},{40,296},{48,304},{56,3... | collective-permute-start | bytes 237608 | tf_op jit(solution)/shard_map/ppermute | solution.py:58
  126.6 2.3 %collective-permute-done.7 = bf16[96,3,134]{0,2,1:T(8,128)(2,1)S(1)} collective-permute-done((bf16[96,3,134]{0,2,1:T(8,128)(2,1)S(1)}, bf16[96,3,134]{0,2,1:T(8,128)(2,1)S(1)}, u32[]{:S(2)}, u32[]{:S(2)}) %collective-permute-start.7) | collective-permute-done | bytes 77216 | tf_op jit(solution)/shard_map/ppermute | solution.py:17
  129.2 4.8 %collective-permute-done.16 = f32[19800]{0:T(1024)S(1)} collective-permute-done((f32[19800]{0:T(1024)S(1)}, f32[19800]{0:T(1024)S(1)}, u32[]{:S(2)}, u32[]{:S(2)}) %collective-permute-start.16) | collective-permute-done | bytes 79232 | tf_op jit(solution)/shard_map/ppermute | solution.py:58
  134.0 3.3 %collective-permute-start.17 = (f32[19800]{0:T(1024)S(1)}, f32[19800]{0:T(1024)S(1)}, u32[]{:S(2)}, u32[]{:S(2)}) collective-permute-start(f32[19800]{0:T(1024)S(1)} %add.511), channel_id=1, source_target_pairs={{0,16},{8,24},{16,0},{24,8},{32,48},{40,56},{48,32},{56,40},{64,80... | collective-permute-start | bytes 237608 | tf_op jit(solution)/shard_map/ppermute | solution.py:58
  137.4 1.7 %collective-permute-done.17 = f32[19800]{0:T(1024)S(1)} collective-permute-done((f32[19800]{0:T(1024)S(1)}, f32[19800]{0:T(1024)S(1)}, u32[]{:S(2)}, u32[]{:S(2)}) %collective-permute-start.17) | collective-permute-done | bytes 79232 | tf_op jit(solution)/shard_map/ppermute | solution.py:58
  139.3 6.1 %collective-permute-start.18 = (f32[39600]{0:T(1024)S(1)}, f32[39600]{0:T(1024)S(1)}, u32[]{:S(2)}, u32[]{:S(2)}) collective-permute-start(f32[39600]{0:T(1024)S(1)} %maximum_select_fusion.1), channel_id=1, source_target_pairs={{0,8},{8,0},{16,24},{24,16},{32,40},{40,32},{48,56},{56,48},{64,72... | collective-permute-start | bytes 475208 | tf_op jit(solution)/shard_map/ppermute | solution.py:58
  145.6 4.0 %fusion.144 = bf16[96,8,128]{0,2,1:T(8,128)(2,1)S(1)} fusion(f32[96,11,134]{0,2,1:T(8,128)S(1)} %get-tuple-element.93, f32[96,8,3]{0,2,1:T(4,128)S(1)} %collective-permute-done.5, f32[96,8,128]{0,2,1:T(8,128)S(1)} %bitcast.262, f32[96,8,3]{0,2,1:T(4,128)S(1)} %collective-permute-done.4, f32[96,11,134]{0,2,1:T(8,128)S(1)} %get-tuple-element.92, ...), kind=kLoop, calls=%fused_computation.260 | loop fusion | flops 10420224 | bytes 17338752 | tf_op jit(solution)/shard_map/convert_element_type | solution.py:158
  149.6 0.8 copy.91
  (215 shorter events, 9.4 us)
Async XLA Ops:
  0.6 37.6 %copy-start = (bf16[96,384]{1,0:T(8,128)(2,1)S(1)}, bf16[96,384]{1,0:T(8,128)(2,1)}, u32[]{:S(2)}) copy-start(bf16[96,384]{1,0:T(8,128)(2,1)} %param.16) | copy-start | bytes 221188
  1.8 7.8 %collective-permute-start = (bf16[96,8,3]{0,2,1:T(4,128)(2,1)S(1)}, bf16[96,8,3]{0,2,1:T(4,128)(2,1)S(1)}, u32[]{:S(2)}, u32[]{:S(2)}) collective-permute-start(bf16[96,8,3]{0,2,1:T(4,128)(2,1)S(1)} %get-tuple-element.112), channel_id=1, source_target_pairs={{0,8},{8,16},{16,24},{24,32},{32,40},{40,48},{48,56},{56,64},{64,7... | collective-permute-start | bytes 13832 | tf_op jit(solution)/shard_map/ppermute | solution.py:14
  5.6 5.0 %collective-permute-start.1 = (bf16[96,8,3]{0,2,1:T(4,128)(2,1)S(1)}, bf16[96,8,3]{0,2,1:T(4,128)(2,1)S(1)}, u32[]{:S(2)}, u32[]{:S(2)}) collective-permute-start(bf16[96,8,3]{0,2,1:T(4,128)(2,1)S(1)} %get-tuple-element.113), channel_id=1, source_target_pairs={{8,0},{16,8},{24,16},{32,24},{40,32},{48,40},{56,48},{64,56},{72,6... | collective-permute-start | bytes 13832 | tf_op jit(solution)/shard_map/ppermute | solution.py:17
  9.5 23.6 %copy-start.6 = (f32[96]{0:T(128)}, f32[96]{0:T(128)S(1)}, u32[]{:S(2)}) copy-start(f32[96]{0:T(128)S(1)} %get-tuple-element.142) | copy-start | bytes 1156
  9.5 23.6 %copy-start.8 = (f32[96]{0:T(128)}, f32[96]{0:T(128)S(1)}, u32[]{:S(2)}) copy-start(f32[96]{0:T(128)S(1)} %get-tuple-element.143) | copy-start | bytes 1156
  9.6 23.6 %copy-start.10 = (f32[96]{0:T(128)}, f32[96]{0:T(128)S(1)}, u32[]{:S(2)}) copy-start(f32[96]{0:T(128)S(1)} %get-tuple-element.144) | copy-start | bytes 1156
  9.6 23.6 %copy-start.12 = (f32[96]{0:T(128)}, f32[96]{0:T(128)S(1)}, u32[]{:S(2)}) copy-start(f32[96]{0:T(128)S(1)} %get-tuple-element.145) | copy-start | bytes 1156
  9.6 23.6 %copy-start.14 = (f32[96]{0:T(128)}, f32[96]{0:T(128)S(1)}, u32[]{:S(2)}) copy-start(f32[96]{0:T(128)S(1)} %get-tuple-element.146) | copy-start | bytes 1156
  9.6 23.6 %copy-start.16 = (f32[96]{0:T(128)}, f32[96]{0:T(128)S(1)}, u32[]{:S(2)}) copy-start(f32[96]{0:T(128)S(1)} %get-tuple-element.147) | copy-start | bytes 1156
  9.6 23.6 %copy-start.18 = (f32[96]{0:T(128)}, f32[96]{0:T(128)S(1)}, u32[]{:S(2)}) copy-start(f32[96]{0:T(128)S(1)} %get-tuple-element.148) | copy-start | bytes 1156
  9.6 23.6 %copy-start.20 = (f32[96]{0:T(128)}, f32[96]{0:T(128)S(1)}, u32[]{:S(2)}) copy-start(f32[96]{0:T(128)S(1)} %get-tuple-element.149) | copy-start | bytes 1156
  9.6 23.6 %copy-start.22 = (f32[96]{0:T(128)}, f32[96]{0:T(128)S(1)}, u32[]{:S(2)}) copy-start(f32[96]{0:T(128)S(1)} %get-tuple-element.150) | copy-start | bytes 1156
  9.6 23.6 %copy-start.24 = (f32[96]{0:T(128)}, f32[96]{0:T(128)S(1)}, u32[]{:S(2)}) copy-start(f32[96]{0:T(128)S(1)} %get-tuple-element.151) | copy-start | bytes 1156
  10.7 15.8 %collective-permute-start.2 = (bf16[96,3,134]{0,2,1:T(8,128)(2,1)S(1)}, bf16[96,3,134]{0,2,1:T(8,128)(2,1)S(1)}, u32[]{:S(2)}, u32[]{:S(2)}) collective-permute-start(bf16[96,3,134]{0,2,1:T(8,128)(2,1)S(1)} %get-tuple-element.110), channel_id=1, source_target_pairs={{0,1},{1,2},{2,3},{3,4},{4,5},{5,6},{6,7},{8,9},{9,10},{10,11},{11... | collective-permute-start | bytes 231560 | tf_op jit(solution)/shard_map/ppermute | solution.py:14
  21.3 11.7 %collective-permute-start.3 = (bf16[96,3,134]{0,2,1:T(8,128)(2,1)S(1)}, bf16[96,3,134]{0,2,1:T(8,128)(2,1)S(1)}, u32[]{:S(2)}, u32[]{:S(2)}) collective-permute-start(bf16[96,3,134]{0,2,1:T(8,128)(2,1)S(1)} %get-tuple-element.111), channel_id=1, source_target_pairs={{1,0},{2,1},{3,2},{4,3},{5,4},{6,5},{7,6},{9,8},{10,9},{11,10},{12... | collective-permute-start | bytes 231560 | tf_op jit(solution)/shard_map/ppermute | solution.py:17
  54.0 3.4 %collective-permute-start.8 = (f32[39600]{0:T(1024)S(1)}, f32[39600]{0:T(1024)S(1)}, u32[]{:S(2)}, u32[]{:S(2)}) collective-permute-start(f32[39600]{0:T(1024)S(1)} %dynamic_slice.13), channel_id=1, source_target_pairs={{0,8},{8,0},{16,24},{24,16},{32,40},{40,32},{48,56},{56,48},{64,72... | collective-permute-start | bytes 475208 | tf_op jit(solution)/shard_map/ppermute | solution.py:58
  57.6 6.9 %collective-permute-start.9 = (f32[19800]{0:T(1024)S(1)}, f32[19800]{0:T(1024)S(1)}, u32[]{:S(2)}, u32[]{:S(2)}) collective-permute-start(f32[19800]{0:T(1024)S(1)} %dynamic_slice.15), channel_id=1, source_target_pairs={{0,16},{8,24},{16,0},{24,8},{32,48},{40,56},{48,32},{56,40},{64,80... | collective-permute-start | bytes 237608 | tf_op jit(solution)/shard_map/ppermute | solution.py:58
  64.5 9.2 %collective-permute-start.10 = (f32[19800]{0:T(1024)S(1)}, f32[19800]{0:T(1024)S(1)}, u32[]{:S(2)}, u32[]{:S(2)}) collective-permute-start(f32[19800]{0:T(1024)S(1)} %dynamic-slice_add_fusion.1), channel_id=1, source_target_pairs={{0,1},{1,0},{2,3},{3,2},{4,5},{5,4},{6,7},{7,6},{8,9},{9,8},{10,11... | collective-permute-start | bytes 237608 | tf_op jit(solution)/shard_map/ppermute | solution.py:58
  73.7 5.2 %collective-permute-start.11 = (f32[19800]{0:T(1024)S(1)}, f32[19800]{0:T(1024)S(1)}, u32[]{:S(2)}, u32[]{:S(2)}) collective-permute-start(f32[19800]{0:T(1024)S(1)} %add.505), channel_id=1, source_target_pairs={{0,2},{1,3},{2,0},{3,1},{4,6},{5,7},{6,4},{7,5},{8,10},{9,11},{10,... | collective-permute-start | bytes 237608 | tf_op jit(solution)/shard_map/ppermute | solution.py:58
  78.9 6.7 %collective-permute-start.12 = (f32[19800]{0:T(1024)S(1)}, f32[19800]{0:T(1024)S(1)}, u32[]{:S(2)}, u32[]{:S(2)}) collective-permute-start(f32[19800]{0:T(1024)S(1)} %add.506), channel_id=1, source_target_pairs={{0,4},{1,5},{2,6},{3,7},{4,0},{5,1},{6,2},{7,3},{8,12},{9,13},{10,... | collective-permute-start | bytes 237608 | tf_op jit(solution)/shard_map/ppermute | solution.py:58
  85.7 13.2 %collective-permute-start.13 = (f32[19800]{0:T(1024)S(1)}, f32[19800]{0:T(1024)S(1)}, u32[]{:S(2)}, u32[]{:S(2)}) collective-permute-start(f32[19800]{0:T(1024)S(1)} %add.507), channel_id=1, source_target_pairs={{0,32},{8,40},{16,48},{24,56},{32,0},{40,8},{48,16},{56,24},{64,96... | collective-permute-start | bytes 237608 | tf_op jit(solution)/shard_map/ppermute | solution.py:58
  89.7 16.7 %collective-permute-start.4 = (f32[96,8,3]{0,2,1:T(4,128)S(1)}, f32[96,8,3]{0,2,1:T(4,128)S(1)}, u32[]{:S(2)}, u32[]{:S(2)}) collective-permute-start(f32[96,8,3]{0,2,1:T(4,128)S(1)} %get-tuple-element.94), channel_id=1, source_target_pairs={{0,8},{8,16},{16,24},{24,32},{32,40},{40,48},{48,56},{56,64},{64,7... | collective-permute-start | bytes 27656 | tf_op jit(solution)/shard_map/ppermute | solution.py:14
  96.9 9.5 %collective-permute-start.5 = (f32[96,8,3]{0,2,1:T(4,128)S(1)}, f32[96,8,3]{0,2,1:T(4,128)S(1)}, u32[]{:S(2)}, u32[]{:S(2)}) collective-permute-start(f32[96,8,3]{0,2,1:T(4,128)S(1)} %get-tuple-element.95), channel_id=1, source_target_pairs={{8,0},{16,8},{24,16},{32,24},{40,32},{48,40},{56,48},{64,56},{72,6... | collective-permute-start | bytes 27656 | tf_op jit(solution)/shard_map/ppermute | solution.py:17
  98.8 9.2 %collective-permute-start.14 = (f32[19800]{0:T(1024)S(1)}, f32[19800]{0:T(1024)S(1)}, u32[]{:S(2)}, u32[]{:S(2)}) collective-permute-start(f32[19800]{0:T(1024)S(1)} %add.508), channel_id=1, source_target_pairs={{0,64},{8,72},{16,80},{24,88},{32,96},{40,104},{48,112},{56,120},{... | collective-permute-start | bytes 237608 | tf_op jit(solution)/shard_map/ppermute | solution.py:58
  108.0 16.6 %collective-permute-start.15 = (f32[19800]{0:T(1024)S(1)}, f32[19800]{0:T(1024)S(1)}, u32[]{:S(2)}, u32[]{:S(2)}) collective-permute-start(f32[19800]{0:T(1024)S(1)} %add.509), channel_id=1, source_target_pairs={{0,128},{8,136},{16,144},{24,152},{32,160},{40,168},{48,176},{56,1... | collective-permute-start | bytes 237608 | tf_op jit(solution)/shard_map/ppermute | solution.py:58
  113.8 12.8 %collective-permute-start.6 = (bf16[96,3,134]{0,2,1:T(8,128)(2,1)S(1)}, bf16[96,3,134]{0,2,1:T(8,128)(2,1)S(1)}, u32[]{:S(2)}, u32[]{:S(2)}) collective-permute-start(bf16[96,3,134]{0,2,1:T(8,128)(2,1)S(1)} %get-tuple-element.106), channel_id=1, source_target_pairs={{0,1},{1,2},{2,3},{3,4},{4,5},{5,6},{6,7},{8,9},{9,10},{10,11},{11... | collective-permute-start | bytes 231560 | tf_op jit(solution)/shard_map/ppermute | solution.py:14
  117.9 11.0 %collective-permute-start.7 = (bf16[96,3,134]{0,2,1:T(8,128)(2,1)S(1)}, bf16[96,3,134]{0,2,1:T(8,128)(2,1)S(1)}, u32[]{:S(2)}, u32[]{:S(2)}) collective-permute-start(bf16[96,3,134]{0,2,1:T(8,128)(2,1)S(1)} %get-tuple-element.107), channel_id=1, source_target_pairs={{1,0},{2,1},{3,2},{4,3},{5,4},{6,5},{7,6},{9,8},{10,9},{11,10},{12... | collective-permute-start | bytes 231560 | tf_op jit(solution)/shard_map/ppermute | solution.py:17
  124.7 9.3 %collective-permute-start.16 = (f32[19800]{0:T(1024)S(1)}, f32[19800]{0:T(1024)S(1)}, u32[]{:S(2)}, u32[]{:S(2)}) collective-permute-start(f32[19800]{0:T(1024)S(1)} %add.510), channel_id=1, source_target_pairs={{0,256},{8,264},{16,272},{24,280},{32,288},{40,296},{48,304},{56,3... | collective-permute-start | bytes 237608 | tf_op jit(solution)/shard_map/ppermute | solution.py:58
  129.0 16.4 %copy-start.2 = (bf16[96,8,128]{0,2,1:T(8,128)(2,1)S(1)}, bf16[96,8,128]{0,2,1:T(8,128)(2,1)}, u32[]{:S(2)}) copy-start(bf16[96,8,128]{0,2,1:T(8,128)(2,1)} %copy-done.1) | copy-start | bytes 589828
  129.0 16.4 %copy-start.7 = (f32[96]{0:T(128)S(1)}, f32[96]{0:T(128)}, u32[]{:S(2)}) copy-start(f32[96]{0:T(128)} %copy-done.6) | copy-start | bytes 1156
  129.0 16.4 %copy-start.9 = (f32[96]{0:T(128)S(1)}, f32[96]{0:T(128)}, u32[]{:S(2)}) copy-start(f32[96]{0:T(128)} %copy-done.8) | copy-start | bytes 1156
  129.0 16.4 %copy-start.11 = (f32[96]{0:T(128)S(1)}, f32[96]{0:T(128)}, u32[]{:S(2)}) copy-start(f32[96]{0:T(128)} %copy-done.10) | copy-start | bytes 1156
  129.0 16.4 %copy-start.13 = (f32[96]{0:T(128)S(1)}, f32[96]{0:T(128)}, u32[]{:S(2)}) copy-start(f32[96]{0:T(128)} %copy-done.12) | copy-start | bytes 1156
  129.0 16.4 %copy-start.15 = (f32[96]{0:T(128)S(1)}, f32[96]{0:T(128)}, u32[]{:S(2)}) copy-start(f32[96]{0:T(128)} %copy-done.14) | copy-start | bytes 1156
  129.0 16.4 %copy-start.17 = (f32[96]{0:T(128)S(1)}, f32[96]{0:T(128)}, u32[]{:S(2)}) copy-start(f32[96]{0:T(128)} %copy-done.16) | copy-start | bytes 1156
  129.1 16.4 %copy-start.19 = (f32[96]{0:T(128)S(1)}, f32[96]{0:T(128)}, u32[]{:S(2)}) copy-start(f32[96]{0:T(128)} %copy-done.18) | copy-start | bytes 1156
  129.1 16.4 %copy-start.21 = (f32[96]{0:T(128)S(1)}, f32[96]{0:T(128)}, u32[]{:S(2)}) copy-start(f32[96]{0:T(128)} %copy-done.20) | copy-start | bytes 1156
  129.1 16.4 %copy-start.23 = (f32[96]{0:T(128)S(1)}, f32[96]{0:T(128)}, u32[]{:S(2)}) copy-start(f32[96]{0:T(128)} %copy-done.22) | copy-start | bytes 1156
  129.1 16.4 %copy-start.25 = (f32[96]{0:T(128)S(1)}, f32[96]{0:T(128)}, u32[]{:S(2)}) copy-start(f32[96]{0:T(128)} %copy-done.24) | copy-start | bytes 1156
  129.1 16.4 %copy-start.27 = (f32[96]{0:T(128)S(1)}, f32[96]{0:T(128)}, u32[]{:S(2)}) copy-start(f32[96]{0:T(128)} %copy-done.26) | copy-start | bytes 1156
  129.1 16.4 %copy-start.29 = (f32[96]{0:T(128)S(1)}, f32[96]{0:T(128)}, u32[]{:S(2)}) copy-start(f32[96]{0:T(128)} %copy-done.28) | copy-start | bytes 1156
  129.1 16.4 %copy-start.31 = (f32[96]{0:T(128)S(1)}, f32[96]{0:T(128)}, u32[]{:S(2)}) copy-start(f32[96]{0:T(128)} %copy-done.30) | copy-start | bytes 1156
  129.1 16.4 %copy-start.33 = (f32[96]{0:T(128)S(1)}, f32[96]{0:T(128)}, u32[]{:S(2)}) copy-start(f32[96]{0:T(128)} %copy-done.32) | copy-start | bytes 1156
  129.1 16.4 %copy-start.35 = (f32[96]{0:T(128)S(1)}, f32[96]{0:T(128)}, u32[]{:S(2)}) copy-start(f32[96]{0:T(128)} %copy-done.34) | copy-start | bytes 1156
  129.1 16.4 %copy-start.37 = (f32[96]{0:T(128)S(1)}, f32[96]{0:T(128)}, u32[]{:S(2)}) copy-start(f32[96]{0:T(128)} %copy-done.36) | copy-start | bytes 1156
  129.2 16.4 %copy-start.39 = (f32[96]{0:T(128)S(1)}, f32[96]{0:T(128)}, u32[]{:S(2)}) copy-start(f32[96]{0:T(128)} %copy-done.38) | copy-start | bytes 1156
  134.0 5.2 %collective-permute-start.17 = (f32[19800]{0:T(1024)S(1)}, f32[19800]{0:T(1024)S(1)}, u32[]{:S(2)}, u32[]{:S(2)}) collective-permute-start(f32[19800]{0:T(1024)S(1)} %add.511), channel_id=1, source_target_pairs={{0,16},{8,24},{16,0},{24,8},{32,48},{40,56},{48,32},{56,40},{64,80... | collective-permute-start | bytes 237608 | tf_op jit(solution)/shard_map/ppermute | solution.py:58
  139.3 11.2 %collective-permute-start.18 = (f32[39600]{0:T(1024)S(1)}, f32[39600]{0:T(1024)S(1)}, u32[]{:S(2)}, u32[]{:S(2)}) collective-permute-start(f32[39600]{0:T(1024)S(1)} %maximum_select_fusion.1), channel_id=1, source_target_pairs={{0,8},{8,0},{16,24},{24,16},{32,40},{40,32},{48,56},{56,48},{64,72... | collective-permute-start | bytes 475208 | tf_op jit(solution)/shard_map/ppermute | solution.py:58
  (51 other events, 258.3 us)

commit v9 on v8

--- a/solution.py
+++ b/solution.py
@@ -83,7 +83,7 @@
         flat = flat + xor_partner(flat, axis, mask)
     for (axis, mask), side in zip(reversed(halving), reversed(sides)):
         other = xor_partner(flat, axis, mask)
-        flat = jnp.where(side == 0, jnp.concatenate([flat, other]), jnp.concatenate([other, flat]))
+        flat = lax.dynamic_update_slice_in_dim(jnp.concatenate([other, other]), flat, side * flat.shape[0], 0)
     out, start = [], 0
     for shape in shapes:
         size = math.prod(shape)

time: 155 us -> 164 us (1.058)
  the two profiles are of different devices: /device:TPU:5 before, /device:TPU:7 now
where the time goes in v9:
time: 164 us; the launch traced here: 163 us
  starting transfers between devices  83.7 us (51%)
  waiting for transfers between devices  31.1 us (19%)
  local copies, waits for them, and re-layouts  20.5 us (12%)
  other arithmetic  19.2 us (12%)
  matrix products  5.72 us (3%)
  between operations  2.89 us (2%)
    ppermute x11, starting transfers between devices, xor_partner(): lax.ppermute(value, axis, [(i, i ^ mask) for i in range(lax.axis_size(axi...  45.4 us
    ppermute x11, waiting for transfers between devices, xor_partner(): lax.ppermute(value, axis, [(i, i ^ mask) for i in range(lax.axis_size(axi...  26.2 us
    ppermute x4, starting transfers between devices, padded_2(): lax.ppermute(lax.slice_in_dim(block, block.shape[dim] - width, None, axis...  25.6 us
    ppermute x4, starting transfers between devices, padded_2(): lax.ppermute(lax.slice_in_dim(block, 0, width, axis=dim), axis, backward)  12.7 us
    unnamed x230, local copies, waits for them, and re-layouts  5.9 us
    dot_general x6, matrix products, product(): return jnp.einsum(form, left, right, preferred_element_type=jnp.float32)  5.72 us
    reduce_sum x4, other arithmetic, kernel_terms(): jnp.sum(conv_grad * padded[:, row_step:row_step + height, col_step:col_st...  5.48 us
    reduce_sum x1, other arithmetic, mixing(): average = jnp.mean(conv_flat, axis=0, keepdims=True)  4.93 us
  transfers between devices with their start and end apart: 19, of which 11 were waited for; matrix products, arithmetic and copies ran while one was open for 7% of the time, Pallas kernels for 0%

profile of v9, /device:TPU:7, one launch (start us, length us, event | category | flops | bytes accessed | tf_op | source)
XLA Modules:
  0.0 163.0 jit_solution(2323444756024888770)
XLA Ops:
  0.7 1.2 copy.24
  1.8 3.8 %collective-permute-start = (bf16[96,8,3]{0,2,1:T(4,128)(2,1)S(1)}, bf16[96,8,3]{0,2,1:T(4,128)(2,1)S(1)}, u32[]{:S(2)}, u32[]{:S(2)}) collective-permute-start(bf16[96,8,3]{0,2,1:T(4,128)(2,1)S(1)} %get-tuple-element.112), channel_id=1, source_target_pairs={{0,8},{8,16},{16,24},{24,32},{32,40},{40,48},{48,56},{56,64},{64,7... | collective-permute-start | bytes 13832 | tf_op jit(solution)/shard_map/ppermute | solution.py:14
  5.6 1.9 %collective-permute-start.1 = (bf16[96,8,3]{0,2,1:T(4,128)(2,1)S(1)}, bf16[96,8,3]{0,2,1:T(4,128)(2,1)S(1)}, u32[]{:S(2)}, u32[]{:S(2)}) collective-permute-start(bf16[96,8,3]{0,2,1:T(4,128)(2,1)S(1)} %get-tuple-element.113), channel_id=1, source_target_pairs={{8,0},{16,8},{24,16},{32,24},{40,32},{48,40},{56,48},{64,56},{72,6... | collective-permute-start | bytes 13832 | tf_op jit(solution)/shard_map/ppermute | solution.py:17
  7.5 1.0 slice_bitcast_fusion.48
  8.7 1.0 slice_bitcast_fusion.47
  10.7 10.6 %collective-permute-start.2 = (bf16[96,3,134]{0,2,1:T(8,128)(2,1)S(1)}, bf16[96,3,134]{0,2,1:T(8,128)(2,1)S(1)}, u32[]{:S(2)}, u32[]{:S(2)}) collective-permute-start(bf16[96,3,134]{0,2,1:T(8,128)(2,1)S(1)} %get-tuple-element.110), channel_id=1, source_target_pairs={{0,1},{1,2},{2,3},{3,4},{4,5},{5,6},{6,7},{8,9},{9,10},{10,11},{11... | collective-permute-start | bytes 231560 | tf_op jit(solution)/shard_map/ppermute | solution.py:14
  21.3 2.2 %collective-permute-start.3 = (bf16[96,3,134]{0,2,1:T(8,128)(2,1)S(1)}, bf16[96,3,134]{0,2,1:T(8,128)(2,1)S(1)}, u32[]{:S(2)}, u32[]{:S(2)}) collective-permute-start(bf16[96,3,134]{0,2,1:T(8,128)(2,1)S(1)} %get-tuple-element.111), channel_id=1, source_target_pairs={{1,0},{2,1},{3,2},{4,3},{5,4},{6,5},{7,6},{9,8},{10,9},{11,10},{12... | collective-permute-start | bytes 231560 | tf_op jit(solution)/shard_map/ppermute | solution.py:17
  23.5 1.5 slice_bitcast_fusion.46
  25.0 1.1 copy.32
  26.3 0.9 copy.95
  27.2 3.6 %collective-permute-done.3 = bf16[96,3,134]{0,2,1:T(8,128)(2,1)S(1)} collective-permute-done((bf16[96,3,134]{0,2,1:T(8,128)(2,1)S(1)}, bf16[96,3,134]{0,2,1:T(8,128)(2,1)S(1)}, u32[]{:S(2)}, u32[]{:S(2)}) %collective-permute-start.3) | collective-permute-done | bytes 77216 | tf_op jit(solution)/shard_map/ppermute | solution.py:17
  31.3 4.9 %fusion.180 = (f32[8,128]{1,0:T(8,128)S(1)}, f32[96,8,128]{0,2,1:T(8,128)S(1)}) fusion(f32[96]{0:T(128)S(1)} %copy-done.109, bf16[96,11,134]{0,2,1:T(8,128)(2,1)S(1)} %get-tuple-element.109, f32[96]{0:T(128)} %get-tuple-element.161, f32[96]{0:T(128)} %get-tuple-element.162, f32[96]{0:T(128)S(1)} %get-tuple-element.115, f32[96]{0:T(128)S(1)} %get-tuple-element.116, ...), kind=kLoop, calls=%fused_computation.429 | loop fusion | flops 16317440 | bytes 8879872 | tf_op jit(solution)/shard_map/reduce_sum | solution.py:100
  37.8 2.0 %convert_reduce_fusion = (f32[384]{0:T(512)}, bf16[384,1024]{0,1:T(8,128)(2,1)S(1)}) fusion(f32[1024,384]{1,0:T(8,128)S(1)} %get-tuple-element.166, bf16[384,96]{0,1:T(8,128)(2,1)S(1)} %copy-done.3, f32[96,1024]{1,0:T(8,128)S(1)} %copy.97, f32[96]{0:T(128)S(1)} %copy-done.83), kind=kOutput, calls=%fused_computation.16 | convolution fusion | flops 84344448 | bytes 2828160 | tf_op jit(solution)/shard_map/hc,cp->hp/dot_general | solution.py:96
  39.8 1.0 fusion.178
  40.8 1.0 fusion.168
  41.8 1.5 fusion.179
  43.3 1.2 copy.98
  44.5 1.1 fusion.123
  45.6 1.9 %fusion.141 = (f32[96]{0:T(128)}, f32[96]{0:T(128)}, f32[96]{0:T(128)}, f32[96]{0:T(128)}, f32[96]{0:T(128)}, /*index=5*/f32[96]{0:T(128)}, f32[96]{0:T(128)}, f...) fusion(bf16[96,11,134]{0,2,1:T(8,128)(2,1)S(1)} %get-tuple-elem, ...), kind=kLoop, calls=%fused_computation.256 | loop fusion | flops 5306688 | bytes 3939072 | tf_op jit(solution)/shard_map/reduce_sum | solution.py:48
  47.7 1.9 %fusion.91 = (f32[96]{0:T(128)}, f32[96]{0:T(128)}, f32[96]{0:T(128)}, f32[96]{0:T(128)}, f32[96]{0:T(128)}, /*index=5*/f32[96]{0:T(128)}, f32[96]{0:T(128)}, f3...) fusion(bf16[96,11,134]{0,2,1:T(8,128)(2,1)S(1)} %get-tuple-elem, ...), kind=kLoop, calls=%fused_computation.206 | loop fusion | flops 5306688 | bytes 3939072 | tf_op jit(solution)/shard_map/reduce_sum | solution.py:48
  50.4 3.5 %stack.199 = f32[96,49]{0,1:T(8,128)S(1)} concatenate(f32[96,1]{0,1:T(1,128)S(1)} %bitcast.270, f32[96,1]{0,1:T(1,128)S(1)} %bitcast.271, f32[96,1]{0,1:T(1,128)S(1)} %bitcast.272, f32[96,1]{0,1:T(1,128)} %bitcast.308, f32[96,1]{0,1:T(1,128)} %bitcast.307, f32[96,1]{0,1:T(1,128)} %bitcast.306, f32[96,1]{0,1:T(1,128)} %bitcast.305, f32[96,1]{0,1:T(1,128)} %bitcast.304, ...), dimensions={1} | concatenate | bytes 37632 | tf_op jit(solution)/shard_map/stack | solution.py:54
  55.4 1.6 concatenate.143
  57.1 1.9 %collective-permute-start.8 = (f32[39600]{0:T(1024)S(1)}, f32[39600]{0:T(1024)S(1)}, u32[]{:S(2)}, u32[]{:S(2)}) collective-permute-start(f32[39600]{0:T(1024)S(1)} %dynamic_slice.13), channel_id=1, source_target_pairs={{0,8},{8,0},{16,24},{24,16},{32,40},{40,32},{48,56},{56,48},{64,72... | collective-permute-start | bytes 475208 | tf_op jit(solution)/shard_map/ppermute | solution.py:58
  59.1 1.3 collective-permute-done.8
  60.6 4.6 %collective-permute-start.9 = (f32[19800]{0:T(1024)S(1)}, f32[19800]{0:T(1024)S(1)}, u32[]{:S(2)}, u32[]{:S(2)}) collective-permute-start(f32[19800]{0:T(1024)S(1)} %dynamic_slice.15), channel_id=1, source_target_pairs={{0,16},{8,24},{16,0},{24,8},{32,48},{40,56},{48,32},{56,40},{64,80... | collective-permute-start | bytes 237608 | tf_op jit(solution)/shard_map/ppermute | solution.py:58
  65.3 2.5 %collective-permute-done.9 = f32[19800]{0:T(1024)S(1)} collective-permute-done((f32[19800]{0:T(1024)S(1)}, f32[19800]{0:T(1024)S(1)}, u32[]{:S(2)}, u32[]{:S(2)}) %collective-permute-start.9) | collective-permute-done | bytes 79232 | tf_op jit(solution)/shard_map/ppermute | solution.py:58
  67.9 2.1 %collective-permute-start.10 = (f32[19800]{0:T(1024)S(1)}, f32[19800]{0:T(1024)S(1)}, u32[]{:S(2)}, u32[]{:S(2)}) collective-permute-start(f32[19800]{0:T(1024)S(1)} %dynamic-slice_add_fusion.1), channel_id=1, source_target_pairs={{0,1},{1,0},{2,3},{3,2},{4,5},{5,4},{6,7},{7,6},{8,9},{9,8},{10,11... | collective-permute-start | bytes 237608 | tf_op jit(solution)/shard_map/ppermute | solution.py:58
  69.9 7.0 %collective-permute-done.10 = f32[19800]{0:T(1024)S(1)} collective-permute-done((f32[19800]{0:T(1024)S(1)}, f32[19800]{0:T(1024)S(1)}, u32[]{:S(2)}, u32[]{:S(2)}) %collective-permute-start.10) | collective-permute-done | bytes 79232 | tf_op jit(solution)/shard_map/ppermute | solution.py:58
  77.0 4.7 %collective-permute-start.11 = (f32[19800]{0:T(1024)S(1)}, f32[19800]{0:T(1024)S(1)}, u32[]{:S(2)}, u32[]{:S(2)}) collective-permute-start(f32[19800]{0:T(1024)S(1)} %add.507), channel_id=1, source_target_pairs={{0,2},{1,3},{2,0},{3,1},{4,6},{5,7},{6,4},{7,5},{8,10},{9,11},{10,... | collective-permute-start | bytes 237608 | tf_op jit(solution)/shard_map/ppermute | solution.py:58
  81.7 1.8 %collective-permute-done.11 = f32[19800]{0:T(1024)S(1)} collective-permute-done((f32[19800]{0:T(1024)S(1)}, f32[19800]{0:T(1024)S(1)}, u32[]{:S(2)}, u32[]{:S(2)}) %collective-permute-start.11) | collective-permute-done | bytes 79232 | tf_op jit(solution)/shard_map/ppermute | solution.py:58
  83.5 3.9 %collective-permute-start.12 = (f32[19800]{0:T(1024)S(1)}, f32[19800]{0:T(1024)S(1)}, u32[]{:S(2)}, u32[]{:S(2)}) collective-permute-start(f32[19800]{0:T(1024)S(1)} %add.508), channel_id=1, source_target_pairs={{0,4},{1,5},{2,6},{3,7},{4,0},{5,1},{6,2},{7,3},{8,12},{9,13},{10,... | collective-permute-start | bytes 237608 | tf_op jit(solution)/shard_map/ppermute | solution.py:58
  87.5 2.7 %collective-permute-done.12 = f32[19800]{0:T(1024)S(1)} collective-permute-done((f32[19800]{0:T(1024)S(1)}, f32[19800]{0:T(1024)S(1)}, u32[]{:S(2)}, u32[]{:S(2)}) %collective-permute-start.12) | collective-permute-done | bytes 79232 | tf_op jit(solution)/shard_map/ppermute | solution.py:58
  90.2 4.0 %collective-permute-start.13 = (f32[19800]{0:T(1024)S(1)}, f32[19800]{0:T(1024)S(1)}, u32[]{:S(2)}, u32[]{:S(2)}) collective-permute-start(f32[19800]{0:T(1024)S(1)} %add.509), channel_id=1, source_target_pairs={{0,32},{8,40},{16,48},{24,56},{32,0},{40,8},{48,16},{56,24},{64,96... | collective-permute-start | bytes 237608 | tf_op jit(solution)/shard_map/ppermute | solution.py:58
  94.3 7.8 %collective-permute-start.4 = (f32[96,8,3]{0,2,1:T(4,128)S(1)}, f32[96,8,3]{0,2,1:T(4,128)S(1)}, u32[]{:S(2)}, u32[]{:S(2)}) collective-permute-start(f32[96,8,3]{0,2,1:T(4,128)S(1)} %get-tuple-element.94), channel_id=1, source_target_pairs={{0,8},{8,16},{16,24},{24,32},{32,40},{40,48},{48,56},{56,64},{64,7... | collective-permute-start | bytes 27656 | tf_op jit(solution)/shard_map/ppermute | solution.py:14
  102.1 1.9 %collective-permute-start.5 = (f32[96,8,3]{0,2,1:T(4,128)S(1)}, f32[96,8,3]{0,2,1:T(4,128)S(1)}, u32[]{:S(2)}, u32[]{:S(2)}) collective-permute-start(f32[96,8,3]{0,2,1:T(4,128)S(1)} %get-tuple-element.95), channel_id=1, source_target_pairs={{8,0},{16,8},{24,16},{32,24},{40,32},{48,40},{56,48},{64,56},{72,6... | collective-permute-start | bytes 27656 | tf_op jit(solution)/shard_map/ppermute | solution.py:17
  104.0 8.8 %collective-permute-start.14 = (f32[19800]{0:T(1024)S(1)}, f32[19800]{0:T(1024)S(1)}, u32[]{:S(2)}, u32[]{:S(2)}) collective-permute-start(f32[19800]{0:T(1024)S(1)} %add.510), channel_id=1, source_target_pairs={{0,64},{8,72},{16,80},{24,88},{32,96},{40,104},{48,112},{56,120},{... | collective-permute-start | bytes 237608 | tf_op jit(solution)/shard_map/ppermute | solution.py:58
  112.9 1.5 collective-permute-done.14
  114.5 4.7 %collective-permute-start.15 = (f32[19800]{0:T(1024)S(1)}, f32[19800]{0:T(1024)S(1)}, u32[]{:S(2)}, u32[]{:S(2)}) collective-permute-start(f32[19800]{0:T(1024)S(1)} %add.511), channel_id=1, source_target_pairs={{0,128},{8,136},{16,144},{24,152},{32,160},{40,168},{48,176},{56,1... | collective-permute-start | bytes 237608 | tf_op jit(solution)/shard_map/ppermute | solution.py:58
  119.2 3.4 %collective-permute-start.6 = (bf16[96,3,134]{0,2,1:T(8,128)(2,1)S(1)}, bf16[96,3,134]{0,2,1:T(8,128)(2,1)S(1)}, u32[]{:S(2)}, u32[]{:S(2)}) collective-permute-start(bf16[96,3,134]{0,2,1:T(8,128)(2,1)S(1)} %get-tuple-element.106), channel_id=1, source_target_pairs={{0,1},{1,2},{2,3},{3,4},{4,5},{5,6},{6,7},{8,9},{9,10},{10,11},{11... | collective-permute-start | bytes 231560 | tf_op jit(solution)/shard_map/ppermute | solution.py:14
  122.6 6.7 %collective-permute-start.7 = (bf16[96,3,134]{0,2,1:T(8,128)(2,1)S(1)}, bf16[96,3,134]{0,2,1:T(8,128)(2,1)S(1)}, u32[]{:S(2)}, u32[]{:S(2)}) collective-permute-start(bf16[96,3,134]{0,2,1:T(8,128)(2,1)S(1)} %get-tuple-element.107), channel_id=1, source_target_pairs={{1,0},{2,1},{3,2},{4,3},{5,4},{6,5},{7,6},{9,8},{10,9},{11,10},{12... | collective-permute-start | bytes 231560 | tf_op jit(solution)/shard_map/ppermute | solution.py:17
  130.0 1.9 %collective-permute-start.16 = (f32[19800]{0:T(1024)S(1)}, f32[19800]{0:T(1024)S(1)}, u32[]{:S(2)}, u32[]{:S(2)}) collective-permute-start(f32[19800]{0:T(1024)S(1)} %add.512), channel_id=1, source_target_pairs={{0,256},{8,264},{16,272},{24,280},{32,288},{40,296},{48,304},{56,3... | collective-permute-start | bytes 237608 | tf_op jit(solution)/shard_map/ppermute | solution.py:58
  133.0 6.1 %collective-permute-done.16 = f32[19800]{0:T(1024)S(1)} collective-permute-done((f32[19800]{0:T(1024)S(1)}, f32[19800]{0:T(1024)S(1)}, u32[]{:S(2)}, u32[]{:S(2)}) %collective-permute-start.16) | collective-permute-done | bytes 79232 | tf_op jit(solution)/shard_map/ppermute | solution.py:58
  139.2 1.9 %collective-permute-start.17 = (f32[19800]{0:T(1024)S(1)}, f32[19800]{0:T(1024)S(1)}, u32[]{:S(2)}, u32[]{:S(2)}) collective-permute-start(f32[19800]{0:T(1024)S(1)} %add.513), channel_id=1, source_target_pairs={{0,16},{8,24},{16,0},{24,8},{32,48},{40,56},{48,32},{56,40},{64,80... | collective-permute-start | bytes 237608 | tf_op jit(solution)/shard_map/ppermute | solution.py:58
  141.3 3.1 %collective-permute-done.17 = f32[19800]{0:T(1024)S(1)} collective-permute-done((f32[19800]{0:T(1024)S(1)}, f32[19800]{0:T(1024)S(1)}, u32[]{:S(2)}, u32[]{:S(2)}) %collective-permute-start.17) | collective-permute-done | bytes 79232 | tf_op jit(solution)/shard_map/ppermute | solution.py:58
  145.3 6.8 %collective-permute-start.18 = (f32[39600]{0:T(1024)S(1)}, f32[39600]{0:T(1024)S(1)}, u32[]{:S(2)}, u32[]{:S(2)}) collective-permute-start(f32[39600]{0:T(1024)S(1)} %dynamic_update_slice.6), channel_id=1, source_target_pairs={{0,8},{8,0},{16,24},{24,16},{32,40},{40,32},{48,56},{56,48},{64,72... | collective-permute-start | bytes 475208 | tf_op jit(solution)/shard_map/ppermute | solution.py:58
  152.5 4.6 %fusion.144 = bf16[96,8,128]{0,2,1:T(8,128)(2,1)S(1)} fusion(f32[96,11,134]{0,2,1:T(8,128)S(1)} %get-tuple-element.93, f32[96,8,3]{0,2,1:T(4,128)S(1)} %collective-permute-done.5, f32[96,8,128]{0,2,1:T(8,128)S(1)} %bitcast.262, f32[96,8,3]{0,2,1:T(4,128)S(1)} %collective-permute-done.4, f32[96,11,134]{0,2,1:T(8,128)S(1)} %get-tuple-element.92, ...), kind=kLoop, calls=%fused_computation.260 | loop fusion | flops 10420224 | bytes 17338752 | tf_op jit(solution)/shard_map/convert_element_type | solution.py:158
  157.1 0.8 copy.91
  158.0 1.2 dynamic_update_slice.7
  (281 shorter events, 11.9 us)
Async XLA Ops:
  0.6 36.2 %copy-start = (bf16[96,384]{1,0:T(8,128)(2,1)S(1)}, bf16[96,384]{1,0:T(8,128)(2,1)}, u32[]{:S(2)}) copy-start(bf16[96,384]{1,0:T(8,128)(2,1)} %param.16) | copy-start | bytes 221188
  1.8 8.1 %collective-permute-start = (bf16[96,8,3]{0,2,1:T(4,128)(2,1)S(1)}, bf16[96,8,3]{0,2,1:T(4,128)(2,1)S(1)}, u32[]{:S(2)}, u32[]{:S(2)}) collective-permute-start(bf16[96,8,3]{0,2,1:T(4,128)(2,1)S(1)} %get-tuple-element.112), channel_id=1, source_target_pairs={{0,8},{8,16},{16,24},{24,32},{32,40},{40,48},{48,56},{56,64},{64,7... | collective-permute-start | bytes 13832 | tf_op jit(solution)/shard_map/ppermute | solution.py:14
  5.6 5.0 %collective-permute-start.1 = (bf16[96,8,3]{0,2,1:T(4,128)(2,1)S(1)}, bf16[96,8,3]{0,2,1:T(4,128)(2,1)S(1)}, u32[]{:S(2)}, u32[]{:S(2)}) collective-permute-start(bf16[96,8,3]{0,2,1:T(4,128)(2,1)S(1)} %get-tuple-element.113), channel_id=1, source_target_pairs={{8,0},{16,8},{24,16},{32,24},{40,32},{48,40},{56,48},{64,56},{72,6... | collective-permute-start | bytes 13832 | tf_op jit(solution)/shard_map/ppermute | solution.py:17
  8.5 22.4 %copy-start.5 = (f32[96]{0:T(128)}, f32[96]{0:T(128)S(1)}, u32[]{:S(2)}) copy-start(f32[96]{0:T(128)S(1)} %get-tuple-element.114) | copy-start | bytes 1156
  8.5 22.4 %copy-start.7 = (f32[96]{0:T(128)}, f32[96]{0:T(128)S(1)}, u32[]{:S(2)}) copy-start(f32[96]{0:T(128)S(1)} %get-tuple-element.115) | copy-start | bytes 1156
  8.5 22.4 %copy-start.9 = (f32[96]{0:T(128)}, f32[96]{0:T(128)S(1)}, u32[]{:S(2)}) copy-start(f32[96]{0:T(128)S(1)} %get-tuple-element.116) | copy-start | bytes 1156
  8.5 22.4 %copy-start.11 = (f32[96]{0:T(128)}, f32[96]{0:T(128)S(1)}, u32[]{:S(2)}) copy-start(f32[96]{0:T(128)S(1)} %get-tuple-element.117) | copy-start | bytes 1156
  8.6 22.4 %copy-start.13 = (f32[96]{0:T(128)}, f32[96]{0:T(128)S(1)}, u32[]{:S(2)}) copy-start(f32[96]{0:T(128)S(1)} %get-tuple-element.118) | copy-start | bytes 1156
  8.6 22.4 %copy-start.15 = (f32[96]{0:T(128)}, f32[96]{0:T(128)S(1)}, u32[]{:S(2)}) copy-start(f32[96]{0:T(128)S(1)} %get-tuple-element.119) | copy-start | bytes 1156
  8.6 22.4 %copy-start.17 = (f32[96]{0:T(128)}, f32[96]{0:T(128)S(1)}, u32[]{:S(2)}) copy-start(f32[96]{0:T(128)S(1)} %get-tuple-element.120) | copy-start | bytes 1156
  8.6 22.4 %copy-start.19 = (f32[96]{0:T(128)}, f32[96]{0:T(128)S(1)}, u32[]{:S(2)}) copy-start(f32[96]{0:T(128)S(1)} %get-tuple-element.121) | copy-start | bytes 1156
  8.6 22.4 %copy-start.21 = (f32[96]{0:T(128)}, f32[96]{0:T(128)S(1)}, u32[]{:S(2)}) copy-start(f32[96]{0:T(128)S(1)} %get-tuple-element.122) | copy-start | bytes 1156
  8.6 22.4 %copy-start.23 = (f32[96]{0:T(128)}, f32[96]{0:T(128)S(1)}, u32[]{:S(2)}) copy-start(f32[96]{0:T(128)S(1)} %get-tuple-element.123) | copy-start | bytes 1156
  8.6 22.4 %copy-start.25 = (f32[96]{0:T(128)}, f32[96]{0:T(128)S(1)}, u32[]{:S(2)}) copy-start(f32[96]{0:T(128)S(1)} %get-tuple-element.124) | copy-start | bytes 1156
  8.6 22.4 %copy-start.27 = (f32[96]{0:T(128)}, f32[96]{0:T(128)S(1)}, u32[]{:S(2)}) copy-start(f32[96]{0:T(128)S(1)} %get-tuple-element.125) | copy-start | bytes 1156
  8.6 22.4 %copy-start.29 = (f32[96]{0:T(128)}, f32[96]{0:T(128)S(1)}, u32[]{:S(2)}) copy-start(f32[96]{0:T(128)S(1)} %get-tuple-element.126) | copy-start | bytes 1156
  8.6 22.4 %copy-start.31 = (f32[96]{0:T(128)}, f32[96]{0:T(128)S(1)}, u32[]{:S(2)}) copy-start(f32[96]{0:T(128)S(1)} %get-tuple-element.127) | copy-start | bytes 1156
  8.7 22.4 %copy-start.33 = (f32[96]{0:T(128)}, f32[96]{0:T(128)S(1)}, u32[]{:S(2)}) copy-start(f32[96]{0:T(128)S(1)} %get-tuple-element.128) | copy-start | bytes 1156
  8.7 22.4 %copy-start.35 = (f32[96]{0:T(128)}, f32[96]{0:T(128)S(1)}, u32[]{:S(2)}) copy-start(f32[96]{0:T(128)S(1)} %get-tuple-element.129) | copy-start | bytes 1156
  8.7 22.4 %copy-start.37 = (f32[96]{0:T(128)}, f32[96]{0:T(128)S(1)}, u32[]{:S(2)}) copy-start(f32[96]{0:T(128)S(1)} %get-tuple-element.130) | copy-start | bytes 1156
  8.7 22.4 %copy-start.39 = (f32[96]{0:T(128)}, f32[96]{0:T(128)S(1)}, u32[]{:S(2)}) copy-start(f32[96]{0:T(128)S(1)} %get-tuple-element.131) | copy-start | bytes 1156
  8.7 22.4 %copy-start.41 = (f32[96]{0:T(128)}, f32[96]{0:T(128)S(1)}, u32[]{:S(2)}) copy-start(f32[96]{0:T(128)S(1)} %get-tuple-element.132) | copy-start | bytes 1156
  9.7 21.4 %copy-start.43 = (f32[96]{0:T(128)}, f32[96]{0:T(128)S(1)}, u32[]{:S(2)}) copy-start(f32[96]{0:T(128)S(1)} %get-tuple-element.133) | copy-start | bytes 1156
  9.7 21.4 %copy-start.45 = (f32[96]{0:T(128)}, f32[96]{0:T(128)S(1)}, u32[]{:S(2)}) copy-start(f32[96]{0:T(128)S(1)} %get-tuple-element.134) | copy-start | bytes 1156
  9.7 21.4 %copy-start.47 = (f32[96]{0:T(128)}, f32[96]{0:T(128)S(1)}, u32[]{:S(2)}) copy-start(f32[96]{0:T(128)S(1)} %get-tuple-element.135) | copy-start | bytes 1156
  9.7 21.4 %copy-start.49 = (f32[96]{0:T(128)}, f32[96]{0:T(128)S(1)}, u32[]{:S(2)}) copy-start(f32[96]{0:T(128)S(1)} %get-tuple-element.136) | copy-start | bytes 1156
  9.8 21.4 %copy-start.51 = (f32[96]{0:T(128)}, f32[96]{0:T(128)S(1)}, u32[]{:S(2)}) copy-start(f32[96]{0:T(128)S(1)} %get-tuple-element.137) | copy-start | bytes 1156
  9.8 21.4 %copy-start.53 = (f32[96]{0:T(128)}, f32[96]{0:T(128)S(1)}, u32[]{:S(2)}) copy-start(f32[96]{0:T(128)S(1)} %get-tuple-element.138) | copy-start | bytes 1156
  9.8 21.4 %copy-start.55 = (f32[96]{0:T(128)}, f32[96]{0:T(128)S(1)}, u32[]{:S(2)}) copy-start(f32[96]{0:T(128)S(1)} %get-tuple-element.139) | copy-start | bytes 1156
  9.8 21.4 %copy-start.57 = (f32[96]{0:T(128)}, f32[96]{0:T(128)S(1)}, u32[]{:S(2)}) copy-start(f32[96]{0:T(128)S(1)} %get-tuple-element.140) | copy-start | bytes 1156
  9.8 21.4 %copy-start.59 = (f32[96]{0:T(128)}, f32[96]{0:T(128)S(1)}, u32[]{:S(2)}) copy-start(f32[96]{0:T(128)S(1)} %get-tuple-element.141) | copy-start | bytes 1156
  10.7 16.5 %collective-permute-start.2 = (bf16[96,3,134]{0,2,1:T(8,128)(2,1)S(1)}, bf16[96,3,134]{0,2,1:T(8,128)(2,1)S(1)}, u32[]{:S(2)}, u32[]{:S(2)}) collective-permute-start(bf16[96,3,134]{0,2,1:T(8,128)(2,1)S(1)} %get-tuple-element.110), channel_id=1, source_target_pairs={{0,1},{1,2},{2,3},{3,4},{4,5},{5,6},{6,7},{8,9},{9,10},{10,11},{11... | collective-permute-start | bytes 231560 | tf_op jit(solution)/shard_map/ppermute | solution.py:14
  21.3 9.4 %collective-permute-start.3 = (bf16[96,3,134]{0,2,1:T(8,128)(2,1)S(1)}, bf16[96,3,134]{0,2,1:T(8,128)(2,1)S(1)}, u32[]{:S(2)}, u32[]{:S(2)}) collective-permute-start(bf16[96,3,134]{0,2,1:T(8,128)(2,1)S(1)} %get-tuple-element.111), channel_id=1, source_target_pairs={{1,0},{2,1},{3,2},{4,3},{5,4},{6,5},{7,6},{9,8},{10,9},{11,10},{12... | collective-permute-start | bytes 231560 | tf_op jit(solution)/shard_map/ppermute | solution.py:17
  57.1 3.3 %collective-permute-start.8 = (f32[39600]{0:T(1024)S(1)}, f32[39600]{0:T(1024)S(1)}, u32[]{:S(2)}, u32[]{:S(2)}) collective-permute-start(f32[39600]{0:T(1024)S(1)} %dynamic_slice.13), channel_id=1, source_target_pairs={{0,8},{8,0},{16,24},{24,16},{32,40},{40,32},{48,56},{56,48},{64,72... | collective-permute-start | bytes 475208 | tf_op jit(solution)/shard_map/ppermute | solution.py:58
  60.6 7.1 %collective-permute-start.9 = (f32[19800]{0:T(1024)S(1)}, f32[19800]{0:T(1024)S(1)}, u32[]{:S(2)}, u32[]{:S(2)}) collective-permute-start(f32[19800]{0:T(1024)S(1)} %dynamic_slice.15), channel_id=1, source_target_pairs={{0,16},{8,24},{16,0},{24,8},{32,48},{40,56},{48,32},{56,40},{64,80... | collective-permute-start | bytes 237608 | tf_op jit(solution)/shard_map/ppermute | solution.py:58
  67.9 9.1 %collective-permute-start.10 = (f32[19800]{0:T(1024)S(1)}, f32[19800]{0:T(1024)S(1)}, u32[]{:S(2)}, u32[]{:S(2)}) collective-permute-start(f32[19800]{0:T(1024)S(1)} %dynamic-slice_add_fusion.1), channel_id=1, source_target_pairs={{0,1},{1,0},{2,3},{3,2},{4,5},{5,4},{6,7},{7,6},{8,9},{9,8},{10,11... | collective-permute-start | bytes 237608 | tf_op jit(solution)/shard_map/ppermute | solution.py:58
  77.0 6.5 %collective-permute-start.11 = (f32[19800]{0:T(1024)S(1)}, f32[19800]{0:T(1024)S(1)}, u32[]{:S(2)}, u32[]{:S(2)}) collective-permute-start(f32[19800]{0:T(1024)S(1)} %add.507), channel_id=1, source_target_pairs={{0,2},{1,3},{2,0},{3,1},{4,6},{5,7},{6,4},{7,5},{8,10},{9,11},{10,... | collective-permute-start | bytes 237608 | tf_op jit(solution)/shard_map/ppermute | solution.py:58
  83.5 6.7 %collective-permute-start.12 = (f32[19800]{0:T(1024)S(1)}, f32[19800]{0:T(1024)S(1)}, u32[]{:S(2)}, u32[]{:S(2)}) collective-permute-start(f32[19800]{0:T(1024)S(1)} %add.508), channel_id=1, source_target_pairs={{0,4},{1,5},{2,6},{3,7},{4,0},{5,1},{6,2},{7,3},{8,12},{9,13},{10,... | collective-permute-start | bytes 237608 | tf_op jit(solution)/shard_map/ppermute | solution.py:58
  90.2 13.8 %collective-permute-start.13 = (f32[19800]{0:T(1024)S(1)}, f32[19800]{0:T(1024)S(1)}, u32[]{:S(2)}, u32[]{:S(2)}) collective-permute-start(f32[19800]{0:T(1024)S(1)} %add.509), channel_id=1, source_target_pairs={{0,32},{8,40},{16,48},{24,56},{32,0},{40,8},{48,16},{56,24},{64,96... | collective-permute-start | bytes 237608 | tf_op jit(solution)/shard_map/ppermute | solution.py:58
  94.3 18.5 %collective-permute-start.4 = (f32[96,8,3]{0,2,1:T(4,128)S(1)}, f32[96,8,3]{0,2,1:T(4,128)S(1)}, u32[]{:S(2)}, u32[]{:S(2)}) collective-permute-start(f32[96,8,3]{0,2,1:T(4,128)S(1)} %get-tuple-element.94), channel_id=1, source_target_pairs={{0,8},{8,16},{16,24},{24,32},{32,40},{40,48},{48,56},{56,64},{64,7... | collective-permute-start | bytes 27656 | tf_op jit(solution)/shard_map/ppermute | solution.py:14
  102.1 10.8 %collective-permute-start.5 = (f32[96,8,3]{0,2,1:T(4,128)S(1)}, f32[96,8,3]{0,2,1:T(4,128)S(1)}, u32[]{:S(2)}, u32[]{:S(2)}) collective-permute-start(f32[96,8,3]{0,2,1:T(4,128)S(1)} %get-tuple-element.95), channel_id=1, source_target_pairs={{8,0},{16,8},{24,16},{32,24},{40,32},{48,40},{56,48},{64,56},{72,6... | collective-permute-start | bytes 27656 | tf_op jit(solution)/shard_map/ppermute | solution.py:17
  104.0 10.5 %collective-permute-start.14 = (f32[19800]{0:T(1024)S(1)}, f32[19800]{0:T(1024)S(1)}, u32[]{:S(2)}, u32[]{:S(2)}) collective-permute-start(f32[19800]{0:T(1024)S(1)} %add.510), channel_id=1, source_target_pairs={{0,64},{8,72},{16,80},{24,88},{32,96},{40,104},{48,112},{56,120},{... | collective-permute-start | bytes 237608 | tf_op jit(solution)/shard_map/ppermute | solution.py:58
  114.5 15.5 %collective-permute-start.15 = (f32[19800]{0:T(1024)S(1)}, f32[19800]{0:T(1024)S(1)}, u32[]{:S(2)}, u32[]{:S(2)}) collective-permute-start(f32[19800]{0:T(1024)S(1)} %add.511), channel_id=1, source_target_pairs={{0,128},{8,136},{16,144},{24,152},{32,160},{40,168},{48,176},{56,1... | collective-permute-start | bytes 237608 | tf_op jit(solution)/shard_map/ppermute | solution.py:58
  119.2 12.8 %collective-permute-start.6 = (bf16[96,3,134]{0,2,1:T(8,128)(2,1)S(1)}, bf16[96,3,134]{0,2,1:T(8,128)(2,1)S(1)}, u32[]{:S(2)}, u32[]{:S(2)}) collective-permute-start(bf16[96,3,134]{0,2,1:T(8,128)(2,1)S(1)} %get-tuple-element.106), channel_id=1, source_target_pairs={{0,1},{1,2},{2,3},{3,4},{4,5},{5,6},{6,7},{8,9},{9,10},{10,11},{11... | collective-permute-start | bytes 231560 | tf_op jit(solution)/shard_map/ppermute | solution.py:14
  122.6 10.0 %collective-permute-start.7 = (bf16[96,3,134]{0,2,1:T(8,128)(2,1)S(1)}, bf16[96,3,134]{0,2,1:T(8,128)(2,1)S(1)}, u32[]{:S(2)}, u32[]{:S(2)}) collective-permute-start(bf16[96,3,134]{0,2,1:T(8,128)(2,1)S(1)} %get-tuple-element.107), channel_id=1, source_target_pairs={{1,0},{2,1},{3,2},{4,3},{5,4},{6,5},{7,6},{9,8},{10,9},{11,10},{12... | collective-permute-start | bytes 231560 | tf_op jit(solution)/shard_map/ppermute | solution.py:17
  130.0 9.1 %collective-permute-start.16 = (f32[19800]{0:T(1024)S(1)}, f32[19800]{0:T(1024)S(1)}, u32[]{:S(2)}, u32[]{:S(2)}) collective-permute-start(f32[19800]{0:T(1024)S(1)} %add.512), channel_id=1, source_target_pairs={{0,256},{8,264},{16,272},{24,280},{32,288},{40,296},{48,304},{56,3... | collective-permute-start | bytes 237608 | tf_op jit(solution)/shard_map/ppermute | solution.py:58
  139.2 5.2 %collective-permute-start.17 = (f32[19800]{0:T(1024)S(1)}, f32[19800]{0:T(1024)S(1)}, u32[]{:S(2)}, u32[]{:S(2)}) collective-permute-start(f32[19800]{0:T(1024)S(1)} %add.513), channel_id=1, source_target_pairs={{0,16},{8,24},{16,0},{24,8},{32,48},{40,56},{48,32},{56,40},{64,80... | collective-permute-start | bytes 237608 | tf_op jit(solution)/shard_map/ppermute | solution.py:58
  145.3 12.6 %collective-permute-start.18 = (f32[39600]{0:T(1024)S(1)}, f32[39600]{0:T(1024)S(1)}, u32[]{:S(2)}, u32[]{:S(2)}) collective-permute-start(f32[39600]{0:T(1024)S(1)} %dynamic_update_slice.6), channel_id=1, source_target_pairs={{0,8},{8,0},{16,24},{24,16},{32,40},{40,32},{48,56},{56,48},{64,72... | collective-permute-start | bytes 475208 | tf_op jit(solution)/shard_map/ppermute | solution.py:58
  (83 other events, 1076.9 us)

commit v10 on v8

--- a/solution.py
+++ b/solution.py
@@ -58,7 +58,7 @@
     return lax.ppermute(value, axis, [(i, i ^ mask) for i in range(lax.axis_size(axis))])
 
 
-def butterfly_sum(parts, halving=(("col", 1), ("col", 2))):
+def butterfly_sum(parts, halving=(("col", 1), ("col", 16))):
     shapes = [p.shape for p in parts]
     flat = jnp.concatenate([p.reshape(-1) for p in parts])
     total = flat.shape[0]

time: 155 us -> 155 us (level)
  waiting for transfers between devices: 36.5 us -> 34.1 us
  starting transfers between devices: 78.7 us -> 80.7 us
    ppermute x11, starting transfers between devices: 41.2 us -> 43.9 us  [xor_partner(): lax.ppermute(value, axis, [(i, i ^ mask) for i in range(lax.axis_size(axi...]
    ppermute x11, waiting for transfers between devices: 26.6 us -> 24.8 us  [xor_partner(): lax.ppermute(value, axis, [(i, i ^ mask) for i in range(lax.axis_size(axi...]
where the time goes in v10:
time: 155 us; the launch traced here: 154 us
  starting transfers between devices  80.7 us (52%)
  waiting for transfers between devices  34.1 us (22%)
  other arithmetic  17.4 us (11%)
  local copies, waits for them, and re-layouts  14.5 us (9%)
  matrix products  5.05 us (3%)
  between operations  2.41 us (2%)
    ppermute x11, starting transfers between devices, xor_partner(): lax.ppermute(value, axis, [(i, i ^ mask) for i in range(lax.axis_size(axi...  43.9 us
    ppermute x4, starting transfers between devices, padded_2(): lax.ppermute(lax.slice_in_dim(block, block.shape[dim] - width, None, axis...  25.3 us
    ppermute x11, waiting for transfers between devices, xor_partner(): lax.ppermute(value, axis, [(i, i ^ mask) for i in range(lax.axis_size(axi...  24.8 us
    ppermute x4, starting transfers between devices, padded_2(): lax.ppermute(lax.slice_in_dim(block, 0, width, axis=dim), axis, backward)  11.6 us
    ppermute x4, waiting for transfers between devices, padded_2(): lax.ppermute(lax.slice_in_dim(block, 0, width, axis=dim), axis, backward)  9.33 us
    unnamed x166, local copies, waits for them, and re-layouts  5.8 us
    dot_general x6, matrix products, product(): return jnp.einsum(form, left, right, preferred_element_type=jnp.float32)  5.05 us
    reduce_sum x4, other arithmetic, kernel_terms(): jnp.sum(conv_grad * padded[:, row_step:row_step + height, col_step:col_st...  4.87 us
  transfers between devices with their start and end apart: 19, of which 11 were waited for; matrix products, arithmetic and copies ran while one was open for 7% of the time, Pallas kernels for 0%

profile of v10, /device:TPU:5, one launch (start us, length us, event | category | flops | bytes accessed | tf_op | source)
XLA Modules:
  0.0 154.1 jit_solution(2364224155842901442)
XLA Ops:
  0.7 1.2 copy.24
  1.8 3.8 %collective-permute-start = (bf16[96,8,3]{0,2,1:T(4,128)(2,1)S(1)}, bf16[96,8,3]{0,2,1:T(4,128)(2,1)S(1)}, u32[]{:S(2)}, u32[]{:S(2)}) collective-permute-start(bf16[96,8,3]{0,2,1:T(4,128)(2,1)S(1)} %get-tuple-element.112), channel_id=1, source_target_pairs={{0,8},{8,16},{16,24},{24,32},{32,40},{40,48},{48,56},{56,64},{64,7... | collective-permute-start | bytes 13832 | tf_op jit(solution)/shard_map/ppermute | solution.py:14
  5.6 1.9 %collective-permute-start.1 = (bf16[96,8,3]{0,2,1:T(4,128)(2,1)S(1)}, bf16[96,8,3]{0,2,1:T(4,128)(2,1)S(1)}, u32[]{:S(2)}, u32[]{:S(2)}) collective-permute-start(bf16[96,8,3]{0,2,1:T(4,128)(2,1)S(1)} %get-tuple-element.113), channel_id=1, source_target_pairs={{8,0},{16,8},{24,16},{32,24},{40,32},{48,40},{56,48},{64,56},{72,6... | collective-permute-start | bytes 13832 | tf_op jit(solution)/shard_map/ppermute | solution.py:17
  7.5 1.0 slice_bitcast_fusion.48
  8.5 1.0 slice_bitcast_fusion.47
  9.6 0.9 collective-permute-done.1
  10.7 10.6 %collective-permute-start.2 = (bf16[96,3,134]{0,2,1:T(8,128)(2,1)S(1)}, bf16[96,3,134]{0,2,1:T(8,128)(2,1)S(1)}, u32[]{:S(2)}, u32[]{:S(2)}) collective-permute-start(bf16[96,3,134]{0,2,1:T(8,128)(2,1)S(1)} %get-tuple-element.110), channel_id=1, source_target_pairs={{0,1},{1,2},{2,3},{3,4},{4,5},{5,6},{6,7},{8,9},{9,10},{10,11},{11... | collective-permute-start | bytes 231560 | tf_op jit(solution)/shard_map/ppermute | solution.py:14
  21.3 1.9 %collective-permute-start.3 = (bf16[96,3,134]{0,2,1:T(8,128)(2,1)S(1)}, bf16[96,3,134]{0,2,1:T(8,128)(2,1)S(1)}, u32[]{:S(2)}, u32[]{:S(2)}) collective-permute-start(bf16[96,3,134]{0,2,1:T(8,128)(2,1)S(1)} %get-tuple-element.111), channel_id=1, source_target_pairs={{1,0},{2,1},{3,2},{4,3},{5,4},{6,5},{7,6},{9,8},{10,9},{11,10},{12... | collective-permute-start | bytes 231560 | tf_op jit(solution)/shard_map/ppermute | solution.py:17
  23.2 0.9 slice_bitcast_fusion.46
  24.3 1.1 copy.32
  25.5 0.9 copy.95
  26.4 6.6 %collective-permute-done.3 = bf16[96,3,134]{0,2,1:T(8,128)(2,1)S(1)} collective-permute-done((bf16[96,3,134]{0,2,1:T(8,128)(2,1)S(1)}, bf16[96,3,134]{0,2,1:T(8,128)(2,1)S(1)}, u32[]{:S(2)}, u32[]{:S(2)}) %collective-permute-start.3) | collective-permute-done | bytes 77216 | tf_op jit(solution)/shard_map/ppermute | solution.py:17
  33.4 4.3 %fusion.180 = (f32[8,128]{1,0:T(8,128)S(1)}, f32[96,8,128]{0,2,1:T(8,128)S(1)}) fusion(f32[96]{0:T(128)S(1)} %copy-done.77, bf16[96,11,134]{0,2,1:T(8,128)(2,1)S(1)} %get-tuple-element.109, f32[96]{0:T(128)S(1)} %get-tuple-element.161, f32[96]{0:T(128)S(1)} %get-tuple-element.162, f32[96]{0:T(128)S(1)} %get-tuple-element.115, f32[96]{0:T(128)S(1)} %get-tuple-element.116, ...), kind=kLoop, calls=%fused_computation.429 | loop fusion | flops 16317440 | bytes 8879872 | tf_op jit(solution)/shard_map/reduce_sum | solution.py:100
  38.3 0.8 fusion.10
  39.2 2.0 %convert_reduce_fusion = (f32[384]{0:T(512)}, bf16[384,1024]{0,1:T(8,128)(2,1)S(1)}) fusion(f32[1024,384]{1,0:T(8,128)S(1)} %get-tuple-element.166, bf16[384,96]{0,1:T(8,128)(2,1)S(1)} %copy-done.4, f32[96,1024]{1,0:T(8,128)S(1)} %copy.97, f32[96]{0:T(128)S(1)} %copy-done.48), kind=kOutput, calls=%fused_computation.16 | convolution fusion | flops 84344448 | bytes 2828160 | tf_op jit(solution)/shard_map/hc,cp->hp/dot_general | solution.py:96
  41.5 1.0 fusion.168
  42.5 1.5 fusion.179
  44.0 1.2 copy.98
  45.2 1.1 fusion.123
  46.3 1.9 %fusion.141 = (f32[96]{0:T(128)}, f32[96]{0:T(128)}, f32[96]{0:T(128)}, f32[96]{0:T(128)}, f32[96]{0:T(128)}, /*index=5*/f32[96]{0:T(128)}, f32[96]{0:T(128)}, f...) fusion(bf16[96,11,134]{0,2,1:T(8,128)(2,1)S(1)} %get-tuple-elem, ...), kind=kLoop, calls=%fused_computation.256 | loop fusion | flops 5306688 | bytes 3939072 | tf_op jit(solution)/shard_map/reduce_sum | solution.py:48
  48.4 1.3 fusion.91
  52.3 1.6 %concatenate.149 = f32[79200]{0:T(1024)S(1)} concatenate(f32[4704]{0:T(1024)S(1)} %reshape_reshape.3, f32[96]{0:T(128)S(1)} %copy-done.52, f32[96]{0:T(128)S(1)} %copy-done.51, f32[96]{0:T(128)S(1)} %reduce_sum.577, f32[36864]{0:T(1024)S(1)} %reshape.104, f32[384]{0:T(512)S(1)} %copy-done.50, f32[36864]{0:T(1024)S(1)} %reshape.105, f32[96]{0:T(128)S(1)} %get-tuple-element.98), dimensions={0} | concatenate | bytes 633600 | tf_op jit(solution)/shard_map/concatenate | solution.py:63
  54.0 2.4 %collective-permute-start.8 = (f32[39600]{0:T(1024)S(1)}, f32[39600]{0:T(1024)S(1)}, u32[]{:S(2)}, u32[]{:S(2)}) collective-permute-start(f32[39600]{0:T(1024)S(1)} %dynamic_slice.13), channel_id=1, source_target_pairs={{0,8},{8,0},{16,24},{24,16},{32,40},{40,32},{48,56},{56,48},{64,72... | collective-permute-start | bytes 475208 | tf_op jit(solution)/shard_map/ppermute | solution.py:58
  56.4 1.0 collective-permute-done.8
  57.6 3.9 %collective-permute-start.9 = (f32[19800]{0:T(1024)S(1)}, f32[19800]{0:T(1024)S(1)}, u32[]{:S(2)}, u32[]{:S(2)}) collective-permute-start(f32[19800]{0:T(1024)S(1)} %dynamic_slice.15), channel_id=1, source_target_pairs={{0,128},{8,136},{16,144},{24,152},{32,160},{40,168},{48,176},{56,1... | collective-permute-start | bytes 237608 | tf_op jit(solution)/shard_map/ppermute | solution.py:58
  61.5 2.5 %collective-permute-done.9 = f32[19800]{0:T(1024)S(1)} collective-permute-done((f32[19800]{0:T(1024)S(1)}, f32[19800]{0:T(1024)S(1)}, u32[]{:S(2)}, u32[]{:S(2)}) %collective-permute-start.9) | collective-permute-done | bytes 79232 | tf_op jit(solution)/shard_map/ppermute | solution.py:58
  64.1 6.2 %collective-permute-start.10 = (f32[19800]{0:T(1024)S(1)}, f32[19800]{0:T(1024)S(1)}, u32[]{:S(2)}, u32[]{:S(2)}) collective-permute-start(f32[19800]{0:T(1024)S(1)} %dynamic-slice_add_fusion.1), channel_id=1, source_target_pairs={{0,1},{1,0},{2,3},{3,2},{4,5},{5,4},{6,7},{7,6},{8,9},{9,8},{10,11... | collective-permute-start | bytes 237608 | tf_op jit(solution)/shard_map/ppermute | solution.py:58
  70.4 2.9 %collective-permute-done.10 = f32[19800]{0:T(1024)S(1)} collective-permute-done((f32[19800]{0:T(1024)S(1)}, f32[19800]{0:T(1024)S(1)}, u32[]{:S(2)}, u32[]{:S(2)}) %collective-permute-start.10) | collective-permute-done | bytes 79232 | tf_op jit(solution)/shard_map/ppermute | solution.py:58
  73.3 4.7 %collective-permute-start.11 = (f32[19800]{0:T(1024)S(1)}, f32[19800]{0:T(1024)S(1)}, u32[]{:S(2)}, u32[]{:S(2)}) collective-permute-start(f32[19800]{0:T(1024)S(1)} %add.505), channel_id=1, source_target_pairs={{0,2},{1,3},{2,0},{3,1},{4,6},{5,7},{6,4},{7,5},{8,10},{9,11},{10,... | collective-permute-start | bytes 237608 | tf_op jit(solution)/shard_map/ppermute | solution.py:58
  78.0 1.8 %collective-permute-done.11 = f32[19800]{0:T(1024)S(1)} collective-permute-done((f32[19800]{0:T(1024)S(1)}, f32[19800]{0:T(1024)S(1)}, u32[]{:S(2)}, u32[]{:S(2)}) %collective-permute-start.11) | collective-permute-done | bytes 79232 | tf_op jit(solution)/shard_map/ppermute | solution.py:58
  79.8 1.9 %collective-permute-start.12 = (f32[19800]{0:T(1024)S(1)}, f32[19800]{0:T(1024)S(1)}, u32[]{:S(2)}, u32[]{:S(2)}) collective-permute-start(f32[19800]{0:T(1024)S(1)} %add.506), channel_id=1, source_target_pairs={{0,4},{1,5},{2,6},{3,7},{4,0},{5,1},{6,2},{7,3},{8,12},{9,13},{10,... | collective-permute-start | bytes 237608 | tf_op jit(solution)/shard_map/ppermute | solution.py:58
  81.7 4.8 %collective-permute-done.12 = f32[19800]{0:T(1024)S(1)} collective-permute-done((f32[19800]{0:T(1024)S(1)}, f32[19800]{0:T(1024)S(1)}, u32[]{:S(2)}, u32[]{:S(2)}) %collective-permute-start.12) | collective-permute-done | bytes 79232 | tf_op jit(solution)/shard_map/ppermute | solution.py:58
  86.5 2.2 %collective-permute-start.13 = (f32[19800]{0:T(1024)S(1)}, f32[19800]{0:T(1024)S(1)}, u32[]{:S(2)}, u32[]{:S(2)}) collective-permute-start(f32[19800]{0:T(1024)S(1)} %add.507), channel_id=1, source_target_pairs={{0,16},{8,24},{16,0},{24,8},{32,48},{40,56},{48,32},{56,40},{64,80... | collective-permute-start | bytes 237608 | tf_op jit(solution)/shard_map/ppermute | solution.py:58
  88.7 6.6 %collective-permute-start.4 = (f32[96,8,3]{0,2,1:T(4,128)S(1)}, f32[96,8,3]{0,2,1:T(4,128)S(1)}, u32[]{:S(2)}, u32[]{:S(2)}) collective-permute-start(f32[96,8,3]{0,2,1:T(4,128)S(1)} %get-tuple-element.94), channel_id=1, source_target_pairs={{0,8},{8,16},{16,24},{24,32},{32,40},{40,48},{48,56},{56,64},{64,7... | collective-permute-start | bytes 27656 | tf_op jit(solution)/shard_map/ppermute | solution.py:14
  95.3 1.9 %collective-permute-start.5 = (f32[96,8,3]{0,2,1:T(4,128)S(1)}, f32[96,8,3]{0,2,1:T(4,128)S(1)}, u32[]{:S(2)}, u32[]{:S(2)}) collective-permute-start(f32[96,8,3]{0,2,1:T(4,128)S(1)} %get-tuple-element.95), channel_id=1, source_target_pairs={{8,0},{16,8},{24,16},{32,24},{40,32},{48,40},{56,48},{64,56},{72,6... | collective-permute-start | bytes 27656 | tf_op jit(solution)/shard_map/ppermute | solution.py:17
  97.3 5.1 %collective-permute-start.14 = (f32[19800]{0:T(1024)S(1)}, f32[19800]{0:T(1024)S(1)}, u32[]{:S(2)}, u32[]{:S(2)}) collective-permute-start(f32[19800]{0:T(1024)S(1)} %add.508), channel_id=1, source_target_pairs={{0,32},{8,40},{16,48},{24,56},{32,0},{40,8},{48,16},{56,24},{64,96... | collective-permute-start | bytes 237608 | tf_op jit(solution)/shard_map/ppermute | solution.py:58
  102.5 1.6 %collective-permute-done.14 = f32[19800]{0:T(1024)S(1)} collective-permute-done((f32[19800]{0:T(1024)S(1)}, f32[19800]{0:T(1024)S(1)}, u32[]{:S(2)}, u32[]{:S(2)}) %collective-permute-start.14) | collective-permute-done | bytes 79232 | tf_op jit(solution)/shard_map/ppermute | solution.py:58
  104.2 8.8 %collective-permute-start.15 = (f32[19800]{0:T(1024)S(1)}, f32[19800]{0:T(1024)S(1)}, u32[]{:S(2)}, u32[]{:S(2)}) collective-permute-start(f32[19800]{0:T(1024)S(1)} %add.509), channel_id=1, source_target_pairs={{0,64},{8,72},{16,80},{24,88},{32,96},{40,104},{48,112},{56,120},{... | collective-permute-start | bytes 237608 | tf_op jit(solution)/shard_map/ppermute | solution.py:58
  113.0 4.3 %collective-permute-start.6 = (bf16[96,3,134]{0,2,1:T(8,128)(2,1)S(1)}, bf16[96,3,134]{0,2,1:T(8,128)(2,1)S(1)}, u32[]{:S(2)}, u32[]{:S(2)}) collective-permute-start(bf16[96,3,134]{0,2,1:T(8,128)(2,1)S(1)} %get-tuple-element.106), channel_id=1, source_target_pairs={{0,1},{1,2},{2,3},{3,4},{4,5},{5,6},{6,7},{8,9},{9,10},{10,11},{11... | collective-permute-start | bytes 231560 | tf_op jit(solution)/shard_map/ppermute | solution.py:14
  117.3 5.8 %collective-permute-start.7 = (bf16[96,3,134]{0,2,1:T(8,128)(2,1)S(1)}, bf16[96,3,134]{0,2,1:T(8,128)(2,1)S(1)}, u32[]{:S(2)}, u32[]{:S(2)}) collective-permute-start(bf16[96,3,134]{0,2,1:T(8,128)(2,1)S(1)} %get-tuple-element.107), channel_id=1, source_target_pairs={{1,0},{2,1},{3,2},{4,3},{5,4},{6,5},{7,6},{9,8},{10,9},{11,10},{12... | collective-permute-start | bytes 231560 | tf_op jit(solution)/shard_map/ppermute | solution.py:17
  123.9 2.5 %collective-permute-start.16 = (f32[19800]{0:T(1024)S(1)}, f32[19800]{0:T(1024)S(1)}, u32[]{:S(2)}, u32[]{:S(2)}) collective-permute-start(f32[19800]{0:T(1024)S(1)} %add.510), channel_id=1, source_target_pairs={{0,256},{8,264},{16,272},{24,280},{32,288},{40,296},{48,304},{56,3... | collective-permute-start | bytes 237608 | tf_op jit(solution)/shard_map/ppermute | solution.py:58
  126.4 1.8 %collective-permute-done.7 = bf16[96,3,134]{0,2,1:T(8,128)(2,1)S(1)} collective-permute-done((bf16[96,3,134]{0,2,1:T(8,128)(2,1)S(1)}, bf16[96,3,134]{0,2,1:T(8,128)(2,1)S(1)}, u32[]{:S(2)}, u32[]{:S(2)}) %collective-permute-start.7) | collective-permute-done | bytes 77216 | tf_op jit(solution)/shard_map/ppermute | solution.py:17
  128.5 7.1 %collective-permute-done.16 = f32[19800]{0:T(1024)S(1)} collective-permute-done((f32[19800]{0:T(1024)S(1)}, f32[19800]{0:T(1024)S(1)}, u32[]{:S(2)}, u32[]{:S(2)}) %collective-permute-start.16) | collective-permute-done | bytes 79232 | tf_op jit(solution)/shard_map/ppermute | solution.py:58
  135.6 1.9 %collective-permute-start.17 = (f32[19800]{0:T(1024)S(1)}, f32[19800]{0:T(1024)S(1)}, u32[]{:S(2)}, u32[]{:S(2)}) collective-permute-start(f32[19800]{0:T(1024)S(1)} %add.511), channel_id=1, source_target_pairs={{0,128},{8,136},{16,144},{24,152},{32,160},{40,168},{48,176},{56,1... | collective-permute-start | bytes 237608 | tf_op jit(solution)/shard_map/ppermute | solution.py:58
  137.7 3.1 %collective-permute-done.17 = f32[19800]{0:T(1024)S(1)} collective-permute-done((f32[19800]{0:T(1024)S(1)}, f32[19800]{0:T(1024)S(1)}, u32[]{:S(2)}, u32[]{:S(2)}) %collective-permute-start.17) | collective-permute-done | bytes 79232 | tf_op jit(solution)/shard_map/ppermute | solution.py:58
  140.9 4.2 %collective-permute-start.18 = (f32[39600]{0:T(1024)S(1)}, f32[39600]{0:T(1024)S(1)}, u32[]{:S(2)}, u32[]{:S(2)}) collective-permute-start(f32[39600]{0:T(1024)S(1)} %maximum_select_fusion.1), channel_id=1, source_target_pairs={{0,8},{8,0},{16,24},{24,16},{32,40},{40,32},{48,56},{56,48},{64,72... | collective-permute-start | bytes 475208 | tf_op jit(solution)/shard_map/ppermute | solution.py:58
  145.3 4.0 %fusion.144 = bf16[96,8,128]{0,2,1:T(8,128)(2,1)S(1)} fusion(f32[96,11,134]{0,2,1:T(8,128)S(1)} %get-tuple-element.93, f32[96,8,3]{0,2,1:T(4,128)S(1)} %collective-permute-done.5, f32[96,8,128]{0,2,1:T(8,128)S(1)} %bitcast.262, f32[96,8,3]{0,2,1:T(4,128)S(1)} %collective-permute-done.4, f32[96,11,134]{0,2,1:T(8,128)S(1)} %get-tuple-element.92, ...), kind=kLoop, calls=%fused_computation.260 | loop fusion | flops 10420224 | bytes 17338752 | tf_op jit(solution)/shard_map/convert_element_type | solution.py:158
  149.3 0.8 copy.91
  (215 shorter events, 9.4 us)
Async XLA Ops:
  0.6 37.6 %copy-start = (bf16[96,384]{1,0:T(8,128)(2,1)S(1)}, bf16[96,384]{1,0:T(8,128)(2,1)}, u32[]{:S(2)}) copy-start(bf16[96,384]{1,0:T(8,128)(2,1)} %param.16) | copy-start | bytes 221188
  1.8 7.8 %collective-permute-start = (bf16[96,8,3]{0,2,1:T(4,128)(2,1)S(1)}, bf16[96,8,3]{0,2,1:T(4,128)(2,1)S(1)}, u32[]{:S(2)}, u32[]{:S(2)}) collective-permute-start(bf16[96,8,3]{0,2,1:T(4,128)(2,1)S(1)} %get-tuple-element.112), channel_id=1, source_target_pairs={{0,8},{8,16},{16,24},{24,32},{32,40},{40,48},{48,56},{56,64},{64,7... | collective-permute-start | bytes 13832 | tf_op jit(solution)/shard_map/ppermute | solution.py:14
  5.6 5.0 %collective-permute-start.1 = (bf16[96,8,3]{0,2,1:T(4,128)(2,1)S(1)}, bf16[96,8,3]{0,2,1:T(4,128)(2,1)S(1)}, u32[]{:S(2)}, u32[]{:S(2)}) collective-permute-start(bf16[96,8,3]{0,2,1:T(4,128)(2,1)S(1)} %get-tuple-element.113), channel_id=1, source_target_pairs={{8,0},{16,8},{24,16},{32,24},{40,32},{48,40},{56,48},{64,56},{72,6... | collective-permute-start | bytes 13832 | tf_op jit(solution)/shard_map/ppermute | solution.py:17
  9.5 23.6 %copy-start.6 = (f32[96]{0:T(128)}, f32[96]{0:T(128)S(1)}, u32[]{:S(2)}) copy-start(f32[96]{0:T(128)S(1)} %get-tuple-element.142) | copy-start | bytes 1156
  9.5 23.6 %copy-start.8 = (f32[96]{0:T(128)}, f32[96]{0:T(128)S(1)}, u32[]{:S(2)}) copy-start(f32[96]{0:T(128)S(1)} %get-tuple-element.143) | copy-start | bytes 1156
  9.6 23.6 %copy-start.10 = (f32[96]{0:T(128)}, f32[96]{0:T(128)S(1)}, u32[]{:S(2)}) copy-start(f32[96]{0:T(128)S(1)} %get-tuple-element.144) | copy-start | bytes 1156
  9.6 23.6 %copy-start.12 = (f32[96]{0:T(128)}, f32[96]{0:T(128)S(1)}, u32[]{:S(2)}) copy-start(f32[96]{0:T(128)S(1)} %get-tuple-element.145) | copy-start | bytes 1156
  9.6 23.6 %copy-start.14 = (f32[96]{0:T(128)}, f32[96]{0:T(128)S(1)}, u32[]{:S(2)}) copy-start(f32[96]{0:T(128)S(1)} %get-tuple-element.146) | copy-start | bytes 1156
  9.6 23.6 %copy-start.16 = (f32[96]{0:T(128)}, f32[96]{0:T(128)S(1)}, u32[]{:S(2)}) copy-start(f32[96]{0:T(128)S(1)} %get-tuple-element.147) | copy-start | bytes 1156
  9.6 23.6 %copy-start.18 = (f32[96]{0:T(128)}, f32[96]{0:T(128)S(1)}, u32[]{:S(2)}) copy-start(f32[96]{0:T(128)S(1)} %get-tuple-element.148) | copy-start | bytes 1156
  9.6 23.6 %copy-start.20 = (f32[96]{0:T(128)}, f32[96]{0:T(128)S(1)}, u32[]{:S(2)}) copy-start(f32[96]{0:T(128)S(1)} %get-tuple-element.149) | copy-start | bytes 1156
  9.6 23.6 %copy-start.22 = (f32[96]{0:T(128)}, f32[96]{0:T(128)S(1)}, u32[]{:S(2)}) copy-start(f32[96]{0:T(128)S(1)} %get-tuple-element.150) | copy-start | bytes 1156
  9.6 23.6 %copy-start.24 = (f32[96]{0:T(128)}, f32[96]{0:T(128)S(1)}, u32[]{:S(2)}) copy-start(f32[96]{0:T(128)S(1)} %get-tuple-element.151) | copy-start | bytes 1156
  10.7 15.8 %collective-permute-start.2 = (bf16[96,3,134]{0,2,1:T(8,128)(2,1)S(1)}, bf16[96,3,134]{0,2,1:T(8,128)(2,1)S(1)}, u32[]{:S(2)}, u32[]{:S(2)}) collective-permute-start(bf16[96,3,134]{0,2,1:T(8,128)(2,1)S(1)} %get-tuple-element.110), channel_id=1, source_target_pairs={{0,1},{1,2},{2,3},{3,4},{4,5},{5,6},{6,7},{8,9},{9,10},{10,11},{11... | collective-permute-start | bytes 231560 | tf_op jit(solution)/shard_map/ppermute | solution.py:14
  21.3 11.7 %collective-permute-start.3 = (bf16[96,3,134]{0,2,1:T(8,128)(2,1)S(1)}, bf16[96,3,134]{0,2,1:T(8,128)(2,1)S(1)}, u32[]{:S(2)}, u32[]{:S(2)}) collective-permute-start(bf16[96,3,134]{0,2,1:T(8,128)(2,1)S(1)} %get-tuple-element.111), channel_id=1, source_target_pairs={{1,0},{2,1},{3,2},{4,3},{5,4},{6,5},{7,6},{9,8},{10,9},{11,10},{12... | collective-permute-start | bytes 231560 | tf_op jit(solution)/shard_map/ppermute | solution.py:17
  54.0 3.4 %collective-permute-start.8 = (f32[39600]{0:T(1024)S(1)}, f32[39600]{0:T(1024)S(1)}, u32[]{:S(2)}, u32[]{:S(2)}) collective-permute-start(f32[39600]{0:T(1024)S(1)} %dynamic_slice.13), channel_id=1, source_target_pairs={{0,8},{8,0},{16,24},{24,16},{32,40},{40,32},{48,56},{56,48},{64,72... | collective-permute-start | bytes 475208 | tf_op jit(solution)/shard_map/ppermute | solution.py:58
  57.6 6.4 %collective-permute-start.9 = (f32[19800]{0:T(1024)S(1)}, f32[19800]{0:T(1024)S(1)}, u32[]{:S(2)}, u32[]{:S(2)}) collective-permute-start(f32[19800]{0:T(1024)S(1)} %dynamic_slice.15), channel_id=1, source_target_pairs={{0,128},{8,136},{16,144},{24,152},{32,160},{40,168},{48,176},{56,1... | collective-permute-start | bytes 237608 | tf_op jit(solution)/shard_map/ppermute | solution.py:58
  64.1 9.1 %collective-permute-start.10 = (f32[19800]{0:T(1024)S(1)}, f32[19800]{0:T(1024)S(1)}, u32[]{:S(2)}, u32[]{:S(2)}) collective-permute-start(f32[19800]{0:T(1024)S(1)} %dynamic-slice_add_fusion.1), channel_id=1, source_target_pairs={{0,1},{1,0},{2,3},{3,2},{4,5},{5,4},{6,7},{7,6},{8,9},{9,8},{10,11... | collective-permute-start | bytes 237608 | tf_op jit(solution)/shard_map/ppermute | solution.py:58
  73.3 6.5 %collective-permute-start.11 = (f32[19800]{0:T(1024)S(1)}, f32[19800]{0:T(1024)S(1)}, u32[]{:S(2)}, u32[]{:S(2)}) collective-permute-start(f32[19800]{0:T(1024)S(1)} %add.505), channel_id=1, source_target_pairs={{0,2},{1,3},{2,0},{3,1},{4,6},{5,7},{6,4},{7,5},{8,10},{9,11},{10,... | collective-permute-start | bytes 237608 | tf_op jit(solution)/shard_map/ppermute | solution.py:58
  79.8 6.7 %collective-permute-start.12 = (f32[19800]{0:T(1024)S(1)}, f32[19800]{0:T(1024)S(1)}, u32[]{:S(2)}, u32[]{:S(2)}) collective-permute-start(f32[19800]{0:T(1024)S(1)} %add.506), channel_id=1, source_target_pairs={{0,4},{1,5},{2,6},{3,7},{4,0},{5,1},{6,2},{7,3},{8,12},{9,13},{10,... | collective-permute-start | bytes 237608 | tf_op jit(solution)/shard_map/ppermute | solution.py:58
  86.5 10.8 %collective-permute-start.13 = (f32[19800]{0:T(1024)S(1)}, f32[19800]{0:T(1024)S(1)}, u32[]{:S(2)}, u32[]{:S(2)}) collective-permute-start(f32[19800]{0:T(1024)S(1)} %add.507), channel_id=1, source_target_pairs={{0,16},{8,24},{16,0},{24,8},{32,48},{40,56},{48,32},{56,40},{64,80... | collective-permute-start | bytes 237608 | tf_op jit(solution)/shard_map/ppermute | solution.py:58
  88.7 13.7 %collective-permute-start.4 = (f32[96,8,3]{0,2,1:T(4,128)S(1)}, f32[96,8,3]{0,2,1:T(4,128)S(1)}, u32[]{:S(2)}, u32[]{:S(2)}) collective-permute-start(f32[96,8,3]{0,2,1:T(4,128)S(1)} %get-tuple-element.94), channel_id=1, source_target_pairs={{0,8},{8,16},{16,24},{24,32},{32,40},{40,48},{48,56},{56,64},{64,7... | collective-permute-start | bytes 27656 | tf_op jit(solution)/shard_map/ppermute | solution.py:14
  95.3 7.1 %collective-permute-start.5 = (f32[96,8,3]{0,2,1:T(4,128)S(1)}, f32[96,8,3]{0,2,1:T(4,128)S(1)}, u32[]{:S(2)}, u32[]{:S(2)}) collective-permute-start(f32[96,8,3]{0,2,1:T(4,128)S(1)} %get-tuple-element.95), channel_id=1, source_target_pairs={{8,0},{16,8},{24,16},{32,24},{40,32},{48,40},{56,48},{64,56},{72,6... | collective-permute-start | bytes 27656 | tf_op jit(solution)/shard_map/ppermute | solution.py:17
  97.3 6.9 %collective-permute-start.14 = (f32[19800]{0:T(1024)S(1)}, f32[19800]{0:T(1024)S(1)}, u32[]{:S(2)}, u32[]{:S(2)}) collective-permute-start(f32[19800]{0:T(1024)S(1)} %add.508), channel_id=1, source_target_pairs={{0,32},{8,40},{16,48},{24,56},{32,0},{40,8},{48,16},{56,24},{64,96... | collective-permute-start | bytes 237608 | tf_op jit(solution)/shard_map/ppermute | solution.py:58
  104.2 19.7 %collective-permute-start.15 = (f32[19800]{0:T(1024)S(1)}, f32[19800]{0:T(1024)S(1)}, u32[]{:S(2)}, u32[]{:S(2)}) collective-permute-start(f32[19800]{0:T(1024)S(1)} %add.509), channel_id=1, source_target_pairs={{0,64},{8,72},{16,80},{24,88},{32,96},{40,104},{48,112},{56,120},{... | collective-permute-start | bytes 237608 | tf_op jit(solution)/shard_map/ppermute | solution.py:58
  113.0 13.3 %collective-permute-start.6 = (bf16[96,3,134]{0,2,1:T(8,128)(2,1)S(1)}, bf16[96,3,134]{0,2,1:T(8,128)(2,1)S(1)}, u32[]{:S(2)}, u32[]{:S(2)}) collective-permute-start(bf16[96,3,134]{0,2,1:T(8,128)(2,1)S(1)} %get-tuple-element.106), channel_id=1, source_target_pairs={{0,1},{1,2},{2,3},{3,4},{4,5},{5,6},{6,7},{8,9},{9,10},{10,11},{11... | collective-permute-start | bytes 231560 | tf_op jit(solution)/shard_map/ppermute | solution.py:14
  117.3 10.9 %collective-permute-start.7 = (bf16[96,3,134]{0,2,1:T(8,128)(2,1)S(1)}, bf16[96,3,134]{0,2,1:T(8,128)(2,1)S(1)}, u32[]{:S(2)}, u32[]{:S(2)}) collective-permute-start(bf16[96,3,134]{0,2,1:T(8,128)(2,1)S(1)} %get-tuple-element.107), channel_id=1, source_target_pairs={{1,0},{2,1},{3,2},{4,3},{5,4},{6,5},{7,6},{9,8},{10,9},{11,10},{12... | collective-permute-start | bytes 231560 | tf_op jit(solution)/shard_map/ppermute | solution.py:17
  123.9 11.7 %collective-permute-start.16 = (f32[19800]{0:T(1024)S(1)}, f32[19800]{0:T(1024)S(1)}, u32[]{:S(2)}, u32[]{:S(2)}) collective-permute-start(f32[19800]{0:T(1024)S(1)} %add.510), channel_id=1, source_target_pairs={{0,256},{8,264},{16,272},{24,280},{32,288},{40,296},{48,304},{56,3... | collective-permute-start | bytes 237608 | tf_op jit(solution)/shard_map/ppermute | solution.py:58
  128.3 16.9 %copy-start.2 = (bf16[96,8,128]{0,2,1:T(8,128)(2,1)S(1)}, bf16[96,8,128]{0,2,1:T(8,128)(2,1)}, u32[]{:S(2)}) copy-start(bf16[96,8,128]{0,2,1:T(8,128)(2,1)} %copy-done.1) | copy-start | bytes 589828
  128.3 16.9 %copy-start.7 = (f32[96]{0:T(128)S(1)}, f32[96]{0:T(128)}, u32[]{:S(2)}) copy-start(f32[96]{0:T(128)} %copy-done.6) | copy-start | bytes 1156
  128.3 16.9 %copy-start.9 = (f32[96]{0:T(128)S(1)}, f32[96]{0:T(128)}, u32[]{:S(2)}) copy-start(f32[96]{0:T(128)} %copy-done.8) | copy-start | bytes 1156
  128.3 16.9 %copy-start.11 = (f32[96]{0:T(128)S(1)}, f32[96]{0:T(128)}, u32[]{:S(2)}) copy-start(f32[96]{0:T(128)} %copy-done.10) | copy-start | bytes 1156
  128.3 16.8 %copy-start.13 = (f32[96]{0:T(128)S(1)}, f32[96]{0:T(128)}, u32[]{:S(2)}) copy-start(f32[96]{0:T(128)} %copy-done.12) | copy-start | bytes 1156
  128.3 16.8 %copy-start.15 = (f32[96]{0:T(128)S(1)}, f32[96]{0:T(128)}, u32[]{:S(2)}) copy-start(f32[96]{0:T(128)} %copy-done.14) | copy-start | bytes 1156
  128.3 16.8 %copy-start.17 = (f32[96]{0:T(128)S(1)}, f32[96]{0:T(128)}, u32[]{:S(2)}) copy-start(f32[96]{0:T(128)} %copy-done.16) | copy-start | bytes 1156
  128.3 16.8 %copy-start.19 = (f32[96]{0:T(128)S(1)}, f32[96]{0:T(128)}, u32[]{:S(2)}) copy-start(f32[96]{0:T(128)} %copy-done.18) | copy-start | bytes 1156
  128.3 16.8 %copy-start.21 = (f32[96]{0:T(128)S(1)}, f32[96]{0:T(128)}, u32[]{:S(2)}) copy-start(f32[96]{0:T(128)} %copy-done.20) | copy-start | bytes 1156
  128.4 16.8 %copy-start.23 = (f32[96]{0:T(128)S(1)}, f32[96]{0:T(128)}, u32[]{:S(2)}) copy-start(f32[96]{0:T(128)} %copy-done.22) | copy-start | bytes 1156
  128.4 16.8 %copy-start.25 = (f32[96]{0:T(128)S(1)}, f32[96]{0:T(128)}, u32[]{:S(2)}) copy-start(f32[96]{0:T(128)} %copy-done.24) | copy-start | bytes 1156
  128.4 16.8 %copy-start.27 = (f32[96]{0:T(128)S(1)}, f32[96]{0:T(128)}, u32[]{:S(2)}) copy-start(f32[96]{0:T(128)} %copy-done.26) | copy-start | bytes 1156
  128.4 16.8 %copy-start.29 = (f32[96]{0:T(128)S(1)}, f32[96]{0:T(128)}, u32[]{:S(2)}) copy-start(f32[96]{0:T(128)} %copy-done.28) | copy-start | bytes 1156
  128.4 16.8 %copy-start.31 = (f32[96]{0:T(128)S(1)}, f32[96]{0:T(128)}, u32[]{:S(2)}) copy-start(f32[96]{0:T(128)} %copy-done.30) | copy-start | bytes 1156
  128.4 16.8 %copy-start.33 = (f32[96]{0:T(128)S(1)}, f32[96]{0:T(128)}, u32[]{:S(2)}) copy-start(f32[96]{0:T(128)} %copy-done.32) | copy-start | bytes 1156
  128.4 16.8 %copy-start.35 = (f32[96]{0:T(128)S(1)}, f32[96]{0:T(128)}, u32[]{:S(2)}) copy-start(f32[96]{0:T(128)} %copy-done.34) | copy-start | bytes 1156
  128.4 16.8 %copy-start.37 = (f32[96]{0:T(128)S(1)}, f32[96]{0:T(128)}, u32[]{:S(2)}) copy-start(f32[96]{0:T(128)} %copy-done.36) | copy-start | bytes 1156
  128.4 16.8 %copy-start.39 = (f32[96]{0:T(128)S(1)}, f32[96]{0:T(128)}, u32[]{:S(2)}) copy-start(f32[96]{0:T(128)} %copy-done.38) | copy-start | bytes 1156
  135.6 5.2 %collective-permute-start.17 = (f32[19800]{0:T(1024)S(1)}, f32[19800]{0:T(1024)S(1)}, u32[]{:S(2)}, u32[]{:S(2)}) collective-permute-start(f32[19800]{0:T(1024)S(1)} %add.511), channel_id=1, source_target_pairs={{0,128},{8,136},{16,144},{24,152},{32,160},{40,168},{48,176},{56,1... | collective-permute-start | bytes 237608 | tf_op jit(solution)/shard_map/ppermute | solution.py:58
  140.9 9.2 %collective-permute-start.18 = (f32[39600]{0:T(1024)S(1)}, f32[39600]{0:T(1024)S(1)}, u32[]{:S(2)}, u32[]{:S(2)}) collective-permute-start(f32[39600]{0:T(1024)S(1)} %maximum_select_fusion.1), channel_id=1, source_target_pairs={{0,8},{8,0},{16,24},{24,16},{32,40},{40,32},{48,56},{56,48},{64,72... | collective-permute-start | bytes 475208 | tf_op jit(solution)/shard_map/ppermute | solution.py:58
  (51 other events, 260.0 us)
